TPU v7x, 256 devices: a whole 4x4x8 slice. The times are simulated.
256 devices in a mesh: group: 8 (over y, core), expert: 32 (over z, x).
Axes of the slice: x: 4, y: 4, z: 8, core: 2. Of those that a mesh axis runs over, the one named last changes fastest.
Arguments:
- context: bfloat16 [32768, 1024], P(('group', 'expert')), may hold values from -6 to 6
- residual: bfloat16 [32768, 2048], P(('group', 'expert')), may hold values from -0.8984375 to 0.8984375
- attn_out_w: bfloat16 [1024, 2048], P('group'), may hold values from -0.02734375 to 0.02734375
- norm_gain: float32 [2048], replicated, may hold values from 0.25 to 1.75
- router_w: bfloat16 [2048, 32], replicated, may hold values from -0.047851562 to 0.047851562
- shared_in: bfloat16 [2048, 2816], P('group'), may hold values from -0.125 to 0.125
- shared_out: bfloat16 [1408, 2048], P(None, 'group'), may hold values from -0.0234375 to 0.0234375
- expert_in: bfloat16 [32, 2048, 1536], P('expert'), may hold values from -0.125 to 0.125
- expert_out_w: bfloat16 [32, 768, 2048], P('expert'), may hold values from -0.21875 to 0.21875
- routes: int32 [32768, 6], P(('group', 'expert')), may hold values from 0 to 31, all different within a row; in each aligned block of 128 rows (0 to 127, 128 to 255, ...) at most 32 rows name the same one
Outputs:
- layer_out: bfloat16 [32768, 2048], P(('group', 'expert'))
Inputs may be any that keep to these rules, and one draw needn't show every extreme that they name: `routes`: the 6 experts of a token differ. Among the rows of one device, no expert is named by more than 32 rows, a bound that some block reaches.
All inputs are finite; a program needn't handle non-finite values.
Results may differ from a plain program's by a relative error of at most 0.022.
Values may be sent and summed in bfloat16 or wider, within the bound.
No kernel may reach another device: no remote copies, remote signals or barrier semaphores. Data moves between devices by JAX's collectives and lax.ppermute only.
A program may use at most 128 MiB of HBM per device.

v0:
```python
import jax
import jax.numpy as jnp
from jax import lax
from jax.sharding import PartitionSpec as P


def swiglu_rows(rows, w_in, w_out):
    width = w_out.shape[0]
    mid = jnp.dot(rows, w_in, preferred_element_type=jnp.float32)
    act = (jax.nn.silu(mid[:, :width]) * mid[:, width:]).astype(jnp.bfloat16)
    return jnp.dot(act, w_out, preferred_element_type=jnp.float32)


def per_device(
    context,
    residual,
    attn_out_w,
    norm_gain,
    router_w,
    shared_in,
    shared_out,
    expert_in,
    expert_out_w,
    routes,
):
    tok_rows = residual.shape[0]
    width = residual.shape[1]
    picks = routes.shape[1]
    experts = lax.axis_size("expert")
    capacity = 4 * tok_rows * picks // (3 * experts)
    columns = context
    attn = jnp.dot(
        columns,
        lax.all_gather(attn_out_w, "group", axis=0, tiled=True),
        preferred_element_type=jnp.float32,
    )
    hidden_state = (residual.astype(jnp.float32) + attn).astype(jnp.bfloat16)
    hidden_f = hidden_state.astype(jnp.float32)
    scale = lax.rsqrt(jnp.mean(hidden_f * hidden_f, axis=-1, keepdims=True) + 1e-06)
    normed = (hidden_f * scale * norm_gain).astype(jnp.bfloat16)
    logits = jnp.dot(normed, router_w, preferred_element_type=jnp.float32)
    chosen = routes[:, :, None] == jnp.arange(experts, dtype=jnp.int32)[None, None, :]
    picked = jnp.sum(jnp.where(chosen, logits[:, None, :], 0.0), axis=-1)
    sig = jax.nn.sigmoid(picked)
    gates = sig / jnp.sum(sig, axis=1, keepdims=True)
    flat_e = routes.reshape(-1)
    onehot = (flat_e[:, None] == jnp.arange(experts, dtype=jnp.int32)[None, :]).astype(jnp.int32)
    rank = jnp.cumsum(onehot, axis=0) - onehot
    position = jnp.sum(rank * onehot, axis=1)
    slot_of = flat_e * capacity + position
    token_of = jnp.arange(tok_rows * picks, dtype=jnp.int32) // picks
    source = jnp.zeros((experts * capacity,), jnp.int32).at[slot_of].set(token_of)
    filled = jnp.zeros((experts * capacity,), jnp.int32).at[slot_of].set(1)
    outgoing = jnp.where(filled[:, None] > 0, normed[source], jnp.zeros((), jnp.bfloat16))
    outgoing = outgoing.reshape(experts, capacity, width)
    local_in = expert_in[0]
    local_out = expert_out_w[0]
    arrived = lax.all_to_all(outgoing, "expert", split_axis=0, concat_axis=0, tiled=True)
    flat_rows = arrived.reshape(-1, width)
    returned = lax.all_to_all(
        swiglu_rows(flat_rows, local_in, local_out).astype(jnp.bfloat16).reshape(arrived.shape),
        "expert",
        split_axis=0,
        concat_axis=0,
        tiled=True,
    )
    gathered = returned.reshape(experts * capacity, width)[slot_of]
    weighted = gates.reshape(-1, 1) * gathered.astype(jnp.float32)
    routed = jnp.sum(weighted.reshape(tok_rows, picks, width), axis=1)
    shared_hidden = shared_out.shape[0]
    columns = normed
    shared_mid = jnp.dot(
        columns,
        lax.all_gather(shared_in, "group", axis=0, tiled=True),
        preferred_element_type=jnp.float32,
    )
    shared_act = (
        jax.nn.silu(shared_mid[:, :shared_hidden]) * shared_mid[:, shared_hidden:]
    ).astype(jnp.bfloat16)
    shared_y = jnp.dot(
        shared_act,
        lax.all_gather(shared_out, "group", axis=1, tiled=True),
        preferred_element_type=jnp.float32,
    )
    return (hidden_f + shared_y + routed).astype(jnp.bfloat16)


def solution(mesh):
    placed = (
        P(("group", "expert"), None),
        P(("group", "expert"), None),
        P("group", None),
        P(),
        P(),
        P("group", None),
        P(None, "group"),
        P("expert", None, None),
        P("expert", None, None),
        P(("group", "expert"), None),
    )
    return jax.shard_map(
        per_device,
        mesh=mesh,
        in_specs=placed,
        out_specs=P(("group", "expert"), None),
        check_vma=False,
    )
```

profile of v0, /device:TPU:32, one launch (start us, length us, event | category | flops | bytes accessed | tf_op | source)
XLA Modules:
  0.0 321.9 jit_solution(1857204493511975896)
XLA Ops:
  6.5 0.0 copy-start
  6.5 0.0 all-gather.4.cloned.1.call-start
  6.5 0.7 all-gather.4.cloned.1.call-update
  7.3 0.0 copy-start.6
  7.3 0.0 all-gather.6.cloned.1.call-start
  7.3 0.7 all-gather.6.cloned.1.call-update
  8.0 0.8 copy.21
  8.8 0.1 eq.45
  9.0 0.1 eq.41
  9.1 1.7 reduce-window.6
  10.9 0.3 slice_reduce_fusion
  11.1 0.7 broadcast_multiply_fusion
  11.8 0.1 copy.20
  12.0 0.1 mul.71
  12.1 0.1 fusion.15
  12.2 3.4 %scatter_custom_fusion.1 = s32[1024]{0:T(1024)S(1)} fusion(s32[768]{0:T(1024)S(1)} %fusion.21, s32[768]{0:T(1024)S(1)} %add_select_fusion, s32[]{:T(128)} %constant.16.clone.1), kind=kCustom, calls=%fused_computation.51 | custom fusion | bytes 4100 | tf_op jit(solution)/shard_map/scatter | solution.py:52
  15.6 3.4 %scatter_custom_fusion = s32[1024]{0:T(1024)S(1)} fusion(s32[768]{0:T(1024)S(1)} %fusion.21, s32[768]{0:T(1024)S(1)} %broadcast.97, s32[]{:T(128)} %constant.16.clone.1), kind=kCustom, calls=%fused_computation.54 | custom fusion | bytes 4100 | tf_op jit(solution)/shard_map/scatter | solution.py:53
  19.0 0.1 broadcast_in_dim.46
  19.1 27.4 %all-gather.4.cloned.1.call-done = bf16[1024,2048]{1,0:T(8,128)(2,1)} async-done(((bf16[128,2048]{1,0:T(8,128)(2,1)}), bf16[1024,2048]{1,0:T(8,128)(2,1)}) %all-gather.4.cloned.1.call-update) | async-done | bytes 4194320 | tf_op jit(solution)/shard_map/all_gather | solution.py:34
  46.6 3.2 multiply_reduce_fusion.1
  49.8 0.0 copy-start.3
  49.8 0.9 copy-done.3
  50.7 0.0 copy-done.6
  50.7 1.0 multiply_convert_fusion
  51.7 9.9 %gather_fusion = bf16[1024,2048]{1,0:T(8,128)(2,1)} fusion(bf16[128,2048]{1,0:T(8,128)(2,1)} %multiply_convert_fusion, s32[1024]{0:T(1024)S(1)} %fusion.19), kind=kCustom, calls=%fused_computation | custom fusion | bytes 8392704 | tf_op jit(solution)/shard_map/gather | solution.py:54
  61.6 5.2 %broadcast_select_fusion = bf16[32,32,2048]{2,1,0:T(8,128)(2,1)} fusion(bf16[32,32,2048]{2,1,0:T(8,128)(2,1)} %bitcast.38, pred[32,32]{1,0:T(8,128)(4,1)S(1)} %broadcast_in_dim.46), kind=kLoop, calls=%fused_computation.7 | loop fusion | flops 2097152 | bytes 8389632 | tf_op jit(solution)/shard_map/jit(_where)/select_n | solution.py:54
  66.8 10.1 %all-to-all-start = ((bf16[32,32,2048]{2,1,0:T(8,128)(2,1)}), bf16[32,32,2048]{2,1,0:T(8,128)(2,1)}, u32[]{:S(2)}, u32[]{:S(2)}) async-start(bf16[32,32,2048]{2,1,0:T(8,128)(2,1)} %broadcast_select_fusion), calls=%async_computation | async-start | bytes 8388608 | tf_op jit(solution)/shard_map/all_to_all | solution.py:58
  76.9 0.0 all-gather.8.cloned.1.call-start
  77.0 0.7 all-gather.8.cloned.1.call-update
  77.7 94.4 %all-to-all-done = bf16[32,32,2048]{2,1,0:T(8,128)(2,1)} async-done(((bf16[32,32,2048]{2,1,0:T(8,128)(2,1)}), bf16[32,32,2048]{2,1,0:T(8,128)(2,1)}, u32[]{:S(2)}, u32[]{:S(2)}) %all-to-all-start) | async-done | bytes 4194336 | tf_op jit(solution)/shard_map/all_to_all | solution.py:58
  172.1 10.0 %fusion = f32[1024,1536]{1,0:T(8,128)S(1)} fusion(bf16[1024,2048]{1,0:T(8,128)(2,1)} %bitcast.2, bf16[1,2048,1536]{2,1,0:T(8,128)(2,1)} %param.17), kind=kOutput, calls=%fused_computation.5 | convolution fusion | flops 6442450944 | bytes 16777216 | tf_op jit(solution)/shard_map/dot_general | solution.py:9
  182.1 0.0 copy-done
  182.1 5.1 %convolution_convert_fusion = bf16[1024,2048]{1,0:T(8,128)(2,1)} fusion(bf16[1,768,2048]{2,1,0:T(8,128)(2,1)S(1)} %copy-done, f32[1024,1536]{1,0:T(8,128)S(1)} %fusion), kind=kOutput, calls=%fused_computation.8 | convolution fusion | flops 3228041216 | bytes 13631488 | tf_op jit(solution)/shard_map/dot_general | solution.py:11
  187.2 0.0 copy-start.2
  187.2 7.3 %all-to-all-start.1 = ((bf16[32,32,2048]{2,1,0:T(8,128)(2,1)}), bf16[32,32,2048]{2,1,0:T(8,128)(2,1)}, u32[]{:S(2)}, u32[]{:S(2)}) async-start(bf16[32,32,2048]{2,1,0:T(8,128)(2,1)} %bitcast.39), calls=%async_computation.1 | async-start | bytes 8388608 | tf_op jit(solution)/shard_map/all_to_all | solution.py:60
  194.5 0.0 copy-done.2
  194.5 0.0 copy-done.4
  194.5 0.3 fusion.29
  194.8 0.0 copy-done.5
  194.9 0.1 copy.19
  195.0 0.0 all-gather.6.cloned.1.call-done
  195.1 7.1 %fusion.28 = f32[128,2816]{1,0:T(8,128)} fusion(bf16[128,2048]{1,0:T(8,128)(2,1)S(1)} %copy-done.2, bf16[2048,2816]{1,0:T(8,128)(2,1)} %all-gather.6.cloned.1.call-done), kind=kOutput, calls=%fused_computation.59 | convolution fusion | flops 1476395008 | bytes 13500416 | tf_op jit(solution)/shard_map/dot_general | solution.py:72
  202.2 87.2 %all-to-all-done.1 = bf16[32,32,2048]{2,1,0:T(8,128)(2,1)} async-done(((bf16[32,32,2048]{2,1,0:T(8,128)(2,1)}), bf16[32,32,2048]{2,1,0:T(8,128)(2,1)}, u32[]{:S(2)}, u32[]{:S(2)}) %all-to-all-start.1) | async-done | bytes 4194336 | tf_op jit(solution)/shard_map/all_to_all | solution.py:60
  289.4 9.1 %gather_fusion.1 = bf16[768,2048]{1,0:T(8,128)(2,1)S(1)} fusion(bf16[1024,2048]{1,0:T(8,128)(2,1)} %bitcast.6, s32[1024]{0:T(1024)S(1)} %pad_clamp_fusion), kind=kCustom, calls=%fused_computation.1 | custom fusion | bytes 6294528 | tf_op jit(solution)/shard_map/gather | solution.py:67
  298.4 3.7 %reshape.103 = f32[128,6,2048]{2,1,0:T(8,128)} reshape(bf16[768,2048]{1,0:T(8,128)(2,1)S(1)} %gather_fusion.1) | data formatting | bytes 9437184 | tf_op jit(solution)/shard_map/convert_element_type | solution.py:68
  302.2 7.8 %multiply_reduce_fusion = f32[128,2048]{1,0:T(8,128)} fusion(f32[128,6,2048]{2,1,0:T(8,128)} %reshape.103, f32[128,6]{1,0:T(8,128)S(1)} %copy.19), kind=kLoop, calls=%fused_computation.4 | loop fusion | flops 2883584 | bytes 7343104 | tf_op jit(solution)/shard_map/reduce_sum | solution.py:69
  309.9 5.5 %fusion.5 = bf16[128,2048]{1,0:T(8,128)(2,1)} fusion(f32[128,2048]{1,0:T(8,128)} %multiply_reduce_fusion, f32[128,2048]{1,0:T(8,128)} %copy-done.3, bf16[1408,2048]{1,0:T(8,128)(2,1)} %all-gather.8.cloned.1.call-done, f32[128,2816]{1,0:T(8,128)} %fusion.28), kind=kOutput, calls=%fused_computation.15 | convolution fusion | flops 740065280 | bytes 9830400 | tf_op jit(solution)/shard_map/dot_general | solution.py:80
  315.4 0.0 copy-done.1
  (16 shorter events, 0.2 us)
Async XLA Ops:
  6.5 175.6 %copy-start = (bf16[1,768,2048]{2,1,0:T(8,128)(2,1)S(1)}, bf16[1,768,2048]{2,1,0:T(8,128)(2,1)}, u32[]{:S(2)}) copy-start(bf16[1,768,2048]{2,1,0:T(8,128)(2,1)} %param.18) | copy-start | bytes 9437188
  6.5 40.0 %all-gather.4.cloned.1.call-start = ((), (), s32[]{:S(2)}) async-start(), calls=%async_computation.2 | async-start | bytes 4718592 | tf_op jit(solution)/shard_map/all_gather | solution.py:34
  7.3 43.5 %copy-start.6 = (f32[2048]{0:T(1024)S(1)}, f32[2048]{0:T(1024)}, u32[]{:S(2)}) copy-start(f32[2048]{0:T(1024)} %param.13) | copy-start | bytes 24580
  7.3 187.8 %all-gather.6.cloned.1.call-start = ((), (), s32[]{:S(2)}) async-start(), calls=%async_computation.3 | async-start | bytes 12976128 | tf_op jit(solution)/shard_map/all_gather | solution.py:74
  49.8 1.0 copy-start.3
  66.8 105.3 %all-to-all-start = ((bf16[32,32,2048]{2,1,0:T(8,128)(2,1)}), bf16[32,32,2048]{2,1,0:T(8,128)(2,1)}, u32[]{:S(2)}, u32[]{:S(2)}) async-start(bf16[32,32,2048]{2,1,0:T(8,128)(2,1)} %broadcast_select_fusion), calls=%async_computation | async-start | bytes 8388608 | tf_op jit(solution)/shard_map/all_to_all | solution.py:58
  76.9 233.0 %all-gather.8.cloned.1.call-start = ((), (), s32[]{:S(2)}) async-start(), calls=%async_computation.4 | async-start | bytes 6488064 | tf_op jit(solution)/shard_map/all_gather | solution.py:82
  187.2 7.3 %copy-start.2 = (bf16[128,2048]{1,0:T(8,128)(2,1)S(1)}, bf16[128,2048]{1,0:T(8,128)(2,1)}, u32[]{:S(2)}) copy-start(bf16[128,2048]{1,0:T(8,128)(2,1)} %multiply_convert_fusion) | copy-start | bytes 1572868
  187.2 7.3 %copy-start.4 = (bf16[2048,32]{0,1:T(8,128)(2,1)S(1)}, bf16[2048,32]{0,1:T(8,128)(2,1)}, u32[]{:S(2)}) copy-start(bf16[2048,32]{0,1:T(8,128)(2,1)} %param.14) | copy-start | bytes 393220
  187.2 7.6 %copy-start.5 = (s32[128,6]{0,1:T(8,128)S(1)}, s32[128,6]{0,1:T(8,128)}, u32[]{:S(2)}) copy-start(s32[128,6]{0,1:T(8,128)} %param.19) | copy-start | bytes 9220
  187.2 102.2 %all-to-all-start.1 = ((bf16[32,32,2048]{2,1,0:T(8,128)(2,1)}), bf16[32,32,2048]{2,1,0:T(8,128)(2,1)}, u32[]{:S(2)}, u32[]{:S(2)}) async-start(bf16[32,32,2048]{2,1,0:T(8,128)(2,1)} %bitcast.39), calls=%async_computation.1 | async-start | bytes 8388608 | tf_op jit(solution)/shard_map/all_to_all | solution.py:60
  302.2 13.3 %copy-start.1 = (bf16[1,768,2048]{2,1,0:T(8,128)(2,1)S(1)}, bf16[1,768,2048]{2,1,0:T(8,128)(2,1)}, u32[]{:S(2)}) copy-start(bf16[1,768,2048]{2,1,0:T(8,128)(2,1)} %param.18) | copy-start | bytes 9437188
Sparse Core Ops, SparseCore 0:
  9.2 37.2 all-gather.3
  48.4 65.4 all-gather.5
  115.7 45.6 all-gather.7
where the time goes:
time: 324 us; the launch traced here: 322 us
  waiting for transfers between devices  211 us (65%)
  local copies, waits for them, and re-layouts  32.2 us (10%)
  matrix products  31.2 us (10%)
  starting transfers between devices  17.5 us (5%)
  other arithmetic  16.6 us (5%)
  between operations  13.3 us (4%)
    all_to_all x1, waiting for transfers between devices, per_device(): lax.all_to_all(outgoing, 'expert', split_axis=0, concat_axis=0, tiled=True)  94.4 us
    all_to_all x1, waiting for transfers between devices, per_device(): lax.all_to_all(swiglu_rows(flat_rows, local_in, local_out).astype(jnp.bfl...  87.2 us
    all_gather x1, waiting for transfers between devices, per_device(): lax.all_gather(attn_out_w, 'group', axis=0, tiled=True)  27.4 us
    all_to_all x1, starting transfers between devices, per_device(): lax.all_to_all(outgoing, 'expert', split_axis=0, concat_axis=0, tiled=True)  10.1 us
    dot_general x1, matrix products, swiglu_rows(): mid = jnp.dot(rows, w_in, preferred_element_type=jnp.float32)  10 us
    gather x1, local copies, waits for them, and re-layouts, per_device(): normed[source]  9.94 us
    gather x1, local copies, waits for them, and re-layouts, per_device(): gathered = returned.reshape(experts * capacity, width)[slot_of]  9.06 us
    reduce_sum x1, other arithmetic, per_device(): routed = jnp.sum(weighted.reshape(tok_rows, picks, width), axis=1)  7.77 us
  transfers between devices with their start and end apart: 5, of which 3 were waited for; matrix products, arithmetic and copies ran while one was open for 23% of the time, Pallas kernels for 0%

commit v1 on v0

--- a/solution.py
+++ b/solution.py
@@ -28,9 +28,9 @@
     picks = routes.shape[1]
     experts = lax.axis_size("expert")
     capacity = 4 * tok_rows * picks // (3 * experts)
-    columns = context
+    slots = experts * capacity
     attn = jnp.dot(
-        columns,
+        context,
         lax.all_gather(attn_out_w, "group", axis=0, tiled=True),
         preferred_element_type=jnp.float32,
     )
@@ -47,12 +47,14 @@
     onehot = (flat_e[:, None] == jnp.arange(experts, dtype=jnp.int32)[None, :]).astype(jnp.int32)
     rank = jnp.cumsum(onehot, axis=0) - onehot
     position = jnp.sum(rank * onehot, axis=1)
-    slot_of = flat_e * capacity + position
-    token_of = jnp.arange(tok_rows * picks, dtype=jnp.int32) // picks
-    source = jnp.zeros((experts * capacity,), jnp.int32).at[slot_of].set(token_of)
-    filled = jnp.zeros((experts * capacity,), jnp.int32).at[slot_of].set(1)
-    outgoing = jnp.where(filled[:, None] > 0, normed[source], jnp.zeros((), jnp.bfloat16))
-    outgoing = outgoing.reshape(experts, capacity, width)
+    slot_of = (flat_e * capacity + position).reshape(tok_rows, picks)
+    hit = slot_of[:, :, None] == jnp.arange(slots, dtype=jnp.int32)[None, None, :]
+    dispatch = jnp.any(hit, axis=1).astype(jnp.bfloat16)
+    outgoing = jnp.dot(dispatch.T, normed, preferred_element_type=jnp.float32)
+    outgoing = outgoing.astype(jnp.bfloat16).reshape(experts, capacity, width)
+    combine = jnp.sum(jnp.where(hit, gates[:, :, None], 0.0), axis=1)
+    combine_hi = combine.astype(jnp.bfloat16)
+    combine_lo = (combine - combine_hi.astype(jnp.float32)).astype(jnp.bfloat16)
     local_in = expert_in[0]
     local_out = expert_out_w[0]
     arrived = lax.all_to_all(outgoing, "expert", split_axis=0, concat_axis=0, tiled=True)
@@ -64,13 +66,12 @@
         concat_axis=0,
         tiled=True,
     )
-    gathered = returned.reshape(experts * capacity, width)[slot_of]
-    weighted = gates.reshape(-1, 1) * gathered.astype(jnp.float32)
-    routed = jnp.sum(weighted.reshape(tok_rows, picks, width), axis=1)
+    returned = returned.reshape(slots, width)
+    routed = jnp.dot(combine_hi, returned, preferred_element_type=jnp.float32)
+    routed = routed + jnp.dot(combine_lo, returned, preferred_element_type=jnp.float32)
     shared_hidden = shared_out.shape[0]
-    columns = normed
     shared_mid = jnp.dot(
-        columns,
+        normed,
         lax.all_gather(shared_in, "group", axis=0, tiled=True),
         preferred_element_type=jnp.float32,
     )

time: 324 us -> 293 us (0.904)
  local copies, waits for them, and re-layouts: 32.2 us -> 3.27 us
  other arithmetic: 16.6 us -> 4.53 us
  matrix products: 31.2 us -> 42.6 us
    gather x2 -> x0, local copies, waits for them, and re-layouts: 19 us -> none  [the longest x1 9.94 us: per_device(): normed[source]]
    dot_general x2 -> x5, matrix products: 10.3 us -> 20.8 us  [the longest x1 7.27 us: per_device(): jnp.dot(normed, lax.all_gather(shared_in, 'group', axis=0, tiled=True), p...]
    all_to_all x1, waiting for transfers between devices: 87.2 us -> 79.5 us  [per_device(): lax.all_to_all(swiglu_rows(flat_rows, local_in, local_out).astype(jnp.bfl...]
    scatter x2 -> x0, local copies, waits for them, and re-layouts: 6.76 us -> none  [the longest x1 3.38 us: per_device(): jnp.zeros((experts * capacity,), jnp.int32).at[slot_of].set(token_of)]
    reduce_sum x1, other arithmetic: 7.77 us -> 1.22 us  [per_device(): combine = jnp.sum(jnp.where(hit, gates[:, :, None], 0.0), axis=1)]
    all_gather x1, waiting for transfers between devices: 27.4 us -> 33.9 us  [per_device(): lax.all_gather(attn_out_w, 'group', axis=0, tiled=True)]
    select_n x3 -> x0, other arithmetic: 5.22 us -> none  [the longest x1 5.19 us: per_device(): jnp.where(filled[:, None] > 0, normed[source], jnp.zeros((), jnp.bfloat16))]
    convert_element_type x1 -> x0, local copies, waits for them, and re-layouts: 3.72 us -> none  [per_device(): weighted = gates.reshape(-1, 1) * gathered.astype(jnp.float32)]
  transfers between devices with their start and end apart: 5 -> 5, of which waited for: 3 -> 3; matrix products, arithmetic and copies ran while one was open for 23% -> 14% of each run, Pallas kernels for 0% -> 0%
where the time goes in v1:
time: 293 us; the launch traced here: 291 us
  waiting for transfers between devices  210 us (72%)
  matrix products  42.6 us (15%)
  starting transfers between devices  17.6 us (6%)
  between operations  13.3 us (5%)
  other arithmetic  4.53 us (2%)
  local copies, waits for them, and re-layouts  3.27 us (1%)
    all_to_all x1, waiting for transfers between devices, per_device(): lax.all_to_all(outgoing, 'expert', split_axis=0, concat_axis=0, tiled=True)  94.4 us
    all_to_all x1, waiting for transfers between devices, per_device(): lax.all_to_all(swiglu_rows(flat_rows, local_in, local_out).astype(jnp.bfl...  79.5 us
    all_gather x1, waiting for transfers between devices, per_device(): lax.all_gather(attn_out_w, 'group', axis=0, tiled=True)  33.9 us
    all_to_all x1, starting transfers between devices, per_device(): lax.all_to_all(outgoing, 'expert', split_axis=0, concat_axis=0, tiled=True)  10.1 us
    dot_general x1, matrix products, swiglu_rows(): mid = jnp.dot(rows, w_in, preferred_element_type=jnp.float32)  10 us
    all_to_all x1, starting transfers between devices, per_device(): lax.all_to_all(swiglu_rows(flat_rows, local_in, local_out).astype(jnp.bfl...  7.38 us
    dot_general x1, matrix products, per_device(): jnp.dot(normed, lax.all_gather(shared_in, 'group', axis=0, tiled=True), p...  7.27 us
  transfers between devices with their start and end apart: 5, of which 3 were waited for; matrix products, arithmetic and copies ran while one was open for 14% of the time, Pallas kernels for 0%

profile of v1, /device:TPU:32, one launch (start us, length us, event | category | flops | bytes accessed | tf_op | source)
XLA Modules:
  0.0 291.1 jit_solution(9251911207652139209)
XLA Ops:
  6.5 0.0 copy-start
  6.5 0.0 all-gather.4.cloned.1.call-start
  6.5 0.7 all-gather.4.cloned.1.call-update
  7.3 0.0 copy-start.7
  7.3 0.0 all-gather.6.cloned.1.call-start
  7.3 0.7 all-gather.6.cloned.1.call-update
  8.0 0.8 copy.27
  8.8 0.1 eq.55
  9.0 0.1 eq.51
  9.1 1.7 reduce-window.6
  10.9 0.3 slice_reduce_fusion
  11.1 0.1 fusion.19
  11.3 0.1 reduce_sum.49
  11.4 0.1 copy.30
  11.5 0.7 multiply_add_fusion
  12.2 0.5 fusion.4
  12.7 33.9 %all-gather.4.cloned.1.call-done = bf16[1024,2048]{1,0:T(8,128)(2,1)} async-done(((bf16[128,2048]{1,0:T(8,128)(2,1)}), bf16[1024,2048]{1,0:T(8,128)(2,1)}) %all-gather.4.cloned.1.call-update) | async-done | bytes 4194320 | tf_op jit(solution)/shard_map/all_gather | solution.py:34
  46.6 3.2 %multiply_reduce_fusion = (f32[128]{0:T(128)S(1)}, f32[128,2048]{1,0:T(8,128)S(1)}) fusion(bf16[128,1024]{1,0:T(8,128)(2,1)} %param.10, bf16[1024,2048]{1,0:T(8,128)(2,1)} %all-gather.4.cloned.1.call-done, bf16[128,2048]{1,0:T(8,128)(2,1)} %param.11), kind=kOutput, calls=%fused_computation.19 | convolution fusion | flops 538443648 | bytes 6029824 | tf_op jit(solution)/shard_map/dot_general | solution.py:32
  49.8 0.0 copy-start.3
  49.8 0.9 copy-done.3
  50.7 0.0 copy-done.7
  50.7 0.2 multiply_convert_fusion
  50.9 0.0 copy-start.1
  50.9 0.8 copy-done.1
  51.7 3.3 %convolution_convert_fusion.1 = bf16[1024,2048]{1,0:T(8,128)(2,1)} fusion(pred[128,1024]{1,0:T(8,128)(4,1)S(1)} %fusion.4, bf16[128,2048]{1,0:T(8,128)(2,1)S(1)} %multiply_convert_fusion), kind=kOutput, calls=%fused_computation.3 | convolution fusion | flops 538968064 | bytes 4849664 | tf_op jit(solution)/shard_map/dot_general | solution.py:53
  55.0 10.1 %all-to-all-start = ((bf16[32,32,2048]{2,1,0:T(8,128)(2,1)}), bf16[32,32,2048]{2,1,0:T(8,128)(2,1)}, u32[]{:S(2)}, u32[]{:S(2)}) async-start(bf16[32,32,2048]{2,1,0:T(8,128)(2,1)} %bitcast.42), calls=%async_computation | async-start | bytes 8388608 | tf_op jit(solution)/shard_map/all_to_all | solution.py:60
  65.1 0.0 all-gather.8.cloned.1.call-start
  65.2 0.7 all-gather.8.cloned.1.call-update
  65.9 94.4 %all-to-all-done = bf16[32,32,2048]{2,1,0:T(8,128)(2,1)} async-done(((bf16[32,32,2048]{2,1,0:T(8,128)(2,1)}), bf16[32,32,2048]{2,1,0:T(8,128)(2,1)}, u32[]{:S(2)}, u32[]{:S(2)}) %all-to-all-start) | async-done | bytes 4194336 | tf_op jit(solution)/shard_map/all_to_all | solution.py:60
  160.2 10.0 %fusion = f32[1024,1536]{1,0:T(8,128)S(1)} fusion(bf16[1024,2048]{1,0:T(8,128)(2,1)} %bitcast.2, bf16[1,2048,1536]{2,1,0:T(8,128)(2,1)} %param.17), kind=kOutput, calls=%fused_computation | convolution fusion | flops 6442450944 | bytes 16777216 | tf_op jit(solution)/shard_map/dot_general | solution.py:9
  170.3 0.0 copy-done
  170.3 5.1 %convolution_convert_fusion = bf16[1024,2048]{1,0:T(8,128)(2,1)} fusion(bf16[1,768,2048]{2,1,0:T(8,128)(2,1)S(1)} %copy-done, f32[1024,1536]{1,0:T(8,128)S(1)} %fusion), kind=kOutput, calls=%fused_computation.2 | convolution fusion | flops 3228041216 | bytes 13631488 | tf_op jit(solution)/shard_map/dot_general | solution.py:11
  175.4 0.0 copy-start.5
  175.4 0.0 copy-start.6
  175.4 7.4 %all-to-all-start.1 = ((bf16[32,32,2048]{2,1,0:T(8,128)(2,1)}), bf16[32,32,2048]{2,1,0:T(8,128)(2,1)}, u32[]{:S(2)}, u32[]{:S(2)}) async-start(bf16[32,32,2048]{2,1,0:T(8,128)(2,1)} %bitcast.43), calls=%async_computation.1 | async-start | bytes 8388608 | tf_op jit(solution)/shard_map/all_to_all | solution.py:62
  182.8 0.0 copy-done.5
  182.8 1.3 fusion.24
  184.1 0.0 copy-done.6
  184.2 1.2 select_reduce_fusion
  185.4 0.0 all-gather.6.cloned.1.call-done
  185.4 7.3 %fusion.23 = f32[128,2816]{1,0:T(8,128)} fusion(bf16[128,2048]{1,0:T(8,128)(2,1)} %copy-done.1, bf16[2048,2816]{1,0:T(8,128)(2,1)} %all-gather.6.cloned.1.call-done), kind=kOutput, calls=%fused_computation.45 | convolution fusion | flops 1476395008 | bytes 13500416 | tf_op jit(solution)/shard_map/dot_general | solution.py:73
  192.7 0.0 all-gather.8.cloned.1.call-done
  192.7 5.3 %convolution_add_fusion.1 = f32[128,2048]{1,0:T(8,128)} fusion(f32[128,2048]{1,0:T(8,128)} %copy-done.3, bf16[1408,2048]{1,0:T(8,128)(2,1)} %all-gather.8.cloned.1.call-done, f32[128,2816]{1,0:T(8,128)} %fusion.23), kind=kOutput, calls=%fused_computation.12 | convolution fusion | flops 739540992 | bytes 9306112 | tf_op jit(solution)/shard_map/dot_general | solution.py:81
  198.0 79.5 %all-to-all-done.1 = bf16[32,32,2048]{2,1,0:T(8,128)(2,1)} async-done(((bf16[32,32,2048]{2,1,0:T(8,128)(2,1)}), bf16[32,32,2048]{2,1,0:T(8,128)(2,1)}, u32[]{:S(2)}, u32[]{:S(2)}) %all-to-all-start.1) | async-done | bytes 4194336 | tf_op jit(solution)/shard_map/all_to_all | solution.py:62
  277.5 3.2 %fusion.15 = f32[128,2048]{1,0:T(8,128)S(1)} fusion(bf16[1024,2048]{1,0:T(8,128)(2,1)} %bitcast.6, f32[128,1024]{1,0:T(8,128)} %select_reduce_fusion), kind=kOutput, calls=%fused_computation.25 | convolution fusion | flops 537001984 | bytes 5767168 | tf_op jit(solution)/shard_map/dot_general | solution.py:70
  280.7 0.0 copy-done.2
  280.7 0.0 copy-done.4
  280.7 3.8 %fusion.8 = bf16[128,2048]{1,0:T(8,128)(2,1)} fusion(f32[128,2048]{1,0:T(8,128)S(1)} %copy-done.4, f32[128,2048]{1,0:T(8,128)S(1)} %fusion.15, bf16[1024,2048]{1,0:T(8,128)(2,1)} %bitcast.6, f32[128,1024]{1,0:T(8,128)S(1)} %copy-done.2), kind=kOutput, calls=%fused_computation.16 | convolution fusion | flops 538181632 | bytes 7340032 | tf_op jit(solution)/shard_map/dot_general | solution.py:71
  (8 shorter events, 0.1 us)
Async XLA Ops:
  6.5 163.7 %copy-start = (bf16[1,768,2048]{2,1,0:T(8,128)(2,1)S(1)}, bf16[1,768,2048]{2,1,0:T(8,128)(2,1)}, u32[]{:S(2)}) copy-start(bf16[1,768,2048]{2,1,0:T(8,128)(2,1)} %param.18) | copy-start | bytes 9437188
  6.5 40.0 %all-gather.4.cloned.1.call-start = ((), (), s32[]{:S(2)}) async-start(), calls=%async_computation.2 | async-start | bytes 4718592 | tf_op jit(solution)/shard_map/all_gather | solution.py:34
  7.3 43.5 %copy-start.7 = (f32[2048]{0:T(1024)S(1)}, f32[2048]{0:T(1024)}, u32[]{:S(2)}) copy-start(f32[2048]{0:T(1024)} %param.13) | copy-start | bytes 24580
  7.3 178.1 %all-gather.6.cloned.1.call-start = ((), (), s32[]{:S(2)}) async-start(), calls=%async_computation.3 | async-start | bytes 12976128 | tf_op jit(solution)/shard_map/all_gather | solution.py:75
  49.8 1.0 copy-start.3
  50.9 0.8 copy-start.1
  55.0 105.2 %all-to-all-start = ((bf16[32,32,2048]{2,1,0:T(8,128)(2,1)}), bf16[32,32,2048]{2,1,0:T(8,128)(2,1)}, u32[]{:S(2)}, u32[]{:S(2)}) async-start(bf16[32,32,2048]{2,1,0:T(8,128)(2,1)} %bitcast.42), calls=%async_computation | async-start | bytes 8388608 | tf_op jit(solution)/shard_map/all_to_all | solution.py:60
  65.1 127.5 %all-gather.8.cloned.1.call-start = ((), (), s32[]{:S(2)}) async-start(), calls=%async_computation.4 | async-start | bytes 6488064 | tf_op jit(solution)/shard_map/all_gather | solution.py:83
  175.4 7.4 %copy-start.5 = (bf16[2048,32]{0,1:T(8,128)(2,1)S(1)}, bf16[2048,32]{0,1:T(8,128)(2,1)}, u32[]{:S(2)}) copy-start(bf16[2048,32]{0,1:T(8,128)(2,1)} %param.14) | copy-start | bytes 393220
  175.4 8.7 %copy-start.6 = (s32[128,6]{0,1:T(8,128)S(1)}, s32[128,6]{0,1:T(8,128)}, u32[]{:S(2)}) copy-start(s32[128,6]{0,1:T(8,128)} %param.19) | copy-start | bytes 9220
  175.4 102.1 %all-to-all-start.1 = ((bf16[32,32,2048]{2,1,0:T(8,128)(2,1)}), bf16[32,32,2048]{2,1,0:T(8,128)(2,1)}, u32[]{:S(2)}, u32[]{:S(2)}) async-start(bf16[32,32,2048]{2,1,0:T(8,128)(2,1)} %bitcast.43), calls=%async_computation.1 | async-start | bytes 8388608 | tf_op jit(solution)/shard_map/all_to_all | solution.py:62
  277.5 3.2 %copy-start.2 = (f32[128,1024]{1,0:T(8,128)S(1)}, f32[128,1024]{1,0:T(8,128)}, u32[]{:S(2)}) copy-start(f32[128,1024]{1,0:T(8,128)} %select_reduce_fusion) | copy-start | bytes 1572868
  277.5 3.2 %copy-start.4 = (f32[128,2048]{1,0:T(8,128)S(1)}, f32[128,2048]{1,0:T(8,128)}, u32[]{:S(2)}) copy-start(f32[128,2048]{1,0:T(8,128)} %convolution_add_fusion.1) | copy-start | bytes 3145732
Sparse Core Ops, SparseCore 0:
  9.2 37.2 all-gather.3
  48.4 65.4 all-gather.5
  115.7 45.6 all-gather.7

commit v2 on v1

--- a/solution.py
+++ b/solution.py
@@ -29,9 +29,12 @@
     experts = lax.axis_size("expert")
     capacity = 4 * tok_rows * picks // (3 * experts)
     slots = experts * capacity
+    piece = attn_out_w.shape[1] // experts
+    mine = lax.dynamic_slice_in_dim(attn_out_w, lax.axis_index("expert") * piece, piece, axis=1)
+    mine = lax.all_gather(mine, "group", axis=0, tiled=True)
     attn = jnp.dot(
         context,
-        lax.all_gather(attn_out_w, "group", axis=0, tiled=True),
+        lax.all_gather(mine, "expert", axis=1, tiled=True),
         preferred_element_type=jnp.float32,
     )
     hidden_state = (residual.astype(jnp.float32) + attn).astype(jnp.bfloat16)

time: 293 us -> 344 us (1.17)
  waiting for transfers between devices: 210 us -> 244 us
  blocking collectives: 0 us -> 13.2 us
  local copies, waits for them, and re-layouts: 3.27 us -> 8.42 us
  starting transfers between devices: 17.6 us -> 12.7 us
  matrix products: 42.6 us -> 46.1 us
    all_gather x1, waiting for transfers between devices: 33.9 us -> 76.3 us  [per_device(): lax.all_gather(mine, 'expert', axis=1, tiled=True)]
    all_gather x0 -> x1, blocking collectives: none -> 13.2 us  [per_device(): mine = lax.all_gather(mine, 'group', axis=0, tiled=True)]
    all_to_all x1, waiting for transfers between devices: 79.5 us -> 75.1 us  [per_device(): lax.all_to_all(swiglu_rows(flat_rows, local_in, local_out).astype(jnp.bfl...]
    all_to_all x1, starting transfers between devices: 10.1 us -> 5.93 us  [per_device(): lax.all_to_all(outgoing, 'expert', split_axis=0, concat_axis=0, tiled=True)]
  transfers between devices with their start and end apart: 5 -> 5, of which waited for: 3 -> 3; matrix products, arithmetic and copies ran while one was open for 14% -> 13% of each run, Pallas kernels for 0% -> 0%
where the time goes in v2:
time: 344 us; the launch traced here: 343 us
  waiting for transfers between devices  244 us (71%)
  matrix products  46.1 us (13%)
  between operations  13.3 us (4%)
  blocking collectives  13.2 us (4%)
  starting transfers between devices  12.7 us (4%)
  local copies, waits for them, and re-layouts  8.42 us (2%)
  other arithmetic  4.71 us (1%)
    all_to_all x1, waiting for transfers between devices, per_device(): lax.all_to_all(outgoing, 'expert', split_axis=0, concat_axis=0, tiled=True)  91.3 us
    all_gather x1, waiting for transfers between devices, per_device(): lax.all_gather(mine, 'expert', axis=1, tiled=True)  76.3 us
    all_to_all x1, waiting for transfers between devices, per_device(): lax.all_to_all(swiglu_rows(flat_rows, local_in, local_out).astype(jnp.bfl...  75.1 us
    all_gather x1, blocking collectives, per_device(): mine = lax.all_gather(mine, 'group', axis=0, tiled=True)  13.2 us
    dot_general x1, matrix products, swiglu_rows(): mid = jnp.dot(rows, w_in, preferred_element_type=jnp.float32)  10 us
    dot_general x1, matrix products, per_device(): jnp.dot(normed, lax.all_gather(shared_in, 'group', axis=0, tiled=True), p...  7.3 us
  transfers between devices with their start and end apart: 5, of which 3 were waited for; matrix products, arithmetic and copies ran while one was open for 13% of the time, Pallas kernels for 0%

profile of v2, /device:TPU:32, one launch (start us, length us, event | category | flops | bytes accessed | tf_op | source)
XLA Modules:
  0.0 342.5 jit_solution(10734988011702027874)
XLA Ops:
  6.5 0.0 copy-start
  6.5 0.0 all-gather.4.cloned.1.call-start
  6.5 1.0 constant_dynamic-slice_fusion
  7.5 0.1 copy.69
  7.6 13.2 %all_gather.12 = bf16[1024,64]{0,1:T(8,128)(2,1)} all-gather(bf16[128,64]{0,1:T(8,128)(2,1)S(1)} %copy.69), channel_id=1, replica_groups=mesh['group'=8,'expert'=32] {'group'}, dimensions={0}, use_global_device_ids=true | all-gather | bytes 147456 | tf_op jit(solution)/shard_map/all_gather | solution.py:34
  20.8 0.0 all-gather.4.cloned.1.call-update
  20.9 0.0 all-gather.6.cloned.1.call-start
  20.9 0.7 all-gather.6.cloned.1.call-update
  21.6 0.8 copy.59
  22.4 0.1 eq.55
  22.6 0.1 eq.51
  22.7 2.0 copy.56
  24.7 0.0 copy-start.7
  24.8 1.7 reduce-window.6
  26.5 0.3 slice_reduce_fusion
  26.8 0.1 fusion.21
  26.9 0.1 reduce_sum.49
  27.0 0.1 copy.62
  27.1 0.7 multiply_add_fusion
  27.8 0.5 fusion.4
  28.3 76.3 %all-gather.4.cloned.1.call-done = bf16[1024,2048]{0,1:T(8,128)(2,1)} async-done(((bf16[1024,64]{0,1:T(8,128)(2,1)}), bf16[1024,2048]{0,1:T(8,128)(2,1)}) %all-gather.4.cloned.1.call-update) | async-done | bytes 4194320 | tf_op jit(solution)/shard_map/all_gather | solution.py:37
  104.6 3.7 %multiply_reduce_fusion = (f32[128]{0:T(128)S(1)}, f32[128,2048]{0,1:T(8,128)S(1)}) fusion(bf16[1024,2048]{0,1:T(8,128)(2,1)} %all-gather.4.cloned.1.call-done, bf16[128,1024]{1,0:T(8,128)(2,1)} %param.10, bf16[128,2048]{0,1:T(8,128)(2,1)} %copy.56), kind=kOutput, calls=%fused_computation.20 | convolution fusion | flops 538443648 | bytes 6029824 | tf_op jit(solution)/shard_map/dot_general | solution.py:35
  108.3 0.9 copy-done.2
  109.2 0.0 copy-done.7
  109.2 0.3 multiply_convert_fusion
  109.6 0.0 copy-start.1
  109.6 0.8 copy-done.1
  110.3 3.3 convolution_convert_fusion
  113.7 5.9 %all-to-all-start = ((bf16[32,32,2048]{2,1,0:T(8,128)(2,1)}), bf16[32,32,2048]{2,1,0:T(8,128)(2,1)}, u32[]{:S(2)}, u32[]{:S(2)}) async-start(bf16[32,32,2048]{2,1,0:T(8,128)(2,1)} %bitcast.49), calls=%async_computation | async-start | bytes 8388608 | tf_op jit(solution)/shard_map/all_to_all | solution.py:63
  119.6 0.0 all-gather.8.cloned.1.call-start
  119.6 0.7 all-gather.8.cloned.1.call-update
  120.3 91.3 %all-to-all-done = bf16[32,32,2048]{2,1,0:T(8,128)(2,1)} async-done(((bf16[32,32,2048]{2,1,0:T(8,128)(2,1)}), bf16[32,32,2048]{2,1,0:T(8,128)(2,1)}, u32[]{:S(2)}, u32[]{:S(2)}) %all-to-all-start) | async-done | bytes 4194336 | tf_op jit(solution)/shard_map/all_to_all | solution.py:63
  211.6 10.0 %fusion = f32[1024,1536]{1,0:T(8,128)S(1)} fusion(bf16[1024,2048]{1,0:T(8,128)(2,1)} %bitcast.3, bf16[1,2048,1536]{2,1,0:T(8,128)(2,1)} %param.17), kind=kOutput, calls=%fused_computation | convolution fusion | flops 6442450944 | bytes 16777216 | tf_op jit(solution)/shard_map/dot_general | solution.py:9
  221.6 0.0 copy-done
  221.6 5.1 %convolution_convert_fusion.1 = bf16[1024,2048]{1,0:T(8,128)(2,1)} fusion(bf16[1,768,2048]{2,1,0:T(8,128)(2,1)S(1)} %copy-done, f32[1024,1536]{1,0:T(8,128)S(1)} %fusion), kind=kOutput, calls=%fused_computation.3 | convolution fusion | flops 3228041216 | bytes 13631488 | tf_op jit(solution)/shard_map/dot_general | solution.py:11
  226.8 6.7 %all-to-all-start.1 = ((bf16[32,32,2048]{2,1,0:T(8,128)(2,1)}), bf16[32,32,2048]{2,1,0:T(8,128)(2,1)}, u32[]{:S(2)}, u32[]{:S(2)}) async-start(bf16[32,32,2048]{2,1,0:T(8,128)(2,1)} %bitcast.50), calls=%async_computation.1 | async-start | bytes 8388608 | tf_op jit(solution)/shard_map/all_to_all | solution.py:65
  233.4 0.0 copy-done.5
  233.4 1.2 fusion.26
  234.7 0.0 copy-done.6
  234.8 1.2 select_reduce_fusion
  236.0 7.3 %fusion.25 = f32[128,2816]{1,0:T(8,128)} fusion(bf16[128,2048]{0,1:T(8,128)(2,1)} %copy-done.1, bf16[2048,2816]{1,0:T(8,128)(2,1)} %all-gather.6.cloned.1.call-done), kind=kOutput, calls=%fused_computation.48 | convolution fusion | flops 1476395008 | bytes 13500416 | tf_op jit(solution)/shard_map/dot_general | solution.py:76
  243.3 6.7 %convolution_add_fusion.1 = f32[128,2048]{0,1:T(8,128)} fusion(f32[128,2048]{0,1:T(8,128)} %copy-done.2, bf16[1408,2048]{1,0:T(8,128)(2,1)} %all-gather.8.cloned.1.call-done, f32[128,2816]{1,0:T(8,128)} %fusion.25), kind=kOutput, calls=%fused_computation.12 | convolution fusion | flops 739540992 | bytes 9306112 | tf_op jit(solution)/shard_map/dot_general | solution.py:84
  249.9 75.1 %all-to-all-done.1 = bf16[32,32,2048]{2,1,0:T(8,128)(2,1)} async-done(((bf16[32,32,2048]{2,1,0:T(8,128)(2,1)}), bf16[32,32,2048]{2,1,0:T(8,128)(2,1)}, u32[]{:S(2)}, u32[]{:S(2)}) %all-to-all-start.1) | async-done | bytes 4194336 | tf_op jit(solution)/shard_map/all_to_all | solution.py:65
  325.1 4.2 %fusion.17 = f32[128,2048]{0,1:T(8,128)S(1)} fusion(bf16[1024,2048]{1,0:T(8,128)(2,1)} %bitcast.7, f32[128,1024]{1,0:T(8,128)} %select_reduce_fusion), kind=kOutput, calls=%fused_computation.27 | convolution fusion | flops 537001984 | bytes 5767168 | tf_op jit(solution)/shard_map/dot_general | solution.py:73
  329.3 0.0 copy-done.3
  329.3 0.0 copy-done.4
  329.3 4.7 %fusion.9 = bf16[128,2048]{0,1:T(8,128)(2,1)} fusion(f32[128,2048]{0,1:T(8,128)S(1)} %copy-done.4, f32[128,2048]{0,1:T(8,128)S(1)} %fusion.17, bf16[1024,2048]{1,0:T(8,128)(2,1)} %bitcast.7, f32[128,1024]{1,0:T(8,128)S(1)} %copy-done.3), kind=kOutput, calls=%fused_computation.17 | convolution fusion | flops 538181632 | bytes 7340032 | tf_op jit(solution)/shard_map/dot_general | solution.py:74
  334.0 2.0 copy.65
  (13 shorter events, 0.1 us)
Async XLA Ops:
  6.5 215.1 %copy-start = (bf16[1,768,2048]{2,1,0:T(8,128)(2,1)S(1)}, bf16[1,768,2048]{2,1,0:T(8,128)(2,1)}, u32[]{:S(2)}) copy-start(bf16[1,768,2048]{2,1,0:T(8,128)(2,1)} %param.18) | copy-start | bytes 9437188
  6.5 98.0 %all-gather.4.cloned.1.call-start = ((), (), s32[]{:S(2)}) async-start(), calls=%async_computation.2 | async-start | bytes 4325376 | tf_op jit(solution)/shard_map/all_gather | solution.py:37
  20.9 215.1 %all-gather.6.cloned.1.call-start = ((), (), s32[]{:S(2)}) async-start(), calls=%async_computation.3 | async-start | bytes 12976128 | tf_op jit(solution)/shard_map/all_gather | solution.py:78
  24.7 84.5 %copy-start.7 = (f32[2048]{0:T(1024)S(1)}, f32[2048]{0:T(1024)}, u32[]{:S(2)}) copy-start(f32[2048]{0:T(1024)} %param.13) | copy-start | bytes 24580
  108.2 1.0 copy-start.2
  109.6 0.8 copy-start.1
  113.7 98.0 %all-to-all-start = ((bf16[32,32,2048]{2,1,0:T(8,128)(2,1)}), bf16[32,32,2048]{2,1,0:T(8,128)(2,1)}, u32[]{:S(2)}, u32[]{:S(2)}) async-start(bf16[32,32,2048]{2,1,0:T(8,128)(2,1)} %bitcast.49), calls=%async_computation | async-start | bytes 8388608 | tf_op jit(solution)/shard_map/all_to_all | solution.py:63
  119.6 123.7 %all-gather.8.cloned.1.call-start = ((), (), s32[]{:S(2)}) async-start(), calls=%async_computation.4 | async-start | bytes 6488064 | tf_op jit(solution)/shard_map/all_gather | solution.py:86
  226.7 6.7 %copy-start.5 = (bf16[2048,32]{0,1:T(8,128)(2,1)S(1)}, bf16[2048,32]{0,1:T(8,128)(2,1)}, u32[]{:S(2)}) copy-start(bf16[2048,32]{0,1:T(8,128)(2,1)} %param.14) | copy-start | bytes 393220
  226.7 7.9 %copy-start.6 = (s32[128,6]{0,1:T(8,128)S(1)}, s32[128,6]{0,1:T(8,128)}, u32[]{:S(2)}) copy-start(s32[128,6]{0,1:T(8,128)} %param.19) | copy-start | bytes 9220
  226.8 98.3 %all-to-all-start.1 = ((bf16[32,32,2048]{2,1,0:T(8,128)(2,1)}), bf16[32,32,2048]{2,1,0:T(8,128)(2,1)}, u32[]{:S(2)}, u32[]{:S(2)}) async-start(bf16[32,32,2048]{2,1,0:T(8,128)(2,1)} %bitcast.50), calls=%async_computation.1 | async-start | bytes 8388608 | tf_op jit(solution)/shard_map/all_to_all | solution.py:65
  325.1 4.2 %copy-start.3 = (f32[128,1024]{1,0:T(8,128)S(1)}, f32[128,1024]{1,0:T(8,128)}, u32[]{:S(2)}) copy-start(f32[128,1024]{1,0:T(8,128)} %select_reduce_fusion) | copy-start | bytes 1572868
  325.1 4.2 %copy-start.4 = (f32[128,2048]{0,1:T(8,128)S(1)}, f32[128,2048]{0,1:T(8,128)}, u32[]{:S(2)}) copy-start(f32[128,2048]{0,1:T(8,128)} %convolution_add_fusion.1) | copy-start | bytes 3145732
Sparse Core Ops, SparseCore 0:
  21.0 83.5 all-gather.3
  106.4 62.6 all-gather.5
  170.9 45.6 all-gather.7

commit v3 on v1

--- a/solution.py
+++ b/solution.py
@@ -57,18 +57,23 @@
     combine_lo = (combine - combine_hi.astype(jnp.float32)).astype(jnp.bfloat16)
     local_in = expert_in[0]
     local_out = expert_out_w[0]
-    arrived = lax.all_to_all(outgoing, "expert", split_axis=0, concat_axis=0, tiled=True)
-    flat_rows = arrived.reshape(-1, width)
-    returned = lax.all_to_all(
-        swiglu_rows(flat_rows, local_in, local_out).astype(jnp.bfloat16).reshape(arrived.shape),
-        "expert",
-        split_axis=0,
-        concat_axis=0,
-        tiled=True,
-    )
-    returned = returned.reshape(slots, width)
-    routed = jnp.dot(combine_hi, returned, preferred_element_type=jnp.float32)
-    routed = routed + jnp.dot(combine_lo, returned, preferred_element_type=jnp.float32)
+    chunks = 2
+    part = capacity // chunks
+    outgoing = outgoing.reshape(experts, chunks, part, width)
+    combine_hi = combine_hi.reshape(tok_rows, experts, chunks, part)
+    combine_lo = combine_lo.reshape(tok_rows, experts, chunks, part)
+    routed = None
+    for c in range(chunks):
+        arrived = lax.all_to_all(outgoing[:, c], "expert", split_axis=0, concat_axis=0, tiled=True)
+        done = swiglu_rows(arrived.reshape(-1, width), local_in, local_out).astype(jnp.bfloat16)
+        returned = lax.all_to_all(
+            done.reshape(arrived.shape), "expert", split_axis=0, concat_axis=0, tiled=True
+        ).reshape(experts * part, width)
+        hi = combine_hi[:, :, c].reshape(tok_rows, experts * part)
+        lo = combine_lo[:, :, c].reshape(tok_rows, experts * part)
+        step = jnp.dot(hi, returned, preferred_element_type=jnp.float32)
+        step = step + jnp.dot(lo, returned, preferred_element_type=jnp.float32)
+        routed = step if routed is None else routed + step
     shared_hidden = shared_out.shape[0]
     shared_mid = jnp.dot(
         normed,

time: 293 us -> 307 us (1.048)
  blocking collectives: 0 us -> 60 us
  waiting for transfers between devices: 210 us -> 152 us
  matrix products: 42.6 us -> 48.5 us
  local copies, waits for them, and re-layouts: 3.27 us -> 6.49 us
    all_to_all x0 -> x1, blocking collectives: none -> 60 us  [per_device(): lax.all_to_all(outgoing[:, c], 'expert', split_axis=0, concat_axis=0, til...]
    all_to_all x2 -> x3, waiting for transfers between devices: 174 us -> 115 us  [the longest x2 76.7 us: per_device(): lax.all_to_all(done.reshape(arrived.shape), 'expert', split_axis=0, conca...]
    dot_general x2 -> x4, matrix products: 7.01 us -> 12.1 us  [the longest x2 6.21 us: per_device(): step = jnp.dot(hi, returned, preferred_element_type=jnp.float32)]
    dot_general x1 -> x2, matrix products: 10 us -> 12.3 us  [swiglu_rows(): mid = jnp.dot(rows, w_in, preferred_element_type=jnp.float32)]
    all_to_all x2 -> x3, starting transfers between devices: 17.5 us -> 19.7 us  [the longest x2 13.2 us: per_device(): lax.all_to_all(done.reshape(arrived.shape), 'expert', split_axis=0, conca...]
    dot_general x1 -> x2, matrix products: 5.09 us -> 6.48 us  [swiglu_rows(): return jnp.dot(act, w_out, preferred_element_type=jnp.float32)]
  transfers between devices with their start and end apart: 5 -> 6, of which waited for: 3 -> 4; matrix products, arithmetic and copies ran while one was open for 14% -> 17% of each run, Pallas kernels for 0% -> 0%
where the time goes in v3:
time: 307 us; the launch traced here: 305 us
  waiting for transfers between devices  152 us (50%)
  blocking collectives  60 us (20%)
  matrix products  48.5 us (16%)
  starting transfers between devices  19.8 us (6%)
  between operations  13.3 us (4%)
  local copies, waits for them, and re-layouts  6.49 us (2%)
  other arithmetic  5.17 us (2%)
    all_to_all x2, waiting for transfers between devices, per_device(): lax.all_to_all(done.reshape(arrived.shape), 'expert', split_axis=0, conca...  76.7 us
    all_to_all x1, blocking collectives, per_device(): lax.all_to_all(outgoing[:, c], 'expert', split_axis=0, concat_axis=0, til...  60 us
    all_to_all x1, waiting for transfers between devices, per_device(): lax.all_to_all(outgoing[:, c], 'expert', split_axis=0, concat_axis=0, til...  38.5 us
    all_gather x1, waiting for transfers between devices, per_device(): lax.all_gather(attn_out_w, 'group', axis=0, tiled=True)  34.6 us
    all_to_all x2, starting transfers between devices, per_device(): lax.all_to_all(done.reshape(arrived.shape), 'expert', split_axis=0, conca...  13.2 us
    dot_general x2, matrix products, swiglu_rows(): mid = jnp.dot(rows, w_in, preferred_element_type=jnp.float32)  12.3 us
    dot_general x1, matrix products, per_device(): jnp.dot(normed, lax.all_gather(shared_in, 'group', axis=0, tiled=True), p...  7.23 us
    all_to_all x1, starting transfers between devices, per_device(): lax.all_to_all(outgoing[:, c], 'expert', split_axis=0, concat_axis=0, til...  6.51 us
  transfers between devices with their start and end apart: 6, of which 4 were waited for; matrix products, arithmetic and copies ran while one was open for 17% of the time, Pallas kernels for 0%

profile of v3, /device:TPU:32, one launch (start us, length us, event | category | flops | bytes accessed | tf_op | source)
XLA Modules:
  0.0 305.3 jit_solution(4275384464395332200)
XLA Ops:
  6.5 0.0 copy-start
  6.5 0.0 all-gather.4.cloned.1.call-start
  6.5 0.7 all-gather.4.cloned.1.call-update
  7.3 0.0 all-gather.6.cloned.1.call-start
  7.3 0.7 all-gather.6.cloned.1.call-update
  8.0 0.8 copy.28
  8.8 0.1 eq.55
  8.9 0.1 eq.51
  9.1 1.7 reduce-window.6
  10.8 0.3 slice_reduce_fusion
  11.1 0.1 fusion.31
  11.2 0.1 reduce_sum.51
  11.4 0.1 copy.31
  11.4 0.0 copy-done.7
  11.5 0.5 fusion.8
  12.0 0.0 copy-start.8
  12.0 34.6 %all-gather.4.cloned.1.call-done = bf16[1024,2048]{1,0:T(8,128)(2,1)} async-done(((bf16[128,2048]{1,0:T(8,128)(2,1)}), bf16[1024,2048]{1,0:T(8,128)(2,1)}) %all-gather.4.cloned.1.call-update) | async-done | bytes 4194320 | tf_op jit(solution)/shard_map/all_gather | solution.py:34
  46.6 3.2 %multiply_reduce_fusion = (f32[128]{0:T(128)S(1)}, f32[128,2048]{1,0:T(8,128)S(1)}) fusion(bf16[128,1024]{1,0:T(8,128)(2,1)} %param.10, bf16[1024,2048]{1,0:T(8,128)(2,1)} %all-gather.4.cloned.1.call-done, bf16[128,2048]{1,0:T(8,128)(2,1)} %param.11), kind=kOutput, calls=%fused_computation.30 | convolution fusion | flops 538443648 | bytes 6029824 | tf_op jit(solution)/shard_map/dot_general | solution.py:32
  49.9 1.0 copy-done.4
  50.9 0.2 multiply_convert_fusion
  51.0 0.0 copy-start.1
  51.0 1.3 convolution_convert_fusion
  52.4 1.9 slice_bitcast_fusion
  54.2 60.0 %all_to_all.20 = bf16[32,16,2048]{2,1,0:T(8,128)(2,1)} all-to-all(bf16[32,16,2048]{2,1,0:T(8,128)(2,1)S(1)} %get-tuple-element.8), channel_id=1, replica_groups=mesh['group'=8,'expert'=32] {'expert'}, dimensions={0} | all-to-all | bytes 4194304 | tf_op jit(solution)/shard_map/all_to_all | solution.py:67
  114.2 6.5 %all-to-all-start.2 = ((bf16[32,16,2048]{2,1,0:T(8,128)(2,1)}), bf16[32,16,2048]{2,1,0:T(8,128)(2,1)}, u32[]{:S(2)}, u32[]{:S(2)}) async-start(bf16[32,16,2048]{2,1,0:T(8,128)(2,1)} %get-tuple-element.7), calls=%async_computation.2 | async-start | bytes 4194304 | tf_op jit(solution)/shard_map/all_to_all | solution.py:67
  120.8 0.0 all-gather.8.cloned.1.call-start
  120.8 0.7 all-gather.8.cloned.1.call-update
  121.5 6.2 %fusion.2 = f32[512,1536]{1,0:T(8,128)S(1)} fusion(bf16[512,2048]{1,0:T(8,128)(2,1)} %bitcast.71, bf16[1,2048,1536]{2,1,0:T(8,128)(2,1)} %param.17), kind=kOutput, calls=%fused_computation.2 | convolution fusion | flops 3221225472 | bytes 11534336 | tf_op jit(solution)/shard_map/dot_general | solution.py:9
  127.7 3.2 %fusion.9 = bf16[512,2048]{1,0:T(8,128)(2,1)} fusion(bf16[1,768,2048]{2,1,0:T(8,128)(2,1)S(1)} %copy-done, f32[512,1536]{1,0:T(8,128)S(1)} %fusion.2), kind=kOutput, calls=%fused_computation.12 | convolution fusion | flops 1614020608 | bytes 8388608 | tf_op jit(solution)/shard_map/dot_general | solution.py:11
  130.9 38.5 %all-to-all-done.2 = bf16[32,16,2048]{2,1,0:T(8,128)(2,1)} async-done(((bf16[32,16,2048]{2,1,0:T(8,128)(2,1)}), bf16[32,16,2048]{2,1,0:T(8,128)(2,1)}, u32[]{:S(2)}, u32[]{:S(2)}) %all-to-all-start.2) | async-done | bytes 2097184 | tf_op jit(solution)/shard_map/all_to_all | solution.py:67
  169.5 6.5 %all-to-all-start.1 = ((bf16[32,16,2048]{2,1,0:T(8,128)(2,1)}), bf16[32,16,2048]{2,1,0:T(8,128)(2,1)}, u32[]{:S(2)}, u32[]{:S(2)}) async-start(bf16[32,16,2048]{2,1,0:T(8,128)(2,1)} %bitcast.72), calls=%async_computation.1 | async-start | bytes 4194304 | tf_op jit(solution)/shard_map/all_to_all | solution.py:69
  176.0 6.2 %fusion = f32[512,1536]{1,0:T(8,128)S(1)} fusion(bf16[512,2048]{1,0:T(8,128)(2,1)} %bitcast.13, bf16[1,2048,1536]{2,1,0:T(8,128)(2,1)} %param.17), kind=kOutput, calls=%fused_computation | convolution fusion | flops 3221225472 | bytes 11534336 | tf_op jit(solution)/shard_map/dot_general | solution.py:9
  182.2 3.2 %fusion.12 = bf16[512,2048]{1,0:T(8,128)(2,1)} fusion(bf16[1,768,2048]{2,1,0:T(8,128)(2,1)S(1)} %copy-done, f32[512,1536]{1,0:T(8,128)S(1)} %fusion), kind=kOutput, calls=%fused_computation.13 | convolution fusion | flops 1614020608 | bytes 8388608 | tf_op jit(solution)/shard_map/dot_general | solution.py:11
  185.4 38.7 %all-to-all-done.1 = bf16[32,16,2048]{2,1,0:T(8,128)(2,1)} async-done(((bf16[32,16,2048]{2,1,0:T(8,128)(2,1)}), bf16[32,16,2048]{2,1,0:T(8,128)(2,1)}, u32[]{:S(2)}, u32[]{:S(2)}) %all-to-all-start.1) | async-done | bytes 2097184 | tf_op jit(solution)/shard_map/all_to_all | solution.py:69
  224.1 6.7 %all-to-all-start.3 = ((bf16[32,16,2048]{2,1,0:T(8,128)(2,1)}), bf16[32,16,2048]{2,1,0:T(8,128)(2,1)}, u32[]{:S(2)}, u32[]{:S(2)}) async-start(bf16[32,16,2048]{2,1,0:T(8,128)(2,1)} %bitcast.70), calls=%async_computation.3 | async-start | bytes 4194304 | tf_op jit(solution)/shard_map/all_to_all | solution.py:69
  230.8 1.3 fusion.39
  232.2 1.2 select_reduce_fusion
  233.4 2.0 copy.32
  235.5 1.3 subtract_convert_fusion
  236.8 3.0 fusion.40
  239.8 38.0 %all-to-all-done.3 = bf16[32,16,2048]{2,1,0:T(8,128)(2,1)} async-done(((bf16[32,16,2048]{2,1,0:T(8,128)(2,1)}), bf16[32,16,2048]{2,1,0:T(8,128)(2,1)}, u32[]{:S(2)}, u32[]{:S(2)}) %all-to-all-start.3) | async-done | bytes 2097184 | tf_op jit(solution)/shard_map/all_to_all | solution.py:69
  277.9 3.2 %fusion.41 = f32[128,2048]{1,0:T(8,128)} fusion(bf16[128,512]{0,1:T(8,128)(2,1)S(1)} %bitcast.76, bf16[512,2048]{1,0:T(8,128)(2,1)} %bitcast.15), kind=kOutput, calls=%fused_computation.61 | convolution fusion | flops 268435456 | bytes 3276800 | tf_op jit(solution)/shard_map/dot_general | solution.py:74
  281.0 3.1 %convolution_add_fusion.1 = f32[128,2048]{1,0:T(8,128)} fusion(f32[128,2048]{1,0:T(8,128)S(1)} %copy-done.3, bf16[128,512]{0,1:T(8,128)(2,1)S(1)} %bitcast.75, bf16[512,2048]{1,0:T(8,128)(2,1)} %bitcast.9), kind=kOutput, calls=%fused_computation.17 | convolution fusion | flops 268697600 | bytes 4325376 | tf_op jit(solution)/shard_map/dot_general | solution.py:75
  284.1 7.2 %fusion.38 = f32[128,2816]{1,0:T(8,128)} fusion(bf16[128,2048]{1,0:T(8,128)(2,1)} %copy-done.1, bf16[2048,2816]{1,0:T(8,128)(2,1)} %all-gather.6.cloned.1.call-done), kind=kOutput, calls=%fused_computation.58 | convolution fusion | flops 1476395008 | bytes 13500416 | tf_op jit(solution)/shard_map/dot_general | solution.py:78
  291.4 4.5 %convolution_add_fusion.2 = f32[128,2048]{1,0:T(8,128)S(1)} fusion(f32[128,2048]{1,0:T(8,128)} %copy-done.4, bf16[1408,2048]{1,0:T(8,128)(2,1)} %all-gather.8.cloned.1.call-done, f32[128,2816]{1,0:T(8,128)} %fusion.38), kind=kOutput, calls=%fused_computation.18 | convolution fusion | flops 739540992 | bytes 9306112 | tf_op jit(solution)/shard_map/dot_general | solution.py:86
  295.8 0.0 copy-done.2
  295.9 0.0 copy-done.5
  295.9 2.9 fusion.19
  (21 shorter events, 0.2 us)
Async XLA Ops:
  6.5 121.1 %copy-start = (bf16[1,768,2048]{2,1,0:T(8,128)(2,1)S(1)}, bf16[1,768,2048]{2,1,0:T(8,128)(2,1)}, u32[]{:S(2)}) copy-start(bf16[1,768,2048]{2,1,0:T(8,128)(2,1)} %param.18) | copy-start | bytes 9437188
  6.5 4.9 %copy-start.7 = (s32[128,6]{0,1:T(8,128)S(1)}, s32[128,6]{0,1:T(8,128)}, u32[]{:S(2)}) copy-start(s32[128,6]{0,1:T(8,128)} %param.19) | copy-start | bytes 9220
  6.5 40.0 %all-gather.4.cloned.1.call-start = ((), (), s32[]{:S(2)}) async-start(), calls=%async_computation.4 | async-start | bytes 4718592 | tf_op jit(solution)/shard_map/all_gather | solution.py:34
  7.3 276.9 %all-gather.6.cloned.1.call-start = ((), (), s32[]{:S(2)}) async-start(), calls=%async_computation.5 | async-start | bytes 12976128 | tf_op jit(solution)/shard_map/all_gather | solution.py:80
  12.0 38.9 %copy-start.8 = (f32[2048]{0:T(1024)S(1)}, f32[2048]{0:T(1024)}, u32[]{:S(2)}) copy-start(f32[2048]{0:T(1024)} %param.13) | copy-start | bytes 24580
  49.8 1.0 copy-start.4
  51.0 1.3 copy-start.1
  114.2 55.2 %all-to-all-start.2 = ((bf16[32,16,2048]{2,1,0:T(8,128)(2,1)}), bf16[32,16,2048]{2,1,0:T(8,128)(2,1)}, u32[]{:S(2)}, u32[]{:S(2)}) async-start(bf16[32,16,2048]{2,1,0:T(8,128)(2,1)} %get-tuple-element.7), calls=%async_computation.2 | async-start | bytes 4194304 | tf_op jit(solution)/shard_map/all_to_all | solution.py:67
  120.8 170.6 %all-gather.8.cloned.1.call-start = ((), (), s32[]{:S(2)}) async-start(), calls=%async_computation.6 | async-start | bytes 6488064 | tf_op jit(solution)/shard_map/all_gather | solution.py:88
  169.5 54.6 %all-to-all-start.1 = ((bf16[32,16,2048]{2,1,0:T(8,128)(2,1)}), bf16[32,16,2048]{2,1,0:T(8,128)(2,1)}, u32[]{:S(2)}, u32[]{:S(2)}) async-start(bf16[32,16,2048]{2,1,0:T(8,128)(2,1)} %bitcast.72), calls=%async_computation.1 | async-start | bytes 4194304 | tf_op jit(solution)/shard_map/all_to_all | solution.py:69
  224.1 6.7 %copy-start.6 = (bf16[2048,32]{0,1:T(8,128)(2,1)S(1)}, bf16[2048,32]{0,1:T(8,128)(2,1)}, u32[]{:S(2)}) copy-start(bf16[2048,32]{0,1:T(8,128)(2,1)} %param.14) | copy-start | bytes 393220
  224.1 53.7 %all-to-all-start.3 = ((bf16[32,16,2048]{2,1,0:T(8,128)(2,1)}), bf16[32,16,2048]{2,1,0:T(8,128)(2,1)}, u32[]{:S(2)}, u32[]{:S(2)}) async-start(bf16[32,16,2048]{2,1,0:T(8,128)(2,1)} %bitcast.70), calls=%async_computation.3 | async-start | bytes 4194304 | tf_op jit(solution)/shard_map/all_to_all | solution.py:69
  277.9 3.2 %copy-start.3 = (f32[128,2048]{1,0:T(8,128)S(1)}, f32[128,2048]{1,0:T(8,128)}, u32[]{:S(2)}) copy-start(f32[128,2048]{1,0:T(8,128)} %fusion.40) | copy-start | bytes 3145732
  291.3 4.5 %copy-start.2 = (f32[128,2048]{1,0:T(8,128)S(1)}, f32[128,2048]{1,0:T(8,128)}, u32[]{:S(2)}) copy-start(f32[128,2048]{1,0:T(8,128)} %fusion.41) | copy-start | bytes 3145732
  291.4 4.5 %copy-start.5 = (f32[128,2048]{1,0:T(8,128)S(1)}, f32[128,2048]{1,0:T(8,128)}, u32[]{:S(2)}) copy-start(f32[128,2048]{1,0:T(8,128)} %convolution_add_fusion.1) | copy-start | bytes 3145732
Sparse Core Ops, SparseCore 0:
  9.2 37.3 all-gather.3
  48.4 65.4 all-gather.5
  123.4 44.9 all-gather.7

commit v4 on v1

--- a/solution.py
+++ b/solution.py
@@ -9,6 +9,22 @@
     mid = jnp.dot(rows, w_in, preferred_element_type=jnp.float32)
     act = (jax.nn.silu(mid[:, :width]) * mid[:, width:]).astype(jnp.bfloat16)
     return jnp.dot(act, w_out, preferred_element_type=jnp.float32)
+
+
+def gather_rows_by_chip(w):
+    groups = lax.axis_size("group")
+    ring = groups // 2
+    g = lax.axis_index("group")
+    y, c = g // 2, g % 2
+    shifts = [0] + sorted(range(1, ring), key=lambda s: min(s, ring - s))
+    got = [w]
+    for s in shifts[1:]:
+        pairs = [(2 * q + k, 2 * ((q + s) % ring) + k) for q in range(ring) for k in range(2)]
+        got.append(lax.ppermute(w, "group", pairs))
+    mine = jnp.stack(got)
+    sib = lax.ppermute(mine, "group", [(i, i ^ 1) for i in range(groups)])
+    order = [2 * ((y - s) % ring) + c for s in shifts] + [2 * ((y - s) % ring) + 1 - c for s in shifts]
+    return jnp.concatenate([mine, sib]).reshape(-1, w.shape[1]), order
 
 
 def per_device(
@@ -29,11 +45,12 @@
     experts = lax.axis_size("expert")
     capacity = 4 * tok_rows * picks // (3 * experts)
     slots = experts * capacity
-    attn = jnp.dot(
-        context,
-        lax.all_gather(attn_out_w, "group", axis=0, tiled=True),
-        preferred_element_type=jnp.float32,
+    w_perm, order = gather_rows_by_chip(attn_out_w)
+    block = attn_out_w.shape[0]
+    ctx_perm = jnp.concatenate(
+        [lax.dynamic_slice_in_dim(context, b * block, block, axis=1) for b in order], axis=1
     )
+    attn = jnp.dot(ctx_perm, w_perm, preferred_element_type=jnp.float32)
     hidden_state = (residual.astype(jnp.float32) + attn).astype(jnp.bfloat16)
     hidden_f = hidden_state.astype(jnp.float32)
     scale = lax.rsqrt(jnp.mean(hidden_f * hidden_f, axis=-1, keepdims=True) + 1e-06)

time: 293 us -> 310 us (1.058)
  local copies, waits for them, and re-layouts: 3.27 us -> 13.2 us
  starting transfers between devices: 17.6 us -> 27.5 us
  matrix products: 42.6 us -> 38.9 us
    all_gather x1 -> x0, waiting for transfers between devices: 33.9 us -> none  [per_device(): lax.all_gather(attn_out_w, 'group', axis=0, tiled=True)]
    ppermute x0 -> x4, waiting for transfers between devices: none -> 19.5 us  [the longest x3 19.5 us: gather_rows_by_chip(): got.append(lax.ppermute(w, 'group', pairs))]
    all_to_all x1, waiting for transfers between devices: 79.5 us -> 94.1 us  [per_device(): lax.all_to_all(swiglu_rows(flat_rows, local_in, local_out).astype(jnp.bfl...]
    unnamed x17 -> x38, local copies, waits for them, and re-layouts: 2.57 us -> 11.5 us
    ppermute x0 -> x4, starting transfers between devices: none -> 5.39 us  [the longest x3 5.3 us: gather_rows_by_chip(): got.append(lax.ppermute(w, 'group', pairs))]
  transfers between devices with their start and end apart: 5 -> 8, of which waited for: 3 -> 5; matrix products, arithmetic and copies ran while one was open for 14% -> 15% of each run, Pallas kernels for 0% -> 0%
where the time goes in v4:
time: 310 us; the launch traced here: 307 us
  waiting for transfers between devices  208 us (67%)
  matrix products  38.9 us (13%)
  starting transfers between devices  27.5 us (9%)
  between operations  13.7 us (4%)
  local copies, waits for them, and re-layouts  13.2 us (4%)
  other arithmetic  5.49 us (2%)
    all_to_all x1, waiting for transfers between devices, per_device(): lax.all_to_all(swiglu_rows(flat_rows, local_in, local_out).astype(jnp.bfl...  94.1 us
    all_to_all x1, waiting for transfers between devices, per_device(): lax.all_to_all(outgoing, 'expert', split_axis=0, concat_axis=0, tiled=True)  93.1 us
    ppermute x3, waiting for transfers between devices, gather_rows_by_chip(): got.append(lax.ppermute(w, 'group', pairs))  19.5 us
    all_to_all x1, starting transfers between devices, per_device(): lax.all_to_all(outgoing, 'expert', split_axis=0, concat_axis=0, tiled=True)  12.5 us
    unnamed x38, local copies, waits for them, and re-layouts  11.5 us
    dot_general x1, matrix products, swiglu_rows(): mid = jnp.dot(rows, w_in, preferred_element_type=jnp.float32)  10 us
    all_to_all x1, starting transfers between devices, per_device(): lax.all_to_all(swiglu_rows(flat_rows, local_in, local_out).astype(jnp.bfl...  9.59 us
    dot_general x1, matrix products, per_device(): jnp.dot(normed, lax.all_gather(shared_in, 'group', axis=0, tiled=True), p...  7.09 us
  transfers between devices with their start and end apart: 8, of which 5 were waited for; matrix products, arithmetic and copies ran while one was open for 15% of the time, Pallas kernels for 0%

profile of v4, /device:TPU:32, one launch (start us, length us, event | category | flops | bytes accessed | tf_op | source)
XLA Modules:
  0.0 306.9 jit_solution(260802176206228977)
XLA Ops:
  6.5 0.7 all-gather.3.cloned.1.call-update
  7.3 1.7 collective-permute-start
  8.9 1.7 collective-permute-start.1
  10.6 2.0 collective-permute-start.2
  12.6 0.8 copy.27
  13.3 0.1 eq.65
  13.5 0.1 eq.61
  13.6 1.7 reduce-window.6
  15.4 0.3 slice_reduce_fusion
  15.7 0.1 fusion.19
  15.8 0.1 reduce_sum.49
  16.0 0.8 dynamic-slice_dynamic-update-slice_fusion.7
  16.8 0.8 dynamic-slice_dynamic-update-slice_fusion.6
  17.6 0.8 dynamic-slice_dynamic-update-slice_fusion.5
  18.4 0.8 dynamic-slice_dynamic-update-slice_fusion.4
  19.2 0.8 dynamic-slice_dynamic-update-slice_fusion.3
  19.9 0.8 dynamic-slice_dynamic-update-slice_fusion.2
  20.7 0.8 dynamic-slice_dynamic-update-slice_fusion.1
  21.5 0.7 multiply_add_fusion
  22.2 0.4 collective-permute-done
  22.6 5.8 %collective-permute-done.1 = bf16[128,2048]{1,0:T(8,128)(2,1)} collective-permute-done((bf16[128,2048]{1,0:T(8,128)(2,1)}, bf16[128,2048]{1,0:T(8,128)(2,1)}, u32[]{:S(2)}, u32[]{:S(2)}) %collective-permute-start.1) | collective-permute-done | bytes 524320 | tf_op jit(solution)/shard_map/ppermute | solution.py:23
  28.4 13.3 %collective-permute-done.2 = bf16[128,2048]{1,0:T(8,128)(2,1)} collective-permute-done((bf16[128,2048]{1,0:T(8,128)(2,1)}, bf16[128,2048]{1,0:T(8,128)(2,1)}, u32[]{:S(2)}, u32[]{:S(2)}) %collective-permute-start.2) | collective-permute-done | bytes 524320 | tf_op jit(solution)/shard_map/ppermute | solution.py:23
  41.6 1.8 pad_maximum_fusion
  43.4 0.1 collective-permute-start.3
  43.5 0.8 dynamic-slice_dynamic-update-slice_fusion
  44.3 0.5 fusion.4
  44.9 1.1 constant_dynamic-update-slice_fusion.3
  46.0 1.1 constant_dynamic-update-slice_fusion.2
  47.1 1.1 constant_dynamic-update-slice_fusion.1
  48.2 0.2 constant_dynamic-update-slice_fusion
  48.5 0.9 multiply_reduce_fusion
  49.4 1.0 copy-done.7
  50.4 0.2 multiply_convert_fusion
  50.6 0.8 copy-done.2
  51.4 3.3 %convolution_convert_fusion.1 = bf16[1024,2048]{1,0:T(8,128)(2,1)} fusion(pred[128,1024]{1,0:T(8,128)(4,1)S(1)} %fusion.4, bf16[128,2048]{1,0:T(8,128)(2,1)S(1)} %multiply_convert_fusion), kind=kOutput, calls=%fused_computation.3 | convolution fusion | flops 538968064 | bytes 4849664 | tf_op jit(solution)/shard_map/dot_general | solution.py:70
  54.7 12.5 %all-to-all-start = ((bf16[32,32,2048]{2,1,0:T(8,128)(2,1)}), bf16[32,32,2048]{2,1,0:T(8,128)(2,1)}, u32[]{:S(2)}, u32[]{:S(2)}) async-start(bf16[32,32,2048]{2,1,0:T(8,128)(2,1)} %bitcast.51), calls=%async_computation | async-start | bytes 8388608 | tf_op jit(solution)/shard_map/all_to_all | solution.py:77
  67.2 0.7 all-gather.5.cloned.1.call-update
  67.9 93.1 %all-to-all-done = bf16[32,32,2048]{2,1,0:T(8,128)(2,1)} async-done(((bf16[32,32,2048]{2,1,0:T(8,128)(2,1)}), bf16[32,32,2048]{2,1,0:T(8,128)(2,1)}, u32[]{:S(2)}, u32[]{:S(2)}) %all-to-all-start) | async-done | bytes 4194336 | tf_op jit(solution)/shard_map/all_to_all | solution.py:77
  161.1 10.0 %fusion = f32[1024,1536]{1,0:T(8,128)S(1)} fusion(bf16[1024,2048]{1,0:T(8,128)(2,1)} %bitcast.7, bf16[1,2048,1536]{2,1,0:T(8,128)(2,1)} %param.17), kind=kOutput, calls=%fused_computation | convolution fusion | flops 6442450944 | bytes 16777216 | tf_op jit(solution)/shard_map/dot_general | solution.py:9
  171.1 5.1 %convolution_convert_fusion = bf16[1024,2048]{1,0:T(8,128)(2,1)} fusion(bf16[1,768,2048]{2,1,0:T(8,128)(2,1)S(1)} %copy-done, f32[1024,1536]{1,0:T(8,128)S(1)} %fusion), kind=kOutput, calls=%fused_computation.2 | convolution fusion | flops 3228041216 | bytes 13631488 | tf_op jit(solution)/shard_map/dot_general | solution.py:11
  176.2 9.6 %all-to-all-start.1 = ((bf16[32,32,2048]{2,1,0:T(8,128)(2,1)}), bf16[32,32,2048]{2,1,0:T(8,128)(2,1)}, u32[]{:S(2)}, u32[]{:S(2)}) async-start(bf16[32,32,2048]{2,1,0:T(8,128)(2,1)} %bitcast.53), calls=%async_computation.1 | async-start | bytes 8388608 | tf_op jit(solution)/shard_map/all_to_all | solution.py:79
  185.8 0.3 fusion.24
  186.2 0.4 select_reduce_fusion
  186.6 94.1 %all-to-all-done.1 = bf16[32,32,2048]{2,1,0:T(8,128)(2,1)} async-done(((bf16[32,32,2048]{2,1,0:T(8,128)(2,1)}), bf16[32,32,2048]{2,1,0:T(8,128)(2,1)}, u32[]{:S(2)}, u32[]{:S(2)}) %all-to-all-start.1) | async-done | bytes 4194336 | tf_op jit(solution)/shard_map/all_to_all | solution.py:79
  280.7 3.9 %fusion.15 = f32[128,2048]{1,0:T(8,128)} fusion(bf16[1024,2048]{1,0:T(8,128)(2,1)} %bitcast.11, f32[128,1024]{1,0:T(8,128)S(1)} %select_reduce_fusion), kind=kOutput, calls=%fused_computation.26 | convolution fusion | flops 537001984 | bytes 5767168 | tf_op jit(solution)/shard_map/dot_general | solution.py:87
  284.6 7.1 %fusion.23 = f32[128,2816]{1,0:T(8,128)} fusion(bf16[128,2048]{1,0:T(8,128)(2,1)S(1)} %copy-done.3, bf16[2048,2816]{1,0:T(8,128)(2,1)} %all-gather.3.cloned.1.call-done), kind=kOutput, calls=%fused_computation.59 | convolution fusion | flops 1476395008 | bytes 13500416 | tf_op jit(solution)/shard_map/dot_general | solution.py:90
  291.7 4.5 %convolution_add_fusion.1 = f32[128,2048]{1,0:T(8,128)S(1)} fusion(f32[128,2048]{1,0:T(8,128)} %copy-done.7, bf16[1408,2048]{1,0:T(8,128)(2,1)} %all-gather.5.cloned.1.call-done, f32[128,2816]{1,0:T(8,128)} %fusion.23), kind=kOutput, calls=%fused_computation.12 | convolution fusion | flops 739540992 | bytes 9306112 | tf_op jit(solution)/shard_map/dot_general | solution.py:98
  296.2 3.8 %fusion.8 = bf16[128,2048]{1,0:T(8,128)(2,1)} fusion(f32[128,2048]{1,0:T(8,128)S(1)} %convolution_add_fusion.1, f32[128,2048]{1,0:T(8,128)S(1)} %copy-done.6, bf16[1024,2048]{1,0:T(8,128)(2,1)} %bitcast.11, f32[128,1024]{1,0:T(8,128)S(1)} %copy-done.5), kind=kOutput, calls=%fused_computation.16 | convolution fusion | flops 538181632 | bytes 7340032 | tf_op jit(solution)/shard_map/dot_general | solution.py:88
  (37 shorter events, 0.3 us)
Async XLA Ops:
  6.5 164.6 %copy-start = (bf16[1,768,2048]{2,1,0:T(8,128)(2,1)S(1)}, bf16[1,768,2048]{2,1,0:T(8,128)(2,1)}, u32[]{:S(2)}) copy-start(bf16[1,768,2048]{2,1,0:T(8,128)(2,1)} %param.18) | copy-start | bytes 9437188
  6.5 278.1 %all-gather.3.cloned.1.call-start = ((), (), s32[]{:S(2)}) async-start(), calls=%async_computation.2 | async-start | bytes 12976128 | tf_op jit(solution)/shard_map/all_gather | solution.py:92
  7.3 15.3 %collective-permute-start = (bf16[128,2048]{1,0:T(8,128)(2,1)}, bf16[128,2048]{1,0:T(8,128)(2,1)}, u32[]{:S(2)}, u32[]{:S(2)}) collective-permute-start(bf16[128,2048]{1,0:T(8,128)(2,1)} %param.12), channel_id=1, source_target_pairs={{0,64},{32,96},{64,128},{96,160},{128,192},{160,224},{192,0},{224,... | collective-permute-start | bytes 1572872 | tf_op jit(solution)/shard_map/ppermute | solution.py:23
  8.9 19.4 %collective-permute-start.1 = (bf16[128,2048]{1,0:T(8,128)(2,1)}, bf16[128,2048]{1,0:T(8,128)(2,1)}, u32[]{:S(2)}, u32[]{:S(2)}) collective-permute-start(bf16[128,2048]{1,0:T(8,128)(2,1)} %param.12), channel_id=1, source_target_pairs={{0,192},{32,224},{64,0},{96,32},{128,64},{160,96},{192,128},{224,1... | collective-permute-start | bytes 1572872 | tf_op jit(solution)/shard_map/ppermute | solution.py:23
  10.6 31.1 %collective-permute-start.2 = (bf16[128,2048]{1,0:T(8,128)(2,1)}, bf16[128,2048]{1,0:T(8,128)(2,1)}, u32[]{:S(2)}, u32[]{:S(2)}) collective-permute-start(bf16[128,2048]{1,0:T(8,128)(2,1)} %param.12), channel_id=1, source_target_pairs={{0,128},{32,160},{64,192},{96,224},{128,0},{160,32},{192,64},{224,... | collective-permute-start | bytes 1572872 | tf_op jit(solution)/shard_map/ppermute | solution.py:23
  16.0 28.8 %copy-start.8 = (bf16[128,2048]{1,0:T(8,128)(2,1)S(1)}, bf16[128,2048]{1,0:T(8,128)(2,1)}, u32[]{:S(2)}) copy-start(bf16[128,2048]{1,0:T(8,128)(2,1)} %param.12) | copy-start | bytes 1572868
  43.4 4.8 %collective-permute-start.3 = (bf16[4,128,2048]{2,1,0:T(8,128)(2,1)S(1)}, bf16[4,128,2048]{2,1,0:T(8,128)(2,1)S(1)}, u32[]{:S(2)}, u32[]{:S(2)}) collective-permute-start(bf16[4,128,2048]{2,1,0:T(8,128)(2,1)S(1)} %pad_maximum_fusion), channel_id=1, source_target_pairs={{0,32},{32,0},{64,96},{96,64},{128,160},{160,128},{192,224},{224,1... | collective-permute-start | bytes 6291464 | tf_op jit(solution)/shard_map/ppermute | solution.py:25
  44.8 3.7 %copy-start.9 = (bf16[128,2048]{1,0:T(8,128)(2,1)S(1)}, bf16[128,2048]{1,0:T(8,128)(2,1)}, u32[]{:S(2)}) copy-start(bf16[128,2048]{1,0:T(8,128)(2,1)} %param.11) | copy-start | bytes 1572868
  48.2 2.2 copy-start.12
  49.4 1.0 copy-start.7
  50.6 0.8 copy-start.2
  54.7 106.4 %all-to-all-start = ((bf16[32,32,2048]{2,1,0:T(8,128)(2,1)}), bf16[32,32,2048]{2,1,0:T(8,128)(2,1)}, u32[]{:S(2)}, u32[]{:S(2)}) async-start(bf16[32,32,2048]{2,1,0:T(8,128)(2,1)} %bitcast.51), calls=%async_computation | async-start | bytes 8388608 | tf_op jit(solution)/shard_map/all_to_all | solution.py:77
  67.2 224.5 %all-gather.5.cloned.1.call-start = ((), (), s32[]{:S(2)}) async-start(), calls=%async_computation.3 | async-start | bytes 6488064 | tf_op jit(solution)/shard_map/all_gather | solution.py:100
  176.2 9.6 %copy-start.3 = (bf16[128,2048]{1,0:T(8,128)(2,1)S(1)}, bf16[128,2048]{1,0:T(8,128)(2,1)}, u32[]{:S(2)}) copy-start(bf16[128,2048]{1,0:T(8,128)(2,1)} %copy-done.2) | copy-start | bytes 1572868
  176.2 9.6 %copy-start.10 = (bf16[2048,32]{0,1:T(8,128)(2,1)S(1)}, bf16[2048,32]{0,1:T(8,128)(2,1)}, u32[]{:S(2)}) copy-start(bf16[2048,32]{0,1:T(8,128)(2,1)} %param.14) | copy-start | bytes 393220
  176.2 9.9 %copy-start.11 = (s32[128,6]{0,1:T(8,128)S(1)}, s32[128,6]{0,1:T(8,128)}, u32[]{:S(2)}) copy-start(s32[128,6]{0,1:T(8,128)} %param.19) | copy-start | bytes 9220
  176.2 104.5 %all-to-all-start.1 = ((bf16[32,32,2048]{2,1,0:T(8,128)(2,1)}), bf16[32,32,2048]{2,1,0:T(8,128)(2,1)}, u32[]{:S(2)}, u32[]{:S(2)}) async-start(bf16[32,32,2048]{2,1,0:T(8,128)(2,1)} %bitcast.53), calls=%async_computation.1 | async-start | bytes 8388608 | tf_op jit(solution)/shard_map/all_to_all | solution.py:79
  186.6 105.1 %copy-start.4 = (f32[128,1024]{1,0:T(8,128)}, f32[128,1024]{1,0:T(8,128)S(1)}, u32[]{:S(2)}) copy-start(f32[128,1024]{1,0:T(8,128)S(1)} %select_reduce_fusion) | copy-start | bytes 1572868
  291.7 4.5 %copy-start.5 = (f32[128,1024]{1,0:T(8,128)S(1)}, f32[128,1024]{1,0:T(8,128)}, u32[]{:S(2)}) copy-start(f32[128,1024]{1,0:T(8,128)} %copy-done.4) | copy-start | bytes 1572868
  291.7 4.5 %copy-start.6 = (f32[128,2048]{1,0:T(8,128)S(1)}, f32[128,2048]{1,0:T(8,128)}, u32[]{:S(2)}) copy-start(f32[128,2048]{1,0:T(8,128)} %fusion.15) | copy-start | bytes 3145732
  291.7 8.3 %copy-start.1 = (bf16[1,768,2048]{2,1,0:T(8,128)(2,1)S(1)}, bf16[1,768,2048]{2,1,0:T(8,128)(2,1)}, u32[]{:S(2)}) copy-start(bf16[1,768,2048]{2,1,0:T(8,128)(2,1)} %param.18) | copy-start | bytes 9437188
Sparse Core Ops, SparseCore 0:
  9.2 73.9 all-gather.2
  85.0 46.3 all-gather.4

commit v5 on v4

--- a/solution.py
+++ b/solution.py
@@ -46,6 +46,9 @@
     capacity = 4 * tok_rows * picks // (3 * experts)
     slots = experts * capacity
     w_perm, order = gather_rows_by_chip(attn_out_w)
+    w_perm, shared_in, shared_out = lax.optimization_barrier((w_perm, shared_in, shared_out))
+    shared_in = lax.all_gather(shared_in, "group", axis=0, tiled=True)
+    shared_out = lax.all_gather(shared_out, "group", axis=1, tiled=True)
     block = attn_out_w.shape[0]
     ctx_perm = jnp.concatenate(
         [lax.dynamic_slice_in_dim(context, b * block, block, axis=1) for b in order], axis=1
@@ -76,8 +79,10 @@
     local_out = expert_out_w[0]
     arrived = lax.all_to_all(outgoing, "expert", split_axis=0, concat_axis=0, tiled=True)
     flat_rows = arrived.reshape(-1, width)
+    expert_rows = swiglu_rows(flat_rows, local_in, local_out).astype(jnp.bfloat16)
+    expert_rows, shared_in, shared_out = lax.optimization_barrier((expert_rows, shared_in, shared_out))
     returned = lax.all_to_all(
-        swiglu_rows(flat_rows, local_in, local_out).astype(jnp.bfloat16).reshape(arrived.shape),
+        expert_rows.reshape(arrived.shape),
         "expert",
         split_axis=0,
         concat_axis=0,
@@ -89,7 +94,7 @@
     shared_hidden = shared_out.shape[0]
     shared_mid = jnp.dot(
         normed,
-        lax.all_gather(shared_in, "group", axis=0, tiled=True),
+        shared_in,
         preferred_element_type=jnp.float32,
     )
     shared_act = (
@@ -97,7 +102,7 @@
     ).astype(jnp.bfloat16)
     shared_y = jnp.dot(
         shared_act,
-        lax.all_gather(shared_out, "group", axis=1, tiled=True),
+        shared_out,
         preferred_element_type=jnp.float32,
     )
     return (hidden_f + shared_y + routed).astype(jnp.bfloat16)

time: 310 us -> 291 us (0.939)
  blocking collectives: 0 us -> 106 us
  waiting for transfers between devices: 208 us -> 108 us
  starting transfers between devices: 27.5 us -> 12 us
  matrix products: 38.9 us -> 31.7 us
    all_to_all x0 -> x1, blocking collectives: none -> 106 us  [per_device(): lax.all_to_all(outgoing, 'expert', split_axis=0, concat_axis=0, tiled=True)]
    all_to_all x2 -> x1, waiting for transfers between devices: 187 us -> 84.1 us  [per_device(): lax.all_to_all(expert_rows.reshape(arrived.shape), 'expert', split_axis=0...]
    all_to_all x2 -> x1, starting transfers between devices: 22.1 us -> 6.65 us  [per_device(): lax.all_to_all(expert_rows.reshape(arrived.shape), 'expert', split_axis=0...]
    dot_general x2, matrix products: 11.6 us -> 8.19 us  [the longest x1 6.18 us: per_device(): shared_mid = jnp.dot(normed, shared_in, preferred_element_type=jnp.float32)]
    dot_general x1, matrix products: 10 us -> 6.64 us  [swiglu_rows(): mid = jnp.dot(rows, w_in, preferred_element_type=jnp.float32)]
    unnamed x38 -> x44, local copies, waits for them, and re-layouts: 11.5 us -> 9.92 us
  transfers between devices with their start and end apart: 8 -> 7, of which waited for: 5 -> 5; matrix products, arithmetic and copies ran while one was open for 15% -> 13% of each run, Pallas kernels for 0% -> 0%
where the time goes in v5:
time: 291 us; the launch traced here: 290 us
  waiting for transfers between devices  108 us (37%)
  blocking collectives  106 us (36%)
  matrix products  31.7 us (11%)
  between operations  13.8 us (5%)
  local copies, waits for them, and re-layouts  12.9 us (4%)
  starting transfers between devices  12 us (4%)
  other arithmetic  5.14 us (2%)
    all_to_all x1, blocking collectives, per_device(): lax.all_to_all(outgoing, 'expert', split_axis=0, concat_axis=0, tiled=True)  106 us
    all_to_all x1, waiting for transfers between devices, per_device(): lax.all_to_all(expert_rows.reshape(arrived.shape), 'expert', split_axis=0...  84.1 us
    ppermute x3, waiting for transfers between devices, gather_rows_by_chip(): got.append(lax.ppermute(w, 'group', pairs))  22.3 us
    unnamed x44, local copies, waits for them, and re-layouts  9.92 us
    all_to_all x1, starting transfers between devices, per_device(): lax.all_to_all(expert_rows.reshape(arrived.shape), 'expert', split_axis=0...  6.65 us
    dot_general x1, matrix products, swiglu_rows(): mid = jnp.dot(rows, w_in, preferred_element_type=jnp.float32)  6.64 us
    dot_general x1, matrix products, per_device(): shared_mid = jnp.dot(normed, shared_in, preferred_element_type=jnp.float32)  6.18 us
  transfers between devices with their start and end apart: 7, of which 5 were waited for; matrix products, arithmetic and copies ran while one was open for 13% of the time, Pallas kernels for 0%

profile of v5, /device:TPU:32, one launch (start us, length us, event | category | flops | bytes accessed | tf_op | source)
XLA Modules:
  0.0 289.9 jit_solution(11533095339086568513)
XLA Ops:
  6.5 1.6 collective-permute-start
  8.1 1.7 collective-permute-start.1
  9.8 2.0 collective-permute-start.2
  11.8 10.0 %collective-permute-done = bf16[128,2048]{1,0:T(8,128)(2,1)S(1)} collective-permute-done((bf16[128,2048]{1,0:T(8,128)(2,1)}, bf16[128,2048]{1,0:T(8,128)(2,1)S(1)}, u32[]{:S(2)}, u32[]{:S(2)}) %collective-permute-start) | collective-permute-done | bytes 524320 | tf_op jit(solution)/shard_map/ppermute | solution.py:23
  21.7 10.7 %collective-permute-done.1 = bf16[128,2048]{1,0:T(8,128)(2,1)S(1)} collective-permute-done((bf16[128,2048]{1,0:T(8,128)(2,1)}, bf16[128,2048]{1,0:T(8,128)(2,1)S(1)}, u32[]{:S(2)}, u32[]{:S(2)}) %collective-permute-start.1) | collective-permute-done | bytes 524320 | tf_op jit(solution)/shard_map/ppermute | solution.py:23
  32.4 1.7 collective-permute-done.2
  34.1 1.3 pad_maximum_fusion
  35.4 0.1 collective-permute-start.3
  35.5 0.8 constant_dynamic-update-slice_fusion.4
  36.3 0.8 constant_dynamic-update-slice_fusion.3
  37.2 0.8 constant_dynamic-update-slice_fusion.2
  38.0 0.8 constant_dynamic-update-slice_fusion.1
  38.9 0.8 collective-permute-done.3
  39.7 1.5 constant_dynamic-update-slice_fusion
  41.1 0.0 all-gather.3.cloned.1.call-start
  41.2 0.7 all-gather.3.cloned.1.call-update
  42.0 0.1 copy.27
  42.2 0.1 eq.61
  42.3 0.1 eq.65
  42.4 1.7 reduce-window.6
  44.2 0.3 slice_reduce_fusion
  44.5 0.1 fusion.19
  44.6 0.1 reduce_sum.49
  44.7 0.1 copy.30
  44.8 0.8 dynamic-slice_dynamic-update-slice_fusion.7
  45.6 0.8 dynamic-slice_dynamic-update-slice_fusion.6
  46.4 0.8 dynamic-slice_dynamic-update-slice_fusion.5
  47.1 0.8 dynamic-slice_dynamic-update-slice_fusion.4
  47.9 0.8 dynamic-slice_dynamic-update-slice_fusion.3
  48.7 0.8 dynamic-slice_dynamic-update-slice_fusion.2
  49.4 0.8 dynamic-slice_dynamic-update-slice_fusion.1
  50.2 0.8 dynamic-slice_dynamic-update-slice_fusion
  51.0 0.5 fusion.4
  51.5 3.2 %multiply_reduce_fusion = (f32[128]{0:T(128)S(1)}, f32[128,2048]{1,0:T(8,128)S(1)}) fusion(bf16[128,1024]{1,0:T(8,128)(2,1)S(1)} %dynamic-slice_dynamic-update-slice_fusion, bf16[1024,2048]{1,0:T(8,128)(2,1)} %bitcast.4, bf16[128,2048]{1,0:T(8,128)(2,1)} %param.11), kind=kOutput, calls=%fused_computation.20 | convolution fusion | flops 538443648 | bytes 6029824 | tf_op jit(solution)/shard_map/dot_general | solution.py:56
  54.7 1.0 copy-done.5
  55.7 0.2 multiply_convert_fusion
  55.9 1.3 convolution_convert_fusion.1
  57.2 106.4 %all_to_all.10 = bf16[32,32,2048]{2,1,0:T(8,128)(2,1)S(1)} all-to-all(bf16[32,32,2048]{2,1,0:T(8,128)(2,1)S(1)} %bitcast.51), channel_id=1, replica_groups=mesh['group'=8,'expert'=32] {'expert'}, dimensions={0} | all-to-all | bytes 8388608 | tf_op jit(solution)/shard_map/all_to_all | solution.py:80
  163.6 6.6 %fusion = f32[1024,1536]{1,0:T(8,128)S(1)} fusion(bf16[1024,2048]{1,0:T(8,128)(2,1)S(1)} %bitcast.53, bf16[1,2048,1536]{2,1,0:T(8,128)(2,1)S(1)} %bitcast.60), kind=kOutput, calls=%fused_computation | convolution fusion | flops 6442450944 | bytes 16777216 | tf_op jit(solution)/shard_map/dot_general | solution.py:9
  170.3 5.1 %convolution_convert_fusion = bf16[1024,2048]{1,0:T(8,128)(2,1)} fusion(bf16[1,768,2048]{2,1,0:T(8,128)(2,1)S(1)} %copy-done, f32[1024,1536]{1,0:T(8,128)S(1)} %fusion), kind=kOutput, calls=%fused_computation.2 | convolution fusion | flops 3228041216 | bytes 13631488 | tf_op jit(solution)/shard_map/dot_general | solution.py:11
  175.4 6.6 %all-to-all-start.1 = ((bf16[32,32,2048]{2,1,0:T(8,128)(2,1)}), bf16[32,32,2048]{2,1,0:T(8,128)(2,1)}, u32[]{:S(2)}, u32[]{:S(2)}) async-start(bf16[32,32,2048]{2,1,0:T(8,128)(2,1)} %bitcast.52), calls=%async_computation.1 | async-start | bytes 8388608 | tf_op jit(solution)/shard_map/all_to_all | solution.py:84
  182.1 0.3 fusion.24
  182.4 1.2 select_reduce_fusion
  183.7 6.2 %fusion.23 = f32[128,2816]{1,0:T(8,128)S(1)} fusion(bf16[128,2048]{1,0:T(8,128)(2,1)S(1)} %copy-done.3, bf16[2048,2816]{1,0:T(8,128)(2,1)} %all-gather.3.cloned.1.call-done), kind=kOutput, calls=%fused_computation.59 | convolution fusion | flops 1476395008 | bytes 13500416 | tf_op jit(solution)/shard_map/dot_general | solution.py:95
  189.9 2.0 convolution_add_fusion.1
  191.9 84.1 %all-to-all-done.1 = bf16[32,32,2048]{2,1,0:T(8,128)(2,1)} async-done(((bf16[32,32,2048]{2,1,0:T(8,128)(2,1)}), bf16[32,32,2048]{2,1,0:T(8,128)(2,1)}, u32[]{:S(2)}, u32[]{:S(2)}) %all-to-all-start.1) | async-done | bytes 4194336 | tf_op jit(solution)/shard_map/all_to_all | solution.py:84
  276.0 3.2 %fusion.15 = f32[128,2048]{1,0:T(8,128)S(1)} fusion(bf16[1024,2048]{1,0:T(8,128)(2,1)} %bitcast.11, f32[128,1024]{1,0:T(8,128)} %select_reduce_fusion), kind=kOutput, calls=%fused_computation.26 | convolution fusion | flops 537001984 | bytes 5767168 | tf_op jit(solution)/shard_map/dot_general | solution.py:92
  279.3 3.8 %fusion.8 = bf16[128,2048]{1,0:T(8,128)(2,1)} fusion(f32[128,2048]{1,0:T(8,128)S(1)} %copy-done.8, f32[128,2048]{1,0:T(8,128)S(1)} %fusion.15, bf16[1024,2048]{1,0:T(8,128)(2,1)} %bitcast.11, f32[128,1024]{1,0:T(8,128)S(1)} %copy-done.4), kind=kOutput, calls=%fused_computation.16 | convolution fusion | flops 538181632 | bytes 7340032 | tf_op jit(solution)/shard_map/dot_general | solution.py:93
  (44 shorter events, 0.2 us)
Async XLA Ops:
  6.5 163.7 %copy-start = (bf16[1,768,2048]{2,1,0:T(8,128)(2,1)S(1)}, bf16[1,768,2048]{2,1,0:T(8,128)(2,1)}, u32[]{:S(2)}) copy-start(bf16[1,768,2048]{2,1,0:T(8,128)(2,1)} %param.18) | copy-start | bytes 9437188
  6.5 168.9 %all-gather.5.cloned.1.call-start = ((), (), s32[]{:S(2)}) async-start(), calls=%async_computation.3 | async-start | bytes 6488064 | tf_op jit(solution)/shard_map/all_gather | solution.py:51
  6.5 29.0 %copy-start.7 = (bf16[128,2048]{1,0:T(8,128)(2,1)S(1)}, bf16[128,2048]{1,0:T(8,128)(2,1)}, u32[]{:S(2)}) copy-start(bf16[128,2048]{1,0:T(8,128)(2,1)} %param.12) | copy-start | bytes 1572868
  6.5 15.2 %collective-permute-start = (bf16[128,2048]{1,0:T(8,128)(2,1)}, bf16[128,2048]{1,0:T(8,128)(2,1)S(1)}, u32[]{:S(2)}, u32[]{:S(2)}) collective-permute-start(bf16[128,2048]{1,0:T(8,128)(2,1)} %param.12), channel_id=1, source_target_pairs={{0,64},{32,96},{64,128},{96,160},{128,192},{160,224},{192,0},{224,... | collective-permute-start | bytes 1572872 | tf_op jit(solution)/shard_map/ppermute | solution.py:23
  8.1 24.3 %collective-permute-start.1 = (bf16[128,2048]{1,0:T(8,128)(2,1)}, bf16[128,2048]{1,0:T(8,128)(2,1)S(1)}, u32[]{:S(2)}, u32[]{:S(2)}) collective-permute-start(bf16[128,2048]{1,0:T(8,128)(2,1)} %param.12), channel_id=1, source_target_pairs={{0,192},{32,224},{64,0},{96,32},{128,64},{160,96},{192,128},{224,1... | collective-permute-start | bytes 1572872 | tf_op jit(solution)/shard_map/ppermute | solution.py:23
  9.8 24.3 %collective-permute-start.2 = (bf16[128,2048]{1,0:T(8,128)(2,1)}, bf16[128,2048]{1,0:T(8,128)(2,1)S(1)}, u32[]{:S(2)}, u32[]{:S(2)}) collective-permute-start(bf16[128,2048]{1,0:T(8,128)(2,1)} %param.12), channel_id=1, source_target_pairs={{0,128},{32,160},{64,192},{96,224},{128,0},{160,32},{192,64},{224,... | collective-permute-start | bytes 1572872 | tf_op jit(solution)/shard_map/ppermute | solution.py:23
  35.4 4.2 %collective-permute-start.3 = (bf16[4,128,2048]{2,1,0:T(8,128)(2,1)S(1)}, bf16[4,128,2048]{2,1,0:T(8,128)(2,1)S(1)}, u32[]{:S(2)}, u32[]{:S(2)}) collective-permute-start(bf16[4,128,2048]{2,1,0:T(8,128)(2,1)S(1)} %pad_maximum_fusion), channel_id=1, source_target_pairs={{0,32},{32,0},{64,96},{96,64},{128,160},{160,128},{192,224},{224,1... | collective-permute-start | bytes 6291464 | tf_op jit(solution)/shard_map/ppermute | solution.py:25
  37.2 4.8 %copy-start.10 = (s32[128,6]{0,1:T(8,128)S(1)}, s32[128,6]{0,1:T(8,128)}, u32[]{:S(2)}) copy-start(s32[128,6]{0,1:T(8,128)} %param.19) | copy-start | bytes 9220
  41.1 134.3 %all-gather.3.cloned.1.call-start = ((), (), s32[]{:S(2)}) async-start(), calls=%async_computation.2 | async-start | bytes 12976128 | tf_op jit(solution)/shard_map/all_gather | solution.py:50
  41.9 13.8 %copy-start.11 = (f32[2048]{0:T(1024)S(1)}, f32[2048]{0:T(1024)}, u32[]{:S(2)}) copy-start(f32[2048]{0:T(1024)} %param.13) | copy-start | bytes 24580
  54.7 1.0 copy-start.5
  55.8 107.7 %copy-start.2 = (bf16[128,2048]{1,0:T(8,128)(2,1)}, bf16[128,2048]{1,0:T(8,128)(2,1)S(1)}, u32[]{:S(2)}) copy-start(bf16[128,2048]{1,0:T(8,128)(2,1)S(1)} %multiply_convert_fusion) | copy-start | bytes 1572868
  55.9 107.7 %slice-start = ((s8[6291456]{0:T(1024)(128)(4,1)}), s8[4194304]{0:T(1024)(128)(4,1)S(1)}, s32[]{:S(2)}) async-start(s8[6291456]{0:T(1024)(128)(4,1)} %bitcast.59), calls=%async_computation.4 | async-start | bytes 8388608
  57.2 106.4 %slice-start.1 = ((s8[6291456]{0:T(1024)(128)(4,1)}), s8[2097152]{0:T(1024)(128)(4,1)S(1)}, s32[]{:S(2)}) async-start(s8[6291456]{0:T(1024)(128)(4,1)} %bitcast.59), calls=%async_computation.5 | async-start | bytes 4194304
  175.4 6.7 %copy-start.3 = (bf16[128,2048]{1,0:T(8,128)(2,1)S(1)}, bf16[128,2048]{1,0:T(8,128)(2,1)}, u32[]{:S(2)}) copy-start(bf16[128,2048]{1,0:T(8,128)(2,1)} %copy-done.2) | copy-start | bytes 1572868
  175.4 6.7 %copy-start.9 = (bf16[2048,32]{0,1:T(8,128)(2,1)S(1)}, bf16[2048,32]{0,1:T(8,128)(2,1)}, u32[]{:S(2)}) copy-start(bf16[2048,32]{0,1:T(8,128)(2,1)} %param.14) | copy-start | bytes 393220
  175.4 100.6 %all-to-all-start.1 = ((bf16[32,32,2048]{2,1,0:T(8,128)(2,1)}), bf16[32,32,2048]{2,1,0:T(8,128)(2,1)}, u32[]{:S(2)}, u32[]{:S(2)}) async-start(bf16[32,32,2048]{2,1,0:T(8,128)(2,1)} %bitcast.52), calls=%async_computation.1 | async-start | bytes 8388608 | tf_op jit(solution)/shard_map/all_to_all | solution.py:84
  182.4 7.4 %slice-start.2 = ((s8[5767168]{0:T(1024)(128)(4,1)}), s8[4194304]{0:T(1024)(128)(4,1)S(1)}, s32[]{:S(2)}) async-start(s8[5767168]{0:T(1024)(128)(4,1)} %bitcast.61), calls=%async_computation.6 | async-start | bytes 8388608
  183.7 6.2 %copy-start.6 = (f32[128,2048]{1,0:T(8,128)S(1)}, f32[128,2048]{1,0:T(8,128)}, u32[]{:S(2)}) copy-start(f32[128,2048]{1,0:T(8,128)} %copy-done.5) | copy-start | bytes 3145732
  183.7 6.2 %slice-start.3 = ((s8[5767168]{0:T(1024)(128)(4,1)}), s8[1572864]{0:T(1024)(128)(4,1)S(1)}, s32[]{:S(2)}) async-start(s8[5767168]{0:T(1024)(128)(4,1)} %bitcast.61), calls=%async_computation.7 | async-start | bytes 3145728
  276.0 3.2 %copy-start.4 = (f32[128,1024]{1,0:T(8,128)S(1)}, f32[128,1024]{1,0:T(8,128)}, u32[]{:S(2)}) copy-start(f32[128,1024]{1,0:T(8,128)} %select_reduce_fusion) | copy-start | bytes 1572868
  276.0 3.2 %copy-start.8 = (f32[128,2048]{1,0:T(8,128)S(1)}, f32[128,2048]{1,0:T(8,128)}, u32[]{:S(2)}) copy-start(f32[128,2048]{1,0:T(8,128)} %convolution_add_fusion.1) | copy-start | bytes 3145732
  276.0 7.1 %copy-start.1 = (bf16[1,768,2048]{2,1,0:T(8,128)(2,1)S(1)}, bf16[1,768,2048]{2,1,0:T(8,128)(2,1)}, u32[]{:S(2)}) copy-start(bf16[1,768,2048]{2,1,0:T(8,128)(2,1)} %param.18) | copy-start | bytes 9437188
Sparse Core Ops, SparseCore 0:
  41.3 46.5 all-gather.4
  89.7 66.4 all-gather.2

commit v6 on v5

--- a/solution.py
+++ b/solution.py
@@ -16,15 +16,24 @@
     ring = groups // 2
     g = lax.axis_index("group")
     y, c = g // 2, g % 2
-    shifts = [0] + sorted(range(1, ring), key=lambda s: min(s, ring - s))
-    got = [w]
-    for s in shifts[1:]:
+
+    def shift(x, s):
         pairs = [(2 * q + k, 2 * ((q + s) % ring) + k) for q in range(ring) for k in range(2)]
-        got.append(lax.ppermute(w, "group", pairs))
-    mine = jnp.stack(got)
-    sib = lax.ppermute(mine, "group", [(i, i ^ 1) for i in range(groups)])
-    order = [2 * ((y - s) % ring) + c for s in shifts] + [2 * ((y - s) % ring) + 1 - c for s in shifts]
-    return jnp.concatenate([mine, sib]).reshape(-1, w.shape[1]), order
+        return lax.ppermute(x, "group", pairs)
+
+    def sib(x):
+        return lax.ppermute(x, "group", [(i, i ^ 1) for i in range(groups)])
+
+    half = w.shape[0] // 2
+    from_left = shift(w, 1)
+    from_right = shift(w, -1)
+    far = jnp.concatenate(
+        [shift(from_right[:half], -1), shift(from_left[half:], 1)], axis=0
+    )
+    pieces = [w, from_left, from_right, far, sib(w), sib(from_left), sib(from_right), sib(far)]
+    ys = [y, y - 1, y + 1, y + 2]
+    order = [2 * (q % ring) + c for q in ys] + [2 * (q % ring) + 1 - c for q in ys]
+    return pieces, order
 
 
 def per_device(
@@ -45,15 +54,21 @@
     experts = lax.axis_size("expert")
     capacity = 4 * tok_rows * picks // (3 * experts)
     slots = experts * capacity
-    w_perm, order = gather_rows_by_chip(attn_out_w)
-    w_perm, shared_in, shared_out = lax.optimization_barrier((w_perm, shared_in, shared_out))
+    if lax.axis_size("group") == 8:
+        pieces, order = gather_rows_by_chip(attn_out_w)
+    else:
+        pieces = [lax.all_gather(attn_out_w, "group", axis=0, tiled=True)]
+        order = [0]
+    pieces, shared_in, shared_out = lax.optimization_barrier((pieces, shared_in, shared_out))
     shared_in = lax.all_gather(shared_in, "group", axis=0, tiled=True)
     shared_out = lax.all_gather(shared_out, "group", axis=1, tiled=True)
-    block = attn_out_w.shape[0]
-    ctx_perm = jnp.concatenate(
-        [lax.dynamic_slice_in_dim(context, b * block, block, axis=1) for b in order], axis=1
-    )
-    attn = jnp.dot(ctx_perm, w_perm, preferred_element_type=jnp.float32)
+    block = pieces[0].shape[0]
+    ctx_blocks = context.reshape(tok_rows, -1, block)
+    ctx_perm = jnp.take(ctx_blocks, jnp.stack(order), axis=1)
+    attn = None
+    for i, piece in enumerate(pieces):
+        term = jnp.dot(ctx_perm[:, i, :], piece, preferred_element_type=jnp.float32)
+        attn = term if attn is None else attn + term
     hidden_state = (residual.astype(jnp.float32) + attn).astype(jnp.bfloat16)
     hidden_f = hidden_state.astype(jnp.float32)
     scale = lax.rsqrt(jnp.mean(hidden_f * hidden_f, axis=-1, keepdims=True) + 1e-06)

time: 291 us -> 285 us (0.979)
  local copies, waits for them, and re-layouts: 12.9 us -> 7.44 us
  waiting for transfers between devices: 108 us -> 104 us
    unnamed x44 -> x59, local copies, waits for them, and re-layouts: 9.92 us -> 4.07 us
    ppermute x4 -> x8, waiting for transfers between devices: 23.1 us -> 19.1 us  [the longest x4 18.9 us: shift(): return lax.ppermute(x, 'group', pairs)]
    ppermute x4 -> x8, starting transfers between devices: 5.31 us -> 7.55 us  [the longest x4 6.76 us: shift(): return lax.ppermute(x, 'group', pairs)]
  transfers between devices with their start and end apart: 7 -> 11, of which waited for: 5 -> 5; matrix products, arithmetic and copies ran while one was open for 13% -> 12% of each run, Pallas kernels for 0% -> 0%
where the time goes in v6:
time: 285 us; the launch traced here: 283 us
  blocking collectives  106 us (37%)
  waiting for transfers between devices  104 us (36%)
  matrix products  33.4 us (12%)
  starting transfers between devices  14.2 us (5%)
  between operations  14 us (5%)
  local copies, waits for them, and re-layouts  7.44 us (3%)
  other arithmetic  3.94 us (1%)
    all_to_all x1, blocking collectives, per_device(): lax.all_to_all(outgoing, 'expert', split_axis=0, concat_axis=0, tiled=True)  106 us
    all_to_all x1, waiting for transfers between devices, per_device(): lax.all_to_all(expert_rows.reshape(arrived.shape), 'expert', split_axis=0...  83.8 us
    ppermute x4, waiting for transfers between devices, shift(): return lax.ppermute(x, 'group', pairs)  18.9 us
    ppermute x4, starting transfers between devices, shift(): return lax.ppermute(x, 'group', pairs)  6.76 us
    all_to_all x1, starting transfers between devices, per_device(): lax.all_to_all(expert_rows.reshape(arrived.shape), 'expert', split_axis=0...  6.66 us
    dot_general x1, matrix products, swiglu_rows(): mid = jnp.dot(rows, w_in, preferred_element_type=jnp.float32)  6.64 us
    dot_general x1, matrix products, per_device(): shared_mid = jnp.dot(normed, shared_in, preferred_element_type=jnp.float32)  6.18 us
  transfers between devices with their start and end apart: 11, of which 5 were waited for; matrix products, arithmetic and copies ran while one was open for 12% of the time, Pallas kernels for 0%

profile of v6, /device:TPU:32, one launch (start us, length us, event | category | flops | bytes accessed | tf_op | source)
XLA Modules:
  0.0 282.9 jit_solution(4594844658367597479)
XLA Ops:
  6.5 3.0 %collective-permute-start.1 = (bf16[128,2048]{1,0:T(8,128)(2,1)}, bf16[128,2048]{1,0:T(8,128)(2,1)S(1)}, u32[]{:S(2)}, u32[]{:S(2)}) collective-permute-start(bf16[128,2048]{1,0:T(8,128)(2,1)} %param.12), channel_id=1, source_target_pairs={{0,192},{32,224},{64,0},{96,32},{128,64},{160,96},{192,128},{224,1... | collective-permute-start | bytes 1572872 | tf_op jit(solution)/shard_map/ppermute | solution.py:22
  9.6 11.5 %collective-permute-done.1 = bf16[128,2048]{1,0:T(8,128)(2,1)S(1)} collective-permute-done((bf16[128,2048]{1,0:T(8,128)(2,1)}, bf16[128,2048]{1,0:T(8,128)(2,1)S(1)}, u32[]{:S(2)}, u32[]{:S(2)}) %collective-permute-start.1) | collective-permute-done | bytes 524320 | tf_op jit(solution)/shard_map/ppermute | solution.py:22
  21.1 3.7 %collective-permute-start.2 = (bf16[64,2048]{1,0:T(8,128)(2,1)S(1)}, bf16[64,2048]{1,0:T(8,128)(2,1)S(1)}, u32[]{:S(2)}, u32[]{:S(2)}) collective-permute-start(bf16[64,2048]{1,0:T(8,128)(2,1)S(1)} %slice.67), channel_id=1, source_target_pairs={{0,192},{32,224},{64,0},{96,32},{128,64},{160,96},{192,128},{224,1... | collective-permute-start | bytes 786440 | tf_op jit(solution)/shard_map/ppermute | solution.py:22
  24.9 0.1 collective-permute-start.4
  25.0 0.5 collective-permute-start.5
  25.5 0.1 collective-permute-start.6
  25.6 3.9 %collective-permute-done.2 = bf16[64,2048]{1,0:T(8,128)(2,1)S(1)} collective-permute-done((bf16[64,2048]{1,0:T(8,128)(2,1)S(1)}, bf16[64,2048]{1,0:T(8,128)(2,1)S(1)}, u32[]{:S(2)}, u32[]{:S(2)}) %collective-permute-start.2) | collective-permute-done | bytes 262176 | tf_op jit(solution)/shard_map/ppermute | solution.py:22
  29.5 3.5 %collective-permute-done.3 = bf16[64,2048]{1,0:T(8,128)(2,1)S(1)} collective-permute-done((bf16[64,2048]{1,0:T(8,128)(2,1)S(1)}, bf16[64,2048]{1,0:T(8,128)(2,1)S(1)}, u32[]{:S(2)}, u32[]{:S(2)}) %collective-permute-start.3) | collective-permute-done | bytes 262176 | tf_op jit(solution)/shard_map/ppermute | solution.py:22
  33.1 0.6 copy-done.11
  33.8 0.2 copy-done.16
  34.0 0.2 copy-done.18
  34.1 0.8 copy-done.20
  34.9 0.2 collective-permute-done.7
  35.2 0.7 all-gather.3.cloned.1.call-update
  36.0 0.1 copy.40
  36.1 0.1 eq.61
  36.2 0.1 eq.65
  36.4 1.1 copy.38
  37.5 0.8 copy.39
  38.4 1.7 reduce-window.6
  40.1 0.3 slice_reduce_fusion
  40.4 0.1 fusion.26
  40.5 0.1 reduce_sum.49
  40.7 0.1 stack.62
  40.9 1.5 gather_fusion
  42.5 0.5 fusion.4
  43.1 1.4 fusion.28
  44.5 1.4 fusion.29
  46.0 0.3 fusion.30
  46.3 0.3 fusion.31
  46.6 0.3 fusion.32
  46.9 0.3 fusion.33
  47.2 0.3 fusion.34
  47.5 0.7 multiply_reduce_fusion
  48.2 0.9 copy-done.5
  49.2 0.2 multiply_convert_fusion
  49.3 1.3 convolution_convert_fusion.1
  50.7 106.3 %all_to_all.10 = bf16[32,32,2048]{2,1,0:T(8,128)(2,1)S(1)} all-to-all(bf16[32,32,2048]{2,1,0:T(8,128)(2,1)S(1)} %bitcast.95), channel_id=1, replica_groups=mesh['group'=8,'expert'=32] {'expert'}, dimensions={0} | all-to-all | bytes 8388608 | tf_op jit(solution)/shard_map/all_to_all | solution.py:95
  157.0 6.6 %fusion = f32[1024,1536]{1,0:T(8,128)S(1)} fusion(bf16[1024,2048]{1,0:T(8,128)(2,1)S(1)} %bitcast.97, bf16[1,2048,1536]{2,1,0:T(8,128)(2,1)S(1)} %bitcast.101), kind=kOutput, calls=%fused_computation.1 | convolution fusion | flops 6442450944 | bytes 16777216 | tf_op jit(solution)/shard_map/dot_general | solution.py:9
  163.6 5.1 %convolution_convert_fusion = bf16[1024,2048]{1,0:T(8,128)(2,1)} fusion(bf16[1,768,2048]{2,1,0:T(8,128)(2,1)S(1)} %copy-done, f32[1024,1536]{1,0:T(8,128)S(1)} %fusion), kind=kOutput, calls=%fused_computation.3 | convolution fusion | flops 3228041216 | bytes 13631488 | tf_op jit(solution)/shard_map/dot_general | solution.py:11
  168.7 6.7 %all-to-all-start.1 = ((bf16[32,32,2048]{2,1,0:T(8,128)(2,1)}), bf16[32,32,2048]{2,1,0:T(8,128)(2,1)}, u32[]{:S(2)}, u32[]{:S(2)}) async-start(bf16[32,32,2048]{2,1,0:T(8,128)(2,1)} %bitcast.96), calls=%async_computation.1 | async-start | bytes 8388608 | tf_op jit(solution)/shard_map/all_to_all | solution.py:99
  175.4 0.3 fusion.39
  175.7 1.2 select_reduce_fusion
  177.0 6.2 %fusion.38 = f32[128,2816]{1,0:T(8,128)S(1)} fusion(bf16[128,2048]{1,0:T(8,128)(2,1)S(1)} %copy-done.3, bf16[2048,2816]{1,0:T(8,128)(2,1)} %all-gather.3.cloned.1.call-done), kind=kOutput, calls=%fused_computation.76 | convolution fusion | flops 1476395008 | bytes 13500416 | tf_op jit(solution)/shard_map/dot_general | solution.py:110
  183.2 2.0 convolution_add_fusion.1
  185.2 83.8 %all-to-all-done.1 = bf16[32,32,2048]{2,1,0:T(8,128)(2,1)} async-done(((bf16[32,32,2048]{2,1,0:T(8,128)(2,1)}), bf16[32,32,2048]{2,1,0:T(8,128)(2,1)}, u32[]{:S(2)}, u32[]{:S(2)}) %all-to-all-start.1) | async-done | bytes 4194336 | tf_op jit(solution)/shard_map/all_to_all | solution.py:99
  269.0 3.2 %fusion.22 = f32[128,2048]{1,0:T(8,128)S(1)} fusion(bf16[1024,2048]{1,0:T(8,128)(2,1)} %bitcast.33, f32[128,1024]{1,0:T(8,128)} %select_reduce_fusion), kind=kOutput, calls=%fused_computation.34 | convolution fusion | flops 537001984 | bytes 5767168 | tf_op jit(solution)/shard_map/dot_general | solution.py:107
  272.3 3.8 %fusion.15 = bf16[128,2048]{1,0:T(8,128)(2,1)} fusion(f32[128,2048]{1,0:T(8,128)S(1)} %copy-done.13, f32[128,2048]{1,0:T(8,128)S(1)} %fusion.22, bf16[1024,2048]{1,0:T(8,128)(2,1)} %bitcast.33, f32[128,1024]{1,0:T(8,128)S(1)} %copy-done.4), kind=kOutput, calls=%fused_computation.24 | convolution fusion | flops 538181632 | bytes 7340032 | tf_op jit(solution)/shard_map/dot_general | solution.py:108
  (82 shorter events, 0.8 us)
Async XLA Ops:
  6.5 157.1 %copy-start = (bf16[1,768,2048]{2,1,0:T(8,128)(2,1)S(1)}, bf16[1,768,2048]{2,1,0:T(8,128)(2,1)}, u32[]{:S(2)}) copy-start(bf16[1,768,2048]{2,1,0:T(8,128)(2,1)} %param.18) | copy-start | bytes 9437188
  6.5 29.4 %copy-start.22 = (s32[128,6]{0,1:T(8,128)S(1)}, s32[128,6]{0,1:T(8,128)}, u32[]{:S(2)}) copy-start(s32[128,6]{0,1:T(8,128)} %param.19) | copy-start | bytes 9220
  6.5 162.2 %all-gather.5.cloned.1.call-start = ((), (), s32[]{:S(2)}) async-start(), calls=%async_computation.3 | async-start | bytes 6488064 | tf_op jit(solution)/shard_map/all_gather | solution.py:64
  6.5 14.5 %collective-permute-start.1 = (bf16[128,2048]{1,0:T(8,128)(2,1)}, bf16[128,2048]{1,0:T(8,128)(2,1)S(1)}, u32[]{:S(2)}, u32[]{:S(2)}) collective-permute-start(bf16[128,2048]{1,0:T(8,128)(2,1)} %param.12), channel_id=1, source_target_pairs={{0,192},{32,224},{64,0},{96,32},{128,64},{160,96},{192,128},{224,1... | collective-permute-start | bytes 1572872 | tf_op jit(solution)/shard_map/ppermute | solution.py:22
  9.6 15.2 %collective-permute-start = (bf16[128,2048]{1,0:T(8,128)(2,1)}, bf16[128,2048]{1,0:T(8,128)(2,1)S(1)}, u32[]{:S(2)}, u32[]{:S(2)}) collective-permute-start(bf16[128,2048]{1,0:T(8,128)(2,1)} %param.12), channel_id=1, source_target_pairs={{0,64},{32,96},{64,128},{96,160},{128,192},{160,224},{192,0},{224,... | collective-permute-start | bytes 1572872 | tf_op jit(solution)/shard_map/ppermute | solution.py:22
  21.1 4.4 %copy-start.7 = (bf16[128,2048]{1,0:T(8,128)(2,1)}, bf16[128,2048]{1,0:T(8,128)(2,1)S(1)}, u32[]{:S(2)}) copy-start(bf16[128,2048]{1,0:T(8,128)(2,1)S(1)} %collective-permute-done.1) | copy-start | bytes 1572868
  21.1 8.4 %collective-permute-start.2 = (bf16[64,2048]{1,0:T(8,128)(2,1)S(1)}, bf16[64,2048]{1,0:T(8,128)(2,1)S(1)}, u32[]{:S(2)}, u32[]{:S(2)}) collective-permute-start(bf16[64,2048]{1,0:T(8,128)(2,1)S(1)} %slice.67), channel_id=1, source_target_pairs={{0,192},{32,224},{64,0},{96,32},{128,64},{160,96},{192,128},{224,1... | collective-permute-start | bytes 786440 | tf_op jit(solution)/shard_map/ppermute | solution.py:22
  24.7 8.4 %copy-start.9 = (bf16[128,2048]{1,0:T(8,128)(2,1)}, bf16[128,2048]{1,0:T(8,128)(2,1)S(1)}, u32[]{:S(2)}) copy-start(bf16[128,2048]{1,0:T(8,128)(2,1)S(1)} %collective-permute-done) | copy-start | bytes 1572868
  24.8 8.2 %collective-permute-start.3 = (bf16[64,2048]{1,0:T(8,128)(2,1)S(1)}, bf16[64,2048]{1,0:T(8,128)(2,1)S(1)}, u32[]{:S(2)}, u32[]{:S(2)}) collective-permute-start(bf16[64,2048]{1,0:T(8,128)(2,1)S(1)} %slice.68), channel_id=1, source_target_pairs={{0,64},{32,96},{64,128},{96,160},{128,192},{160,224},{192,0},{224,... | collective-permute-start | bytes 786440 | tf_op jit(solution)/shard_map/ppermute | solution.py:22
  24.9 8.2 %collective-permute-start.4 = (bf16[128,2048]{1,0:T(8,128)(2,1)}, bf16[128,2048]{1,0:T(8,128)(2,1)S(1)}, u32[]{:S(2)}, u32[]{:S(2)}) collective-permute-start(bf16[128,2048]{1,0:T(8,128)(2,1)} %param.12), channel_id=1, source_target_pairs={{0,32},{32,0},{64,96},{96,64},{128,160},{160,128},{192,224},{224,1... | collective-permute-start | bytes 1572872 | tf_op jit(solution)/shard_map/ppermute | solution.py:25
  25.0 8.1 %collective-permute-start.5 = (bf16[128,2048]{1,0:T(8,128)(2,1)S(1)}, bf16[128,2048]{1,0:T(8,128)(2,1)S(1)}, u32[]{:S(2)}, u32[]{:S(2)}) collective-permute-start(bf16[128,2048]{1,0:T(8,128)(2,1)S(1)} %collective-permute-done), channel_id=1, source_target_pairs={{0,32},{32,0},{64,96},{96,64},{128,160},{160,128},{192,224},{224,1... | collective-permute-start | bytes 1572872 | tf_op jit(solution)/shard_map/ppermute | solution.py:25
  25.5 7.7 %collective-permute-start.6 = (bf16[128,2048]{1,0:T(8,128)(2,1)S(1)}, bf16[128,2048]{1,0:T(8,128)(2,1)S(1)}, u32[]{:S(2)}, u32[]{:S(2)}) collective-permute-start(bf16[128,2048]{1,0:T(8,128)(2,1)S(1)} %collective-permute-done.1), channel_id=1, source_target_pairs={{0,32},{32,0},{64,96},{96,64},{128,160},{160,128},{192,224},{224,1... | collective-permute-start | bytes 1572872 | tf_op jit(solution)/shard_map/ppermute | solution.py:25
  33.0 0.8 copy-start.11
  33.0 2.1 collective-permute-start.7
  33.1 0.9 copy-start.16
  33.1 1.0 copy-start.18
  34.1 0.8 copy-start.20
  35.1 133.6 %all-gather.3.cloned.1.call-start = ((), (), s32[]{:S(2)}) async-start(), calls=%async_computation.2 | async-start | bytes 12976128 | tf_op jit(solution)/shard_map/all_gather | solution.py:63
  42.5 3.4 %copy-start.19 = (bf16[128,2048]{1,0:T(8,128)(2,1)S(1)}, bf16[128,2048]{1,0:T(8,128)(2,1)}, u32[]{:S(2)}) copy-start(bf16[128,2048]{1,0:T(8,128)(2,1)} %copy-done.18) | copy-start | bytes 1572868
  42.5 3.7 %copy-start.17 = (bf16[128,2048]{1,0:T(8,128)(2,1)S(1)}, bf16[128,2048]{1,0:T(8,128)(2,1)}, u32[]{:S(2)}) copy-start(bf16[128,2048]{1,0:T(8,128)(2,1)} %copy-done.16) | copy-start | bytes 1572868
  42.5 4.0 %copy-start.12 = (bf16[128,2048]{1,0:T(8,128)(2,1)S(1)}, bf16[128,2048]{1,0:T(8,128)(2,1)}, u32[]{:S(2)}) copy-start(bf16[128,2048]{1,0:T(8,128)(2,1)} %copy-done.11) | copy-start | bytes 1572868
  43.0 3.8 %copy-start.8 = (bf16[128,2048]{1,0:T(8,128)(2,1)S(1)}, bf16[128,2048]{1,0:T(8,128)(2,1)}, u32[]{:S(2)}) copy-start(bf16[128,2048]{1,0:T(8,128)(2,1)} %copy-done.7) | copy-start | bytes 1572868
  44.5 2.6 copy-start.10
  45.9 1.5 copy-start.14
  45.9 1.5 copy-start.15
  47.5 1.7 copy-start.23
  48.2 1.0 copy-start.5
  49.3 107.6 %copy-start.2 = (bf16[128,2048]{1,0:T(8,128)(2,1)}, bf16[128,2048]{1,0:T(8,128)(2,1)S(1)}, u32[]{:S(2)}) copy-start(bf16[128,2048]{1,0:T(8,128)(2,1)S(1)} %multiply_convert_fusion) | copy-start | bytes 1572868
  49.3 107.6 %slice-start = ((s8[6291456]{0:T(1024)(128)(4,1)}), s8[4194304]{0:T(1024)(128)(4,1)S(1)}, s32[]{:S(2)}) async-start(s8[6291456]{0:T(1024)(128)(4,1)} %bitcast.100), calls=%async_computation.4 | async-start | bytes 8388608
  50.6 106.3 %slice-start.1 = ((s8[6291456]{0:T(1024)(128)(4,1)}), s8[2097152]{0:T(1024)(128)(4,1)S(1)}, s32[]{:S(2)}) async-start(s8[6291456]{0:T(1024)(128)(4,1)} %bitcast.100), calls=%async_computation.5 | async-start | bytes 4194304
  168.7 6.7 %copy-start.3 = (bf16[128,2048]{1,0:T(8,128)(2,1)S(1)}, bf16[128,2048]{1,0:T(8,128)(2,1)}, u32[]{:S(2)}) copy-start(bf16[128,2048]{1,0:T(8,128)(2,1)} %copy-done.2) | copy-start | bytes 1572868
  168.7 6.7 %copy-start.21 = (bf16[2048,32]{0,1:T(8,128)(2,1)S(1)}, bf16[2048,32]{0,1:T(8,128)(2,1)}, u32[]{:S(2)}) copy-start(bf16[2048,32]{0,1:T(8,128)(2,1)} %param.14) | copy-start | bytes 393220
  168.7 100.3 %all-to-all-start.1 = ((bf16[32,32,2048]{2,1,0:T(8,128)(2,1)}), bf16[32,32,2048]{2,1,0:T(8,128)(2,1)}, u32[]{:S(2)}, u32[]{:S(2)}) async-start(bf16[32,32,2048]{2,1,0:T(8,128)(2,1)} %bitcast.96), calls=%async_computation.1 | async-start | bytes 8388608 | tf_op jit(solution)/shard_map/all_to_all | solution.py:99
  175.7 7.4 %slice-start.2 = ((s8[5767168]{0:T(1024)(128)(4,1)}), s8[4194304]{0:T(1024)(128)(4,1)S(1)}, s32[]{:S(2)}) async-start(s8[5767168]{0:T(1024)(128)(4,1)} %bitcast.102), calls=%async_computation.6 | async-start | bytes 8388608
  177.0 6.2 %copy-start.6 = (f32[128,2048]{1,0:T(8,128)S(1)}, f32[128,2048]{1,0:T(8,128)}, u32[]{:S(2)}) copy-start(f32[128,2048]{1,0:T(8,128)} %copy-done.5) | copy-start | bytes 3145732
  177.0 6.2 %slice-start.3 = ((s8[5767168]{0:T(1024)(128)(4,1)}), s8[1572864]{0:T(1024)(128)(4,1)S(1)}, s32[]{:S(2)}) async-start(s8[5767168]{0:T(1024)(128)(4,1)} %bitcast.102), calls=%async_computation.7 | async-start | bytes 3145728
  269.0 3.2 %copy-start.4 = (f32[128,1024]{1,0:T(8,128)S(1)}, f32[128,1024]{1,0:T(8,128)}, u32[]{:S(2)}) copy-start(f32[128,1024]{1,0:T(8,128)} %select_reduce_fusion) | copy-start | bytes 1572868
  269.0 3.2 %copy-start.13 = (f32[128,2048]{1,0:T(8,128)S(1)}, f32[128,2048]{1,0:T(8,128)}, u32[]{:S(2)}) copy-start(f32[128,2048]{1,0:T(8,128)} %convolution_add_fusion.1) | copy-start | bytes 3145732
  269.0 7.1 %copy-start.1 = (bf16[1,768,2048]{2,1,0:T(8,128)(2,1)S(1)}, bf16[1,768,2048]{2,1,0:T(8,128)(2,1)}, u32[]{:S(2)}) copy-start(bf16[1,768,2048]{2,1,0:T(8,128)(2,1)} %param.18) | copy-start | bytes 9437188
Sparse Core Ops, SparseCore 0:
  35.3 45.2 all-gather.4
  82.4 66.5 all-gather.2

commit v7 on v6

--- a/solution.py
+++ b/solution.py
@@ -11,7 +11,7 @@
     return jnp.dot(act, w_out, preferred_element_type=jnp.float32)
 
 
-def gather_rows_by_chip(w):
+def gather_rows_by_chip(w, passenger):
     groups = lax.axis_size("group")
     ring = groups // 2
     g = lax.axis_index("group")
@@ -27,13 +27,20 @@
     half = w.shape[0] // 2
     from_left = shift(w, 1)
     from_right = shift(w, -1)
+    from_left, passenger = lax.optimization_barrier((from_left, passenger))
     far = jnp.concatenate(
         [shift(from_right[:half], -1), shift(from_left[half:], 1)], axis=0
     )
     pieces = [w, from_left, from_right, far, sib(w), sib(from_left), sib(from_right), sib(far)]
-    ys = [y, y - 1, y + 1, y + 2]
-    order = [2 * (q % ring) + c for q in ys] + [2 * (q % ring) + 1 - c for q in ys]
-    return pieces, order
+    return pieces, passenger
+
+
+def chip_gather_order():
+    ring = lax.axis_size("group") // 2
+    g = lax.axis_index("group")
+    y, c = g // 2, g % 2
+    ys = (y + jnp.array([0, -1, 1, 2], jnp.int32) + ring) % ring
+    return jnp.concatenate([2 * ys + c, 2 * ys + 1 - c])
 
 
 def per_device(
@@ -54,19 +61,38 @@
     experts = lax.axis_size("expert")
     capacity = 4 * tok_rows * picks // (3 * experts)
     slots = experts * capacity
-    if lax.axis_size("group") == 8:
-        pieces, order = gather_rows_by_chip(attn_out_w)
+    flat_e = routes.reshape(-1)
+    onehot = (flat_e[:, None] == jnp.arange(experts, dtype=jnp.int32)[None, :]).astype(jnp.int32)
+    rank = jnp.cumsum(onehot, axis=0) - onehot
+    position = jnp.sum(rank * onehot, axis=1)
+    slot_of = (flat_e * capacity + position).reshape(tok_rows, picks)
+    hit = slot_of[:, :, None] == jnp.arange(slots, dtype=jnp.int32)[None, None, :]
+    dispatch = jnp.any(hit, axis=1).astype(jnp.bfloat16)
+    block = attn_out_w.shape[0]
+    ctx_blocks = context.reshape(tok_rows, -1, block)
+    groups = lax.axis_size("group")
+    if groups == 8:
+        own = lax.axis_index("group")
+        first = jnp.dot(
+            lax.dynamic_index_in_dim(ctx_blocks, own, 1, keepdims=False),
+            attn_out_w,
+            preferred_element_type=jnp.float32,
+        )
+        ctx_perm = jnp.take(ctx_blocks, chip_gather_order(), axis=1)
+        pieces, (slot_of, dispatch, first, ctx_perm) = gather_rows_by_chip(
+            attn_out_w, (slot_of, dispatch, first, ctx_perm)
+        )
     else:
         pieces = [lax.all_gather(attn_out_w, "group", axis=0, tiled=True)]
-        order = [0]
+        ctx_perm = context[:, None, :]
+        first = None
     pieces, shared_in, shared_out = lax.optimization_barrier((pieces, shared_in, shared_out))
     shared_in = lax.all_gather(shared_in, "group", axis=0, tiled=True)
     shared_out = lax.all_gather(shared_out, "group", axis=1, tiled=True)
-    block = pieces[0].shape[0]
-    ctx_blocks = context.reshape(tok_rows, -1, block)
-    ctx_perm = jnp.take(ctx_blocks, jnp.stack(order), axis=1)
-    attn = None
+    attn = first
     for i, piece in enumerate(pieces):
+        if first is not None and i == 0:
+            continue
         term = jnp.dot(ctx_perm[:, i, :], piece, preferred_element_type=jnp.float32)
         attn = term if attn is None else attn + term
     hidden_state = (residual.astype(jnp.float32) + attn).astype(jnp.bfloat16)
@@ -78,15 +104,9 @@
     picked = jnp.sum(jnp.where(chosen, logits[:, None, :], 0.0), axis=-1)
     sig = jax.nn.sigmoid(picked)
     gates = sig / jnp.sum(sig, axis=1, keepdims=True)
-    flat_e = routes.reshape(-1)
-    onehot = (flat_e[:, None] == jnp.arange(experts, dtype=jnp.int32)[None, :]).astype(jnp.int32)
-    rank = jnp.cumsum(onehot, axis=0) - onehot
-    position = jnp.sum(rank * onehot, axis=1)
-    slot_of = (flat_e * capacity + position).reshape(tok_rows, picks)
-    hit = slot_of[:, :, None] == jnp.arange(slots, dtype=jnp.int32)[None, None, :]
-    dispatch = jnp.any(hit, axis=1).astype(jnp.bfloat16)
     outgoing = jnp.dot(dispatch.T, normed, preferred_element_type=jnp.float32)
     outgoing = outgoing.astype(jnp.bfloat16).reshape(experts, capacity, width)
+    hit = slot_of[:, :, None] == jnp.arange(slots, dtype=jnp.int32)[None, None, :]
     combine = jnp.sum(jnp.where(hit, gates[:, :, None], 0.0), axis=1)
     combine_hi = combine.astype(jnp.bfloat16)
     combine_lo = (combine - combine_hi.astype(jnp.float32)).astype(jnp.bfloat16)

time: 285 us -> 286 us (level)
  waiting for transfers between devices: 104 us -> 94.5 us
  matrix products: 33.4 us -> 39.8 us
  local copies, waits for them, and re-layouts: 7.44 us -> 11.2 us
  other arithmetic: 3.94 us -> 7.14 us
    ppermute x4, waiting for transfers between devices: 18.9 us -> 7.65 us  [shift(): return lax.ppermute(x, 'group', pairs)]
    dot_general x8 -> x7, matrix products: 4.89 us -> 8.86 us  [per_device(): term = jnp.dot(ctx_perm[:, i, :], piece, preferred_element_type=jnp.float32)]
  transfers between devices with their start and end apart: 11 -> 11, of which waited for: 5 -> 4; matrix products, arithmetic and copies ran while one was open for 12% -> 17% of each run, Pallas kernels for 0% -> 0%
where the time goes in v7:
time: 286 us; the launch traced here: 285 us
  blocking collectives  106 us (37%)
  waiting for transfers between devices  94.5 us (33%)
  matrix products  39.8 us (14%)
  between operations  13.8 us (5%)
  starting transfers between devices  12.6 us (4%)
  local copies, waits for them, and re-layouts  11.2 us (4%)
  other arithmetic  7.14 us (2%)
    all_to_all x1, blocking collectives, per_device(): lax.all_to_all(outgoing, 'expert', split_axis=0, concat_axis=0, tiled=True)  106 us
    all_to_all x1, waiting for transfers between devices, per_device(): lax.all_to_all(expert_rows.reshape(arrived.shape), 'expert', split_axis=0...  84.1 us
    dot_general x7, matrix products, per_device(): term = jnp.dot(ctx_perm[:, i, :], piece, preferred_element_type=jnp.float32)  8.86 us
    ppermute x4, waiting for transfers between devices, shift(): return lax.ppermute(x, 'group', pairs)  7.65 us
    all_to_all x1, starting transfers between devices, per_device(): lax.all_to_all(expert_rows.reshape(arrived.shape), 'expert', split_axis=0...  6.65 us
    dot_general x1, matrix products, swiglu_rows(): mid = jnp.dot(rows, w_in, preferred_element_type=jnp.float32)  6.64 us
    dot_general x1, matrix products, per_device(): shared_mid = jnp.dot(normed, shared_in, preferred_element_type=jnp.float32)  6.18 us
  transfers between devices with their start and end apart: 11, of which 4 were waited for; matrix products, arithmetic and copies ran while one was open for 17% of the time, Pallas kernels for 0%

profile of v7, /device:TPU:32, one launch (start us, length us, event | category | flops | bytes accessed | tf_op | source)
XLA Modules:
  0.0 285.2 jit_solution(5777263171869941194)
XLA Ops:
  6.5 1.6 collective-permute-start
  8.1 1.7 collective-permute-start.1
  9.8 0.8 copy.43
  10.6 0.1 eq.68
  10.7 0.1 eq.72
  10.9 0.7 broadcast_add_fusion
  11.6 1.7 reduce-window.6
  13.3 0.3 slice_reduce_fusion
  13.6 0.1 fusion.25
  13.7 0.1 reduce_sum.48
  13.9 0.7 multiply_add_fusion
  14.7 0.5 fusion.4
  15.3 1.8 copy.47
  17.1 1.8 copy.49
  18.9 2.2 gather_fusion
  21.2 2.4 fusion.27
  23.6 1.0 slice.63
  24.5 1.9 collective-permute-start.2
  26.4 1.8 select_bitcast_fusion
  28.2 1.0 slice.49
  29.1 0.3 collective-permute-start.3
  29.5 0.5 collective-permute-start.5
  30.0 2.2 collective-permute-done.2
  32.2 5.5 %collective-permute-done.3 = bf16[64,2048]{1,0:T(8,128)(2,1)S(1)} collective-permute-done((bf16[64,2048]{1,0:T(8,128)(2,1)S(1)}, bf16[64,2048]{1,0:T(8,128)(2,1)S(1)}, u32[]{:S(2)}, u32[]{:S(2)}) %collective-permute-start.3) | collective-permute-done | bytes 262176 | tf_op jit(solution)/shard_map/ppermute | solution.py:22
  37.7 0.8 copy-done.8
  38.5 2.0 collective-permute-done.7
  40.6 0.7 all-gather.3.cloned.1.call-update
  41.3 1.5 fusion.29
  42.8 1.4 fusion.31
  44.2 1.3 fusion.33
  45.6 1.3 fusion.35
  46.9 0.3 fusion.37
  47.2 1.3 convolution_add_fusion.3
  48.6 1.7 multiply_reduce_fusion
  50.3 1.0 copy-done.5
  51.2 0.2 multiply_convert_fusion
  51.4 1.3 convolution_convert_fusion.1
  52.7 106.1 %all_to_all.10 = bf16[32,32,2048]{2,1,0:T(8,128)(2,1)S(1)} all-to-all(bf16[32,32,2048]{2,1,0:T(8,128)(2,1)S(1)} %bitcast.83), channel_id=1, replica_groups=mesh['group'=8,'expert'=32] {'expert'}, dimensions={0} | all-to-all | bytes 8388608 | tf_op jit(solution)/shard_map/all_to_all | solution.py:115
  158.9 6.6 %fusion = f32[1024,1536]{1,0:T(8,128)S(1)} fusion(bf16[1024,2048]{1,0:T(8,128)(2,1)S(1)} %bitcast.85, bf16[1,2048,1536]{2,1,0:T(8,128)(2,1)S(1)} %bitcast.91), kind=kOutput, calls=%fused_computation.1 | convolution fusion | flops 6442450944 | bytes 16777216 | tf_op jit(solution)/shard_map/dot_general | solution.py:9
  165.5 5.1 %convolution_convert_fusion = bf16[1024,2048]{1,0:T(8,128)(2,1)} fusion(bf16[1,768,2048]{2,1,0:T(8,128)(2,1)S(1)} %copy-done, f32[1024,1536]{1,0:T(8,128)S(1)} %fusion), kind=kOutput, calls=%fused_computation.3 | convolution fusion | flops 3228041216 | bytes 13631488 | tf_op jit(solution)/shard_map/dot_general | solution.py:11
  170.7 6.6 %all-to-all-start.1 = ((bf16[32,32,2048]{2,1,0:T(8,128)(2,1)}), bf16[32,32,2048]{2,1,0:T(8,128)(2,1)}, u32[]{:S(2)}, u32[]{:S(2)}) async-start(bf16[32,32,2048]{2,1,0:T(8,128)(2,1)} %bitcast.84), calls=%async_computation.1 | async-start | bytes 8388608 | tf_op jit(solution)/shard_map/all_to_all | solution.py:119
  177.4 0.3 fusion.57
  177.7 1.2 select_reduce_fusion
  179.0 6.2 %fusion.56 = f32[128,2816]{1,0:T(8,128)S(1)} fusion(bf16[128,2048]{1,0:T(8,128)(2,1)S(1)} %copy-done.3, bf16[2048,2816]{1,0:T(8,128)(2,1)} %all-gather.3.cloned.1.call-done), kind=kOutput, calls=%fused_computation.92 | convolution fusion | flops 1476395008 | bytes 13500416 | tf_op jit(solution)/shard_map/dot_general | solution.py:130
  185.2 2.0 convolution_add_fusion.1
  187.2 84.1 %all-to-all-done.1 = bf16[32,32,2048]{2,1,0:T(8,128)(2,1)} async-done(((bf16[32,32,2048]{2,1,0:T(8,128)(2,1)}), bf16[32,32,2048]{2,1,0:T(8,128)(2,1)}, u32[]{:S(2)}, u32[]{:S(2)}) %all-to-all-start.1) | async-done | bytes 4194336 | tf_op jit(solution)/shard_map/all_to_all | solution.py:119
  271.3 3.2 %fusion.21 = f32[128,2048]{1,0:T(8,128)S(1)} fusion(bf16[1024,2048]{1,0:T(8,128)(2,1)} %bitcast.19, f32[128,1024]{1,0:T(8,128)} %select_reduce_fusion), kind=kOutput, calls=%fused_computation.35 | convolution fusion | flops 537001984 | bytes 5767168 | tf_op jit(solution)/shard_map/dot_general | solution.py:127
  274.5 3.8 %fusion.14 = bf16[128,2048]{1,0:T(8,128)(2,1)} fusion(f32[128,2048]{1,0:T(8,128)S(1)} %copy-done.10, f32[128,2048]{1,0:T(8,128)S(1)} %fusion.21, bf16[1024,2048]{1,0:T(8,128)(2,1)} %bitcast.19, f32[128,1024]{1,0:T(8,128)S(1)} %copy-done.4), kind=kOutput, calls=%fused_computation.25 | convolution fusion | flops 538181632 | bytes 7340032 | tf_op jit(solution)/shard_map/dot_general | solution.py:128
  (68 shorter events, 0.6 us)
Async XLA Ops:
  6.5 159.0 %copy-start = (bf16[1,768,2048]{2,1,0:T(8,128)(2,1)S(1)}, bf16[1,768,2048]{2,1,0:T(8,128)(2,1)}, u32[]{:S(2)}) copy-start(bf16[1,768,2048]{2,1,0:T(8,128)(2,1)} %param.19) | copy-start | bytes 9437188
  6.5 164.1 %all-gather.5.cloned.1.call-start = ((), (), s32[]{:S(2)}) async-start(), calls=%async_computation.3 | async-start | bytes 6488064 | tf_op jit(solution)/shard_map/all_gather | solution.py:91
  6.5 21.6 %collective-permute-start = (bf16[128,2048]{1,0:T(8,128)(2,1)}, bf16[128,2048]{1,0:T(8,128)(2,1)}, u32[]{:S(2)}, u32[]{:S(2)}) collective-permute-start(bf16[128,2048]{1,0:T(8,128)(2,1)} %param.13), channel_id=1, source_target_pairs={{0,64},{32,96},{64,128},{96,160},{128,192},{160,224},{192,0},{224,... | collective-permute-start | bytes 1572872 | tf_op jit(solution)/shard_map/ppermute | solution.py:22
  8.1 15.4 %collective-permute-start.1 = (bf16[128,2048]{1,0:T(8,128)(2,1)}, bf16[128,2048]{1,0:T(8,128)(2,1)}, u32[]{:S(2)}, u32[]{:S(2)}) collective-permute-start(bf16[128,2048]{1,0:T(8,128)(2,1)} %param.13), channel_id=1, source_target_pairs={{0,192},{32,224},{64,0},{96,32},{128,64},{160,96},{192,128},{224,1... | collective-permute-start | bytes 1572872 | tf_op jit(solution)/shard_map/ppermute | solution.py:22
  24.5 7.6 %collective-permute-start.2 = (bf16[64,2048]{1,0:T(8,128)(2,1)S(1)}, bf16[64,2048]{1,0:T(8,128)(2,1)S(1)}, u32[]{:S(2)}, u32[]{:S(2)}) collective-permute-start(bf16[64,2048]{1,0:T(8,128)(2,1)S(1)} %slice.63), channel_id=1, source_target_pairs={{0,192},{32,224},{64,0},{96,32},{128,64},{160,96},{192,128},{224,1... | collective-permute-start | bytes 786440 | tf_op jit(solution)/shard_map/ppermute | solution.py:22
  29.1 8.5 %collective-permute-start.3 = (bf16[64,2048]{1,0:T(8,128)(2,1)S(1)}, bf16[64,2048]{1,0:T(8,128)(2,1)S(1)}, u32[]{:S(2)}, u32[]{:S(2)}) collective-permute-start(bf16[64,2048]{1,0:T(8,128)(2,1)S(1)} %slice.49), channel_id=1, source_target_pairs={{0,64},{32,96},{64,128},{96,160},{128,192},{160,224},{192,0},{224,... | collective-permute-start | bytes 786440 | tf_op jit(solution)/shard_map/ppermute | solution.py:22
  29.4 9.0 %collective-permute-start.4 = (bf16[128,2048]{1,0:T(8,128)(2,1)}, bf16[128,2048]{1,0:T(8,128)(2,1)}, u32[]{:S(2)}, u32[]{:S(2)}) collective-permute-start(bf16[128,2048]{1,0:T(8,128)(2,1)} %param.13), channel_id=1, source_target_pairs={{0,32},{32,0},{64,96},{96,64},{128,160},{160,128},{192,224},{224,1... | collective-permute-start | bytes 1572872 | tf_op jit(solution)/shard_map/ppermute | solution.py:25
  29.5 9.0 %collective-permute-start.5 = (bf16[128,2048]{1,0:T(8,128)(2,1)}, bf16[128,2048]{1,0:T(8,128)(2,1)}, u32[]{:S(2)}, u32[]{:S(2)}) collective-permute-start(bf16[128,2048]{1,0:T(8,128)(2,1)} %collective-permute-done), channel_id=1, source_target_pairs={{0,32},{32,0},{64,96},{96,64},{128,160},{160,128},{192,224},{224,1... | collective-permute-start | bytes 1572872 | tf_op jit(solution)/shard_map/ppermute | solution.py:25
  30.0 8.5 %collective-permute-start.6 = (bf16[128,2048]{1,0:T(8,128)(2,1)}, bf16[128,2048]{1,0:T(8,128)(2,1)}, u32[]{:S(2)}, u32[]{:S(2)}) collective-permute-start(bf16[128,2048]{1,0:T(8,128)(2,1)} %collective-permute-done.1), channel_id=1, source_target_pairs={{0,32},{32,0},{64,96},{96,64},{128,160},{160,128},{192,224},{224,1... | collective-permute-start | bytes 1572872 | tf_op jit(solution)/shard_map/ppermute | solution.py:25
  37.7 0.8 copy-start.8
  38.4 2.0 collective-permute-start.7
  40.5 130.2 %all-gather.3.cloned.1.call-start = ((), (), s32[]{:S(2)}) async-start(), calls=%async_computation.2 | async-start | bytes 12976128 | tf_op jit(solution)/shard_map/all_gather | solution.py:90
  41.3 4.3 %copy-start.11 = (bf16[128,8,128]{2,0,1:T(8,128)(2,1)S(1)}, bf16[128,8,128]{2,0,1:T(8,128)(2,1)}, u32[]{:S(2)}) copy-start(bf16[128,8,128]{2,0,1:T(8,128)(2,1)} %select_bitcast_fusion) | copy-start | bytes 786436
  41.3 5.6 %copy-start.9 = (bf16[128,2048]{1,0:T(8,128)(2,1)S(1)}, bf16[128,2048]{1,0:T(8,128)(2,1)}, u32[]{:S(2)}) copy-start(bf16[128,2048]{1,0:T(8,128)(2,1)} %copy-done.8) | copy-start | bytes 1572868
  41.3 5.9 %copy-start.7 = (f32[128,2048]{1,0:T(8,128)S(1)}, f32[128,2048]{1,0:T(8,128)}, u32[]{:S(2)}) copy-start(f32[128,2048]{1,0:T(8,128)} %fusion.27) | copy-start | bytes 3145732
  42.8 5.8 %copy-start.12 = (bf16[128,2048]{1,0:T(8,128)(2,1)S(1)}, bf16[128,2048]{1,0:T(8,128)(2,1)}, u32[]{:S(2)}) copy-start(bf16[128,2048]{1,0:T(8,128)(2,1)} %param.12) | copy-start | bytes 1572868
  48.5 2.7 copy-start.15
  50.3 1.0 copy-start.5
  51.4 107.5 %copy-start.2 = (bf16[128,2048]{1,0:T(8,128)(2,1)}, bf16[128,2048]{1,0:T(8,128)(2,1)S(1)}, u32[]{:S(2)}) copy-start(bf16[128,2048]{1,0:T(8,128)(2,1)S(1)} %multiply_convert_fusion) | copy-start | bytes 1572868
  51.4 107.5 %slice-start = ((s8[6291456]{0:T(1024)(128)(4,1)}), s8[4194304]{0:T(1024)(128)(4,1)S(1)}, s32[]{:S(2)}) async-start(s8[6291456]{0:T(1024)(128)(4,1)} %bitcast.90), calls=%async_computation.4 | async-start | bytes 8388608
  52.7 106.2 %slice-start.1 = ((s8[6291456]{0:T(1024)(128)(4,1)}), s8[2097152]{0:T(1024)(128)(4,1)S(1)}, s32[]{:S(2)}) async-start(s8[6291456]{0:T(1024)(128)(4,1)} %bitcast.90), calls=%async_computation.5 | async-start | bytes 4194304
  170.7 6.7 %copy-start.3 = (bf16[128,2048]{1,0:T(8,128)(2,1)S(1)}, bf16[128,2048]{1,0:T(8,128)(2,1)}, u32[]{:S(2)}) copy-start(bf16[128,2048]{1,0:T(8,128)(2,1)} %copy-done.2) | copy-start | bytes 1572868
  170.7 6.7 %copy-start.13 = (bf16[2048,32]{0,1:T(8,128)(2,1)S(1)}, bf16[2048,32]{0,1:T(8,128)(2,1)}, u32[]{:S(2)}) copy-start(bf16[2048,32]{0,1:T(8,128)(2,1)} %param.15) | copy-start | bytes 393220
  170.7 7.0 %copy-start.14 = (s32[128,6]{0,1:T(8,128)S(1)}, s32[128,6]{0,1:T(8,128)}, u32[]{:S(2)}) copy-start(s32[128,6]{0,1:T(8,128)} %param.20) | copy-start | bytes 9220
  170.7 100.6 %all-to-all-start.1 = ((bf16[32,32,2048]{2,1,0:T(8,128)(2,1)}), bf16[32,32,2048]{2,1,0:T(8,128)(2,1)}, u32[]{:S(2)}, u32[]{:S(2)}) async-start(bf16[32,32,2048]{2,1,0:T(8,128)(2,1)} %bitcast.84), calls=%async_computation.1 | async-start | bytes 8388608 | tf_op jit(solution)/shard_map/all_to_all | solution.py:119
  177.7 7.4 %slice-start.2 = ((s8[5767168]{0:T(1024)(128)(4,1)}), s8[4194304]{0:T(1024)(128)(4,1)S(1)}, s32[]{:S(2)}) async-start(s8[5767168]{0:T(1024)(128)(4,1)} %bitcast.92), calls=%async_computation.6 | async-start | bytes 8388608
  179.0 6.2 %copy-start.6 = (f32[128,2048]{1,0:T(8,128)S(1)}, f32[128,2048]{1,0:T(8,128)}, u32[]{:S(2)}) copy-start(f32[128,2048]{1,0:T(8,128)} %copy-done.5) | copy-start | bytes 3145732
  179.0 6.2 %slice-start.3 = ((s8[5767168]{0:T(1024)(128)(4,1)}), s8[1572864]{0:T(1024)(128)(4,1)S(1)}, s32[]{:S(2)}) async-start(s8[5767168]{0:T(1024)(128)(4,1)} %bitcast.92), calls=%async_computation.7 | async-start | bytes 3145728
  271.3 3.2 %copy-start.4 = (f32[128,1024]{1,0:T(8,128)S(1)}, f32[128,1024]{1,0:T(8,128)}, u32[]{:S(2)}) copy-start(f32[128,1024]{1,0:T(8,128)} %select_reduce_fusion) | copy-start | bytes 1572868
  271.3 3.2 %copy-start.10 = (f32[128,2048]{1,0:T(8,128)S(1)}, f32[128,2048]{1,0:T(8,128)}, u32[]{:S(2)}) copy-start(f32[128,2048]{1,0:T(8,128)} %convolution_add_fusion.1) | copy-start | bytes 3145732
  271.3 7.1 %copy-start.1 = (bf16[1,768,2048]{2,1,0:T(8,128)(2,1)S(1)}, bf16[1,768,2048]{2,1,0:T(8,128)(2,1)}, u32[]{:S(2)}) copy-start(bf16[1,768,2048]{2,1,0:T(8,128)(2,1)} %param.19) | copy-start | bytes 9437188
Sparse Core Ops, SparseCore 0:
  40.6 45.2 all-gather.4
  87.8 66.4 all-gather.2

commit v8 on v7

--- a/solution.py
+++ b/solution.py
@@ -69,30 +69,23 @@
     hit = slot_of[:, :, None] == jnp.arange(slots, dtype=jnp.int32)[None, None, :]
     dispatch = jnp.any(hit, axis=1).astype(jnp.bfloat16)
     block = attn_out_w.shape[0]
-    ctx_blocks = context.reshape(tok_rows, -1, block)
     groups = lax.axis_size("group")
     if groups == 8:
-        own = lax.axis_index("group")
-        first = jnp.dot(
-            lax.dynamic_index_in_dim(ctx_blocks, own, 1, keepdims=False),
-            attn_out_w,
-            preferred_element_type=jnp.float32,
-        )
-        ctx_perm = jnp.take(ctx_blocks, chip_gather_order(), axis=1)
-        pieces, (slot_of, dispatch, first, ctx_perm) = gather_rows_by_chip(
-            attn_out_w, (slot_of, dispatch, first, ctx_perm)
+        src = chip_gather_order()[:, None] * block + jnp.arange(block, dtype=jnp.int32)[None, :]
+        perm = (jnp.arange(context.shape[1], dtype=jnp.int32)[:, None] == src.reshape(1, -1))
+        ctx_perm = jnp.dot(context, perm.astype(jnp.bfloat16), preferred_element_type=jnp.float32)
+        ctx_perm = ctx_perm.astype(jnp.bfloat16).reshape(tok_rows, groups, block)
+        pieces, (slot_of, dispatch, ctx_perm) = gather_rows_by_chip(
+            attn_out_w, (slot_of, dispatch, ctx_perm)
         )
     else:
         pieces = [lax.all_gather(attn_out_w, "group", axis=0, tiled=True)]
         ctx_perm = context[:, None, :]
-        first = None
     pieces, shared_in, shared_out = lax.optimization_barrier((pieces, shared_in, shared_out))
     shared_in = lax.all_gather(shared_in, "group", axis=0, tiled=True)
     shared_out = lax.all_gather(shared_out, "group", axis=1, tiled=True)
-    attn = first
+    attn = None
     for i, piece in enumerate(pieces):
-        if first is not None and i == 0:
-            continue
         term = jnp.dot(ctx_perm[:, i, :], piece, preferred_element_type=jnp.float32)
         attn = term if attn is None else attn + term
     hidden_state = (residual.astype(jnp.float32) + attn).astype(jnp.bfloat16)

time: 286 us -> 286 us (level)
  local copies, waits for them, and re-layouts: 11.2 us -> 5.32 us
  waiting for transfers between devices: 94.5 us -> 100 us
    ppermute x4, waiting for transfers between devices: 7.65 us -> 13.6 us  [shift(): return lax.ppermute(x, 'group', pairs)]
    dot_general x7 -> x8, matrix products: 8.86 us -> 9.46 us  [per_device(): term = jnp.dot(ctx_perm[:, i, :], piece, preferred_element_type=jnp.float32)]
  transfers between devices with their start and end apart: 11 -> 11, of which waited for: 4 -> 5; matrix products, arithmetic and copies ran while one was open for 17% -> 15% of each run, Pallas kernels for 0% -> 0%
where the time goes in v8:
time: 286 us; the launch traced here: 285 us
  blocking collectives  106 us (37%)
  waiting for transfers between devices  100 us (35%)
  matrix products  40.4 us (14%)
  between operations  13.8 us (5%)
  starting transfers between devices  13.7 us (5%)
  other arithmetic  5.37 us (2%)
  local copies, waits for them, and re-layouts  5.32 us (2%)
    all_to_all x1, blocking collectives, per_device(): lax.all_to_all(outgoing, 'expert', split_axis=0, concat_axis=0, tiled=True)  106 us
    all_to_all x1, waiting for transfers between devices, per_device(): lax.all_to_all(expert_rows.reshape(arrived.shape), 'expert', split_axis=0...  84.1 us
    ppermute x4, waiting for transfers between devices, shift(): return lax.ppermute(x, 'group', pairs)  13.6 us
    dot_general x8, matrix products, per_device(): term = jnp.dot(ctx_perm[:, i, :], piece, preferred_element_type=jnp.float32)  9.46 us
    all_to_all x1, starting transfers between devices, per_device(): lax.all_to_all(expert_rows.reshape(arrived.shape), 'expert', split_axis=0...  6.65 us
    dot_general x1, matrix products, swiglu_rows(): mid = jnp.dot(rows, w_in, preferred_element_type=jnp.float32)  6.64 us
    ppermute x4, starting transfers between devices, shift(): return lax.ppermute(x, 'group', pairs)  6.33 us
    dot_general x1, matrix products, per_device(): shared_mid = jnp.dot(normed, shared_in, preferred_element_type=jnp.float32)  6.18 us
  transfers between devices with their start and end apart: 11, of which 5 were waited for; matrix products, arithmetic and copies ran while one was open for 15% of the time, Pallas kernels for 0%

profile of v8, /device:TPU:32, one launch (start us, length us, event | category | flops | bytes accessed | tf_op | source)
XLA Modules:
  0.0 285.2 jit_solution(16197533553214022133)
XLA Ops:
  6.5 1.6 collective-permute-start
  8.1 1.7 collective-permute-start.1
  9.8 0.8 copy.30
  10.6 0.1 eq.81
  10.7 0.1 eq.85
  10.9 1.7 reduce-window.6
  12.6 0.3 slice_reduce_fusion
  12.9 0.1 fusion.33
  13.0 0.1 reduce_sum.48
  13.2 0.7 multiply_add_fusion
  13.9 0.5 fusion.5
  14.5 0.7 broadcast_add_fusion
  15.3 6.5 %collective-permute-done.1 = bf16[128,2048]{1,0:T(8,128)(2,1)} collective-permute-done((bf16[128,2048]{1,0:T(8,128)(2,1)}, bf16[128,2048]{1,0:T(8,128)(2,1)}, u32[]{:S(2)}, u32[]{:S(2)}) %collective-permute-start.1) | collective-permute-done | bytes 524320 | tf_op jit(solution)/shard_map/ppermute | solution.py:22
  21.8 1.0 slice.65
  22.8 3.0 %collective-permute-start.2 = (bf16[64,2048]{1,0:T(8,128)(2,1)S(1)}, bf16[64,2048]{1,0:T(8,128)(2,1)S(1)}, u32[]{:S(2)}, u32[]{:S(2)}) collective-permute-start(bf16[64,2048]{1,0:T(8,128)(2,1)S(1)} %slice.65), channel_id=1, source_target_pairs={{0,192},{32,224},{64,0},{96,32},{128,64},{160,96},{192,128},{224,1... | collective-permute-start | bytes 786440 | tf_op jit(solution)/shard_map/ppermute | solution.py:22
  25.8 2.4 fusion.22
  28.2 1.0 slice.52
  29.2 0.1 collective-permute-start.3
  29.3 0.1 collective-permute-start.4
  29.4 0.5 collective-permute-start.5
  29.9 0.1 collective-permute-start.6
  30.0 0.2 collective-permute-done.2
  30.3 6.9 %collective-permute-done.3 = bf16[64,2048]{1,0:T(8,128)(2,1)S(1)} collective-permute-done((bf16[64,2048]{1,0:T(8,128)(2,1)S(1)}, bf16[64,2048]{1,0:T(8,128)(2,1)S(1)}, u32[]{:S(2)}, u32[]{:S(2)}) %collective-permute-start.3) | collective-permute-done | bytes 262176 | tf_op jit(solution)/shard_map/ppermute | solution.py:22
  37.2 0.8 copy-done.7
  38.0 2.0 collective-permute-done.7
  40.1 0.7 all-gather.3.cloned.1.call-update
  40.8 1.5 fusion.35
  42.2 1.4 fusion.37
  43.6 1.5 fusion.39
  45.1 1.4 fusion.41
  46.5 0.3 fusion.43
  46.8 1.4 fusion.45
  48.2 1.4 fusion.47
  49.6 0.8 multiply_reduce_fusion
  50.4 1.0 copy-done.5
  51.3 0.2 multiply_convert_fusion
  51.5 1.3 convolution_convert_fusion.1
  52.8 106.1 %all_to_all.10 = bf16[32,32,2048]{2,1,0:T(8,128)(2,1)S(1)} all-to-all(bf16[32,32,2048]{2,1,0:T(8,128)(2,1)S(1)} %bitcast.80), channel_id=1, replica_groups=mesh['group'=8,'expert'=32] {'expert'}, dimensions={0} | all-to-all | bytes 8388608 | tf_op jit(solution)/shard_map/all_to_all | solution.py:108
  159.0 6.6 %fusion = f32[1024,1536]{1,0:T(8,128)S(1)} fusion(bf16[1024,2048]{1,0:T(8,128)(2,1)S(1)} %bitcast.82, bf16[1,2048,1536]{2,1,0:T(8,128)(2,1)S(1)} %bitcast.93), kind=kOutput, calls=%fused_computation | convolution fusion | flops 6442450944 | bytes 16777216 | tf_op jit(solution)/shard_map/dot_general | solution.py:9
  165.6 5.1 %convolution_convert_fusion = bf16[1024,2048]{1,0:T(8,128)(2,1)} fusion(bf16[1,768,2048]{2,1,0:T(8,128)(2,1)S(1)} %copy-done, f32[1024,1536]{1,0:T(8,128)S(1)} %fusion), kind=kOutput, calls=%fused_computation.4 | convolution fusion | flops 3228041216 | bytes 13631488 | tf_op jit(solution)/shard_map/dot_general | solution.py:11
  170.7 6.7 %all-to-all-start.1 = ((bf16[32,32,2048]{2,1,0:T(8,128)(2,1)}), bf16[32,32,2048]{2,1,0:T(8,128)(2,1)}, u32[]{:S(2)}, u32[]{:S(2)}) async-start(bf16[32,32,2048]{2,1,0:T(8,128)(2,1)} %bitcast.81), calls=%async_computation.1 | async-start | bytes 8388608 | tf_op jit(solution)/shard_map/all_to_all | solution.py:112
  177.4 0.3 fusion.64
  177.8 1.2 select_reduce_fusion
  179.0 6.2 %fusion.63 = f32[128,2816]{1,0:T(8,128)S(1)} fusion(bf16[128,2048]{1,0:T(8,128)(2,1)S(1)} %copy-done.3, bf16[2048,2816]{1,0:T(8,128)(2,1)} %all-gather.3.cloned.1.call-done), kind=kOutput, calls=%fused_computation.92 | convolution fusion | flops 1476395008 | bytes 13500416 | tf_op jit(solution)/shard_map/dot_general | solution.py:123
  185.2 2.0 convolution_add_fusion.1
  187.2 84.1 %all-to-all-done.1 = bf16[32,32,2048]{2,1,0:T(8,128)(2,1)} async-done(((bf16[32,32,2048]{2,1,0:T(8,128)(2,1)}), bf16[32,32,2048]{2,1,0:T(8,128)(2,1)}, u32[]{:S(2)}, u32[]{:S(2)}) %all-to-all-start.1) | async-done | bytes 4194336 | tf_op jit(solution)/shard_map/all_to_all | solution.py:112
  271.3 3.2 %fusion.29 = f32[128,2048]{1,0:T(8,128)S(1)} fusion(bf16[1024,2048]{1,0:T(8,128)(2,1)} %bitcast.17, f32[128,1024]{1,0:T(8,128)} %select_reduce_fusion), kind=kOutput, calls=%fused_computation.38 | convolution fusion | flops 537001984 | bytes 5767168 | tf_op jit(solution)/shard_map/dot_general | solution.py:120
  274.6 3.8 %fusion.16 = bf16[128,2048]{1,0:T(8,128)(2,1)} fusion(f32[128,2048]{1,0:T(8,128)S(1)} %copy-done.9, f32[128,2048]{1,0:T(8,128)S(1)} %fusion.29, bf16[1024,2048]{1,0:T(8,128)(2,1)} %bitcast.17, f32[128,1024]{1,0:T(8,128)S(1)} %copy-done.4), kind=kOutput, calls=%fused_computation.26 | convolution fusion | flops 538181632 | bytes 7340032 | tf_op jit(solution)/shard_map/dot_general | solution.py:121
  (63 shorter events, 0.6 us)
Async XLA Ops:
  6.5 159.1 %copy-start = (bf16[1,768,2048]{2,1,0:T(8,128)(2,1)S(1)}, bf16[1,768,2048]{2,1,0:T(8,128)(2,1)}, u32[]{:S(2)}) copy-start(bf16[1,768,2048]{2,1,0:T(8,128)(2,1)} %param.19) | copy-start | bytes 9437188
  6.5 164.2 %all-gather.5.cloned.1.call-start = ((), (), s32[]{:S(2)}) async-start(), calls=%async_computation.3 | async-start | bytes 6488064 | tf_op jit(solution)/shard_map/all_gather | solution.py:86
  6.5 21.7 %collective-permute-start = (bf16[128,2048]{1,0:T(8,128)(2,1)}, bf16[128,2048]{1,0:T(8,128)(2,1)}, u32[]{:S(2)}, u32[]{:S(2)}) collective-permute-start(bf16[128,2048]{1,0:T(8,128)(2,1)} %param.13), channel_id=1, source_target_pairs={{0,64},{32,96},{64,128},{96,160},{128,192},{160,224},{192,0},{224,... | collective-permute-start | bytes 1572872 | tf_op jit(solution)/shard_map/ppermute | solution.py:22
  8.1 13.7 %collective-permute-start.1 = (bf16[128,2048]{1,0:T(8,128)(2,1)}, bf16[128,2048]{1,0:T(8,128)(2,1)}, u32[]{:S(2)}, u32[]{:S(2)}) collective-permute-start(bf16[128,2048]{1,0:T(8,128)(2,1)} %param.13), channel_id=1, source_target_pairs={{0,192},{32,224},{64,0},{96,32},{128,64},{160,96},{192,128},{224,1... | collective-permute-start | bytes 1572872 | tf_op jit(solution)/shard_map/ppermute | solution.py:22
  22.8 7.4 %collective-permute-start.2 = (bf16[64,2048]{1,0:T(8,128)(2,1)S(1)}, bf16[64,2048]{1,0:T(8,128)(2,1)S(1)}, u32[]{:S(2)}, u32[]{:S(2)}) collective-permute-start(bf16[64,2048]{1,0:T(8,128)(2,1)S(1)} %slice.65), channel_id=1, source_target_pairs={{0,192},{32,224},{64,0},{96,32},{128,64},{160,96},{192,128},{224,1... | collective-permute-start | bytes 786440 | tf_op jit(solution)/shard_map/ppermute | solution.py:22
  29.2 7.9 %collective-permute-start.3 = (bf16[64,2048]{1,0:T(8,128)(2,1)S(1)}, bf16[64,2048]{1,0:T(8,128)(2,1)S(1)}, u32[]{:S(2)}, u32[]{:S(2)}) collective-permute-start(bf16[64,2048]{1,0:T(8,128)(2,1)S(1)} %slice.52), channel_id=1, source_target_pairs={{0,64},{32,96},{64,128},{96,160},{128,192},{160,224},{192,0},{224,... | collective-permute-start | bytes 786440 | tf_op jit(solution)/shard_map/ppermute | solution.py:22
  29.3 8.7 %collective-permute-start.4 = (bf16[128,2048]{1,0:T(8,128)(2,1)}, bf16[128,2048]{1,0:T(8,128)(2,1)}, u32[]{:S(2)}, u32[]{:S(2)}) collective-permute-start(bf16[128,2048]{1,0:T(8,128)(2,1)} %param.13), channel_id=1, source_target_pairs={{0,32},{32,0},{64,96},{96,64},{128,160},{160,128},{192,224},{224,1... | collective-permute-start | bytes 1572872 | tf_op jit(solution)/shard_map/ppermute | solution.py:25
  29.4 8.6 %collective-permute-start.5 = (bf16[128,2048]{1,0:T(8,128)(2,1)}, bf16[128,2048]{1,0:T(8,128)(2,1)}, u32[]{:S(2)}, u32[]{:S(2)}) collective-permute-start(bf16[128,2048]{1,0:T(8,128)(2,1)} %collective-permute-done), channel_id=1, source_target_pairs={{0,32},{32,0},{64,96},{96,64},{128,160},{160,128},{192,224},{224,1... | collective-permute-start | bytes 1572872 | tf_op jit(solution)/shard_map/ppermute | solution.py:25
  29.9 8.1 %collective-permute-start.6 = (bf16[128,2048]{1,0:T(8,128)(2,1)}, bf16[128,2048]{1,0:T(8,128)(2,1)}, u32[]{:S(2)}, u32[]{:S(2)}) collective-permute-start(bf16[128,2048]{1,0:T(8,128)(2,1)} %collective-permute-done.1), channel_id=1, source_target_pairs={{0,32},{32,0},{64,96},{96,64},{128,160},{160,128},{192,224},{224,1... | collective-permute-start | bytes 1572872 | tf_op jit(solution)/shard_map/ppermute | solution.py:25
  37.1 0.8 copy-start.7
  37.9 2.0 collective-permute-start.7
  40.0 130.7 %all-gather.3.cloned.1.call-start = ((), (), s32[]{:S(2)}) async-start(), calls=%async_computation.2 | async-start | bytes 12976128 | tf_op jit(solution)/shard_map/all_gather | solution.py:85
  40.8 4.4 %copy-start.12 = (bf16[1024,128]{1,0:T(8,128)(2,1)S(1)}, bf16[1024,128]{1,0:T(8,128)(2,1)}, u32[]{:S(2)}) copy-start(bf16[1024,128]{1,0:T(8,128)(2,1)} %fusion.22) | copy-start | bytes 786436
  40.8 5.7 %copy-start.8 = (bf16[128,2048]{1,0:T(8,128)(2,1)S(1)}, bf16[128,2048]{1,0:T(8,128)(2,1)}, u32[]{:S(2)}) copy-start(bf16[128,2048]{1,0:T(8,128)(2,1)} %copy-done.7) | copy-start | bytes 1572868
  43.6 5.9 %copy-start.10 = (bf16[128,2048]{1,0:T(8,128)(2,1)S(1)}, bf16[128,2048]{1,0:T(8,128)(2,1)}, u32[]{:S(2)}) copy-start(bf16[128,2048]{1,0:T(8,128)(2,1)} %param.13) | copy-start | bytes 1572868
  43.6 5.9 %copy-start.11 = (bf16[128,2048]{1,0:T(8,128)(2,1)S(1)}, bf16[128,2048]{1,0:T(8,128)(2,1)}, u32[]{:S(2)}) copy-start(bf16[128,2048]{1,0:T(8,128)(2,1)} %param.12) | copy-start | bytes 1572868
  49.6 1.7 copy-start.15
  50.3 1.0 copy-start.5
  51.5 107.5 %copy-start.2 = (bf16[128,2048]{1,0:T(8,128)(2,1)}, bf16[128,2048]{1,0:T(8,128)(2,1)S(1)}, u32[]{:S(2)}) copy-start(bf16[128,2048]{1,0:T(8,128)(2,1)S(1)} %multiply_convert_fusion) | copy-start | bytes 1572868
  51.5 107.5 %slice-start = ((s8[6291456]{0:T(1024)(128)(4,1)}), s8[4194304]{0:T(1024)(128)(4,1)S(1)}, s32[]{:S(2)}) async-start(s8[6291456]{0:T(1024)(128)(4,1)} %bitcast.92), calls=%async_computation.4 | async-start | bytes 8388608
  52.8 106.2 %slice-start.1 = ((s8[6291456]{0:T(1024)(128)(4,1)}), s8[2097152]{0:T(1024)(128)(4,1)S(1)}, s32[]{:S(2)}) async-start(s8[6291456]{0:T(1024)(128)(4,1)} %bitcast.92), calls=%async_computation.5 | async-start | bytes 4194304
  170.7 6.7 %copy-start.3 = (bf16[128,2048]{1,0:T(8,128)(2,1)S(1)}, bf16[128,2048]{1,0:T(8,128)(2,1)}, u32[]{:S(2)}) copy-start(bf16[128,2048]{1,0:T(8,128)(2,1)} %copy-done.2) | copy-start | bytes 1572868
  170.7 6.7 %copy-start.13 = (bf16[2048,32]{0,1:T(8,128)(2,1)S(1)}, bf16[2048,32]{0,1:T(8,128)(2,1)}, u32[]{:S(2)}) copy-start(bf16[2048,32]{0,1:T(8,128)(2,1)} %param.15) | copy-start | bytes 393220
  170.7 7.0 %copy-start.14 = (s32[128,6]{0,1:T(8,128)S(1)}, s32[128,6]{0,1:T(8,128)}, u32[]{:S(2)}) copy-start(s32[128,6]{0,1:T(8,128)} %param.20) | copy-start | bytes 9220
  170.7 100.6 %all-to-all-start.1 = ((bf16[32,32,2048]{2,1,0:T(8,128)(2,1)}), bf16[32,32,2048]{2,1,0:T(8,128)(2,1)}, u32[]{:S(2)}, u32[]{:S(2)}) async-start(bf16[32,32,2048]{2,1,0:T(8,128)(2,1)} %bitcast.81), calls=%async_computation.1 | async-start | bytes 8388608 | tf_op jit(solution)/shard_map/all_to_all | solution.py:112
  177.8 7.4 %slice-start.2 = ((s8[5767168]{0:T(1024)(128)(4,1)}), s8[4194304]{0:T(1024)(128)(4,1)S(1)}, s32[]{:S(2)}) async-start(s8[5767168]{0:T(1024)(128)(4,1)} %bitcast.94), calls=%async_computation.6 | async-start | bytes 8388608
  179.0 6.2 %copy-start.6 = (f32[128,2048]{1,0:T(8,128)S(1)}, f32[128,2048]{1,0:T(8,128)}, u32[]{:S(2)}) copy-start(f32[128,2048]{1,0:T(8,128)} %copy-done.5) | copy-start | bytes 3145732
  179.0 6.2 %slice-start.3 = ((s8[5767168]{0:T(1024)(128)(4,1)}), s8[1572864]{0:T(1024)(128)(4,1)S(1)}, s32[]{:S(2)}) async-start(s8[5767168]{0:T(1024)(128)(4,1)} %bitcast.94), calls=%async_computation.7 | async-start | bytes 3145728
  271.3 3.2 %copy-start.4 = (f32[128,1024]{1,0:T(8,128)S(1)}, f32[128,1024]{1,0:T(8,128)}, u32[]{:S(2)}) copy-start(f32[128,1024]{1,0:T(8,128)} %select_reduce_fusion) | copy-start | bytes 1572868
  271.3 3.2 %copy-start.9 = (f32[128,2048]{1,0:T(8,128)S(1)}, f32[128,2048]{1,0:T(8,128)}, u32[]{:S(2)}) copy-start(f32[128,2048]{1,0:T(8,128)} %convolution_add_fusion.1) | copy-start | bytes 3145732
  271.3 7.1 %copy-start.1 = (bf16[1,768,2048]{2,1,0:T(8,128)(2,1)S(1)}, bf16[1,768,2048]{2,1,0:T(8,128)(2,1)}, u32[]{:S(2)}) copy-start(bf16[1,768,2048]{2,1,0:T(8,128)(2,1)} %param.19) | copy-start | bytes 9437188
Sparse Core Ops, SparseCore 0:
  40.1 45.2 all-gather.4
  87.3 66.4 all-gather.2

commit v9 on v8

--- a/solution.py
+++ b/solution.py
@@ -84,10 +84,11 @@
     pieces, shared_in, shared_out = lax.optimization_barrier((pieces, shared_in, shared_out))
     shared_in = lax.all_gather(shared_in, "group", axis=0, tiled=True)
     shared_out = lax.all_gather(shared_out, "group", axis=1, tiled=True)
-    attn = None
-    for i, piece in enumerate(pieces):
-        term = jnp.dot(ctx_perm[:, i, :], piece, preferred_element_type=jnp.float32)
-        attn = term if attn is None else attn + term
+    attn = jnp.dot(
+        ctx_perm.reshape(tok_rows, -1),
+        jnp.concatenate(pieces, axis=0),
+        preferred_element_type=jnp.float32,
+    )
     hidden_state = (residual.astype(jnp.float32) + attn).astype(jnp.bfloat16)
     hidden_f = hidden_state.astype(jnp.float32)
     scale = lax.rsqrt(jnp.mean(hidden_f * hidden_f, axis=-1, keepdims=True) + 1e-06)

time: 286 us -> 286 us (level)
  local copies, waits for them, and re-layouts: 5.32 us -> 14.1 us
  matrix products: 40.4 us -> 31.8 us
    dot_general x8 -> x1, matrix products: 9.46 us -> 0.83 us  [per_device(): jnp.dot(ctx_perm.reshape(tok_rows, -1), jnp.concatenate(pieces, axis=0),...]
    unnamed x42 -> x45, local copies, waits for them, and re-layouts: 2.65 us -> 10.3 us
where the time goes in v9:
time: 286 us; the launch traced here: 285 us
  blocking collectives  106 us (37%)
  waiting for transfers between devices  100 us (35%)
  matrix products  31.8 us (11%)
  local copies, waits for them, and re-layouts  14.1 us (5%)
  between operations  13.9 us (5%)
  starting transfers between devices  13.7 us (5%)
  other arithmetic  5.37 us (2%)
    all_to_all x1, blocking collectives, per_device(): lax.all_to_all(outgoing, 'expert', split_axis=0, concat_axis=0, tiled=True)  106 us
    all_to_all x1, waiting for transfers between devices, per_device(): lax.all_to_all(expert_rows.reshape(arrived.shape), 'expert', split_axis=0...  84.1 us
    ppermute x4, waiting for transfers between devices, shift(): return lax.ppermute(x, 'group', pairs)  13.6 us
    unnamed x45, local copies, waits for them, and re-layouts  10.3 us
    all_to_all x1, starting transfers between devices, per_device(): lax.all_to_all(expert_rows.reshape(arrived.shape), 'expert', split_axis=0...  6.65 us
    dot_general x1, matrix products, swiglu_rows(): mid = jnp.dot(rows, w_in, preferred_element_type=jnp.float32)  6.64 us
    ppermute x4, starting transfers between devices, shift(): return lax.ppermute(x, 'group', pairs)  6.33 us
    dot_general x1, matrix products, per_device(): shared_mid = jnp.dot(normed, shared_in, preferred_element_type=jnp.float32)  6.18 us
  transfers between devices with their start and end apart: 11, of which 5 were waited for; matrix products, arithmetic and copies ran while one was open for 15% of the time, Pallas kernels for 0%

profile of v9, /device:TPU:32, one launch (start us, length us, event | category | flops | bytes accessed | tf_op | source)
XLA Modules:
  0.0 285.4 jit_solution(4307429155874486018)
XLA Ops:
  6.5 1.6 collective-permute-start
  8.1 1.7 collective-permute-start.1
  9.8 0.8 copy.30
  10.6 0.1 eq.81
  10.7 0.1 eq.85
  10.9 1.7 reduce-window.6
  12.6 0.3 slice_reduce_fusion
  12.9 0.1 fusion.26
  13.0 0.1 reduce_sum.48
  13.2 0.7 multiply_add_fusion
  13.9 0.5 fusion.5
  14.5 0.7 broadcast_add_fusion
  15.3 6.5 %collective-permute-done.1 = bf16[128,2048]{1,0:T(8,128)(2,1)} collective-permute-done((bf16[128,2048]{1,0:T(8,128)(2,1)}, bf16[128,2048]{1,0:T(8,128)(2,1)}, u32[]{:S(2)}, u32[]{:S(2)}) %collective-permute-start.1) | collective-permute-done | bytes 524320 | tf_op jit(solution)/shard_map/ppermute | solution.py:22
  21.8 1.0 slice.33
  22.8 3.0 %collective-permute-start.2 = (bf16[64,2048]{1,0:T(8,128)(2,1)S(1)}, bf16[64,2048]{1,0:T(8,128)(2,1)S(1)}, u32[]{:S(2)}, u32[]{:S(2)}) collective-permute-start(bf16[64,2048]{1,0:T(8,128)(2,1)S(1)} %slice.33), channel_id=1, source_target_pairs={{0,192},{32,224},{64,0},{96,32},{128,64},{160,96},{192,128},{224,1... | collective-permute-start | bytes 786440 | tf_op jit(solution)/shard_map/ppermute | solution.py:22
  25.8 2.4 fusion.15
  28.2 1.0 slice.27
  29.3 0.1 collective-permute-start.4
  29.4 0.5 collective-permute-start.5
  29.9 0.1 collective-permute-start.6
  30.0 0.2 collective-permute-done.2
  30.3 6.9 %collective-permute-done.3 = bf16[64,2048]{1,0:T(8,128)(2,1)S(1)} collective-permute-done((bf16[64,2048]{1,0:T(8,128)(2,1)S(1)}, bf16[64,2048]{1,0:T(8,128)(2,1)S(1)}, u32[]{:S(2)}, u32[]{:S(2)}) %collective-permute-start.3) | collective-permute-done | bytes 262176 | tf_op jit(solution)/shard_map/ppermute | solution.py:22
  37.2 0.8 copy-done.7
  38.0 2.0 collective-permute-done.7
  40.1 0.7 all-gather.3.cloned.1.call-update
  40.8 1.2 constant_dynamic-update-slice_fusion.9
  41.9 1.1 constant_dynamic-update-slice_fusion.8
  43.0 1.1 constant_dynamic-update-slice_fusion.7
  44.1 1.1 constant_dynamic-update-slice_fusion.6
  45.2 1.1 constant_dynamic-update-slice_fusion.5
  46.3 1.1 constant_dynamic-update-slice_fusion.4
  47.4 1.1 constant_dynamic-update-slice_fusion.3
  48.5 1.1 constant_dynamic-update-slice_fusion.2
  49.6 0.8 multiply_reduce_fusion
  50.5 1.0 copy-done.5
  51.4 0.2 multiply_convert_fusion
  51.6 1.3 convolution_convert_fusion.1
  52.9 106.1 %all_to_all.10 = bf16[32,32,2048]{2,1,0:T(8,128)(2,1)S(1)} all-to-all(bf16[32,32,2048]{2,1,0:T(8,128)(2,1)S(1)} %bitcast.49), channel_id=1, replica_groups=mesh['group'=8,'expert'=32] {'expert'}, dimensions={0} | all-to-all | bytes 8388608 | tf_op jit(solution)/shard_map/all_to_all | solution.py:109
  159.1 6.6 %fusion = f32[1024,1536]{1,0:T(8,128)S(1)} fusion(bf16[1024,2048]{1,0:T(8,128)(2,1)S(1)} %bitcast.51, bf16[1,2048,1536]{2,1,0:T(8,128)(2,1)S(1)} %bitcast.55), kind=kOutput, calls=%fused_computation | convolution fusion | flops 6442450944 | bytes 16777216 | tf_op jit(solution)/shard_map/dot_general | solution.py:9
  165.7 5.1 %convolution_convert_fusion = bf16[1024,2048]{1,0:T(8,128)(2,1)} fusion(bf16[1,768,2048]{2,1,0:T(8,128)(2,1)S(1)} %copy-done, f32[1024,1536]{1,0:T(8,128)S(1)} %fusion), kind=kOutput, calls=%fused_computation.4 | convolution fusion | flops 3228041216 | bytes 13631488 | tf_op jit(solution)/shard_map/dot_general | solution.py:11
  170.9 6.7 %all-to-all-start.1 = ((bf16[32,32,2048]{2,1,0:T(8,128)(2,1)}), bf16[32,32,2048]{2,1,0:T(8,128)(2,1)}, u32[]{:S(2)}, u32[]{:S(2)}) async-start(bf16[32,32,2048]{2,1,0:T(8,128)(2,1)} %bitcast.50), calls=%async_computation.1 | async-start | bytes 8388608 | tf_op jit(solution)/shard_map/all_to_all | solution.py:113
  177.6 0.3 fusion.34
  177.9 1.2 select_reduce_fusion
  179.1 6.2 %fusion.33 = f32[128,2816]{1,0:T(8,128)S(1)} fusion(bf16[128,2048]{1,0:T(8,128)(2,1)S(1)} %copy-done.3, bf16[2048,2816]{1,0:T(8,128)(2,1)} %all-gather.3.cloned.1.call-done), kind=kOutput, calls=%fused_computation.70 | convolution fusion | flops 1476395008 | bytes 13500416 | tf_op jit(solution)/shard_map/dot_general | solution.py:124
  185.4 2.0 convolution_add_fusion.1
  187.4 84.1 %all-to-all-done.1 = bf16[32,32,2048]{2,1,0:T(8,128)(2,1)} async-done(((bf16[32,32,2048]{2,1,0:T(8,128)(2,1)}), bf16[32,32,2048]{2,1,0:T(8,128)(2,1)}, u32[]{:S(2)}, u32[]{:S(2)}) %all-to-all-start.1) | async-done | bytes 4194336 | tf_op jit(solution)/shard_map/all_to_all | solution.py:113
  271.5 3.2 %fusion.22 = f32[128,2048]{1,0:T(8,128)S(1)} fusion(bf16[1024,2048]{1,0:T(8,128)(2,1)} %bitcast.10, f32[128,1024]{1,0:T(8,128)} %select_reduce_fusion), kind=kOutput, calls=%fused_computation.31 | convolution fusion | flops 537001984 | bytes 5767168 | tf_op jit(solution)/shard_map/dot_general | solution.py:121
  274.7 3.8 %fusion.9 = bf16[128,2048]{1,0:T(8,128)(2,1)} fusion(f32[128,2048]{1,0:T(8,128)S(1)} %copy-done.8, f32[128,2048]{1,0:T(8,128)S(1)} %fusion.22, bf16[1024,2048]{1,0:T(8,128)(2,1)} %bitcast.10, f32[128,1024]{1,0:T(8,128)S(1)} %copy-done.4), kind=kOutput, calls=%fused_computation.19 | convolution fusion | flops 538181632 | bytes 7340032 | tf_op jit(solution)/shard_map/dot_general | solution.py:122
  (60 shorter events, 0.6 us)
Async XLA Ops:
  6.5 159.2 %copy-start = (bf16[1,768,2048]{2,1,0:T(8,128)(2,1)S(1)}, bf16[1,768,2048]{2,1,0:T(8,128)(2,1)}, u32[]{:S(2)}) copy-start(bf16[1,768,2048]{2,1,0:T(8,128)(2,1)} %param.19) | copy-start | bytes 9437188
  6.5 164.3 %all-gather.5.cloned.1.call-start = ((), (), s32[]{:S(2)}) async-start(), calls=%async_computation.3 | async-start | bytes 6488064 | tf_op jit(solution)/shard_map/all_gather | solution.py:86
  6.5 21.7 %collective-permute-start = (bf16[128,2048]{1,0:T(8,128)(2,1)}, bf16[128,2048]{1,0:T(8,128)(2,1)}, u32[]{:S(2)}, u32[]{:S(2)}) collective-permute-start(bf16[128,2048]{1,0:T(8,128)(2,1)} %param.13), channel_id=1, source_target_pairs={{0,64},{32,96},{64,128},{96,160},{128,192},{160,224},{192,0},{224,... | collective-permute-start | bytes 1572872 | tf_op jit(solution)/shard_map/ppermute | solution.py:22
  8.1 13.7 %collective-permute-start.1 = (bf16[128,2048]{1,0:T(8,128)(2,1)}, bf16[128,2048]{1,0:T(8,128)(2,1)}, u32[]{:S(2)}, u32[]{:S(2)}) collective-permute-start(bf16[128,2048]{1,0:T(8,128)(2,1)} %param.13), channel_id=1, source_target_pairs={{0,192},{32,224},{64,0},{96,32},{128,64},{160,96},{192,128},{224,1... | collective-permute-start | bytes 1572872 | tf_op jit(solution)/shard_map/ppermute | solution.py:22
  22.8 7.4 %collective-permute-start.2 = (bf16[64,2048]{1,0:T(8,128)(2,1)S(1)}, bf16[64,2048]{1,0:T(8,128)(2,1)S(1)}, u32[]{:S(2)}, u32[]{:S(2)}) collective-permute-start(bf16[64,2048]{1,0:T(8,128)(2,1)S(1)} %slice.33), channel_id=1, source_target_pairs={{0,192},{32,224},{64,0},{96,32},{128,64},{160,96},{192,128},{224,1... | collective-permute-start | bytes 786440 | tf_op jit(solution)/shard_map/ppermute | solution.py:22
  29.2 7.9 %collective-permute-start.3 = (bf16[64,2048]{1,0:T(8,128)(2,1)S(1)}, bf16[64,2048]{1,0:T(8,128)(2,1)S(1)}, u32[]{:S(2)}, u32[]{:S(2)}) collective-permute-start(bf16[64,2048]{1,0:T(8,128)(2,1)S(1)} %slice.27), channel_id=1, source_target_pairs={{0,64},{32,96},{64,128},{96,160},{128,192},{160,224},{192,0},{224,... | collective-permute-start | bytes 786440 | tf_op jit(solution)/shard_map/ppermute | solution.py:22
  29.3 8.7 %collective-permute-start.4 = (bf16[128,2048]{1,0:T(8,128)(2,1)}, bf16[128,2048]{1,0:T(8,128)(2,1)}, u32[]{:S(2)}, u32[]{:S(2)}) collective-permute-start(bf16[128,2048]{1,0:T(8,128)(2,1)} %param.13), channel_id=1, source_target_pairs={{0,32},{32,0},{64,96},{96,64},{128,160},{160,128},{192,224},{224,1... | collective-permute-start | bytes 1572872 | tf_op jit(solution)/shard_map/ppermute | solution.py:25
  29.4 8.6 %collective-permute-start.5 = (bf16[128,2048]{1,0:T(8,128)(2,1)}, bf16[128,2048]{1,0:T(8,128)(2,1)}, u32[]{:S(2)}, u32[]{:S(2)}) collective-permute-start(bf16[128,2048]{1,0:T(8,128)(2,1)} %collective-permute-done), channel_id=1, source_target_pairs={{0,32},{32,0},{64,96},{96,64},{128,160},{160,128},{192,224},{224,1... | collective-permute-start | bytes 1572872 | tf_op jit(solution)/shard_map/ppermute | solution.py:25
  29.9 8.1 %collective-permute-start.6 = (bf16[128,2048]{1,0:T(8,128)(2,1)}, bf16[128,2048]{1,0:T(8,128)(2,1)}, u32[]{:S(2)}, u32[]{:S(2)}) collective-permute-start(bf16[128,2048]{1,0:T(8,128)(2,1)} %collective-permute-done.1), channel_id=1, source_target_pairs={{0,32},{32,0},{64,96},{96,64},{128,160},{160,128},{192,224},{224,1... | collective-permute-start | bytes 1572872 | tf_op jit(solution)/shard_map/ppermute | solution.py:25
  37.1 0.8 copy-start.7
  37.9 2.0 collective-permute-start.7
  40.0 130.8 %all-gather.3.cloned.1.call-start = ((), (), s32[]{:S(2)}) async-start(), calls=%async_computation.2 | async-start | bytes 12976128 | tf_op jit(solution)/shard_map/all_gather | solution.py:85
  40.8 8.8 %copy-start.9 = (bf16[128,2048]{1,0:T(8,128)(2,1)S(1)}, bf16[128,2048]{1,0:T(8,128)(2,1)}, u32[]{:S(2)}) copy-start(bf16[128,2048]{1,0:T(8,128)(2,1)} %param.12) | copy-start | bytes 1572868
  40.8 8.8 %copy-start.10 = (bf16[1024,128]{1,0:T(8,128)(2,1)S(1)}, bf16[1024,128]{1,0:T(8,128)(2,1)}, u32[]{:S(2)}) copy-start(bf16[1024,128]{1,0:T(8,128)(2,1)} %fusion.15) | copy-start | bytes 786436
  47.4 4.0 %copy-start.13 = (f32[2048]{0:T(1024)S(1)}, f32[2048]{0:T(1024)}, u32[]{:S(2)}) copy-start(f32[2048]{0:T(1024)} %param.14) | copy-start | bytes 24580
  50.4 1.0 copy-start.5
  51.6 107.5 %copy-start.2 = (bf16[128,2048]{1,0:T(8,128)(2,1)}, bf16[128,2048]{1,0:T(8,128)(2,1)S(1)}, u32[]{:S(2)}) copy-start(bf16[128,2048]{1,0:T(8,128)(2,1)S(1)} %multiply_convert_fusion) | copy-start | bytes 1572868
  51.6 107.5 %slice-start = ((s8[6291456]{0:T(1024)(128)(4,1)}), s8[4194304]{0:T(1024)(128)(4,1)S(1)}, s32[]{:S(2)}) async-start(s8[6291456]{0:T(1024)(128)(4,1)} %bitcast.54), calls=%async_computation.4 | async-start | bytes 8388608
  52.9 106.2 %slice-start.1 = ((s8[6291456]{0:T(1024)(128)(4,1)}), s8[2097152]{0:T(1024)(128)(4,1)S(1)}, s32[]{:S(2)}) async-start(s8[6291456]{0:T(1024)(128)(4,1)} %bitcast.54), calls=%async_computation.5 | async-start | bytes 4194304
  170.9 6.7 %copy-start.3 = (bf16[128,2048]{1,0:T(8,128)(2,1)S(1)}, bf16[128,2048]{1,0:T(8,128)(2,1)}, u32[]{:S(2)}) copy-start(bf16[128,2048]{1,0:T(8,128)(2,1)} %copy-done.2) | copy-start | bytes 1572868
  170.9 6.7 %copy-start.11 = (bf16[2048,32]{0,1:T(8,128)(2,1)S(1)}, bf16[2048,32]{0,1:T(8,128)(2,1)}, u32[]{:S(2)}) copy-start(bf16[2048,32]{0,1:T(8,128)(2,1)} %param.15) | copy-start | bytes 393220
  170.9 7.0 %copy-start.12 = (s32[128,6]{0,1:T(8,128)S(1)}, s32[128,6]{0,1:T(8,128)}, u32[]{:S(2)}) copy-start(s32[128,6]{0,1:T(8,128)} %param.20) | copy-start | bytes 9220
  170.9 100.6 %all-to-all-start.1 = ((bf16[32,32,2048]{2,1,0:T(8,128)(2,1)}), bf16[32,32,2048]{2,1,0:T(8,128)(2,1)}, u32[]{:S(2)}, u32[]{:S(2)}) async-start(bf16[32,32,2048]{2,1,0:T(8,128)(2,1)} %bitcast.50), calls=%async_computation.1 | async-start | bytes 8388608 | tf_op jit(solution)/shard_map/all_to_all | solution.py:113
  177.9 7.4 %slice-start.2 = ((s8[5767168]{0:T(1024)(128)(4,1)}), s8[4194304]{0:T(1024)(128)(4,1)S(1)}, s32[]{:S(2)}) async-start(s8[5767168]{0:T(1024)(128)(4,1)} %bitcast.56), calls=%async_computation.6 | async-start | bytes 8388608
  179.1 6.2 %copy-start.6 = (f32[128,2048]{1,0:T(8,128)S(1)}, f32[128,2048]{1,0:T(8,128)}, u32[]{:S(2)}) copy-start(f32[128,2048]{1,0:T(8,128)} %copy-done.5) | copy-start | bytes 3145732
  179.1 6.2 %slice-start.3 = ((s8[5767168]{0:T(1024)(128)(4,1)}), s8[1572864]{0:T(1024)(128)(4,1)S(1)}, s32[]{:S(2)}) async-start(s8[5767168]{0:T(1024)(128)(4,1)} %bitcast.56), calls=%async_computation.7 | async-start | bytes 3145728
  271.5 3.2 %copy-start.4 = (f32[128,1024]{1,0:T(8,128)S(1)}, f32[128,1024]{1,0:T(8,128)}, u32[]{:S(2)}) copy-start(f32[128,1024]{1,0:T(8,128)} %select_reduce_fusion) | copy-start | bytes 1572868
  271.5 3.2 %copy-start.8 = (f32[128,2048]{1,0:T(8,128)S(1)}, f32[128,2048]{1,0:T(8,128)}, u32[]{:S(2)}) copy-start(f32[128,2048]{1,0:T(8,128)} %convolution_add_fusion.1) | copy-start | bytes 3145732
  271.5 7.1 %copy-start.1 = (bf16[1,768,2048]{2,1,0:T(8,128)(2,1)S(1)}, bf16[1,768,2048]{2,1,0:T(8,128)(2,1)}, u32[]{:S(2)}) copy-start(bf16[1,768,2048]{2,1,0:T(8,128)(2,1)} %param.19) | copy-start | bytes 9437188
Sparse Core Ops, SparseCore 0:
  40.1 45.2 all-gather.4
  87.3 66.4 all-gather.2

commit v10 on v8

--- a/solution.py
+++ b/solution.py
@@ -2,6 +2,7 @@
 import jax.numpy as jnp
 from jax import lax
 from jax.sharding import PartitionSpec as P
+from jax.experimental import pallas as pl
 
 
 def swiglu_rows(rows, w_in, w_out):
@@ -41,6 +42,25 @@
     y, c = g // 2, g % 2
     ys = (y + jnp.array([0, -1, 1, 2], jnp.int32) + ring) % ring
     return jnp.concatenate([2 * ys + c, 2 * ys + 1 - c])
+
+
+def _pieces_dot_kernel(ctx_ref, *refs):
+    out_ref = refs[-1]
+    width = refs[0].shape[0]
+    acc = None
+    for i, piece in enumerate(refs[:-1]):
+        term = jnp.dot(
+            ctx_ref[:, i * width:(i + 1) * width], piece[...], preferred_element_type=jnp.float32
+        )
+        acc = term if acc is None else acc + term
+    out_ref[...] = acc
+
+
+def pieces_dot(ctx, pieces):
+    return pl.pallas_call(
+        _pieces_dot_kernel,
+        out_shape=jax.ShapeDtypeStruct((ctx.shape[0], pieces[0].shape[1]), jnp.float32),
+    )(ctx, *pieces)
 
 
 def per_device(
@@ -84,10 +104,7 @@
     pieces, shared_in, shared_out = lax.optimization_barrier((pieces, shared_in, shared_out))
     shared_in = lax.all_gather(shared_in, "group", axis=0, tiled=True)
     shared_out = lax.all_gather(shared_out, "group", axis=1, tiled=True)
-    attn = None
-    for i, piece in enumerate(pieces):
-        term = jnp.dot(ctx_perm[:, i, :], piece, preferred_element_type=jnp.float32)
-        attn = term if attn is None else attn + term
+    attn = pieces_dot(ctx_perm.reshape(tok_rows, -1), pieces)
     hidden_state = (residual.astype(jnp.float32) + attn).astype(jnp.bfloat16)
     hidden_f = hidden_state.astype(jnp.float32)
     scale = lax.rsqrt(jnp.mean(hidden_f * hidden_f, axis=-1, keepdims=True) + 1e-06)

time: 286 us -> 283 us (0.990)
  matrix products: 40.4 us -> 32.3 us
  Pallas kernels: 0 us -> 4.43 us
    dot_general x8 -> x0, matrix products: 9.46 us -> none  [per_device(): term = jnp.dot(ctx_perm[:, i, :], piece, preferred_element_type=jnp.float32)]
    pallas_call x0 -> x1, Pallas kernels: none -> 4.43 us  [pieces_dot(): pl.pallas_call(_pieces_dot_kernel, out_shape=jax.ShapeDtypeStruct((ctx.sh...]
  transfers between devices with their start and end apart: 11 -> 11, of which waited for: 5 -> 5; matrix products, arithmetic and copies ran while one was open for 15% -> 13% of each run, Pallas kernels for 0% -> 2%
where the time goes in v10:
time: 283 us; the launch traced here: 282 us
  blocking collectives  106 us (37%)
  waiting for transfers between devices  99.2 us (35%)
  matrix products  32.3 us (11%)
  starting transfers between devices  13.7 us (5%)
  between operations  13.7 us (5%)
  other arithmetic  6.89 us (2%)
  local copies, waits for them, and re-layouts  6.14 us (2%)
  Pallas kernels  4.43 us (2%)
    all_to_all x1, blocking collectives, per_device(): lax.all_to_all(outgoing, 'expert', split_axis=0, concat_axis=0, tiled=True)  106 us
    all_to_all x1, waiting for transfers between devices, per_device(): lax.all_to_all(expert_rows.reshape(arrived.shape), 'expert', split_axis=0...  82.8 us
    ppermute x4, waiting for transfers between devices, shift(): return lax.ppermute(x, 'group', pairs)  13.6 us
    all_to_all x1, starting transfers between devices, per_device(): lax.all_to_all(expert_rows.reshape(arrived.shape), 'expert', split_axis=0...  6.65 us
    dot_general x1, matrix products, swiglu_rows(): mid = jnp.dot(rows, w_in, preferred_element_type=jnp.float32)  6.64 us
    ppermute x4, starting transfers between devices, shift(): return lax.ppermute(x, 'group', pairs)  6.33 us
    dot_general x1, matrix products, per_device(): shared_mid = jnp.dot(normed, shared_in, preferred_element_type=jnp.float32)  6.32 us
  transfers between devices with their start and end apart: 11, of which 5 were waited for; matrix products, arithmetic and copies ran while one was open for 13% of the time, Pallas kernels for 2%

profile of v10, /device:TPU:32, one launch (start us, length us, event | category | flops | bytes accessed | tf_op | source)
XLA Modules:
  0.0 282.5 jit_solution(4518370355238739744)
XLA Ops:
  6.5 1.6 collective-permute-start
  8.1 1.7 collective-permute-start.1
  9.8 0.8 copy.33
  10.6 0.1 eq.81
  10.7 0.1 eq.85
  10.9 1.7 reduce-window.6
  12.6 0.3 slice_reduce_fusion
  12.9 0.1 fusion.27
  13.0 0.1 reduce_sum.48
  13.2 0.1 copy.36
  13.2 0.7 multiply_add_fusion
  13.9 0.5 fusion.5
  14.5 0.7 broadcast_add_fusion
  15.2 0.1 add_multiply_fusion
  15.2 0.1 add_bitcast_fusion.1
  15.3 6.5 %collective-permute-done.1.refs_2_ = bf16[128,2048]{1,0:T(8,128)(2,1)} collective-permute-done((bf16[128,2048]{1,0:T(8,128)(2,1)}, bf16[128,2048]{1,0:T(8,128)(2,1)}, u32[]{:S(2)}, u32[]{:S(2)}) %collective-permute-start.1) | collective-permute-done | bytes 524320 | tf_op jit(solution)/shard_map/ppermute | solution.py:23
  21.8 1.0 slice.33
  22.8 3.0 %collective-permute-start.2 = (bf16[64,2048]{1,0:T(8,128)(2,1)S(1)}, bf16[64,2048]{1,0:T(8,128)(2,1)S(1)}, u32[]{:S(2)}, u32[]{:S(2)}) collective-permute-start(bf16[64,2048]{1,0:T(8,128)(2,1)S(1)} %slice.33), channel_id=1, source_target_pairs={{0,192},{32,224},{64,0},{96,32},{128,64},{160,96},{192,128},{224,1... | collective-permute-start | bytes 786440 | tf_op jit(solution)/shard_map/ppermute | solution.py:23
  25.8 2.4 fusion.13
  28.2 1.0 slice.27
  29.2 0.1 collective-permute-start.3
  29.3 0.1 collective-permute-start.4
  29.4 0.5 collective-permute-start.5
  29.9 0.1 collective-permute-start.6
  30.0 0.3 collective-permute-done.2
  30.3 6.9 %collective-permute-done.3 = bf16[64,2048]{1,0:T(8,128)(2,1)S(1)} collective-permute-done((bf16[64,2048]{1,0:T(8,128)(2,1)S(1)}, bf16[64,2048]{1,0:T(8,128)(2,1)S(1)}, u32[]{:S(2)}, u32[]{:S(2)}) %collective-permute-start.3) | collective-permute-done | bytes 262176 | tf_op jit(solution)/shard_map/ppermute | solution.py:23
  37.2 0.8 copy-done.4
  38.0 2.0 collective-permute-done.7.refs_7_
  40.0 0.0 all-gather.5.cloned.1.call-update
  40.0 0.0 all-gather.3.cloned.1.call-start
  40.1 0.7 all-gather.3.cloned.1.call-update
  40.8 1.8 copy.38.ctx_ref
  42.6 4.4 %shard_map.109 = f32[128,2048]{1,0:T(8,128)} custom-call(bf16[128,1024]{1,0:T(8,128)(2,1)} %copy.38.ctx_ref, bf16[128,2048]{1,0:T(8,128)(2,1)} %refs_0_, bf16[128,2048]{1,0:T(8,128)(2,1)} %collective-permute-done.refs_1_, bf16[128,2048]{1,0:T(8,128)(2,1)} %collective-permute-done.1.refs_2_, bf16[128,2048]{1,0:T(8,128)(2,1)} %copy-done.4, ...), custom_call_target="tpu_custom_call" | custom-call | tf_op jit(solution)/shard_map/pallas_call | solution.py:60
  47.0 1.6 fusion.16
  48.7 0.0 slice-start
  48.7 1.3 convolution_convert_fusion.1
  50.0 0.0 slice-start.1
  50.0 106.1 %all_to_all.10 = bf16[32,32,2048]{2,1,0:T(8,128)(2,1)S(1)} all-to-all(bf16[32,32,2048]{2,1,0:T(8,128)(2,1)S(1)} %bitcast.44), channel_id=1, replica_groups=mesh['group'=8,'expert'=32] {'expert'}, dimensions={0} | all-to-all | bytes 8388608 | tf_op jit(solution)/shard_map/all_to_all | solution.py:125
  156.2 6.6 %fusion = f32[1024,1536]{1,0:T(8,128)S(1)} fusion(bf16[1024,2048]{1,0:T(8,128)(2,1)S(1)} %bitcast.46, bf16[1,2048,1536]{2,1,0:T(8,128)(2,1)S(1)} %bitcast.50), kind=kOutput, calls=%fused_computation | convolution fusion | flops 6442450944 | bytes 16777216 | tf_op jit(solution)/shard_map/dot_general | solution.py:10
  162.8 5.1 %convolution_convert_fusion = bf16[1024,2048]{1,0:T(8,128)(2,1)} fusion(bf16[1,768,2048]{2,1,0:T(8,128)(2,1)S(1)} %copy-done, f32[1024,1536]{1,0:T(8,128)S(1)} %fusion), kind=kOutput, calls=%fused_computation.4 | convolution fusion | flops 3228041216 | bytes 13631488 | tf_op jit(solution)/shard_map/dot_general | solution.py:12
  168.0 6.7 %all-to-all-start.1 = ((bf16[32,32,2048]{2,1,0:T(8,128)(2,1)}), bf16[32,32,2048]{2,1,0:T(8,128)(2,1)}, u32[]{:S(2)}, u32[]{:S(2)}) async-start(bf16[32,32,2048]{2,1,0:T(8,128)(2,1)} %bitcast.45), calls=%async_computation.1 | async-start | bytes 8388608 | tf_op jit(solution)/shard_map/all_to_all | solution.py:129
  174.7 1.4 fusion.33
  176.1 1.3 select_reduce_fusion
  177.4 6.3 %fusion.35 = f32[128,2816]{1,0:T(8,128)S(1)} fusion(bf16[2048,2816]{1,0:T(8,128)(2,1)} %all-gather.3.cloned.1.call-done, bf16[128,2048]{1,0:T(8,128)(2,1)} %copy-done.1, f32[2048]{0:T(1024)S(1)} %copy-done.6, f32[128]{0:T(128)S(1)} %add_rsqrt_fusion), kind=kOutput, calls=%fused_computation.64 | convolution fusion | flops 1477443584 | bytes 13509120 | tf_op jit(solution)/shard_map/dot_general | solution.py:140
  183.8 2.0 convolution_add_fusion.1
  185.8 82.8 %all-to-all-done.1 = bf16[32,32,2048]{2,1,0:T(8,128)(2,1)} async-done(((bf16[32,32,2048]{2,1,0:T(8,128)(2,1)}), bf16[32,32,2048]{2,1,0:T(8,128)(2,1)}, u32[]{:S(2)}, u32[]{:S(2)}) %all-to-all-start.1) | async-done | bytes 4194336 | tf_op jit(solution)/shard_map/all_to_all | solution.py:129
  268.6 3.2 %fusion.23 = f32[128,2048]{1,0:T(8,128)S(1)} fusion(bf16[1024,2048]{1,0:T(8,128)(2,1)} %bitcast.10, f32[128,1024]{1,0:T(8,128)} %select_reduce_fusion), kind=kOutput, calls=%fused_computation.32 | convolution fusion | flops 537001984 | bytes 5767168 | tf_op jit(solution)/shard_map/dot_general | solution.py:137
  271.8 3.8 %fusion.7 = bf16[128,2048]{1,0:T(8,128)(2,1)} fusion(f32[128,2048]{1,0:T(8,128)S(1)} %copy-done.5, f32[128,2048]{1,0:T(8,128)S(1)} %fusion.23, bf16[1024,2048]{1,0:T(8,128)(2,1)} %bitcast.10, f32[128,1024]{1,0:T(8,128)S(1)} %copy-done.3), kind=kOutput, calls=%fused_computation.16 | convolution fusion | flops 538181632 | bytes 7340032 | tf_op jit(solution)/shard_map/dot_general | solution.py:138
  (43 shorter events, 0.2 us)
Async XLA Ops:
  6.5 156.3 %copy-start = (bf16[1,768,2048]{2,1,0:T(8,128)(2,1)S(1)}, bf16[1,768,2048]{2,1,0:T(8,128)(2,1)}, u32[]{:S(2)}) copy-start(bf16[1,768,2048]{2,1,0:T(8,128)(2,1)} %param.19) | copy-start | bytes 9437188
  6.5 161.5 %all-gather.5.cloned.1.call-start = ((), (), s32[]{:S(2)}) async-start(), calls=%async_computation.3 | async-start | bytes 6488064 | tf_op jit(solution)/shard_map/all_gather | solution.py:106
  6.5 21.7 %collective-permute-start = (bf16[128,2048]{1,0:T(8,128)(2,1)}, bf16[128,2048]{1,0:T(8,128)(2,1)}, u32[]{:S(2)}, u32[]{:S(2)}) collective-permute-start(bf16[128,2048]{1,0:T(8,128)(2,1)} %refs_0_), channel_id=1, source_target_pairs={{0,64},{32,96},{64,128},{96,160},{128,192},{160,224},{192,0},{224,... | collective-permute-start | bytes 1572872 | tf_op jit(solution)/shard_map/ppermute | solution.py:23
  8.1 13.7 %collective-permute-start.1 = (bf16[128,2048]{1,0:T(8,128)(2,1)}, bf16[128,2048]{1,0:T(8,128)(2,1)}, u32[]{:S(2)}, u32[]{:S(2)}) collective-permute-start(bf16[128,2048]{1,0:T(8,128)(2,1)} %refs_0_), channel_id=1, source_target_pairs={{0,192},{32,224},{64,0},{96,32},{128,64},{160,96},{192,128},{224,1... | collective-permute-start | bytes 1572872 | tf_op jit(solution)/shard_map/ppermute | solution.py:23
  22.8 7.4 %collective-permute-start.2 = (bf16[64,2048]{1,0:T(8,128)(2,1)S(1)}, bf16[64,2048]{1,0:T(8,128)(2,1)S(1)}, u32[]{:S(2)}, u32[]{:S(2)}) collective-permute-start(bf16[64,2048]{1,0:T(8,128)(2,1)S(1)} %slice.33), channel_id=1, source_target_pairs={{0,192},{32,224},{64,0},{96,32},{128,64},{160,96},{192,128},{224,1... | collective-permute-start | bytes 786440 | tf_op jit(solution)/shard_map/ppermute | solution.py:23
  29.2 7.9 %collective-permute-start.3 = (bf16[64,2048]{1,0:T(8,128)(2,1)S(1)}, bf16[64,2048]{1,0:T(8,128)(2,1)S(1)}, u32[]{:S(2)}, u32[]{:S(2)}) collective-permute-start(bf16[64,2048]{1,0:T(8,128)(2,1)S(1)} %slice.27), channel_id=1, source_target_pairs={{0,64},{32,96},{64,128},{96,160},{128,192},{160,224},{192,0},{224,... | collective-permute-start | bytes 786440 | tf_op jit(solution)/shard_map/ppermute | solution.py:23
  29.3 8.7 %collective-permute-start.4 = (bf16[128,2048]{1,0:T(8,128)(2,1)}, bf16[128,2048]{1,0:T(8,128)(2,1)}, u32[]{:S(2)}, u32[]{:S(2)}) collective-permute-start(bf16[128,2048]{1,0:T(8,128)(2,1)} %refs_0_), channel_id=1, source_target_pairs={{0,32},{32,0},{64,96},{96,64},{128,160},{160,128},{192,224},{224,1... | collective-permute-start | bytes 1572872 | tf_op jit(solution)/shard_map/ppermute | solution.py:26
  29.4 8.6 %collective-permute-start.5 = (bf16[128,2048]{1,0:T(8,128)(2,1)}, bf16[128,2048]{1,0:T(8,128)(2,1)}, u32[]{:S(2)}, u32[]{:S(2)}) collective-permute-start(bf16[128,2048]{1,0:T(8,128)(2,1)} %collective-permute-done.refs_1_), channel_id=1, source_target_pairs={{0,32},{32,0},{64,96},{96,64},{128,160},{160,128},{192,224},{224,1... | collective-permute-start | bytes 1572872 | tf_op jit(solution)/shard_map/ppermute | solution.py:26
  29.9 8.1 %collective-permute-start.6 = (bf16[128,2048]{1,0:T(8,128)(2,1)}, bf16[128,2048]{1,0:T(8,128)(2,1)}, u32[]{:S(2)}, u32[]{:S(2)}) collective-permute-start(bf16[128,2048]{1,0:T(8,128)(2,1)} %collective-permute-done.1.refs_2_), channel_id=1, source_target_pairs={{0,32},{32,0},{64,96},{96,64},{128,160},{160,128},{192,224},{224,1... | collective-permute-start | bytes 1572872 | tf_op jit(solution)/shard_map/ppermute | solution.py:26
  37.1 0.8 copy-start.4
  37.9 2.0 collective-permute-start.7
  40.0 128.0 %all-gather.3.cloned.1.call-start = ((), (), s32[]{:S(2)}) async-start(), calls=%async_computation.2 | async-start | bytes 12976128 | tf_op jit(solution)/shard_map/all_gather | solution.py:105
  40.8 7.9 %copy-start.6 = (f32[2048]{0:T(1024)S(1)}, f32[2048]{0:T(1024)}, u32[]{:S(2)}) copy-start(f32[2048]{0:T(1024)} %param.14) | copy-start | bytes 24580
  48.6 107.6 %copy-start.1 = (bf16[128,2048]{1,0:T(8,128)(2,1)}, bf16[128,2048]{1,0:T(8,128)(2,1)S(1)}, u32[]{:S(2)}) copy-start(bf16[128,2048]{1,0:T(8,128)(2,1)S(1)} %get-tuple-element.40) | copy-start | bytes 1572868
  48.7 107.5 %slice-start = ((s8[6291456]{0:T(1024)(128)(4,1)}), s8[4194304]{0:T(1024)(128)(4,1)S(1)}, s32[]{:S(2)}) async-start(s8[6291456]{0:T(1024)(128)(4,1)} %bitcast.49), calls=%async_computation.4 | async-start | bytes 8388608
  50.0 106.2 %slice-start.1 = ((s8[6291456]{0:T(1024)(128)(4,1)}), s8[2097152]{0:T(1024)(128)(4,1)S(1)}, s32[]{:S(2)}) async-start(s8[6291456]{0:T(1024)(128)(4,1)} %bitcast.49), calls=%async_computation.5 | async-start | bytes 4194304
  168.0 6.7 %copy-start.8 = (bf16[2048,32]{0,1:T(8,128)(2,1)S(1)}, bf16[2048,32]{0,1:T(8,128)(2,1)}, u32[]{:S(2)}) copy-start(bf16[2048,32]{0,1:T(8,128)(2,1)} %param.15) | copy-start | bytes 393220
  168.0 8.1 %copy-start.7 = (s32[128,6]{0,1:T(8,128)S(1)}, s32[128,6]{0,1:T(8,128)}, u32[]{:S(2)}) copy-start(s32[128,6]{0,1:T(8,128)} %param.20) | copy-start | bytes 9220
  168.0 100.6 %all-to-all-start.1 = ((bf16[32,32,2048]{2,1,0:T(8,128)(2,1)}), bf16[32,32,2048]{2,1,0:T(8,128)(2,1)}, u32[]{:S(2)}, u32[]{:S(2)}) async-start(bf16[32,32,2048]{2,1,0:T(8,128)(2,1)} %bitcast.45), calls=%async_computation.1 | async-start | bytes 8388608 | tf_op jit(solution)/shard_map/all_to_all | solution.py:129
  176.1 7.6 %slice-start.2 = ((s8[5767168]{0:T(1024)(128)(4,1)}), s8[4194304]{0:T(1024)(128)(4,1)S(1)}, s32[]{:S(2)}) async-start(s8[5767168]{0:T(1024)(128)(4,1)} %bitcast.51), calls=%async_computation.6 | async-start | bytes 8388608
  177.4 6.3 %copy-start.2 = (bf16[128,2048]{1,0:T(8,128)(2,1)S(1)}, bf16[128,2048]{1,0:T(8,128)(2,1)}, u32[]{:S(2)}) copy-start(bf16[128,2048]{1,0:T(8,128)(2,1)} %copy-done.1) | copy-start | bytes 1572868
  177.4 6.4 %slice-start.3 = ((s8[5767168]{0:T(1024)(128)(4,1)}), s8[1572864]{0:T(1024)(128)(4,1)S(1)}, s32[]{:S(2)}) async-start(s8[5767168]{0:T(1024)(128)(4,1)} %bitcast.51), calls=%async_computation.7 | async-start | bytes 3145728
  268.6 3.2 %copy-start.3 = (f32[128,1024]{1,0:T(8,128)S(1)}, f32[128,1024]{1,0:T(8,128)}, u32[]{:S(2)}) copy-start(f32[128,1024]{1,0:T(8,128)} %select_reduce_fusion) | copy-start | bytes 1572868
  268.6 3.2 %copy-start.5 = (f32[128,2048]{1,0:T(8,128)S(1)}, f32[128,2048]{1,0:T(8,128)}, u32[]{:S(2)}) copy-start(f32[128,2048]{1,0:T(8,128)} %convolution_add_fusion.1) | copy-start | bytes 3145732
Sparse Core Ops, SparseCore 0:
  40.1 45.2 all-gather.4
  87.3 66.4 all-gather.2

commit v11 on v10

--- a/solution.py
+++ b/solution.py
@@ -134,8 +134,10 @@
         tiled=True,
     )
     returned = returned.reshape(slots, width)
-    routed = jnp.dot(combine_hi, returned, preferred_element_type=jnp.float32)
-    routed = routed + jnp.dot(combine_lo, returned, preferred_element_type=jnp.float32)
+    both = jnp.dot(
+        jnp.concatenate([combine_hi, combine_lo], axis=0), returned, preferred_element_type=jnp.float32
+    )
+    routed = both[:tok_rows] + both[tok_rows:]
     shared_hidden = shared_out.shape[0]
     shared_mid = jnp.dot(
         normed,

time: 283 us -> 284 us (level)
    dot_general x2 -> x1, matrix products: 7 us -> 3.66 us  [per_device(): jnp.dot(jnp.concatenate([combine_hi, combine_lo], axis=0), returned, pref...]
where the time goes in v11:
time: 284 us
  blocking collectives  106 us (37%)
  waiting for transfers between devices  100 us (35%)
  matrix products  32.6 us (11%)
  starting transfers between devices  13.7 us (5%)
  between operations  13.7 us (5%)
  other arithmetic  6.85 us (2%)
  local copies, waits for them, and re-layouts  6.12 us (2%)
  Pallas kernels  4.43 us (2%)
    all_to_all x1, blocking collectives, per_device(): lax.all_to_all(outgoing, 'expert', split_axis=0, concat_axis=0, tiled=True)  106 us
    all_to_all x1, waiting for transfers between devices, per_device(): lax.all_to_all(expert_rows.reshape(arrived.shape), 'expert', split_axis=0...  83.9 us
    ppermute x4, waiting for transfers between devices, shift(): return lax.ppermute(x, 'group', pairs)  13.6 us
    dot_general x1, matrix products, per_device(): shared_mid = jnp.dot(normed, shared_in, preferred_element_type=jnp.float32)  7.32 us
    all_to_all x1, starting transfers between devices, per_device(): lax.all_to_all(expert_rows.reshape(arrived.shape), 'expert', split_axis=0...  6.65 us
    dot_general x1, matrix products, swiglu_rows(): mid = jnp.dot(rows, w_in, preferred_element_type=jnp.float32)  6.64 us
    ppermute x4, starting transfers between devices, shift(): return lax.ppermute(x, 'group', pairs)  6.33 us
  transfers between devices with their start and end apart: 11, of which 5 were waited for; matrix products, arithmetic and copies ran while one was open for 13% of the time, Pallas kernels for 2%

profile of v11, /device:TPU:32, one launch (start us, length us, event | category | flops | bytes accessed | tf_op | source)
XLA Modules:
  0.0 283.8 jit_solution(11019232205932792710)
XLA Ops:
  6.5 1.6 collective-permute-start
  8.1 1.7 collective-permute-start.1
  9.8 0.8 copy.33
  10.6 0.1 eq.85
  10.7 0.1 eq.81
  10.9 1.7 reduce-window.6
  12.6 0.3 slice_reduce_fusion
  12.9 0.1 fusion.28
  13.0 0.1 reduce_sum.48
  13.2 0.1 copy.36
  13.2 0.7 multiply_add_fusion
  13.9 0.5 fusion.5
  14.5 0.7 broadcast_add_fusion
  15.2 0.1 add_multiply_fusion
  15.2 0.1 add_bitcast_fusion.1
  15.3 6.5 %collective-permute-done.1.refs_2_ = bf16[128,2048]{1,0:T(8,128)(2,1)} collective-permute-done((bf16[128,2048]{1,0:T(8,128)(2,1)}, bf16[128,2048]{1,0:T(8,128)(2,1)}, u32[]{:S(2)}, u32[]{:S(2)}) %collective-permute-start.1) | collective-permute-done | bytes 524320 | tf_op jit(solution)/shard_map/ppermute | solution.py:23
  21.8 1.0 slice.41
  22.8 3.0 %collective-permute-start.2 = (bf16[64,2048]{1,0:T(8,128)(2,1)S(1)}, bf16[64,2048]{1,0:T(8,128)(2,1)S(1)}, u32[]{:S(2)}, u32[]{:S(2)}) collective-permute-start(bf16[64,2048]{1,0:T(8,128)(2,1)S(1)} %slice.41), channel_id=1, source_target_pairs={{0,192},{32,224},{64,0},{96,32},{128,64},{160,96},{192,128},{224,1... | collective-permute-start | bytes 786440 | tf_op jit(solution)/shard_map/ppermute | solution.py:23
  25.8 2.4 fusion.13
  28.2 1.0 slice.33
  29.2 0.1 collective-permute-start.3
  29.3 0.1 collective-permute-start.4
  29.4 0.5 collective-permute-start.5
  29.9 0.1 collective-permute-start.6
  30.0 0.3 collective-permute-done.2
  30.3 6.9 %collective-permute-done.3 = bf16[64,2048]{1,0:T(8,128)(2,1)S(1)} collective-permute-done((bf16[64,2048]{1,0:T(8,128)(2,1)S(1)}, bf16[64,2048]{1,0:T(8,128)(2,1)S(1)}, u32[]{:S(2)}, u32[]{:S(2)}) %collective-permute-start.3) | collective-permute-done | bytes 262176 | tf_op jit(solution)/shard_map/ppermute | solution.py:23
  37.1 0.8 copy-done.4
  38.0 2.0 collective-permute-done.7.refs_7_
  40.0 0.0 all-gather.5.cloned.1.call-update
  40.0 0.0 all-gather.3.cloned.1.call-start
  40.0 0.7 all-gather.3.cloned.1.call-update
  40.8 1.8 copy.38.ctx_ref
  42.6 4.4 %shard_map.109 = f32[128,2048]{1,0:T(8,128)} custom-call(bf16[128,1024]{1,0:T(8,128)(2,1)} %copy.38.ctx_ref, bf16[128,2048]{1,0:T(8,128)(2,1)} %refs_0_, bf16[128,2048]{1,0:T(8,128)(2,1)} %collective-permute-done.refs_1_, bf16[128,2048]{1,0:T(8,128)(2,1)} %collective-permute-done.1.refs_2_, bf16[128,2048]{1,0:T(8,128)(2,1)} %copy-done.4, ...), custom_call_target="tpu_custom_call" | custom-call | tf_op jit(solution)/shard_map/pallas_call | solution.py:60
  47.0 1.6 fusion.16
  48.6 0.0 slice-start
  48.6 1.3 convolution_convert_fusion.1
  50.0 0.0 slice-start.1
  50.0 106.1 %all_to_all.10 = bf16[32,32,2048]{2,1,0:T(8,128)(2,1)S(1)} all-to-all(bf16[32,32,2048]{2,1,0:T(8,128)(2,1)S(1)} %bitcast.43), channel_id=1, replica_groups=mesh['group'=8,'expert'=32] {'expert'}, dimensions={0} | all-to-all | bytes 8388608 | tf_op jit(solution)/shard_map/all_to_all | solution.py:125
  156.2 6.6 %fusion = f32[1024,1536]{1,0:T(8,128)S(1)} fusion(bf16[1024,2048]{1,0:T(8,128)(2,1)S(1)} %bitcast.45, bf16[1,2048,1536]{2,1,0:T(8,128)(2,1)S(1)} %bitcast.49), kind=kOutput, calls=%fused_computation | convolution fusion | flops 6442450944 | bytes 16777216 | tf_op jit(solution)/shard_map/dot_general | solution.py:10
  162.8 5.1 %convolution_convert_fusion = bf16[1024,2048]{1,0:T(8,128)(2,1)} fusion(bf16[1,768,2048]{2,1,0:T(8,128)(2,1)S(1)} %copy-done, f32[1024,1536]{1,0:T(8,128)S(1)} %fusion), kind=kOutput, calls=%fused_computation.4 | convolution fusion | flops 3228041216 | bytes 13631488 | tf_op jit(solution)/shard_map/dot_general | solution.py:12
  168.0 6.7 %all-to-all-start.1 = ((bf16[32,32,2048]{2,1,0:T(8,128)(2,1)}), bf16[32,32,2048]{2,1,0:T(8,128)(2,1)}, u32[]{:S(2)}, u32[]{:S(2)}) async-start(bf16[32,32,2048]{2,1,0:T(8,128)(2,1)} %bitcast.44), calls=%async_computation.1 | async-start | bytes 8388608 | tf_op jit(solution)/shard_map/all_to_all | solution.py:129
  174.7 1.4 fusion.35
  176.1 0.4 select_reduce_fusion
  176.6 0.8 subtract_convert_fusion
  177.4 7.3 %fusion.37 = f32[128,2816]{1,0:T(8,128)} fusion(bf16[2048,2816]{1,0:T(8,128)(2,1)} %all-gather.3.cloned.1.call-done, bf16[128,2048]{1,0:T(8,128)(2,1)} %copy-done.1, f32[2048]{0:T(1024)S(1)} %copy-done.5, f32[128]{0:T(128)S(1)} %add_rsqrt_fusion), kind=kOutput, calls=%fused_computation.66 | convolution fusion | flops 1477443584 | bytes 13509120 | tf_op jit(solution)/shard_map/dot_general | solution.py:142
  184.7 83.9 %all-to-all-done.1 = bf16[32,32,2048]{2,1,0:T(8,128)(2,1)} async-done(((bf16[32,32,2048]{2,1,0:T(8,128)(2,1)}), bf16[32,32,2048]{2,1,0:T(8,128)(2,1)}, u32[]{:S(2)}, u32[]{:S(2)}) %all-to-all-start.1) | async-done | bytes 4194336 | tf_op jit(solution)/shard_map/all_to_all | solution.py:129
  268.6 3.7 %fusion.20 = f32[256,2048]{1,0:T(8,128)S(1)} fusion(bf16[1024,2048]{1,0:T(8,128)(2,1)} %bitcast.10, bf16[128,1024]{1,0:T(8,128)(2,1)S(1)} %get-tuple-element.39, bf16[128,1024]{1,0:T(8,128)(2,1)} %get-tuple-element.40), kind=kOutput, calls=%fused_computation.29 | convolution fusion | flops 1074790400 | bytes 6815744 | tf_op jit(solution)/shard_map/dot_general | solution.py:137
  272.3 4.7 %fusion.7 = bf16[128,2048]{1,0:T(8,128)(2,1)} fusion(bf16[1408,2048]{1,0:T(8,128)(2,1)} %all-gather.5.cloned.1.call-done, bf16[128,2048]{1,0:T(8,128)(2,1)S(1)} %copy-done.2, f32[256,2048]{1,0:T(8,128)S(1)} %fusion.20, f32[128,2816]{1,0:T(8,128)S(1)} %copy-done.3), kind=kOutput, calls=%fused_computation.15 | convolution fusion | flops 740589568 | bytes 10354688 | tf_op jit(solution)/shard_map/dot_general | solution.py:150
  (36 shorter events, 0.2 us)
Async XLA Ops:
  6.5 156.3 %copy-start = (bf16[1,768,2048]{2,1,0:T(8,128)(2,1)S(1)}, bf16[1,768,2048]{2,1,0:T(8,128)(2,1)}, u32[]{:S(2)}) copy-start(bf16[1,768,2048]{2,1,0:T(8,128)(2,1)} %param.19) | copy-start | bytes 9437188
  6.5 161.4 %all-gather.5.cloned.1.call-start = ((), (), s32[]{:S(2)}) async-start(), calls=%async_computation.3 | async-start | bytes 6488064 | tf_op jit(solution)/shard_map/all_gather | solution.py:106
  6.5 21.7 %collective-permute-start = (bf16[128,2048]{1,0:T(8,128)(2,1)}, bf16[128,2048]{1,0:T(8,128)(2,1)}, u32[]{:S(2)}, u32[]{:S(2)}) collective-permute-start(bf16[128,2048]{1,0:T(8,128)(2,1)} %refs_0_), channel_id=1, source_target_pairs={{0,64},{32,96},{64,128},{96,160},{128,192},{160,224},{192,0},{224,... | collective-permute-start | bytes 1572872 | tf_op jit(solution)/shard_map/ppermute | solution.py:23
  8.1 13.7 %collective-permute-start.1 = (bf16[128,2048]{1,0:T(8,128)(2,1)}, bf16[128,2048]{1,0:T(8,128)(2,1)}, u32[]{:S(2)}, u32[]{:S(2)}) collective-permute-start(bf16[128,2048]{1,0:T(8,128)(2,1)} %refs_0_), channel_id=1, source_target_pairs={{0,192},{32,224},{64,0},{96,32},{128,64},{160,96},{192,128},{224,1... | collective-permute-start | bytes 1572872 | tf_op jit(solution)/shard_map/ppermute | solution.py:23
  22.8 7.4 %collective-permute-start.2 = (bf16[64,2048]{1,0:T(8,128)(2,1)S(1)}, bf16[64,2048]{1,0:T(8,128)(2,1)S(1)}, u32[]{:S(2)}, u32[]{:S(2)}) collective-permute-start(bf16[64,2048]{1,0:T(8,128)(2,1)S(1)} %slice.41), channel_id=1, source_target_pairs={{0,192},{32,224},{64,0},{96,32},{128,64},{160,96},{192,128},{224,1... | collective-permute-start | bytes 786440 | tf_op jit(solution)/shard_map/ppermute | solution.py:23
  29.2 7.9 %collective-permute-start.3 = (bf16[64,2048]{1,0:T(8,128)(2,1)S(1)}, bf16[64,2048]{1,0:T(8,128)(2,1)S(1)}, u32[]{:S(2)}, u32[]{:S(2)}) collective-permute-start(bf16[64,2048]{1,0:T(8,128)(2,1)S(1)} %slice.33), channel_id=1, source_target_pairs={{0,64},{32,96},{64,128},{96,160},{128,192},{160,224},{192,0},{224,... | collective-permute-start | bytes 786440 | tf_op jit(solution)/shard_map/ppermute | solution.py:23
  29.3 8.7 %collective-permute-start.4 = (bf16[128,2048]{1,0:T(8,128)(2,1)}, bf16[128,2048]{1,0:T(8,128)(2,1)}, u32[]{:S(2)}, u32[]{:S(2)}) collective-permute-start(bf16[128,2048]{1,0:T(8,128)(2,1)} %refs_0_), channel_id=1, source_target_pairs={{0,32},{32,0},{64,96},{96,64},{128,160},{160,128},{192,224},{224,1... | collective-permute-start | bytes 1572872 | tf_op jit(solution)/shard_map/ppermute | solution.py:26
  29.4 8.6 %collective-permute-start.5 = (bf16[128,2048]{1,0:T(8,128)(2,1)}, bf16[128,2048]{1,0:T(8,128)(2,1)}, u32[]{:S(2)}, u32[]{:S(2)}) collective-permute-start(bf16[128,2048]{1,0:T(8,128)(2,1)} %collective-permute-done.refs_1_), channel_id=1, source_target_pairs={{0,32},{32,0},{64,96},{96,64},{128,160},{160,128},{192,224},{224,1... | collective-permute-start | bytes 1572872 | tf_op jit(solution)/shard_map/ppermute | solution.py:26
  29.9 8.1 %collective-permute-start.6 = (bf16[128,2048]{1,0:T(8,128)(2,1)}, bf16[128,2048]{1,0:T(8,128)(2,1)}, u32[]{:S(2)}, u32[]{:S(2)}) collective-permute-start(bf16[128,2048]{1,0:T(8,128)(2,1)} %collective-permute-done.1.refs_2_), channel_id=1, source_target_pairs={{0,32},{32,0},{64,96},{96,64},{128,160},{160,128},{192,224},{224,1... | collective-permute-start | bytes 1572872 | tf_op jit(solution)/shard_map/ppermute | solution.py:26
  37.1 0.8 copy-start.4
  37.9 2.0 collective-permute-start.7
  40.0 128.0 %all-gather.3.cloned.1.call-start = ((), (), s32[]{:S(2)}) async-start(), calls=%async_computation.2 | async-start | bytes 12976128 | tf_op jit(solution)/shard_map/all_gather | solution.py:105
  40.8 7.9 %copy-start.5 = (f32[2048]{0:T(1024)S(1)}, f32[2048]{0:T(1024)}, u32[]{:S(2)}) copy-start(f32[2048]{0:T(1024)} %param.14) | copy-start | bytes 24580
  48.6 107.6 %copy-start.1 = (bf16[128,2048]{1,0:T(8,128)(2,1)}, bf16[128,2048]{1,0:T(8,128)(2,1)S(1)}, u32[]{:S(2)}) copy-start(bf16[128,2048]{1,0:T(8,128)(2,1)S(1)} %get-tuple-element.42) | copy-start | bytes 1572868
  48.6 107.5 %slice-start = ((s8[6291456]{0:T(1024)(128)(4,1)}), s8[4194304]{0:T(1024)(128)(4,1)S(1)}, s32[]{:S(2)}) async-start(s8[6291456]{0:T(1024)(128)(4,1)} %bitcast.48), calls=%async_computation.4 | async-start | bytes 8388608
  50.0 106.2 %slice-start.1 = ((s8[6291456]{0:T(1024)(128)(4,1)}), s8[2097152]{0:T(1024)(128)(4,1)S(1)}, s32[]{:S(2)}) async-start(s8[6291456]{0:T(1024)(128)(4,1)} %bitcast.48), calls=%async_computation.5 | async-start | bytes 4194304
  168.0 6.7 %copy-start.7 = (bf16[2048,32]{0,1:T(8,128)(2,1)S(1)}, bf16[2048,32]{0,1:T(8,128)(2,1)}, u32[]{:S(2)}) copy-start(bf16[2048,32]{0,1:T(8,128)(2,1)} %param.15) | copy-start | bytes 393220
  168.0 8.1 %copy-start.6 = (s32[128,6]{0,1:T(8,128)S(1)}, s32[128,6]{0,1:T(8,128)}, u32[]{:S(2)}) copy-start(s32[128,6]{0,1:T(8,128)} %param.20) | copy-start | bytes 9220
  168.0 100.6 %all-to-all-start.1 = ((bf16[32,32,2048]{2,1,0:T(8,128)(2,1)}), bf16[32,32,2048]{2,1,0:T(8,128)(2,1)}, u32[]{:S(2)}, u32[]{:S(2)}) async-start(bf16[32,32,2048]{2,1,0:T(8,128)(2,1)} %bitcast.44), calls=%async_computation.1 | async-start | bytes 8388608 | tf_op jit(solution)/shard_map/all_to_all | solution.py:129
  268.6 3.7 %copy-start.2 = (bf16[128,2048]{1,0:T(8,128)(2,1)S(1)}, bf16[128,2048]{1,0:T(8,128)(2,1)}, u32[]{:S(2)}) copy-start(bf16[128,2048]{1,0:T(8,128)(2,1)} %copy-done.1) | copy-start | bytes 1572868
  268.6 3.7 %copy-start.3 = (f32[128,2816]{1,0:T(8,128)S(1)}, f32[128,2816]{1,0:T(8,128)}, u32[]{:S(2)}) copy-start(f32[128,2816]{1,0:T(8,128)} %fusion.37) | copy-start | bytes 4325380
Sparse Core Ops, SparseCore 0:
  40.1 45.2 all-gather.4
  87.3 66.4 all-gather.2

commit v12 on v11

--- a/solution.py
+++ b/solution.py
@@ -152,6 +152,7 @@
         shared_out,
         preferred_element_type=jnp.float32,
     )
+    shared_y = lax.optimization_barrier(shared_y)
     return (hidden_f + shared_y + routed).astype(jnp.bfloat16)
 
 

time: 284 us -> 281 us (0.989)
  matrix products: 32.6 us -> 28 us
where the time goes in v12:
time: 281 us; the launch traced here: 280 us
  blocking collectives  106 us (38%)
  waiting for transfers between devices  100 us (36%)
  matrix products  28 us (10%)
  starting transfers between devices  13.7 us (5%)
  between operations  13.7 us (5%)
  other arithmetic  7.92 us (3%)
  local copies, waits for them, and re-layouts  6.13 us (2%)
  Pallas kernels  4.45 us (2%)
    all_to_all x1, blocking collectives, per_device(): lax.all_to_all(outgoing, 'expert', split_axis=0, concat_axis=0, tiled=True)  106 us
    all_to_all x1, waiting for transfers between devices, per_device(): lax.all_to_all(expert_rows.reshape(arrived.shape), 'expert', split_axis=0...  83.7 us
    ppermute x4, waiting for transfers between devices, shift(): return lax.ppermute(x, 'group', pairs)  13.6 us
    all_to_all x1, starting transfers between devices, per_device(): lax.all_to_all(expert_rows.reshape(arrived.shape), 'expert', split_axis=0...  6.67 us
    dot_general x1, matrix products, swiglu_rows(): mid = jnp.dot(rows, w_in, preferred_element_type=jnp.float32)  6.64 us
    dot_general x1, matrix products, per_device(): shared_mid = jnp.dot(normed, shared_in, preferred_element_type=jnp.float32)  6.47 us
    ppermute x4, starting transfers between devices, shift(): return lax.ppermute(x, 'group', pairs)  6.33 us
  transfers between devices with their start and end apart: 11, of which 5 were waited for; matrix products, arithmetic and copies ran while one was open for 13% of the time, Pallas kernels for 2%

profile of v12, /device:TPU:32, one launch (start us, length us, event | category | flops | bytes accessed | tf_op | source)
XLA Modules:
  0.0 280.2 jit_solution(749832230392552417)
XLA Ops:
  6.5 1.6 collective-permute-start
  8.1 1.7 collective-permute-start.1
  9.8 0.8 copy.33
  10.6 0.1 eq.81
  10.7 0.1 eq.85
  10.9 1.7 reduce-window.6
  12.6 0.3 slice_reduce_fusion
  12.9 0.1 fusion.29
  13.0 0.1 reduce_sum.48
  13.2 0.1 copy.36
  13.2 0.7 multiply_add_fusion
  13.9 0.5 fusion.5
  14.5 0.7 broadcast_add_fusion
  15.2 0.1 add_multiply_fusion
  15.2 0.1 add_bitcast_fusion.1
  15.3 6.5 %collective-permute-done.1.refs_2_ = bf16[128,2048]{1,0:T(8,128)(2,1)} collective-permute-done((bf16[128,2048]{1,0:T(8,128)(2,1)}, bf16[128,2048]{1,0:T(8,128)(2,1)}, u32[]{:S(2)}, u32[]{:S(2)}) %collective-permute-start.1) | collective-permute-done | bytes 524320 | tf_op jit(solution)/shard_map/ppermute | solution.py:23
  21.8 1.0 slice.41
  22.8 3.0 %collective-permute-start.2 = (bf16[64,2048]{1,0:T(8,128)(2,1)S(1)}, bf16[64,2048]{1,0:T(8,128)(2,1)S(1)}, u32[]{:S(2)}, u32[]{:S(2)}) collective-permute-start(bf16[64,2048]{1,0:T(8,128)(2,1)S(1)} %slice.41), channel_id=1, source_target_pairs={{0,192},{32,224},{64,0},{96,32},{128,64},{160,96},{192,128},{224,1... | collective-permute-start | bytes 786440 | tf_op jit(solution)/shard_map/ppermute | solution.py:23
  25.8 2.4 fusion.11
  28.2 1.0 slice.33
  29.2 0.1 collective-permute-start.3
  29.3 0.1 collective-permute-start.4
  29.4 0.5 collective-permute-start.5
  29.9 0.1 collective-permute-start.6
  30.0 0.3 collective-permute-done.2
  30.3 6.9 %collective-permute-done.3 = bf16[64,2048]{1,0:T(8,128)(2,1)S(1)} collective-permute-done((bf16[64,2048]{1,0:T(8,128)(2,1)S(1)}, bf16[64,2048]{1,0:T(8,128)(2,1)S(1)}, u32[]{:S(2)}, u32[]{:S(2)}) %collective-permute-start.3) | collective-permute-done | bytes 262176 | tf_op jit(solution)/shard_map/ppermute | solution.py:23
  37.1 0.8 copy-done.5
  37.9 2.0 collective-permute-done.7.refs_7_
  40.0 0.0 all-gather.5.cloned.1.call-update
  40.0 0.0 all-gather.3.cloned.1.call-start
  40.0 0.7 all-gather.3.cloned.1.call-update
  40.8 1.8 copy.38.ctx_ref
  42.6 4.4 %shard_map.109 = f32[128,2048]{1,0:T(8,128)} custom-call(bf16[128,1024]{1,0:T(8,128)(2,1)} %copy.38.ctx_ref, bf16[128,2048]{1,0:T(8,128)(2,1)} %refs_0_, bf16[128,2048]{1,0:T(8,128)(2,1)} %collective-permute-done.refs_1_, bf16[128,2048]{1,0:T(8,128)(2,1)} %collective-permute-done.1.refs_2_, bf16[128,2048]{1,0:T(8,128)(2,1)} %copy-done.5, ...), custom_call_target="tpu_custom_call" | custom-call | tf_op jit(solution)/shard_map/pallas_call | solution.py:60
  47.0 1.6 fusion.14
  48.6 1.3 convolution_convert_fusion.1
  50.0 0.0 slice-start.1
  50.0 106.1 %all_to_all.10 = bf16[32,32,2048]{2,1,0:T(8,128)(2,1)S(1)} all-to-all(bf16[32,32,2048]{2,1,0:T(8,128)(2,1)S(1)} %bitcast.43), channel_id=1, replica_groups=mesh['group'=8,'expert'=32] {'expert'}, dimensions={0} | all-to-all | bytes 8388608 | tf_op jit(solution)/shard_map/all_to_all | solution.py:125
  156.2 6.6 %fusion = f32[1024,1536]{1,0:T(8,128)S(1)} fusion(bf16[1024,2048]{1,0:T(8,128)(2,1)S(1)} %bitcast.45, bf16[1,2048,1536]{2,1,0:T(8,128)(2,1)S(1)} %bitcast.49), kind=kOutput, calls=%fused_computation | convolution fusion | flops 6442450944 | bytes 16777216 | tf_op jit(solution)/shard_map/dot_general | solution.py:10
  162.8 5.1 %convolution_convert_fusion = bf16[1024,2048]{1,0:T(8,128)(2,1)} fusion(bf16[1,768,2048]{2,1,0:T(8,128)(2,1)S(1)} %copy-done, f32[1024,1536]{1,0:T(8,128)S(1)} %fusion), kind=kOutput, calls=%fused_computation.4 | convolution fusion | flops 3228041216 | bytes 13631488 | tf_op jit(solution)/shard_map/dot_general | solution.py:12
  168.0 6.7 %all-to-all-start.1 = ((bf16[32,32,2048]{2,1,0:T(8,128)(2,1)}), bf16[32,32,2048]{2,1,0:T(8,128)(2,1)}, u32[]{:S(2)}, u32[]{:S(2)}) async-start(bf16[32,32,2048]{2,1,0:T(8,128)(2,1)} %bitcast.44), calls=%async_computation.1 | async-start | bytes 8388608 | tf_op jit(solution)/shard_map/all_to_all | solution.py:129
  174.7 0.3 fusion.36
  175.1 0.4 select_reduce_fusion
  175.6 0.8 subtract_convert_fusion
  176.4 6.5 %fusion.38 = f32[128,2816]{1,0:T(8,128)S(1)} fusion(bf16[2048,2816]{1,0:T(8,128)(2,1)} %all-gather.3.cloned.1.call-done, bf16[128,2048]{1,0:T(8,128)(2,1)S(1)} %copy-done.3, f32[2048]{0:T(1024)S(1)} %copy-done.7, f32[128]{0:T(128)S(1)} %add_rsqrt_fusion), kind=kOutput, calls=%fused_computation.67 | convolution fusion | flops 1477443584 | bytes 13509120 | tf_op jit(solution)/shard_map/dot_general | solution.py:142
  182.9 2.0 fusion.24
  184.9 83.7 %all-to-all-done.1 = bf16[32,32,2048]{2,1,0:T(8,128)(2,1)} async-done(((bf16[32,32,2048]{2,1,0:T(8,128)(2,1)}), bf16[32,32,2048]{2,1,0:T(8,128)(2,1)}, u32[]{:S(2)}, u32[]{:S(2)}) %all-to-all-start.1) | async-done | bytes 4194336 | tf_op jit(solution)/shard_map/all_to_all | solution.py:129
  268.6 3.7 %fusion.20 = f32[256,2048]{1,0:T(8,128)S(1)} fusion(bf16[1024,2048]{1,0:T(8,128)(2,1)} %bitcast.10, bf16[128,1024]{1,0:T(8,128)(2,1)S(1)} %get-tuple-element.39, bf16[128,1024]{1,0:T(8,128)(2,1)} %get-tuple-element.40), kind=kOutput, calls=%fused_computation.29 | convolution fusion | flops 1074790400 | bytes 6815744 | tf_op jit(solution)/shard_map/dot_general | solution.py:137
  272.3 1.1 fusion.18
  (46 shorter events, 0.3 us)
Async XLA Ops:
  6.5 156.3 %copy-start = (bf16[1,768,2048]{2,1,0:T(8,128)(2,1)S(1)}, bf16[1,768,2048]{2,1,0:T(8,128)(2,1)}, u32[]{:S(2)}) copy-start(bf16[1,768,2048]{2,1,0:T(8,128)(2,1)} %param.19) | copy-start | bytes 9437188
  6.5 161.4 %all-gather.5.cloned.1.call-start = ((), (), s32[]{:S(2)}) async-start(), calls=%async_computation.3 | async-start | bytes 6488064 | tf_op jit(solution)/shard_map/all_gather | solution.py:106
  6.5 21.7 %collective-permute-start = (bf16[128,2048]{1,0:T(8,128)(2,1)}, bf16[128,2048]{1,0:T(8,128)(2,1)}, u32[]{:S(2)}, u32[]{:S(2)}) collective-permute-start(bf16[128,2048]{1,0:T(8,128)(2,1)} %refs_0_), channel_id=1, source_target_pairs={{0,64},{32,96},{64,128},{96,160},{128,192},{160,224},{192,0},{224,... | collective-permute-start | bytes 1572872 | tf_op jit(solution)/shard_map/ppermute | solution.py:23
  8.1 13.7 %collective-permute-start.1 = (bf16[128,2048]{1,0:T(8,128)(2,1)}, bf16[128,2048]{1,0:T(8,128)(2,1)}, u32[]{:S(2)}, u32[]{:S(2)}) collective-permute-start(bf16[128,2048]{1,0:T(8,128)(2,1)} %refs_0_), channel_id=1, source_target_pairs={{0,192},{32,224},{64,0},{96,32},{128,64},{160,96},{192,128},{224,1... | collective-permute-start | bytes 1572872 | tf_op jit(solution)/shard_map/ppermute | solution.py:23
  22.8 7.4 %collective-permute-start.2 = (bf16[64,2048]{1,0:T(8,128)(2,1)S(1)}, bf16[64,2048]{1,0:T(8,128)(2,1)S(1)}, u32[]{:S(2)}, u32[]{:S(2)}) collective-permute-start(bf16[64,2048]{1,0:T(8,128)(2,1)S(1)} %slice.41), channel_id=1, source_target_pairs={{0,192},{32,224},{64,0},{96,32},{128,64},{160,96},{192,128},{224,1... | collective-permute-start | bytes 786440 | tf_op jit(solution)/shard_map/ppermute | solution.py:23
  29.2 7.9 %collective-permute-start.3 = (bf16[64,2048]{1,0:T(8,128)(2,1)S(1)}, bf16[64,2048]{1,0:T(8,128)(2,1)S(1)}, u32[]{:S(2)}, u32[]{:S(2)}) collective-permute-start(bf16[64,2048]{1,0:T(8,128)(2,1)S(1)} %slice.33), channel_id=1, source_target_pairs={{0,64},{32,96},{64,128},{96,160},{128,192},{160,224},{192,0},{224,... | collective-permute-start | bytes 786440 | tf_op jit(solution)/shard_map/ppermute | solution.py:23
  29.3 8.7 %collective-permute-start.4 = (bf16[128,2048]{1,0:T(8,128)(2,1)}, bf16[128,2048]{1,0:T(8,128)(2,1)}, u32[]{:S(2)}, u32[]{:S(2)}) collective-permute-start(bf16[128,2048]{1,0:T(8,128)(2,1)} %refs_0_), channel_id=1, source_target_pairs={{0,32},{32,0},{64,96},{96,64},{128,160},{160,128},{192,224},{224,1... | collective-permute-start | bytes 1572872 | tf_op jit(solution)/shard_map/ppermute | solution.py:26
  29.4 8.6 %collective-permute-start.5 = (bf16[128,2048]{1,0:T(8,128)(2,1)}, bf16[128,2048]{1,0:T(8,128)(2,1)}, u32[]{:S(2)}, u32[]{:S(2)}) collective-permute-start(bf16[128,2048]{1,0:T(8,128)(2,1)} %collective-permute-done.refs_1_), channel_id=1, source_target_pairs={{0,32},{32,0},{64,96},{96,64},{128,160},{160,128},{192,224},{224,1... | collective-permute-start | bytes 1572872 | tf_op jit(solution)/shard_map/ppermute | solution.py:26
  29.9 8.1 %collective-permute-start.6 = (bf16[128,2048]{1,0:T(8,128)(2,1)}, bf16[128,2048]{1,0:T(8,128)(2,1)}, u32[]{:S(2)}, u32[]{:S(2)}) collective-permute-start(bf16[128,2048]{1,0:T(8,128)(2,1)} %collective-permute-done.1.refs_2_), channel_id=1, source_target_pairs={{0,32},{32,0},{64,96},{96,64},{128,160},{160,128},{192,224},{224,1... | collective-permute-start | bytes 1572872 | tf_op jit(solution)/shard_map/ppermute | solution.py:26
  37.1 0.8 copy-start.5
  37.9 2.0 collective-permute-start.7
  40.0 128.0 %all-gather.3.cloned.1.call-start = ((), (), s32[]{:S(2)}) async-start(), calls=%async_computation.2 | async-start | bytes 12976128 | tf_op jit(solution)/shard_map/all_gather | solution.py:105
  40.7 7.9 %copy-start.7 = (f32[2048]{0:T(1024)S(1)}, f32[2048]{0:T(1024)}, u32[]{:S(2)}) copy-start(f32[2048]{0:T(1024)} %param.14) | copy-start | bytes 24580
  48.6 107.6 %copy-start.2 = (bf16[128,2048]{1,0:T(8,128)(2,1)}, bf16[128,2048]{1,0:T(8,128)(2,1)S(1)}, u32[]{:S(2)}) copy-start(bf16[128,2048]{1,0:T(8,128)(2,1)S(1)} %get-tuple-element.42) | copy-start | bytes 1572868
  48.6 107.5 %slice-start = ((s8[6291456]{0:T(1024)(128)(4,1)}), s8[4194304]{0:T(1024)(128)(4,1)S(1)}, s32[]{:S(2)}) async-start(s8[6291456]{0:T(1024)(128)(4,1)} %bitcast.48), calls=%async_computation.4 | async-start | bytes 8388608
  50.0 106.2 %slice-start.1 = ((s8[6291456]{0:T(1024)(128)(4,1)}), s8[2097152]{0:T(1024)(128)(4,1)S(1)}, s32[]{:S(2)}) async-start(s8[6291456]{0:T(1024)(128)(4,1)} %bitcast.48), calls=%async_computation.5 | async-start | bytes 4194304
  168.0 6.7 %copy-start.3 = (bf16[128,2048]{1,0:T(8,128)(2,1)S(1)}, bf16[128,2048]{1,0:T(8,128)(2,1)}, u32[]{:S(2)}) copy-start(bf16[128,2048]{1,0:T(8,128)(2,1)} %copy-done.2) | copy-start | bytes 1572868
  168.0 6.7 %copy-start.9 = (bf16[2048,32]{0,1:T(8,128)(2,1)S(1)}, bf16[2048,32]{0,1:T(8,128)(2,1)}, u32[]{:S(2)}) copy-start(bf16[2048,32]{0,1:T(8,128)(2,1)} %param.15) | copy-start | bytes 393220
  168.0 7.1 %copy-start.8 = (s32[128,6]{0,1:T(8,128)S(1)}, s32[128,6]{0,1:T(8,128)}, u32[]{:S(2)}) copy-start(s32[128,6]{0,1:T(8,128)} %param.20) | copy-start | bytes 9220
  168.0 100.6 %all-to-all-start.1 = ((bf16[32,32,2048]{2,1,0:T(8,128)(2,1)}), bf16[32,32,2048]{2,1,0:T(8,128)(2,1)}, u32[]{:S(2)}, u32[]{:S(2)}) async-start(bf16[32,32,2048]{2,1,0:T(8,128)(2,1)} %bitcast.44), calls=%async_computation.1 | async-start | bytes 8388608 | tf_op jit(solution)/shard_map/all_to_all | solution.py:129
  175.6 7.3 %slice-start.2 = ((s8[5767168]{0:T(1024)(128)(4,1)}), s8[4194304]{0:T(1024)(128)(4,1)S(1)}, s32[]{:S(2)}) async-start(s8[5767168]{0:T(1024)(128)(4,1)} %bitcast.50), calls=%async_computation.6 | async-start | bytes 8388608
  176.4 6.5 %slice-start.3 = ((s8[5767168]{0:T(1024)(128)(4,1)}), s8[1572864]{0:T(1024)(128)(4,1)S(1)}, s32[]{:S(2)}) async-start(s8[5767168]{0:T(1024)(128)(4,1)} %bitcast.50), calls=%async_computation.7 | async-start | bytes 3145728
  268.6 3.7 %copy-start.4 = (bf16[128,2048]{1,0:T(8,128)(2,1)S(1)}, bf16[128,2048]{1,0:T(8,128)(2,1)}, u32[]{:S(2)}) copy-start(bf16[128,2048]{1,0:T(8,128)(2,1)} %copy-done.2) | copy-start | bytes 1572868
  268.6 3.7 %copy-start.6 = (f32[128,2048]{1,0:T(8,128)S(1)}, f32[128,2048]{1,0:T(8,128)}, u32[]{:S(2)}) copy-start(f32[128,2048]{1,0:T(8,128)} %fusion.24) | copy-start | bytes 3145732
  268.6 4.8 %copy-start.1 = (bf16[1,768,2048]{2,1,0:T(8,128)(2,1)S(1)}, bf16[1,768,2048]{2,1,0:T(8,128)(2,1)}, u32[]{:S(2)}) copy-start(bf16[1,768,2048]{2,1,0:T(8,128)(2,1)} %param.19) | copy-start | bytes 9437188
Sparse Core Ops, SparseCore 0:
  40.1 45.2 all-gather.4
  87.3 66.4 all-gather.2

commit v13 on v12

--- a/solution.py
+++ b/solution.py
@@ -94,17 +94,17 @@
         src = chip_gather_order()[:, None] * block + jnp.arange(block, dtype=jnp.int32)[None, :]
         perm = (jnp.arange(context.shape[1], dtype=jnp.int32)[:, None] == src.reshape(1, -1))
         ctx_perm = jnp.dot(context, perm.astype(jnp.bfloat16), preferred_element_type=jnp.float32)
-        ctx_perm = ctx_perm.astype(jnp.bfloat16).reshape(tok_rows, groups, block)
+        ctx_perm = ctx_perm.astype(jnp.bfloat16)
         pieces, (slot_of, dispatch, ctx_perm) = gather_rows_by_chip(
             attn_out_w, (slot_of, dispatch, ctx_perm)
         )
     else:
         pieces = [lax.all_gather(attn_out_w, "group", axis=0, tiled=True)]
-        ctx_perm = context[:, None, :]
+        ctx_perm = context
     pieces, shared_in, shared_out = lax.optimization_barrier((pieces, shared_in, shared_out))
     shared_in = lax.all_gather(shared_in, "group", axis=0, tiled=True)
     shared_out = lax.all_gather(shared_out, "group", axis=1, tiled=True)
-    attn = pieces_dot(ctx_perm.reshape(tok_rows, -1), pieces)
+    attn = pieces_dot(ctx_perm, pieces)
     hidden_state = (residual.astype(jnp.float32) + attn).astype(jnp.bfloat16)
     hidden_f = hidden_state.astype(jnp.float32)
     scale = lax.rsqrt(jnp.mean(hidden_f * hidden_f, axis=-1, keepdims=True) + 1e-06)

time: 281 us -> 279 us (level)
  no operation moved by 1% of the time
where the time goes in v13:
time: 279 us; the launch traced here: 278 us
  blocking collectives  106 us (38%)
  waiting for transfers between devices  98.9 us (35%)
  matrix products  29.3 us (11%)
  starting transfers between devices  13.7 us (5%)
  between operations  13.7 us (5%)
  other arithmetic  7.94 us (3%)
  Pallas kernels  4.43 us (2%)
  local copies, waits for them, and re-layouts  4.31 us (2%)
    all_to_all x1, blocking collectives, per_device(): lax.all_to_all(outgoing, 'expert', split_axis=0, concat_axis=0, tiled=True)  106 us
    all_to_all x1, waiting for transfers between devices, per_device(): lax.all_to_all(expert_rows.reshape(arrived.shape), 'expert', split_axis=0...  82.5 us
    ppermute x4, waiting for transfers between devices, shift(): return lax.ppermute(x, 'group', pairs)  13.6 us
    all_to_all x1, starting transfers between devices, per_device(): lax.all_to_all(expert_rows.reshape(arrived.shape), 'expert', split_axis=0...  6.66 us
    dot_general x1, matrix products, per_device(): shared_mid = jnp.dot(normed, shared_in, preferred_element_type=jnp.float32)  6.64 us
    dot_general x1, matrix products, swiglu_rows(): mid = jnp.dot(rows, w_in, preferred_element_type=jnp.float32)  6.64 us
    ppermute x4, starting transfers between devices, shift(): return lax.ppermute(x, 'group', pairs)  6.33 us
  transfers between devices with their start and end apart: 11, of which 5 were waited for; matrix products, arithmetic and copies ran while one was open for 13% of the time, Pallas kernels for 2%

profile of v13, /device:TPU:32, one launch (start us, length us, event | category | flops | bytes accessed | tf_op | source)
XLA Modules:
  0.0 278.3 jit_solution(8650613976130072712)
XLA Ops:
  6.5 1.6 collective-permute-start
  8.1 1.7 collective-permute-start.1
  9.8 0.8 copy.33
  10.6 0.1 eq.81
  10.7 0.1 eq.85
  10.9 1.7 reduce-window.6
  12.6 0.3 slice_reduce_fusion
  12.9 0.1 fusion.26
  13.0 0.1 reduce_sum.48
  13.2 0.1 copy.36
  13.2 0.7 multiply_add_fusion
  13.9 0.5 fusion.5
  14.5 0.7 broadcast_add_fusion
  15.2 0.1 add_multiply_fusion
  15.2 0.1 add_bitcast_fusion.1
  15.3 6.5 %collective-permute-done.1.refs_2_ = bf16[128,2048]{1,0:T(8,128)(2,1)} collective-permute-done((bf16[128,2048]{1,0:T(8,128)(2,1)}, bf16[128,2048]{1,0:T(8,128)(2,1)}, u32[]{:S(2)}, u32[]{:S(2)}) %collective-permute-start.1) | collective-permute-done | bytes 524320 | tf_op jit(solution)/shard_map/ppermute | solution.py:23
  21.8 1.0 slice.41
  22.8 3.0 %collective-permute-start.2 = (bf16[64,2048]{1,0:T(8,128)(2,1)S(1)}, bf16[64,2048]{1,0:T(8,128)(2,1)S(1)}, u32[]{:S(2)}, u32[]{:S(2)}) collective-permute-start(bf16[64,2048]{1,0:T(8,128)(2,1)S(1)} %slice.41), channel_id=1, source_target_pairs={{0,192},{32,224},{64,0},{96,32},{128,64},{160,96},{192,128},{224,1... | collective-permute-start | bytes 786440 | tf_op jit(solution)/shard_map/ppermute | solution.py:23
  25.8 2.5 fusion.10.ctx_ref
  28.3 1.0 slice.33
  29.3 0.1 collective-permute-start.3
  29.4 0.1 collective-permute-start.4
  29.5 0.5 collective-permute-start.5
  30.0 0.1 collective-permute-start.6
  30.1 0.2 collective-permute-done.2
  30.3 7.0 %collective-permute-done.3 = bf16[64,2048]{1,0:T(8,128)(2,1)S(1)} collective-permute-done((bf16[64,2048]{1,0:T(8,128)(2,1)S(1)}, bf16[64,2048]{1,0:T(8,128)(2,1)S(1)}, u32[]{:S(2)}, u32[]{:S(2)}) %collective-permute-start.3) | collective-permute-done | bytes 262176 | tf_op jit(solution)/shard_map/ppermute | solution.py:23
  37.2 0.8 copy-done.3
  38.1 2.0 collective-permute-done.7.refs_7_
  40.1 0.0 all-gather.5.cloned.1.call-update
  40.1 0.0 all-gather.3.cloned.1.call-start
  40.2 0.7 all-gather.3.cloned.1.call-update
  40.9 4.4 %shard_map.109 = f32[128,2048]{1,0:T(8,128)} custom-call(bf16[128,1024]{1,0:T(8,128)(2,1)} %fusion.10.ctx_ref, bf16[128,2048]{1,0:T(8,128)(2,1)} %refs_0_, bf16[128,2048]{1,0:T(8,128)(2,1)} %collective-permute-done.refs_1_, bf16[128,2048]{1,0:T(8,128)(2,1)} %collective-permute-done.1.refs_2_, bf16[128,2048]{1,0:T(8,128)(2,1)} %copy-done.3, ...), custom_call_target="tpu_custom_call" | custom-call | tf_op jit(solution)/shard_map/pallas_call | solution.py:60
  45.3 1.6 fusion.11
  46.9 0.0 slice-start
  46.9 1.3 convolution_convert_fusion.1
  48.3 0.0 slice-start.1
  48.3 106.0 %all_to_all.10 = bf16[32,32,2048]{2,1,0:T(8,128)(2,1)S(1)} all-to-all(bf16[32,32,2048]{2,1,0:T(8,128)(2,1)S(1)} %bitcast.41), channel_id=1, replica_groups=mesh['group'=8,'expert'=32] {'expert'}, dimensions={0} | all-to-all | bytes 8388608 | tf_op jit(solution)/shard_map/all_to_all | solution.py:125
  154.3 6.6 %fusion = f32[1024,1536]{1,0:T(8,128)S(1)} fusion(bf16[1024,2048]{1,0:T(8,128)(2,1)S(1)} %bitcast.43, bf16[1,2048,1536]{2,1,0:T(8,128)(2,1)S(1)} %bitcast.46), kind=kOutput, calls=%fused_computation | convolution fusion | flops 6442450944 | bytes 16777216 | tf_op jit(solution)/shard_map/dot_general | solution.py:10
  161.0 5.1 %convolution_convert_fusion = bf16[1024,2048]{1,0:T(8,128)(2,1)} fusion(bf16[1,768,2048]{2,1,0:T(8,128)(2,1)S(1)} %copy-done, f32[1024,1536]{1,0:T(8,128)S(1)} %fusion), kind=kOutput, calls=%fused_computation.4 | convolution fusion | flops 3228041216 | bytes 13631488 | tf_op jit(solution)/shard_map/dot_general | solution.py:12
  166.1 6.7 %all-to-all-start.1 = ((bf16[32,32,2048]{2,1,0:T(8,128)(2,1)}), bf16[32,32,2048]{2,1,0:T(8,128)(2,1)}, u32[]{:S(2)}, u32[]{:S(2)}) async-start(bf16[32,32,2048]{2,1,0:T(8,128)(2,1)} %bitcast.42), calls=%async_computation.1 | async-start | bytes 8388608 | tf_op jit(solution)/shard_map/all_to_all | solution.py:129
  172.8 1.4 fusion.33
  174.3 0.4 select_reduce_fusion
  174.7 0.8 subtract_convert_fusion
  175.5 6.6 %fusion.35 = f32[128,2816]{1,0:T(8,128)S(1)} fusion(bf16[2048,2816]{1,0:T(8,128)(2,1)} %all-gather.3.cloned.1.call-done, bf16[128,2048]{1,0:T(8,128)(2,1)} %copy-done.1, f32[2048]{0:T(1024)S(1)} %copy-done.5, f32[128]{0:T(128)S(1)} %add_rsqrt_fusion), kind=kOutput, calls=%fused_computation.67 | convolution fusion | flops 1477443584 | bytes 13509120 | tf_op jit(solution)/shard_map/dot_general | solution.py:142
  182.2 2.0 fusion.21
  184.2 82.5 %all-to-all-done.1 = bf16[32,32,2048]{2,1,0:T(8,128)(2,1)} async-done(((bf16[32,32,2048]{2,1,0:T(8,128)(2,1)}), bf16[32,32,2048]{2,1,0:T(8,128)(2,1)}, u32[]{:S(2)}, u32[]{:S(2)}) %all-to-all-start.1) | async-done | bytes 4194336 | tf_op jit(solution)/shard_map/all_to_all | solution.py:129
  266.7 3.6 %fusion.17 = f32[256,2048]{1,0:T(8,128)S(1)} fusion(bf16[1024,2048]{1,0:T(8,128)(2,1)} %bitcast.8, bf16[128,1024]{1,0:T(8,128)(2,1)S(1)} %get-tuple-element.39, bf16[128,1024]{1,0:T(8,128)(2,1)} %get-tuple-element.40), kind=kOutput, calls=%fused_computation.29 | convolution fusion | flops 1074790400 | bytes 6815744 | tf_op jit(solution)/shard_map/dot_general | solution.py:137
  270.4 1.1 fusion.15
  (41 shorter events, 0.2 us)
Async XLA Ops:
  6.5 154.4 %copy-start = (bf16[1,768,2048]{2,1,0:T(8,128)(2,1)S(1)}, bf16[1,768,2048]{2,1,0:T(8,128)(2,1)}, u32[]{:S(2)}) copy-start(bf16[1,768,2048]{2,1,0:T(8,128)(2,1)} %param.19) | copy-start | bytes 9437188
  6.5 159.6 %all-gather.5.cloned.1.call-start = ((), (), s32[]{:S(2)}) async-start(), calls=%async_computation.3 | async-start | bytes 6488064 | tf_op jit(solution)/shard_map/all_gather | solution.py:106
  6.5 21.8 %collective-permute-start = (bf16[128,2048]{1,0:T(8,128)(2,1)}, bf16[128,2048]{1,0:T(8,128)(2,1)}, u32[]{:S(2)}, u32[]{:S(2)}) collective-permute-start(bf16[128,2048]{1,0:T(8,128)(2,1)} %refs_0_), channel_id=1, source_target_pairs={{0,64},{32,96},{64,128},{96,160},{128,192},{160,224},{192,0},{224,... | collective-permute-start | bytes 1572872 | tf_op jit(solution)/shard_map/ppermute | solution.py:23
  8.1 13.7 %collective-permute-start.1 = (bf16[128,2048]{1,0:T(8,128)(2,1)}, bf16[128,2048]{1,0:T(8,128)(2,1)}, u32[]{:S(2)}, u32[]{:S(2)}) collective-permute-start(bf16[128,2048]{1,0:T(8,128)(2,1)} %refs_0_), channel_id=1, source_target_pairs={{0,192},{32,224},{64,0},{96,32},{128,64},{160,96},{192,128},{224,1... | collective-permute-start | bytes 1572872 | tf_op jit(solution)/shard_map/ppermute | solution.py:23
  22.8 7.4 %collective-permute-start.2 = (bf16[64,2048]{1,0:T(8,128)(2,1)S(1)}, bf16[64,2048]{1,0:T(8,128)(2,1)S(1)}, u32[]{:S(2)}, u32[]{:S(2)}) collective-permute-start(bf16[64,2048]{1,0:T(8,128)(2,1)S(1)} %slice.41), channel_id=1, source_target_pairs={{0,192},{32,224},{64,0},{96,32},{128,64},{160,96},{192,128},{224,1... | collective-permute-start | bytes 786440 | tf_op jit(solution)/shard_map/ppermute | solution.py:23
  29.3 7.9 %collective-permute-start.3 = (bf16[64,2048]{1,0:T(8,128)(2,1)S(1)}, bf16[64,2048]{1,0:T(8,128)(2,1)S(1)}, u32[]{:S(2)}, u32[]{:S(2)}) collective-permute-start(bf16[64,2048]{1,0:T(8,128)(2,1)S(1)} %slice.33), channel_id=1, source_target_pairs={{0,64},{32,96},{64,128},{96,160},{128,192},{160,224},{192,0},{224,... | collective-permute-start | bytes 786440 | tf_op jit(solution)/shard_map/ppermute | solution.py:23
  29.4 8.7 %collective-permute-start.4 = (bf16[128,2048]{1,0:T(8,128)(2,1)}, bf16[128,2048]{1,0:T(8,128)(2,1)}, u32[]{:S(2)}, u32[]{:S(2)}) collective-permute-start(bf16[128,2048]{1,0:T(8,128)(2,1)} %refs_0_), channel_id=1, source_target_pairs={{0,32},{32,0},{64,96},{96,64},{128,160},{160,128},{192,224},{224,1... | collective-permute-start | bytes 1572872 | tf_op jit(solution)/shard_map/ppermute | solution.py:26
  29.5 8.6 %collective-permute-start.5 = (bf16[128,2048]{1,0:T(8,128)(2,1)}, bf16[128,2048]{1,0:T(8,128)(2,1)}, u32[]{:S(2)}, u32[]{:S(2)}) collective-permute-start(bf16[128,2048]{1,0:T(8,128)(2,1)} %collective-permute-done.refs_1_), channel_id=1, source_target_pairs={{0,32},{32,0},{64,96},{96,64},{128,160},{160,128},{192,224},{224,1... | collective-permute-start | bytes 1572872 | tf_op jit(solution)/shard_map/ppermute | solution.py:26
  30.0 8.1 %collective-permute-start.6 = (bf16[128,2048]{1,0:T(8,128)(2,1)}, bf16[128,2048]{1,0:T(8,128)(2,1)}, u32[]{:S(2)}, u32[]{:S(2)}) collective-permute-start(bf16[128,2048]{1,0:T(8,128)(2,1)} %collective-permute-done.1.refs_2_), channel_id=1, source_target_pairs={{0,32},{32,0},{64,96},{96,64},{128,160},{160,128},{192,224},{224,1... | collective-permute-start | bytes 1572872 | tf_op jit(solution)/shard_map/ppermute | solution.py:26
  37.2 0.8 copy-start.3
  38.0 2.0 collective-permute-start.7
  40.1 6.8 %copy-start.5 = (f32[2048]{0:T(1024)S(1)}, f32[2048]{0:T(1024)}, u32[]{:S(2)}) copy-start(f32[2048]{0:T(1024)} %param.14) | copy-start | bytes 24580
  40.1 126.0 %all-gather.3.cloned.1.call-start = ((), (), s32[]{:S(2)}) async-start(), calls=%async_computation.2 | async-start | bytes 12976128 | tf_op jit(solution)/shard_map/all_gather | solution.py:105
  46.9 107.4 %copy-start.1 = (bf16[128,2048]{1,0:T(8,128)(2,1)}, bf16[128,2048]{1,0:T(8,128)(2,1)S(1)}, u32[]{:S(2)}) copy-start(bf16[128,2048]{1,0:T(8,128)(2,1)S(1)} %get-tuple-element.42) | copy-start | bytes 1572868
  46.9 107.4 %slice-start = ((s8[6291456]{0:T(1024)(128)(4,1)}), s8[4194304]{0:T(1024)(128)(4,1)S(1)}, s32[]{:S(2)}) async-start(s8[6291456]{0:T(1024)(128)(4,1)} %bitcast.45), calls=%async_computation.4 | async-start | bytes 8388608
  48.3 106.0 %slice-start.1 = ((s8[6291456]{0:T(1024)(128)(4,1)}), s8[2097152]{0:T(1024)(128)(4,1)S(1)}, s32[]{:S(2)}) async-start(s8[6291456]{0:T(1024)(128)(4,1)} %bitcast.45), calls=%async_computation.5 | async-start | bytes 4194304
  166.1 6.7 %copy-start.7 = (bf16[2048,32]{0,1:T(8,128)(2,1)S(1)}, bf16[2048,32]{0,1:T(8,128)(2,1)}, u32[]{:S(2)}) copy-start(bf16[2048,32]{0,1:T(8,128)(2,1)} %param.15) | copy-start | bytes 393220
  166.1 8.1 %copy-start.6 = (s32[128,6]{0,1:T(8,128)S(1)}, s32[128,6]{0,1:T(8,128)}, u32[]{:S(2)}) copy-start(s32[128,6]{0,1:T(8,128)} %param.20) | copy-start | bytes 9220
  166.1 100.6 %all-to-all-start.1 = ((bf16[32,32,2048]{2,1,0:T(8,128)(2,1)}), bf16[32,32,2048]{2,1,0:T(8,128)(2,1)}, u32[]{:S(2)}, u32[]{:S(2)}) async-start(bf16[32,32,2048]{2,1,0:T(8,128)(2,1)} %bitcast.42), calls=%async_computation.1 | async-start | bytes 8388608 | tf_op jit(solution)/shard_map/all_to_all | solution.py:129
  174.7 7.5 %slice-start.2 = ((s8[5767168]{0:T(1024)(128)(4,1)}), s8[4194304]{0:T(1024)(128)(4,1)S(1)}, s32[]{:S(2)}) async-start(s8[5767168]{0:T(1024)(128)(4,1)} %bitcast.47), calls=%async_computation.6 | async-start | bytes 8388608
  175.5 6.7 %slice-start.3 = ((s8[5767168]{0:T(1024)(128)(4,1)}), s8[1572864]{0:T(1024)(128)(4,1)S(1)}, s32[]{:S(2)}) async-start(s8[5767168]{0:T(1024)(128)(4,1)} %bitcast.47), calls=%async_computation.7 | async-start | bytes 3145728
  266.7 3.6 %copy-start.2 = (bf16[128,2048]{1,0:T(8,128)(2,1)S(1)}, bf16[128,2048]{1,0:T(8,128)(2,1)}, u32[]{:S(2)}) copy-start(bf16[128,2048]{1,0:T(8,128)(2,1)} %copy-done.1) | copy-start | bytes 1572868
  266.7 3.7 %copy-start.4 = (f32[128,2048]{1,0:T(8,128)S(1)}, f32[128,2048]{1,0:T(8,128)}, u32[]{:S(2)}) copy-start(f32[128,2048]{1,0:T(8,128)} %fusion.21) | copy-start | bytes 3145732
Sparse Core Ops, SparseCore 0:
  40.2 45.2 all-gather.4
  87.4 66.4 all-gather.2

commit v14 on v13

--- a/solution.py
+++ b/solution.py
@@ -61,6 +61,31 @@
         _pieces_dot_kernel,
         out_shape=jax.ShapeDtypeStruct((ctx.shape[0], pieces[0].shape[1]), jnp.float32),
     )(ctx, *pieces)
+
+
+def _combine_kernel(comb_ref, ret_ref, hid_ref, sh_ref, out_ref):
+    rows = hid_ref.shape[0]
+    both = jnp.dot(comb_ref[...], ret_ref[...], preferred_element_type=jnp.float32)
+    routed = both[:rows] + both[rows:]
+    out_ref[...] = (hid_ref[...] + sh_ref[...] + routed).astype(out_ref.dtype)
+
+
+def combine_rows(comb, returned, hidden_f, shared_y, cols=512):
+    rows, width = hidden_f.shape
+    slots = returned.shape[0]
+    cols = min(cols, width)
+    return pl.pallas_call(
+        _combine_kernel,
+        out_shape=jax.ShapeDtypeStruct((rows, width), jnp.bfloat16),
+        grid=(width // cols,),
+        in_specs=[
+            pl.BlockSpec((2 * rows, slots), lambda j: (0, 0)),
+            pl.BlockSpec((slots, cols), lambda j: (0, j)),
+            pl.BlockSpec((rows, cols), lambda j: (0, j)),
+            pl.BlockSpec((rows, cols), lambda j: (0, j)),
+        ],
+        out_specs=pl.BlockSpec((rows, cols), lambda j: (0, j)),
+    )(comb, returned, hidden_f, shared_y)
 
 
 def per_device(
@@ -134,10 +159,6 @@
         tiled=True,
     )
     returned = returned.reshape(slots, width)
-    both = jnp.dot(
-        jnp.concatenate([combine_hi, combine_lo], axis=0), returned, preferred_element_type=jnp.float32
-    )
-    routed = both[:tok_rows] + both[tok_rows:]
     shared_hidden = shared_out.shape[0]
     shared_mid = jnp.dot(
         normed,
@@ -153,7 +174,7 @@
         preferred_element_type=jnp.float32,
     )
     shared_y = lax.optimization_barrier(shared_y)
-    return (hidden_f + shared_y + routed).astype(jnp.bfloat16)
+    return combine_rows(jnp.concatenate([combine_hi, combine_lo], axis=0), returned, hidden_f, shared_y)
 
 
 def solution(mesh):

time: 279 us -> 281 us (level)
  Pallas kernels: 4.43 us -> 9.71 us
  matrix products: 29.3 us -> 25.6 us
    pallas_call x0 -> x1, Pallas kernels: none -> 5.27 us  [combine_rows(): pl.pallas_call(_combine_kernel, out_shape=jax.ShapeDtypeStruct((rows, wid...]
    dot_general x1 -> x0, matrix products: 3.63 us -> none  [per_device(): jnp.dot(jnp.concatenate([combine_hi, combine_lo], axis=0), returned, pref...]
where the time goes in v14:
time: 281 us; the launch traced here: 280 us
  blocking collectives  106 us (38%)
  waiting for transfers between devices  98.9 us (35%)
  matrix products  25.6 us (9%)
  starting transfers between devices  13.7 us (5%)
  between operations  13.7 us (5%)
  Pallas kernels  9.71 us (3%)
  other arithmetic  7.05 us (3%)
  local copies, waits for them, and re-layouts  5.3 us (2%)
    all_to_all x1, blocking collectives, per_device(): lax.all_to_all(outgoing, 'expert', split_axis=0, concat_axis=0, tiled=True)  106 us
    all_to_all x1, waiting for transfers between devices, per_device(): lax.all_to_all(expert_rows.reshape(arrived.shape), 'expert', split_axis=0...  82.5 us
    ppermute x4, waiting for transfers between devices, shift(): return lax.ppermute(x, 'group', pairs)  13.6 us
    dot_general x1, matrix products, per_device(): shared_mid = jnp.dot(normed, shared_in, preferred_element_type=jnp.float32)  6.69 us
    all_to_all x1, starting transfers between devices, per_device(): lax.all_to_all(expert_rows.reshape(arrived.shape), 'expert', split_axis=0...  6.66 us
    dot_general x1, matrix products, swiglu_rows(): mid = jnp.dot(rows, w_in, preferred_element_type=jnp.float32)  6.64 us
    ppermute x4, starting transfers between devices, shift(): return lax.ppermute(x, 'group', pairs)  6.33 us
  transfers between devices with their start and end apart: 11, of which 5 were waited for; matrix products, arithmetic and copies ran while one was open for 13% of the time, Pallas kernels for 2%

profile of v14, /device:TPU:32, one launch (start us, length us, event | category | flops | bytes accessed | tf_op | source)
XLA Modules:
  0.0 280.1 jit_solution(1548722390146116408)
XLA Ops:
  6.5 1.6 collective-permute-start
  8.1 1.7 collective-permute-start.1
  9.8 0.8 copy.33
  10.6 0.1 eq.85
  10.7 0.1 eq.81
  10.9 1.7 reduce-window.6
  12.6 0.3 slice_reduce_fusion
  12.9 0.1 fusion.18
  13.0 0.1 reduce_sum.48
  13.2 0.1 copy.36
  13.2 0.7 multiply_add_fusion
  13.9 0.5 fusion.5
  14.5 0.7 broadcast_add_fusion
  15.2 0.1 add_multiply_fusion
  15.2 0.1 add_bitcast_fusion.1
  15.3 6.5 %collective-permute-done.1.refs_2_ = bf16[128,2048]{1,0:T(8,128)(2,1)} collective-permute-done((bf16[128,2048]{1,0:T(8,128)(2,1)}, bf16[128,2048]{1,0:T(8,128)(2,1)}, u32[]{:S(2)}, u32[]{:S(2)}) %collective-permute-start.1) | collective-permute-done | bytes 524320 | tf_op jit(solution)/shard_map/ppermute | solution.py:23
  21.8 1.0 slice.33
  22.8 3.0 %collective-permute-start.2 = (bf16[64,2048]{1,0:T(8,128)(2,1)S(1)}, bf16[64,2048]{1,0:T(8,128)(2,1)S(1)}, u32[]{:S(2)}, u32[]{:S(2)}) collective-permute-start(bf16[64,2048]{1,0:T(8,128)(2,1)S(1)} %slice.33), channel_id=1, source_target_pairs={{0,192},{32,224},{64,0},{96,32},{128,64},{160,96},{192,128},{224,1... | collective-permute-start | bytes 786440 | tf_op jit(solution)/shard_map/ppermute | solution.py:23
  25.8 2.5 fusion.10.ctx_ref
  28.3 1.0 slice.27
  29.3 0.1 collective-permute-start.3
  29.4 0.1 collective-permute-start.4
  29.5 0.5 collective-permute-start.5
  30.0 0.1 collective-permute-start.6
  30.1 0.2 collective-permute-done.2
  30.3 6.9 %collective-permute-done.3 = bf16[64,2048]{1,0:T(8,128)(2,1)S(1)} collective-permute-done((bf16[64,2048]{1,0:T(8,128)(2,1)S(1)}, bf16[64,2048]{1,0:T(8,128)(2,1)S(1)}, u32[]{:S(2)}, u32[]{:S(2)}) %collective-permute-start.3) | collective-permute-done | bytes 262176 | tf_op jit(solution)/shard_map/ppermute | solution.py:23
  37.2 0.8 copy-done.3
  38.0 2.0 collective-permute-done.7.refs_7_
  40.1 0.0 all-gather.5.cloned.1.call-update
  40.1 0.0 all-gather.3.cloned.1.call-start
  40.1 0.7 all-gather.3.cloned.1.call-update
  40.9 4.4 %shard_map.109 = f32[128,2048]{1,0:T(8,128)} custom-call(bf16[128,1024]{1,0:T(8,128)(2,1)} %fusion.10.ctx_ref, bf16[128,2048]{1,0:T(8,128)(2,1)} %refs_0_, bf16[128,2048]{1,0:T(8,128)(2,1)} %collective-permute-done.refs_1_, bf16[128,2048]{1,0:T(8,128)(2,1)} %collective-permute-done.1.refs_2_, bf16[128,2048]{1,0:T(8,128)(2,1)} %copy-done.3, ...), custom_call_target="tpu_custom_call" | custom-call | tf_op jit(solution)/shard_map/pallas_call | solution.py:60
  45.3 1.6 multiply_reduce_fusion
  46.9 1.0 copy-done.2
  47.9 0.2 multiply_convert_fusion
  48.1 1.3 convolution_convert_fusion.1
  49.4 106.1 %all_to_all.10 = bf16[32,32,2048]{2,1,0:T(8,128)(2,1)S(1)} all-to-all(bf16[32,32,2048]{2,1,0:T(8,128)(2,1)S(1)} %bitcast.43), channel_id=1, replica_groups=mesh['group'=8,'expert'=32] {'expert'}, dimensions={0} | all-to-all | bytes 8388608 | tf_op jit(solution)/shard_map/all_to_all | solution.py:150
  155.5 6.6 %fusion = f32[1024,1536]{1,0:T(8,128)S(1)} fusion(bf16[1024,2048]{1,0:T(8,128)(2,1)S(1)} %bitcast.45, bf16[1,2048,1536]{2,1,0:T(8,128)(2,1)S(1)} %bitcast.48), kind=kOutput, calls=%fused_computation | convolution fusion | flops 6442450944 | bytes 16777216 | tf_op jit(solution)/shard_map/dot_general | solution.py:10
  162.2 5.1 %convolution_convert_fusion = bf16[1024,2048]{1,0:T(8,128)(2,1)} fusion(bf16[1,768,2048]{2,1,0:T(8,128)(2,1)S(1)} %copy-done, f32[1024,1536]{1,0:T(8,128)S(1)} %fusion), kind=kOutput, calls=%fused_computation.4 | convolution fusion | flops 3228041216 | bytes 13631488 | tf_op jit(solution)/shard_map/dot_general | solution.py:12
  167.3 6.7 %all-to-all-start.1 = ((bf16[32,32,2048]{2,1,0:T(8,128)(2,1)}), bf16[32,32,2048]{2,1,0:T(8,128)(2,1)}, u32[]{:S(2)}, u32[]{:S(2)}) async-start(bf16[32,32,2048]{2,1,0:T(8,128)(2,1)} %bitcast.44), calls=%async_computation.1 | async-start | bytes 8388608 | tf_op jit(solution)/shard_map/all_to_all | solution.py:154
  174.0 1.3 fusion.26
  175.4 0.4 select_reduce_fusion
  175.8 0.1 subtract_convert_fusion
  175.9 0.8 pad_maximum_fusion.comb_ref
  176.7 6.7 %fusion.27 = f32[128,2816]{1,0:T(8,128)S(1)} fusion(bf16[128,2048]{1,0:T(8,128)(2,1)} %copy-done.1, bf16[2048,2816]{1,0:T(8,128)(2,1)} %all-gather.3.cloned.1.call-done), kind=kOutput, calls=%fused_computation.57 | convolution fusion | flops 1476395008 | bytes 13500416 | tf_op jit(solution)/shard_map/dot_general | solution.py:163
  183.5 2.0 fusion.13.sh_ref
  185.5 82.5 %all-to-all-done.1 = bf16[32,32,2048]{2,1,0:T(8,128)(2,1)} async-done(((bf16[32,32,2048]{2,1,0:T(8,128)(2,1)}), bf16[32,32,2048]{2,1,0:T(8,128)(2,1)}, u32[]{:S(2)}, u32[]{:S(2)}) %all-to-all-start.1) | async-done | bytes 4194336 | tf_op jit(solution)/shard_map/all_to_all | solution.py:154
  267.9 5.3 %shard_map.110 = bf16[128,2048]{1,0:T(8,128)(2,1)} custom-call(bf16[256,1024]{1,0:T(8,128)(2,1)} %pad_maximum_fusion.comb_ref, bf16[1024,2048]{1,0:T(8,128)(2,1)} %bitcast.8.ret_ref, f32[128,2048]{1,0:T(8,128)} %copy-done.2, f32[128,2048]{1,0:T(8,128)} %fusion.13.sh_ref), custom_call_target="tpu_custom_call" | custom-call | tf_op jit(solution)/shard_map/pallas_call | solution.py:77
  (40 shorter events, 0.2 us)
Async XLA Ops:
  6.5 155.6 %copy-start = (bf16[1,768,2048]{2,1,0:T(8,128)(2,1)S(1)}, bf16[1,768,2048]{2,1,0:T(8,128)(2,1)}, u32[]{:S(2)}) copy-start(bf16[1,768,2048]{2,1,0:T(8,128)(2,1)} %param.19) | copy-start | bytes 9437188
  6.5 160.8 %all-gather.5.cloned.1.call-start = ((), (), s32[]{:S(2)}) async-start(), calls=%async_computation.3 | async-start | bytes 6488064 | tf_op jit(solution)/shard_map/all_gather | solution.py:131
  6.5 21.8 %collective-permute-start = (bf16[128,2048]{1,0:T(8,128)(2,1)}, bf16[128,2048]{1,0:T(8,128)(2,1)}, u32[]{:S(2)}, u32[]{:S(2)}) collective-permute-start(bf16[128,2048]{1,0:T(8,128)(2,1)} %refs_0_), channel_id=1, source_target_pairs={{0,64},{32,96},{64,128},{96,160},{128,192},{160,224},{192,0},{224,... | collective-permute-start | bytes 1572872 | tf_op jit(solution)/shard_map/ppermute | solution.py:23
  8.1 13.7 %collective-permute-start.1 = (bf16[128,2048]{1,0:T(8,128)(2,1)}, bf16[128,2048]{1,0:T(8,128)(2,1)}, u32[]{:S(2)}, u32[]{:S(2)}) collective-permute-start(bf16[128,2048]{1,0:T(8,128)(2,1)} %refs_0_), channel_id=1, source_target_pairs={{0,192},{32,224},{64,0},{96,32},{128,64},{160,96},{192,128},{224,1... | collective-permute-start | bytes 1572872 | tf_op jit(solution)/shard_map/ppermute | solution.py:23
  22.8 7.4 %collective-permute-start.2 = (bf16[64,2048]{1,0:T(8,128)(2,1)S(1)}, bf16[64,2048]{1,0:T(8,128)(2,1)S(1)}, u32[]{:S(2)}, u32[]{:S(2)}) collective-permute-start(bf16[64,2048]{1,0:T(8,128)(2,1)S(1)} %slice.33), channel_id=1, source_target_pairs={{0,192},{32,224},{64,0},{96,32},{128,64},{160,96},{192,128},{224,1... | collective-permute-start | bytes 786440 | tf_op jit(solution)/shard_map/ppermute | solution.py:23
  29.3 7.9 %collective-permute-start.3 = (bf16[64,2048]{1,0:T(8,128)(2,1)S(1)}, bf16[64,2048]{1,0:T(8,128)(2,1)S(1)}, u32[]{:S(2)}, u32[]{:S(2)}) collective-permute-start(bf16[64,2048]{1,0:T(8,128)(2,1)S(1)} %slice.27), channel_id=1, source_target_pairs={{0,64},{32,96},{64,128},{96,160},{128,192},{160,224},{192,0},{224,... | collective-permute-start | bytes 786440 | tf_op jit(solution)/shard_map/ppermute | solution.py:23
  29.4 8.7 %collective-permute-start.4 = (bf16[128,2048]{1,0:T(8,128)(2,1)}, bf16[128,2048]{1,0:T(8,128)(2,1)}, u32[]{:S(2)}, u32[]{:S(2)}) collective-permute-start(bf16[128,2048]{1,0:T(8,128)(2,1)} %refs_0_), channel_id=1, source_target_pairs={{0,32},{32,0},{64,96},{96,64},{128,160},{160,128},{192,224},{224,1... | collective-permute-start | bytes 1572872 | tf_op jit(solution)/shard_map/ppermute | solution.py:26
  29.5 8.6 %collective-permute-start.5 = (bf16[128,2048]{1,0:T(8,128)(2,1)}, bf16[128,2048]{1,0:T(8,128)(2,1)}, u32[]{:S(2)}, u32[]{:S(2)}) collective-permute-start(bf16[128,2048]{1,0:T(8,128)(2,1)} %collective-permute-done.refs_1_), channel_id=1, source_target_pairs={{0,32},{32,0},{64,96},{96,64},{128,160},{160,128},{192,224},{224,1... | collective-permute-start | bytes 1572872 | tf_op jit(solution)/shard_map/ppermute | solution.py:26
  30.0 8.1 %collective-permute-start.6 = (bf16[128,2048]{1,0:T(8,128)(2,1)}, bf16[128,2048]{1,0:T(8,128)(2,1)}, u32[]{:S(2)}, u32[]{:S(2)}) collective-permute-start(bf16[128,2048]{1,0:T(8,128)(2,1)} %collective-permute-done.1.refs_2_), channel_id=1, source_target_pairs={{0,32},{32,0},{64,96},{96,64},{128,160},{160,128},{192,224},{224,1... | collective-permute-start | bytes 1572872 | tf_op jit(solution)/shard_map/ppermute | solution.py:26
  37.2 0.8 copy-start.3
  38.0 2.0 collective-permute-start.7
  40.1 127.2 %all-gather.3.cloned.1.call-start = ((), (), s32[]{:S(2)}) async-start(), calls=%async_computation.2 | async-start | bytes 12976128 | tf_op jit(solution)/shard_map/all_gather | solution.py:130
  40.8 7.0 %copy-start.6 = (f32[2048]{0:T(1024)S(1)}, f32[2048]{0:T(1024)}, u32[]{:S(2)}) copy-start(f32[2048]{0:T(1024)} %param.14) | copy-start | bytes 24580
  46.9 1.0 copy-start.2
  48.0 107.5 %copy-start.1 = (bf16[128,2048]{1,0:T(8,128)(2,1)}, bf16[128,2048]{1,0:T(8,128)(2,1)S(1)}, u32[]{:S(2)}) copy-start(bf16[128,2048]{1,0:T(8,128)(2,1)S(1)} %multiply_convert_fusion) | copy-start | bytes 1572868
  48.0 107.5 %slice-start = ((s8[6291456]{0:T(1024)(128)(4,1)}), s8[4194304]{0:T(1024)(128)(4,1)S(1)}, s32[]{:S(2)}) async-start(s8[6291456]{0:T(1024)(128)(4,1)} %bitcast.47), calls=%async_computation.4 | async-start | bytes 8388608
  49.3 106.2 %slice-start.1 = ((s8[6291456]{0:T(1024)(128)(4,1)}), s8[2097152]{0:T(1024)(128)(4,1)S(1)}, s32[]{:S(2)}) async-start(s8[6291456]{0:T(1024)(128)(4,1)} %bitcast.47), calls=%async_computation.5 | async-start | bytes 4194304
  167.3 6.7 %copy-start.4 = (bf16[2048,32]{0,1:T(8,128)(2,1)S(1)}, bf16[2048,32]{0,1:T(8,128)(2,1)}, u32[]{:S(2)}) copy-start(bf16[2048,32]{0,1:T(8,128)(2,1)} %param.15) | copy-start | bytes 393220
  167.3 8.0 %copy-start.5 = (s32[128,6]{0,1:T(8,128)S(1)}, s32[128,6]{0,1:T(8,128)}, u32[]{:S(2)}) copy-start(s32[128,6]{0,1:T(8,128)} %param.20) | copy-start | bytes 9220
  167.3 100.6 %all-to-all-start.1 = ((bf16[32,32,2048]{2,1,0:T(8,128)(2,1)}), bf16[32,32,2048]{2,1,0:T(8,128)(2,1)}, u32[]{:S(2)}, u32[]{:S(2)}) async-start(bf16[32,32,2048]{2,1,0:T(8,128)(2,1)} %bitcast.44), calls=%async_computation.1 | async-start | bytes 8388608 | tf_op jit(solution)/shard_map/all_to_all | solution.py:154
  175.9 7.5 %slice-start.2 = ((s8[5767168]{0:T(1024)(128)(4,1)}), s8[4194304]{0:T(1024)(128)(4,1)S(1)}, s32[]{:S(2)}) async-start(s8[5767168]{0:T(1024)(128)(4,1)} %bitcast.49), calls=%async_computation.6 | async-start | bytes 8388608
  176.7 6.7 %slice-start.3 = ((s8[5767168]{0:T(1024)(128)(4,1)}), s8[1572864]{0:T(1024)(128)(4,1)S(1)}, s32[]{:S(2)}) async-start(s8[5767168]{0:T(1024)(128)(4,1)} %bitcast.49), calls=%async_computation.7 | async-start | bytes 3145728
Sparse Core Ops, SparseCore 0:
  40.2 45.2 all-gather.4
  87.4 66.4 all-gather.2

commit v15 on v13

--- a/solution.py
+++ b/solution.py
@@ -44,23 +44,31 @@
     return jnp.concatenate([2 * ys + c, 2 * ys + 1 - c])
 
 
-def _pieces_dot_kernel(ctx_ref, *refs):
-    out_ref = refs[-1]
-    width = refs[0].shape[0]
+def _attn_norm_kernel(ctx_ref, res_ref, gain_ref, *refs):
+    hid_ref, normed_ref = refs[-2:]
+    pieces = refs[:-2]
+    width = pieces[0].shape[0]
     acc = None
-    for i, piece in enumerate(refs[:-1]):
+    for i, piece in enumerate(pieces):
         term = jnp.dot(
             ctx_ref[:, i * width:(i + 1) * width], piece[...], preferred_element_type=jnp.float32
         )
         acc = term if acc is None else acc + term
-    out_ref[...] = acc
+    hidden = (res_ref[...].astype(jnp.float32) + acc).astype(jnp.bfloat16).astype(jnp.float32)
+    scale = lax.rsqrt(jnp.mean(hidden * hidden, axis=-1, keepdims=True) + 1e-06)
+    hid_ref[...] = hidden
+    normed_ref[...] = (hidden * scale * gain_ref[...]).astype(jnp.bfloat16)
 
 
-def pieces_dot(ctx, pieces):
+def attn_norm(ctx, pieces, residual, norm_gain):
+    shape = (ctx.shape[0], pieces[0].shape[1])
     return pl.pallas_call(
-        _pieces_dot_kernel,
-        out_shape=jax.ShapeDtypeStruct((ctx.shape[0], pieces[0].shape[1]), jnp.float32),
-    )(ctx, *pieces)
+        _attn_norm_kernel,
+        out_shape=(
+            jax.ShapeDtypeStruct(shape, jnp.float32),
+            jax.ShapeDtypeStruct(shape, jnp.bfloat16),
+        ),
+    )(ctx, residual, norm_gain.reshape(1, -1), *pieces)
 
 
 def per_device(
@@ -104,11 +112,7 @@
     pieces, shared_in, shared_out = lax.optimization_barrier((pieces, shared_in, shared_out))
     shared_in = lax.all_gather(shared_in, "group", axis=0, tiled=True)
     shared_out = lax.all_gather(shared_out, "group", axis=1, tiled=True)
-    attn = pieces_dot(ctx_perm, pieces)
-    hidden_state = (residual.astype(jnp.float32) + attn).astype(jnp.bfloat16)
-    hidden_f = hidden_state.astype(jnp.float32)
-    scale = lax.rsqrt(jnp.mean(hidden_f * hidden_f, axis=-1, keepdims=True) + 1e-06)
-    normed = (hidden_f * scale * norm_gain).astype(jnp.bfloat16)
+    hidden_f, normed = attn_norm(ctx_perm, pieces, residual, norm_gain)
     logits = jnp.dot(normed, router_w, preferred_element_type=jnp.float32)
     chosen = routes[:, :, None] == jnp.arange(experts, dtype=jnp.int32)[None, None, :]
     picked = jnp.sum(jnp.where(chosen, logits[:, None, :], 0.0), axis=-1)

time: 279 us -> 279 us (level)
  no operation moved by 1% of the time
where the time goes in v15:
time: 279 us; the launch traced here: 278 us
  blocking collectives  106 us (38%)
  waiting for transfers between devices  99.1 us (36%)
  matrix products  30.3 us (11%)
  starting transfers between devices  13.7 us (5%)
  between operations  13.7 us (5%)
  other arithmetic  6.26 us (2%)
  Pallas kernels  4.8 us (2%)
  local copies, waits for them, and re-layouts  4.31 us (2%)
    all_to_all x1, blocking collectives, per_device(): lax.all_to_all(outgoing, 'expert', split_axis=0, concat_axis=0, tiled=True)  106 us
    all_to_all x1, waiting for transfers between devices, per_device(): lax.all_to_all(expert_rows.reshape(arrived.shape), 'expert', split_axis=0...  82.7 us
    ppermute x4, waiting for transfers between devices, shift(): return lax.ppermute(x, 'group', pairs)  13.6 us
    all_to_all x1, starting transfers between devices, per_device(): lax.all_to_all(expert_rows.reshape(arrived.shape), 'expert', split_axis=0...  6.64 us
    dot_general x1, matrix products, swiglu_rows(): mid = jnp.dot(rows, w_in, preferred_element_type=jnp.float32)  6.64 us
    dot_general x1, matrix products, per_device(): shared_mid = jnp.dot(normed, shared_in, preferred_element_type=jnp.float32)  6.57 us
    ppermute x4, starting transfers between devices, shift(): return lax.ppermute(x, 'group', pairs)  6.33 us
  transfers between devices with their start and end apart: 11, of which 5 were waited for; matrix products, arithmetic and copies ran while one was open for 13% of the time, Pallas kernels for 2%

profile of v15, /device:TPU:32, one launch (start us, length us, event | category | flops | bytes accessed | tf_op | source)
XLA Modules:
  0.0 278.1 jit_solution(1505010596630001786)
XLA Ops:
  6.5 1.6 collective-permute-start
  8.1 1.7 collective-permute-start.1
  9.8 0.8 copy.33
  10.6 0.1 eq.85
  10.7 0.1 eq.81
  10.9 1.7 reduce-window.6
  12.6 0.3 slice_reduce_fusion
  12.9 0.1 fusion.23
  13.0 0.1 reduce_sum.39
  13.2 0.1 copy.36
  13.2 0.7 multiply_add_fusion
  13.9 0.5 fusion.5
  14.5 0.7 broadcast_add_fusion
  15.2 0.1 add_multiply_fusion
  15.2 0.1 add_bitcast_fusion.1
  15.3 6.5 %collective-permute-done.1.refs_2_ = bf16[128,2048]{1,0:T(8,128)(2,1)} collective-permute-done((bf16[128,2048]{1,0:T(8,128)(2,1)}, bf16[128,2048]{1,0:T(8,128)(2,1)}, u32[]{:S(2)}, u32[]{:S(2)}) %collective-permute-start.1) | collective-permute-done | bytes 524320 | tf_op jit(solution)/shard_map/ppermute | solution.py:23
  21.8 1.0 slice.41
  22.8 3.0 %collective-permute-start.2 = (bf16[64,2048]{1,0:T(8,128)(2,1)S(1)}, bf16[64,2048]{1,0:T(8,128)(2,1)S(1)}, u32[]{:S(2)}, u32[]{:S(2)}) collective-permute-start(bf16[64,2048]{1,0:T(8,128)(2,1)S(1)} %slice.41), channel_id=1, source_target_pairs={{0,192},{32,224},{64,0},{96,32},{128,64},{160,96},{192,128},{224,1... | collective-permute-start | bytes 786440 | tf_op jit(solution)/shard_map/ppermute | solution.py:23
  25.8 2.5 fusion.10.ctx_ref
  28.3 1.0 slice.33
  29.2 0.1 collective-permute-start.3
  29.3 0.1 collective-permute-start.4
  29.4 0.5 collective-permute-start.5
  29.9 0.1 collective-permute-start.6
  30.0 0.2 collective-permute-done.2
  30.3 6.9 %collective-permute-done.3 = bf16[64,2048]{1,0:T(8,128)(2,1)S(1)} collective-permute-done((bf16[64,2048]{1,0:T(8,128)(2,1)S(1)}, bf16[64,2048]{1,0:T(8,128)(2,1)S(1)}, u32[]{:S(2)}, u32[]{:S(2)}) %collective-permute-start.3) | collective-permute-done | bytes 262176 | tf_op jit(solution)/shard_map/ppermute | solution.py:23
  37.2 0.0 copy-start.1
  37.2 0.8 copy-done.1
  38.0 2.0 collective-permute-done.7.refs_7_
  40.0 0.0 all-gather.5.cloned.1.call-update
  40.1 0.0 all-gather.3.cloned.1.call-start
  40.1 0.7 all-gather.3.cloned.1.call-update
  40.8 4.8 %shard_map.109 = (f32[128,2048]{1,0:T(8,128)}, bf16[128,2048]{1,0:T(8,128)(2,1)}) custom-call(bf16[128,1024]{1,0:T(8,128)(2,1)} %fusion.10.ctx_ref, bf16[128,2048]{1,0:T(8,128)(2,1)} %res_ref.1, f32[1,2048]{1,0:T(1,128)} %bitcast.49, bf16[128,2048]{1,0:T(8,128)(2,1)} %refs_0_, bf16[128,2048]{1,0:T(8,128)(2,1)} %collective-permute-done.refs_1_, ...), custom_call_target="tpu_custom_call" | custom-call | tf_op jit(solution)/shard_map/pallas_call | solution.py:65
  45.6 2.5 convolution_convert_fusion.1
  48.1 0.0 slice-start.1
  48.1 106.0 %all_to_all.10 = bf16[32,32,2048]{2,1,0:T(8,128)(2,1)S(1)} all-to-all(bf16[32,32,2048]{2,1,0:T(8,128)(2,1)S(1)} %bitcast.45), channel_id=1, replica_groups=mesh['group'=8,'expert'=32] {'expert'}, dimensions={0} | all-to-all | bytes 8388608 | tf_op jit(solution)/shard_map/all_to_all | solution.py:129
  154.1 6.6 %fusion = f32[1024,1536]{1,0:T(8,128)S(1)} fusion(bf16[1024,2048]{1,0:T(8,128)(2,1)S(1)} %bitcast.47, bf16[1,2048,1536]{2,1,0:T(8,128)(2,1)S(1)} %bitcast.51), kind=kOutput, calls=%fused_computation | convolution fusion | flops 6442450944 | bytes 16777216 | tf_op jit(solution)/shard_map/dot_general | solution.py:10
  160.8 5.2 %convolution_convert_fusion = bf16[1024,2048]{1,0:T(8,128)(2,1)} fusion(bf16[1,768,2048]{2,1,0:T(8,128)(2,1)S(1)} %copy-done, f32[1024,1536]{1,0:T(8,128)S(1)} %fusion), kind=kOutput, calls=%fused_computation.4 | convolution fusion | flops 3228041216 | bytes 13631488 | tf_op jit(solution)/shard_map/dot_general | solution.py:12
  166.0 6.6 %all-to-all-start.1 = ((bf16[32,32,2048]{2,1,0:T(8,128)(2,1)}), bf16[32,32,2048]{2,1,0:T(8,128)(2,1)}, u32[]{:S(2)}, u32[]{:S(2)}) async-start(bf16[32,32,2048]{2,1,0:T(8,128)(2,1)} %bitcast.46), calls=%async_computation.1 | async-start | bytes 8388608 | tf_op jit(solution)/shard_map/all_to_all | solution.py:133
  172.6 1.3 fusion.32
  173.9 0.0 copy-done.5
  174.0 0.4 select_reduce_fusion
  174.5 0.8 subtract_convert_fusion
  175.2 6.6 %fusion.31 = f32[128,2816]{1,0:T(8,128)S(1)} fusion(bf16[128,2048]{1,0:T(8,128)(2,1)} %get-tuple-element.35, bf16[2048,2816]{1,0:T(8,128)(2,1)} %all-gather.3.cloned.1.call-done), kind=kOutput, calls=%fused_computation.58 | convolution fusion | flops 1476395008 | bytes 13500416 | tf_op jit(solution)/shard_map/dot_general | solution.py:146
  181.9 2.0 fusion.18
  183.9 82.7 %all-to-all-done.1 = bf16[32,32,2048]{2,1,0:T(8,128)(2,1)} async-done(((bf16[32,32,2048]{2,1,0:T(8,128)(2,1)}), bf16[32,32,2048]{2,1,0:T(8,128)(2,1)}, u32[]{:S(2)}, u32[]{:S(2)}) %all-to-all-start.1) | async-done | bytes 4194336 | tf_op jit(solution)/shard_map/all_to_all | solution.py:133
  266.5 3.7 %fusion.14 = f32[256,2048]{1,0:T(8,128)S(1)} fusion(bf16[1024,2048]{1,0:T(8,128)(2,1)} %bitcast.9, bf16[128,1024]{1,0:T(8,128)(2,1)S(1)} %get-tuple-element.43, bf16[128,1024]{1,0:T(8,128)(2,1)} %get-tuple-element.44), kind=kOutput, calls=%fused_computation.22 | convolution fusion | flops 1074790400 | bytes 6815744 | tf_op jit(solution)/shard_map/dot_general | solution.py:141
  270.2 1.1 fusion.12
  (35 shorter events, 0.2 us)
Async XLA Ops:
  6.5 154.2 %copy-start = (bf16[1,768,2048]{2,1,0:T(8,128)(2,1)S(1)}, bf16[1,768,2048]{2,1,0:T(8,128)(2,1)}, u32[]{:S(2)}) copy-start(bf16[1,768,2048]{2,1,0:T(8,128)(2,1)} %param.19) | copy-start | bytes 9437188
  6.5 159.4 %all-gather.5.cloned.1.call-start = ((), (), s32[]{:S(2)}) async-start(), calls=%async_computation.3 | async-start | bytes 6488064 | tf_op jit(solution)/shard_map/all_gather | solution.py:114
  6.5 21.7 %collective-permute-start = (bf16[128,2048]{1,0:T(8,128)(2,1)}, bf16[128,2048]{1,0:T(8,128)(2,1)}, u32[]{:S(2)}, u32[]{:S(2)}) collective-permute-start(bf16[128,2048]{1,0:T(8,128)(2,1)} %refs_0_), channel_id=1, source_target_pairs={{0,64},{32,96},{64,128},{96,160},{128,192},{160,224},{192,0},{224,... | collective-permute-start | bytes 1572872 | tf_op jit(solution)/shard_map/ppermute | solution.py:23
  8.1 13.7 %collective-permute-start.1 = (bf16[128,2048]{1,0:T(8,128)(2,1)}, bf16[128,2048]{1,0:T(8,128)(2,1)}, u32[]{:S(2)}, u32[]{:S(2)}) collective-permute-start(bf16[128,2048]{1,0:T(8,128)(2,1)} %refs_0_), channel_id=1, source_target_pairs={{0,192},{32,224},{64,0},{96,32},{128,64},{160,96},{192,128},{224,1... | collective-permute-start | bytes 1572872 | tf_op jit(solution)/shard_map/ppermute | solution.py:23
  22.8 7.4 %collective-permute-start.2 = (bf16[64,2048]{1,0:T(8,128)(2,1)S(1)}, bf16[64,2048]{1,0:T(8,128)(2,1)S(1)}, u32[]{:S(2)}, u32[]{:S(2)}) collective-permute-start(bf16[64,2048]{1,0:T(8,128)(2,1)S(1)} %slice.41), channel_id=1, source_target_pairs={{0,192},{32,224},{64,0},{96,32},{128,64},{160,96},{192,128},{224,1... | collective-permute-start | bytes 786440 | tf_op jit(solution)/shard_map/ppermute | solution.py:23
  29.2 7.9 %collective-permute-start.3 = (bf16[64,2048]{1,0:T(8,128)(2,1)S(1)}, bf16[64,2048]{1,0:T(8,128)(2,1)S(1)}, u32[]{:S(2)}, u32[]{:S(2)}) collective-permute-start(bf16[64,2048]{1,0:T(8,128)(2,1)S(1)} %slice.33), channel_id=1, source_target_pairs={{0,64},{32,96},{64,128},{96,160},{128,192},{160,224},{192,0},{224,... | collective-permute-start | bytes 786440 | tf_op jit(solution)/shard_map/ppermute | solution.py:23
  29.3 8.7 %collective-permute-start.4 = (bf16[128,2048]{1,0:T(8,128)(2,1)}, bf16[128,2048]{1,0:T(8,128)(2,1)}, u32[]{:S(2)}, u32[]{:S(2)}) collective-permute-start(bf16[128,2048]{1,0:T(8,128)(2,1)} %refs_0_), channel_id=1, source_target_pairs={{0,32},{32,0},{64,96},{96,64},{128,160},{160,128},{192,224},{224,1... | collective-permute-start | bytes 1572872 | tf_op jit(solution)/shard_map/ppermute | solution.py:26
  29.4 8.6 %collective-permute-start.5 = (bf16[128,2048]{1,0:T(8,128)(2,1)}, bf16[128,2048]{1,0:T(8,128)(2,1)}, u32[]{:S(2)}, u32[]{:S(2)}) collective-permute-start(bf16[128,2048]{1,0:T(8,128)(2,1)} %collective-permute-done.refs_1_), channel_id=1, source_target_pairs={{0,32},{32,0},{64,96},{96,64},{128,160},{160,128},{192,224},{224,1... | collective-permute-start | bytes 1572872 | tf_op jit(solution)/shard_map/ppermute | solution.py:26
  29.9 8.1 %collective-permute-start.6 = (bf16[128,2048]{1,0:T(8,128)(2,1)}, bf16[128,2048]{1,0:T(8,128)(2,1)}, u32[]{:S(2)}, u32[]{:S(2)}) collective-permute-start(bf16[128,2048]{1,0:T(8,128)(2,1)} %collective-permute-done.1.refs_2_), channel_id=1, source_target_pairs={{0,32},{32,0},{64,96},{96,64},{128,160},{160,128},{192,224},{224,1... | collective-permute-start | bytes 1572872 | tf_op jit(solution)/shard_map/ppermute | solution.py:26
  37.2 0.8 copy-start.1
  38.0 2.0 collective-permute-start.7
  40.1 125.9 %all-gather.3.cloned.1.call-start = ((), (), s32[]{:S(2)}) async-start(), calls=%async_computation.2 | async-start | bytes 12976128 | tf_op jit(solution)/shard_map/all_gather | solution.py:113
  45.6 108.5 %slice-start = ((s8[6291456]{0:T(1024)(128)(4,1)}), s8[4194304]{0:T(1024)(128)(4,1)S(1)}, s32[]{:S(2)}) async-start(s8[6291456]{0:T(1024)(128)(4,1)} %bitcast.50), calls=%async_computation.4 | async-start | bytes 8388608
  48.1 106.0 %slice-start.1 = ((s8[6291456]{0:T(1024)(128)(4,1)}), s8[2097152]{0:T(1024)(128)(4,1)S(1)}, s32[]{:S(2)}) async-start(s8[6291456]{0:T(1024)(128)(4,1)} %bitcast.50), calls=%async_computation.5 | async-start | bytes 4194304
  165.9 6.7 %copy-start.4 = (bf16[2048,32]{0,1:T(8,128)(2,1)S(1)}, bf16[2048,32]{0,1:T(8,128)(2,1)}, u32[]{:S(2)}) copy-start(bf16[2048,32]{0,1:T(8,128)(2,1)} %param.15) | copy-start | bytes 393220
  166.0 8.0 %copy-start.5 = (s32[128,6]{0,1:T(8,128)S(1)}, s32[128,6]{0,1:T(8,128)}, u32[]{:S(2)}) copy-start(s32[128,6]{0,1:T(8,128)} %param.20) | copy-start | bytes 9220
  166.0 100.6 %all-to-all-start.1 = ((bf16[32,32,2048]{2,1,0:T(8,128)(2,1)}), bf16[32,32,2048]{2,1,0:T(8,128)(2,1)}, u32[]{:S(2)}, u32[]{:S(2)}) async-start(bf16[32,32,2048]{2,1,0:T(8,128)(2,1)} %bitcast.46), calls=%async_computation.1 | async-start | bytes 8388608 | tf_op jit(solution)/shard_map/all_to_all | solution.py:133
  174.5 7.4 %slice-start.2 = ((s8[5767168]{0:T(1024)(128)(4,1)}), s8[4194304]{0:T(1024)(128)(4,1)S(1)}, s32[]{:S(2)}) async-start(s8[5767168]{0:T(1024)(128)(4,1)} %bitcast.52), calls=%async_computation.6 | async-start | bytes 8388608
  175.2 6.6 %slice-start.3 = ((s8[5767168]{0:T(1024)(128)(4,1)}), s8[1572864]{0:T(1024)(128)(4,1)S(1)}, s32[]{:S(2)}) async-start(s8[5767168]{0:T(1024)(128)(4,1)} %bitcast.52), calls=%async_computation.7 | async-start | bytes 3145728
  266.5 3.7 %copy-start.2 = (f32[128,2048]{1,0:T(8,128)S(1)}, f32[128,2048]{1,0:T(8,128)}, u32[]{:S(2)}) copy-start(f32[128,2048]{1,0:T(8,128)} %get-tuple-element.34) | copy-start | bytes 3145732
  266.5 3.7 %copy-start.3 = (f32[128,2048]{1,0:T(8,128)S(1)}, f32[128,2048]{1,0:T(8,128)}, u32[]{:S(2)}) copy-start(f32[128,2048]{1,0:T(8,128)} %fusion.18) | copy-start | bytes 3145732
Sparse Core Ops, SparseCore 0:
  40.2 45.2 all-gather.4
  87.3 66.4 all-gather.2

commit v16 on v15

--- a/solution.py
+++ b/solution.py
@@ -109,9 +109,8 @@
     else:
         pieces = [lax.all_gather(attn_out_w, "group", axis=0, tiled=True)]
         ctx_perm = context
-    pieces, shared_in, shared_out = lax.optimization_barrier((pieces, shared_in, shared_out))
+    pieces, shared_in = lax.optimization_barrier((pieces, shared_in))
     shared_in = lax.all_gather(shared_in, "group", axis=0, tiled=True)
-    shared_out = lax.all_gather(shared_out, "group", axis=1, tiled=True)
     hidden_f, normed = attn_norm(ctx_perm, pieces, residual, norm_gain)
     logits = jnp.dot(normed, router_w, preferred_element_type=jnp.float32)
     chosen = routes[:, :, None] == jnp.arange(experts, dtype=jnp.int32)[None, None, :]
@@ -127,9 +126,11 @@
     local_in = expert_in[0]
     local_out = expert_out_w[0]
     arrived = lax.all_to_all(outgoing, "expert", split_axis=0, concat_axis=0, tiled=True)
+    arrived, shared_out = lax.optimization_barrier((arrived, shared_out))
+    shared_out = lax.all_gather(shared_out, "group", axis=1, tiled=True)
     flat_rows = arrived.reshape(-1, width)
     expert_rows = swiglu_rows(flat_rows, local_in, local_out).astype(jnp.bfloat16)
-    expert_rows, shared_in, shared_out = lax.optimization_barrier((expert_rows, shared_in, shared_out))
+    expert_rows, shared_in = lax.optimization_barrier((expert_rows, shared_in))
     returned = lax.all_to_all(
         expert_rows.reshape(arrived.shape),
         "expert",

time: 279 us -> 281 us (level)
  matrix products: 30.3 us -> 37.2 us
  waiting for transfers between devices: 99.1 us -> 94.6 us
    all_to_all x1, waiting for transfers between devices: 82.7 us -> 69.9 us  [per_device(): lax.all_to_all(expert_rows.reshape(arrived.shape), 'expert', split_axis=0...]
    all_gather x1, waiting for transfers between devices: 0.01 us -> 9.02 us  [per_device(): shared_out = lax.all_gather(shared_out, 'group', axis=1, tiled=True)]
    dot_general x1, matrix products: 6.64 us -> 10 us  [swiglu_rows(): mid = jnp.dot(rows, w_in, preferred_element_type=jnp.float32)]
    dot_general x1, matrix products: 2 us -> 5.09 us  [per_device(): jnp.dot(shared_act, shared_out, preferred_element_type=jnp.float32)]
  transfers between devices with their start and end apart: 11 -> 11, of which waited for: 5 -> 6; matrix products, arithmetic and copies ran while one was open for 13% -> 15% of each run, Pallas kernels for 2% -> 2%
where the time goes in v16:
time: 281 us
  blocking collectives  106 us (38%)
  waiting for transfers between devices  94.6 us (34%)
  matrix products  37.2 us (13%)
  starting transfers between devices  13.7 us (5%)
  between operations  13.6 us (5%)
  other arithmetic  6.26 us (2%)
  Pallas kernels  4.8 us (2%)
  local copies, waits for them, and re-layouts  4.29 us (2%)
    all_to_all x1, blocking collectives, per_device(): lax.all_to_all(outgoing, 'expert', split_axis=0, concat_axis=0, tiled=True)  106 us
    all_to_all x1, waiting for transfers between devices, per_device(): lax.all_to_all(expert_rows.reshape(arrived.shape), 'expert', split_axis=0...  69.9 us
    ppermute x4, waiting for transfers between devices, shift(): return lax.ppermute(x, 'group', pairs)  13.6 us
    dot_general x1, matrix products, swiglu_rows(): mid = jnp.dot(rows, w_in, preferred_element_type=jnp.float32)  10 us
    all_gather x1, waiting for transfers between devices, per_device(): shared_out = lax.all_gather(shared_out, 'group', axis=1, tiled=True)  9.02 us
    dot_general x1, matrix products, per_device(): shared_mid = jnp.dot(normed, shared_in, preferred_element_type=jnp.float32)  7.25 us
    all_to_all x1, starting transfers between devices, per_device(): lax.all_to_all(expert_rows.reshape(arrived.shape), 'expert', split_axis=0...  6.64 us
    ppermute x4, starting transfers between devices, shift(): return lax.ppermute(x, 'group', pairs)  6.33 us
  transfers between devices with their start and end apart: 11, of which 6 were waited for; matrix products, arithmetic and copies ran while one was open for 15% of the time, Pallas kernels for 2%

profile of v16, /device:TPU:32, one launch (start us, length us, event | category | flops | bytes accessed | tf_op | source)
XLA Modules:
  0.0 280.6 jit_solution(17379036446139809160)
XLA Ops:
  6.5 1.6 collective-permute-start
  8.1 1.7 collective-permute-start.1
  9.8 0.8 copy.33
  10.6 0.1 eq.85
  10.7 0.1 eq.81
  10.9 1.7 reduce-window.6
  12.6 0.3 slice_reduce_fusion
  12.9 0.1 fusion.23
  13.0 0.1 reduce_sum.39
  13.2 0.1 copy.36
  13.2 0.7 multiply_add_fusion
  13.9 0.5 fusion.5
  14.5 0.7 broadcast_add_fusion
  15.2 0.1 add_multiply_fusion
  15.2 0.1 add_bitcast_fusion.1
  15.3 6.5 %collective-permute-done.1.refs_2_ = bf16[128,2048]{1,0:T(8,128)(2,1)} collective-permute-done((bf16[128,2048]{1,0:T(8,128)(2,1)}, bf16[128,2048]{1,0:T(8,128)(2,1)}, u32[]{:S(2)}, u32[]{:S(2)}) %collective-permute-start.1) | collective-permute-done | bytes 524320 | tf_op jit(solution)/shard_map/ppermute | solution.py:23
  21.8 1.0 slice.41
  22.8 3.0 %collective-permute-start.2 = (bf16[64,2048]{1,0:T(8,128)(2,1)S(1)}, bf16[64,2048]{1,0:T(8,128)(2,1)S(1)}, u32[]{:S(2)}, u32[]{:S(2)}) collective-permute-start(bf16[64,2048]{1,0:T(8,128)(2,1)S(1)} %slice.41), channel_id=1, source_target_pairs={{0,192},{32,224},{64,0},{96,32},{128,64},{160,96},{192,128},{224,1... | collective-permute-start | bytes 786440 | tf_op jit(solution)/shard_map/ppermute | solution.py:23
  25.8 2.5 fusion.10.ctx_ref
  28.3 1.0 slice.33
  29.3 0.1 collective-permute-start.3
  29.4 0.1 collective-permute-start.4
  29.5 0.5 collective-permute-start.5
  30.0 0.1 collective-permute-start.6
  30.1 0.2 collective-permute-done.2
  30.3 6.9 %collective-permute-done.3 = bf16[64,2048]{1,0:T(8,128)(2,1)S(1)} collective-permute-done((bf16[64,2048]{1,0:T(8,128)(2,1)S(1)}, bf16[64,2048]{1,0:T(8,128)(2,1)S(1)}, u32[]{:S(2)}, u32[]{:S(2)}) %collective-permute-start.3) | collective-permute-done | bytes 262176 | tf_op jit(solution)/shard_map/ppermute | solution.py:23
  37.2 0.0 copy-start.1
  37.2 0.8 copy-done.1
  38.0 2.0 collective-permute-done.7.refs_7_
  40.1 0.0 all-gather.3.cloned.1.call-update
  40.1 0.0 all-gather.5.cloned.1.call-start
  40.1 4.8 %shard_map.109 = (f32[128,2048]{1,0:T(8,128)}, bf16[128,2048]{1,0:T(8,128)(2,1)}) custom-call(bf16[128,1024]{1,0:T(8,128)(2,1)} %fusion.10.ctx_ref, bf16[128,2048]{1,0:T(8,128)(2,1)} %res_ref.1, f32[1,2048]{1,0:T(1,128)} %bitcast.49, bf16[128,2048]{1,0:T(8,128)(2,1)} %refs_0_, bf16[128,2048]{1,0:T(8,128)(2,1)} %collective-permute-done.refs_1_, ...), custom_call_target="tpu_custom_call" | custom-call | tf_op jit(solution)/shard_map/pallas_call | solution.py:65
  44.9 2.3 convolution_convert_fusion.1
  47.2 106.0 %all_to_all.10 = bf16[32,32,2048]{2,1,0:T(8,128)(2,1)} all-to-all(bf16[32,32,2048]{2,1,0:T(8,128)(2,1)S(1)} %bitcast.45), channel_id=1, replica_groups=mesh['group'=8,'expert'=32] {'expert'}, dimensions={0} | all-to-all | bytes 8388608 | tf_op jit(solution)/shard_map/all_to_all | solution.py:128
  153.2 0.0 all-gather.5.cloned.1.call-update
  153.3 10.0 %fusion = f32[1024,1536]{1,0:T(8,128)S(1)} fusion(bf16[1024,2048]{1,0:T(8,128)(2,1)} %bitcast.47, bf16[1,2048,1536]{2,1,0:T(8,128)(2,1)} %param.18), kind=kOutput, calls=%fused_computation | convolution fusion | flops 6442450944 | bytes 16777216 | tf_op jit(solution)/shard_map/dot_general | solution.py:10
  163.3 5.1 %convolution_convert_fusion = bf16[1024,2048]{1,0:T(8,128)(2,1)} fusion(bf16[1,768,2048]{2,1,0:T(8,128)(2,1)S(1)} %copy-done, f32[1024,1536]{1,0:T(8,128)S(1)} %fusion), kind=kOutput, calls=%fused_computation.4 | convolution fusion | flops 3228041216 | bytes 13631488 | tf_op jit(solution)/shard_map/dot_general | solution.py:12
  168.4 6.6 %all-to-all-start.1 = ((bf16[32,32,2048]{2,1,0:T(8,128)(2,1)}), bf16[32,32,2048]{2,1,0:T(8,128)(2,1)}, u32[]{:S(2)}, u32[]{:S(2)}) async-start(bf16[32,32,2048]{2,1,0:T(8,128)(2,1)} %bitcast.46), calls=%async_computation.1 | async-start | bytes 8388608 | tf_op jit(solution)/shard_map/all_to_all | solution.py:134
  175.1 1.3 fusion.32
  176.4 0.0 copy-done.5
  176.5 0.4 select_reduce_fusion
  176.9 0.8 subtract_convert_fusion
  177.7 7.3 %fusion.31 = f32[128,2816]{1,0:T(8,128)} fusion(bf16[128,2048]{1,0:T(8,128)(2,1)} %get-tuple-element.35, bf16[2048,2816]{1,0:T(8,128)(2,1)} %all-gather.3.cloned.1.call-done), kind=kOutput, calls=%fused_computation.58 | convolution fusion | flops 1476395008 | bytes 13500416 | tf_op jit(solution)/shard_map/dot_general | solution.py:147
  184.9 9.0 %all-gather.5.cloned.1.call-done = bf16[1408,2048]{1,0:T(8,128)(2,1)} async-done(((bf16[1408,256]{1,0:T(8,128)(2,1)}), bf16[1408,2048]{1,0:T(8,128)(2,1)}) %all-gather.5.cloned.1.call-update) | async-done | bytes 5767184 | tf_op jit(solution)/shard_map/all_gather | solution.py:130
  194.0 5.1 %fusion.18 = f32[128,2048]{1,0:T(8,128)} fusion(bf16[1408,2048]{1,0:T(8,128)(2,1)} %all-gather.5.cloned.1.call-done, f32[128,2816]{1,0:T(8,128)} %fusion.31), kind=kOutput, calls=%fused_computation.27 | convolution fusion | flops 739278848 | bytes 8257536 | tf_op jit(solution)/shard_map/dot_general | solution.py:155
  199.1 69.9 %all-to-all-done.1 = bf16[32,32,2048]{2,1,0:T(8,128)(2,1)} async-done(((bf16[32,32,2048]{2,1,0:T(8,128)(2,1)}), bf16[32,32,2048]{2,1,0:T(8,128)(2,1)}, u32[]{:S(2)}, u32[]{:S(2)}) %all-to-all-start.1) | async-done | bytes 4194336 | tf_op jit(solution)/shard_map/all_to_all | solution.py:134
  269.0 3.7 %fusion.14 = f32[256,2048]{1,0:T(8,128)S(1)} fusion(bf16[1024,2048]{1,0:T(8,128)(2,1)} %bitcast.9, bf16[128,1024]{1,0:T(8,128)(2,1)S(1)} %get-tuple-element.43, bf16[128,1024]{1,0:T(8,128)(2,1)} %get-tuple-element.44), kind=kOutput, calls=%fused_computation.22 | convolution fusion | flops 1074790400 | bytes 6815744 | tf_op jit(solution)/shard_map/dot_general | solution.py:142
  272.7 1.1 fusion.12
  (25 shorter events, 0.2 us)
Async XLA Ops:
  6.5 156.8 %copy-start = (bf16[1,768,2048]{2,1,0:T(8,128)(2,1)S(1)}, bf16[1,768,2048]{2,1,0:T(8,128)(2,1)}, u32[]{:S(2)}) copy-start(bf16[1,768,2048]{2,1,0:T(8,128)(2,1)} %param.19) | copy-start | bytes 9437188
  6.5 161.9 %all-gather.3.cloned.1.call-start = ((), (), s32[]{:S(2)}) async-start(), calls=%async_computation.2 | async-start | bytes 12976128 | tf_op jit(solution)/shard_map/all_gather | solution.py:113
  6.5 21.8 %collective-permute-start = (bf16[128,2048]{1,0:T(8,128)(2,1)}, bf16[128,2048]{1,0:T(8,128)(2,1)}, u32[]{:S(2)}, u32[]{:S(2)}) collective-permute-start(bf16[128,2048]{1,0:T(8,128)(2,1)} %refs_0_), channel_id=1, source_target_pairs={{0,64},{32,96},{64,128},{96,160},{128,192},{160,224},{192,0},{224,... | collective-permute-start | bytes 1572872 | tf_op jit(solution)/shard_map/ppermute | solution.py:23
  8.1 13.7 %collective-permute-start.1 = (bf16[128,2048]{1,0:T(8,128)(2,1)}, bf16[128,2048]{1,0:T(8,128)(2,1)}, u32[]{:S(2)}, u32[]{:S(2)}) collective-permute-start(bf16[128,2048]{1,0:T(8,128)(2,1)} %refs_0_), channel_id=1, source_target_pairs={{0,192},{32,224},{64,0},{96,32},{128,64},{160,96},{192,128},{224,1... | collective-permute-start | bytes 1572872 | tf_op jit(solution)/shard_map/ppermute | solution.py:23
  22.8 7.4 %collective-permute-start.2 = (bf16[64,2048]{1,0:T(8,128)(2,1)S(1)}, bf16[64,2048]{1,0:T(8,128)(2,1)S(1)}, u32[]{:S(2)}, u32[]{:S(2)}) collective-permute-start(bf16[64,2048]{1,0:T(8,128)(2,1)S(1)} %slice.41), channel_id=1, source_target_pairs={{0,192},{32,224},{64,0},{96,32},{128,64},{160,96},{192,128},{224,1... | collective-permute-start | bytes 786440 | tf_op jit(solution)/shard_map/ppermute | solution.py:23
  29.3 7.9 %collective-permute-start.3 = (bf16[64,2048]{1,0:T(8,128)(2,1)S(1)}, bf16[64,2048]{1,0:T(8,128)(2,1)S(1)}, u32[]{:S(2)}, u32[]{:S(2)}) collective-permute-start(bf16[64,2048]{1,0:T(8,128)(2,1)S(1)} %slice.33), channel_id=1, source_target_pairs={{0,64},{32,96},{64,128},{96,160},{128,192},{160,224},{192,0},{224,... | collective-permute-start | bytes 786440 | tf_op jit(solution)/shard_map/ppermute | solution.py:23
  29.4 8.7 %collective-permute-start.4 = (bf16[128,2048]{1,0:T(8,128)(2,1)}, bf16[128,2048]{1,0:T(8,128)(2,1)}, u32[]{:S(2)}, u32[]{:S(2)}) collective-permute-start(bf16[128,2048]{1,0:T(8,128)(2,1)} %refs_0_), channel_id=1, source_target_pairs={{0,32},{32,0},{64,96},{96,64},{128,160},{160,128},{192,224},{224,1... | collective-permute-start | bytes 1572872 | tf_op jit(solution)/shard_map/ppermute | solution.py:26
  29.5 8.6 %collective-permute-start.5 = (bf16[128,2048]{1,0:T(8,128)(2,1)}, bf16[128,2048]{1,0:T(8,128)(2,1)}, u32[]{:S(2)}, u32[]{:S(2)}) collective-permute-start(bf16[128,2048]{1,0:T(8,128)(2,1)} %collective-permute-done.refs_1_), channel_id=1, source_target_pairs={{0,32},{32,0},{64,96},{96,64},{128,160},{160,128},{192,224},{224,1... | collective-permute-start | bytes 1572872 | tf_op jit(solution)/shard_map/ppermute | solution.py:26
  30.0 8.1 %collective-permute-start.6 = (bf16[128,2048]{1,0:T(8,128)(2,1)}, bf16[128,2048]{1,0:T(8,128)(2,1)}, u32[]{:S(2)}, u32[]{:S(2)}) collective-permute-start(bf16[128,2048]{1,0:T(8,128)(2,1)} %collective-permute-done.1.refs_2_), channel_id=1, source_target_pairs={{0,32},{32,0},{64,96},{96,64},{128,160},{160,128},{192,224},{224,1... | collective-permute-start | bytes 1572872 | tf_op jit(solution)/shard_map/ppermute | solution.py:26
  37.2 0.8 copy-start.1
  38.0 2.0 collective-permute-start.7
  40.1 153.9 %all-gather.5.cloned.1.call-start = ((), (), s32[]{:S(2)}) async-start(), calls=%async_computation.3 | async-start | bytes 6488064 | tf_op jit(solution)/shard_map/all_gather | solution.py:130
  168.4 6.7 %copy-start.4 = (bf16[2048,32]{0,1:T(8,128)(2,1)S(1)}, bf16[2048,32]{0,1:T(8,128)(2,1)}, u32[]{:S(2)}) copy-start(bf16[2048,32]{0,1:T(8,128)(2,1)} %param.15) | copy-start | bytes 393220
  168.4 8.0 %copy-start.5 = (s32[128,6]{0,1:T(8,128)S(1)}, s32[128,6]{0,1:T(8,128)}, u32[]{:S(2)}) copy-start(s32[128,6]{0,1:T(8,128)} %param.20) | copy-start | bytes 9220
  168.4 100.6 %all-to-all-start.1 = ((bf16[32,32,2048]{2,1,0:T(8,128)(2,1)}), bf16[32,32,2048]{2,1,0:T(8,128)(2,1)}, u32[]{:S(2)}, u32[]{:S(2)}) async-start(bf16[32,32,2048]{2,1,0:T(8,128)(2,1)} %bitcast.46), calls=%async_computation.1 | async-start | bytes 8388608 | tf_op jit(solution)/shard_map/all_to_all | solution.py:134
  269.0 3.7 %copy-start.2 = (f32[128,2048]{1,0:T(8,128)S(1)}, f32[128,2048]{1,0:T(8,128)}, u32[]{:S(2)}) copy-start(f32[128,2048]{1,0:T(8,128)} %get-tuple-element.34) | copy-start | bytes 3145732
  269.0 3.7 %copy-start.3 = (f32[128,2048]{1,0:T(8,128)S(1)}, f32[128,2048]{1,0:T(8,128)}, u32[]{:S(2)}) copy-start(f32[128,2048]{1,0:T(8,128)} %fusion.18) | copy-start | bytes 3145732
Sparse Core Ops, SparseCore 0:
  40.2 65.4 all-gather.2
  153.4 40.5 all-gather.4

commit v17 on v15

--- a/solution.py
+++ b/solution.py
@@ -44,9 +44,9 @@
     return jnp.concatenate([2 * ys + c, 2 * ys + 1 - c])
 
 
-def _attn_norm_kernel(ctx_ref, res_ref, gain_ref, *refs):
-    hid_ref, normed_ref = refs[-2:]
-    pieces = refs[:-2]
+def _attn_norm_kernel(ctx_ref, res_ref, gain_ref, send_ref, *refs):
+    hid_ref, normed_ref, out_ref = refs[-3:]
+    pieces = refs[:-3]
     width = pieces[0].shape[0]
     acc = None
     for i, piece in enumerate(pieces):
@@ -57,18 +57,23 @@
     hidden = (res_ref[...].astype(jnp.float32) + acc).astype(jnp.bfloat16).astype(jnp.float32)
     scale = lax.rsqrt(jnp.mean(hidden * hidden, axis=-1, keepdims=True) + 1e-06)
     hid_ref[...] = hidden
-    normed_ref[...] = (hidden * scale * gain_ref[...]).astype(jnp.bfloat16)
+    normed = (hidden * scale * gain_ref[...]).astype(jnp.bfloat16)
+    normed_ref[...] = normed
+    out_ref[...] = jnp.dot(send_ref[...], normed, preferred_element_type=jnp.float32).astype(
+        out_ref.dtype
+    )
 
 
-def attn_norm(ctx, pieces, residual, norm_gain):
+def attn_norm(ctx, pieces, residual, norm_gain, send):
     shape = (ctx.shape[0], pieces[0].shape[1])
     return pl.pallas_call(
         _attn_norm_kernel,
         out_shape=(
             jax.ShapeDtypeStruct(shape, jnp.float32),
             jax.ShapeDtypeStruct(shape, jnp.bfloat16),
+            jax.ShapeDtypeStruct((send.shape[0], shape[1]), jnp.bfloat16),
         ),
-    )(ctx, residual, norm_gain.reshape(1, -1), *pieces)
+    )(ctx, residual, norm_gain.reshape(1, -1), send, *pieces)
 
 
 def per_device(
@@ -94,8 +99,8 @@
     rank = jnp.cumsum(onehot, axis=0) - onehot
     position = jnp.sum(rank * onehot, axis=1)
     slot_of = (flat_e * capacity + position).reshape(tok_rows, picks)
-    hit = slot_of[:, :, None] == jnp.arange(slots, dtype=jnp.int32)[None, None, :]
-    dispatch = jnp.any(hit, axis=1).astype(jnp.bfloat16)
+    dispatch = jnp.any(slot_of[None, :, :] == jnp.arange(slots, dtype=jnp.int32)[:, None, None], axis=2)
+    dispatch = dispatch.astype(jnp.bfloat16)
     block = attn_out_w.shape[0]
     groups = lax.axis_size("group")
     if groups == 8:
@@ -112,14 +117,13 @@
     pieces, shared_in, shared_out = lax.optimization_barrier((pieces, shared_in, shared_out))
     shared_in = lax.all_gather(shared_in, "group", axis=0, tiled=True)
     shared_out = lax.all_gather(shared_out, "group", axis=1, tiled=True)
-    hidden_f, normed = attn_norm(ctx_perm, pieces, residual, norm_gain)
+    hidden_f, normed, outgoing = attn_norm(ctx_perm, pieces, residual, norm_gain, dispatch)
     logits = jnp.dot(normed, router_w, preferred_element_type=jnp.float32)
     chosen = routes[:, :, None] == jnp.arange(experts, dtype=jnp.int32)[None, None, :]
     picked = jnp.sum(jnp.where(chosen, logits[:, None, :], 0.0), axis=-1)
     sig = jax.nn.sigmoid(picked)
     gates = sig / jnp.sum(sig, axis=1, keepdims=True)
-    outgoing = jnp.dot(dispatch.T, normed, preferred_element_type=jnp.float32)
-    outgoing = outgoing.astype(jnp.bfloat16).reshape(experts, capacity, width)
+    outgoing = outgoing.reshape(experts, capacity, width)
     hit = slot_of[:, :, None] == jnp.arange(slots, dtype=jnp.int32)[None, None, :]
     combine = jnp.sum(jnp.where(hit, gates[:, :, None], 0.0), axis=1)
     combine_hi = combine.astype(jnp.bfloat16)

time: 279 us -> 280 us (level)
  transfers between devices with their start and end apart: 11 -> 11, of which waited for: 5 -> 5; matrix products, arithmetic and copies ran while one was open for 13% -> 13% of each run, Pallas kernels for 2% -> 3%
where the time goes in v17:
time: 280 us
  blocking collectives  106 us (38%)
  waiting for transfers between devices  98.3 us (35%)
  matrix products  29.9 us (11%)
  starting transfers between devices  13.7 us (5%)
  between operations  13.6 us (5%)
  other arithmetic  7.06 us (3%)
  Pallas kernels  7.05 us (3%)
  local copies, waits for them, and re-layouts  4.3 us (2%)
    all_to_all x1, blocking collectives, per_device(): lax.all_to_all(outgoing, 'expert', split_axis=0, concat_axis=0, tiled=True)  106 us
    all_to_all x1, waiting for transfers between devices, per_device(): lax.all_to_all(expert_rows.reshape(arrived.shape), 'expert', split_axis=0...  82.7 us
    ppermute x4, waiting for transfers between devices, shift(): return lax.ppermute(x, 'group', pairs)  12.9 us
    dot_general x1, matrix products, swiglu_rows(): mid = jnp.dot(rows, w_in, preferred_element_type=jnp.float32)  8.74 us
    pallas_call x1, Pallas kernels, attn_norm(): pl.pallas_call(_attn_norm_kernel, out_shape=(jax.ShapeDtypeStruct(shape,...  7.05 us
    all_to_all x1, starting transfers between devices, per_device(): lax.all_to_all(expert_rows.reshape(arrived.shape), 'expert', split_axis=0...  6.67 us
    dot_general x1, matrix products, per_device(): shared_mid = jnp.dot(normed, shared_in, preferred_element_type=jnp.float32)  6.58 us
    ppermute x4, starting transfers between devices, shift(): return lax.ppermute(x, 'group', pairs)  6.33 us
  transfers between devices with their start and end apart: 11, of which 5 were waited for; matrix products, arithmetic and copies ran while one was open for 13% of the time, Pallas kernels for 3%

profile of v17, /device:TPU:32, one launch (start us, length us, event | category | flops | bytes accessed | tf_op | source)
XLA Modules:
  0.0 280.0 jit_solution(7467768017642391670)
XLA Ops:
  6.5 1.6 collective-permute-start
  8.1 1.7 collective-permute-start.1
  9.8 0.8 copy.33
  10.6 0.1 eq.85
  10.7 0.1 eq.81
  10.9 1.7 reduce-window.6
  12.6 0.3 slice_reduce_fusion
  12.9 0.1 fusion.23
  13.0 0.1 reduce_sum.39
  13.2 0.1 copy.36
  13.2 0.7 multiply_add_fusion
  13.9 0.5 fusion.5
  14.4 0.8 convert_element_type.40.send_ref
  15.2 0.7 broadcast_add_fusion
  15.9 0.1 add_multiply_fusion
  16.0 0.1 add_bitcast_fusion.1
  16.1 5.7 %collective-permute-done.1.refs_2_ = bf16[128,2048]{1,0:T(8,128)(2,1)} collective-permute-done((bf16[128,2048]{1,0:T(8,128)(2,1)}, bf16[128,2048]{1,0:T(8,128)(2,1)}, u32[]{:S(2)}, u32[]{:S(2)}) %collective-permute-start.1) | collective-permute-done | bytes 524320 | tf_op jit(solution)/shard_map/ppermute | solution.py:23
  21.8 1.0 slice.41
  22.8 3.0 %collective-permute-start.2 = (bf16[64,2048]{1,0:T(8,128)(2,1)S(1)}, bf16[64,2048]{1,0:T(8,128)(2,1)S(1)}, u32[]{:S(2)}, u32[]{:S(2)}) collective-permute-start(bf16[64,2048]{1,0:T(8,128)(2,1)S(1)} %slice.41), channel_id=1, source_target_pairs={{0,192},{32,224},{64,0},{96,32},{128,64},{160,96},{192,128},{224,1... | collective-permute-start | bytes 786440 | tf_op jit(solution)/shard_map/ppermute | solution.py:23
  25.8 2.5 fusion.10.ctx_ref
  28.3 0.0 collective-permute-done.refs_1_
  28.3 1.0 slice.33
  29.3 0.1 collective-permute-start.3
  29.3 0.1 collective-permute-start.4
  29.4 0.5 collective-permute-start.5
  29.9 0.1 collective-permute-start.6
  30.0 0.2 collective-permute-done.2
  30.3 6.9 %collective-permute-done.3 = bf16[64,2048]{1,0:T(8,128)(2,1)S(1)} collective-permute-done((bf16[64,2048]{1,0:T(8,128)(2,1)S(1)}, bf16[64,2048]{1,0:T(8,128)(2,1)S(1)}, u32[]{:S(2)}, u32[]{:S(2)}) %collective-permute-start.3) | collective-permute-done | bytes 262176 | tf_op jit(solution)/shard_map/ppermute | solution.py:23
  37.2 0.0 copy-start.1
  37.2 0.8 copy-done.1
  38.0 2.0 collective-permute-done.7.refs_7_
  40.0 0.0 all-gather.5.cloned.1.call-update
  40.1 0.0 all-gather.3.cloned.1.call-start
  40.1 0.7 all-gather.3.cloned.1.call-update
  40.8 7.1 %shard_map.109 = (f32[128,2048]{1,0:T(8,128)}, bf16[128,2048]{1,0:T(8,128)(2,1)}, bf16[1024,2048]{1,0:T(8,128)(2,1)}) custom-call(bf16[128,1024]{1,0:T(8,128)(2,1)} %fusion.10.ctx_ref, bf16[128,2048]{1,0:T(8,128)(2,1)} %res_ref.1, f32[1,2048]{1,0:T(1,128)} %bitcast.47, bf16[1024,128]{1,0:T(8,128)(2,1)} %convert_element_type.40.send_ref, ...), custom_call_target="tpu_custom_call" | custom-call | tf_op jit(solution)/shard_map/pallas_call | solution.py:69
  47.9 106.1 %all_to_all.10 = bf16[32,32,2048]{2,1,0:T(8,128)(2,1)S(1)} all-to-all(bf16[32,32,2048]{2,1,0:T(8,128)(2,1)} %bitcast.44), channel_id=1, replica_groups=mesh['group'=8,'expert'=32] {'expert'}, dimensions={0} | all-to-all | bytes 8388608 | tf_op jit(solution)/shard_map/all_to_all | solution.py:133
  154.0 8.7 %fusion = f32[1024,1536]{1,0:T(8,128)S(1)} fusion(bf16[1024,2048]{1,0:T(8,128)(2,1)S(1)} %bitcast.45, bf16[1,2048,1536]{2,1,0:T(8,128)(2,1)} %param.18), kind=kOutput, calls=%fused_computation | convolution fusion | flops 6442450944 | bytes 16777216 | tf_op jit(solution)/shard_map/dot_general | solution.py:10
  162.7 5.1 %convolution_convert_fusion = bf16[1024,2048]{1,0:T(8,128)(2,1)} fusion(bf16[1,768,2048]{2,1,0:T(8,128)(2,1)S(1)} %copy-done, f32[1024,1536]{1,0:T(8,128)S(1)} %fusion), kind=kOutput, calls=%fused_computation.4 | convolution fusion | flops 3228041216 | bytes 13631488 | tf_op jit(solution)/shard_map/dot_general | solution.py:12
  167.8 6.7 %all-to-all-start.1 = ((bf16[32,32,2048]{2,1,0:T(8,128)(2,1)}), bf16[32,32,2048]{2,1,0:T(8,128)(2,1)}, u32[]{:S(2)}, u32[]{:S(2)}) async-start(bf16[32,32,2048]{2,1,0:T(8,128)(2,1)} %bitcast.43), calls=%async_computation.1 | async-start | bytes 8388608 | tf_op jit(solution)/shard_map/all_to_all | solution.py:137
  174.5 1.3 fusion.32
  175.8 0.0 copy-done.5
  175.9 0.4 select_reduce_fusion
  176.3 0.8 subtract_convert_fusion
  177.1 6.6 %fusion.31 = f32[128,2816]{1,0:T(8,128)S(1)} fusion(bf16[128,2048]{1,0:T(8,128)(2,1)} %get-tuple-element.37, bf16[2048,2816]{1,0:T(8,128)(2,1)} %all-gather.3.cloned.1.call-done), kind=kOutput, calls=%fused_computation.57 | convolution fusion | flops 1476395008 | bytes 13500416 | tf_op jit(solution)/shard_map/dot_general | solution.py:150
  183.7 2.0 fusion.18
  185.7 82.7 %all-to-all-done.1 = bf16[32,32,2048]{2,1,0:T(8,128)(2,1)} async-done(((bf16[32,32,2048]{2,1,0:T(8,128)(2,1)}), bf16[32,32,2048]{2,1,0:T(8,128)(2,1)}, u32[]{:S(2)}, u32[]{:S(2)}) %all-to-all-start.1) | async-done | bytes 4194336 | tf_op jit(solution)/shard_map/all_to_all | solution.py:137
  268.4 3.7 %fusion.14 = f32[256,2048]{1,0:T(8,128)S(1)} fusion(bf16[1024,2048]{1,0:T(8,128)(2,1)} %bitcast.9, bf16[128,1024]{1,0:T(8,128)(2,1)S(1)} %get-tuple-element.45, bf16[128,1024]{1,0:T(8,128)(2,1)} %get-tuple-element.46), kind=kOutput, calls=%fused_computation.21 | convolution fusion | flops 1074790400 | bytes 6815744 | tf_op jit(solution)/shard_map/dot_general | solution.py:145
  272.1 1.1 fusion.12
  (29 shorter events, 0.2 us)
Async XLA Ops:
  6.5 156.2 %copy-start = (bf16[1,768,2048]{2,1,0:T(8,128)(2,1)S(1)}, bf16[1,768,2048]{2,1,0:T(8,128)(2,1)}, u32[]{:S(2)}) copy-start(bf16[1,768,2048]{2,1,0:T(8,128)(2,1)} %param.19) | copy-start | bytes 9437188
  6.5 161.3 %all-gather.5.cloned.1.call-start = ((), (), s32[]{:S(2)}) async-start(), calls=%async_computation.3 | async-start | bytes 6488064 | tf_op jit(solution)/shard_map/all_gather | solution.py:119
  6.5 21.7 %collective-permute-start = (bf16[128,2048]{1,0:T(8,128)(2,1)}, bf16[128,2048]{1,0:T(8,128)(2,1)}, u32[]{:S(2)}, u32[]{:S(2)}) collective-permute-start(bf16[128,2048]{1,0:T(8,128)(2,1)} %refs_0_), channel_id=1, source_target_pairs={{0,64},{32,96},{64,128},{96,160},{128,192},{160,224},{192,0},{224,... | collective-permute-start | bytes 1572872 | tf_op jit(solution)/shard_map/ppermute | solution.py:23
  8.1 13.7 %collective-permute-start.1 = (bf16[128,2048]{1,0:T(8,128)(2,1)}, bf16[128,2048]{1,0:T(8,128)(2,1)}, u32[]{:S(2)}, u32[]{:S(2)}) collective-permute-start(bf16[128,2048]{1,0:T(8,128)(2,1)} %refs_0_), channel_id=1, source_target_pairs={{0,192},{32,224},{64,0},{96,32},{128,64},{160,96},{192,128},{224,1... | collective-permute-start | bytes 1572872 | tf_op jit(solution)/shard_map/ppermute | solution.py:23
  22.8 7.4 %collective-permute-start.2 = (bf16[64,2048]{1,0:T(8,128)(2,1)S(1)}, bf16[64,2048]{1,0:T(8,128)(2,1)S(1)}, u32[]{:S(2)}, u32[]{:S(2)}) collective-permute-start(bf16[64,2048]{1,0:T(8,128)(2,1)S(1)} %slice.41), channel_id=1, source_target_pairs={{0,192},{32,224},{64,0},{96,32},{128,64},{160,96},{192,128},{224,1... | collective-permute-start | bytes 786440 | tf_op jit(solution)/shard_map/ppermute | solution.py:23
  29.3 7.9 %collective-permute-start.3 = (bf16[64,2048]{1,0:T(8,128)(2,1)S(1)}, bf16[64,2048]{1,0:T(8,128)(2,1)S(1)}, u32[]{:S(2)}, u32[]{:S(2)}) collective-permute-start(bf16[64,2048]{1,0:T(8,128)(2,1)S(1)} %slice.33), channel_id=1, source_target_pairs={{0,64},{32,96},{64,128},{96,160},{128,192},{160,224},{192,0},{224,... | collective-permute-start | bytes 786440 | tf_op jit(solution)/shard_map/ppermute | solution.py:23
  29.3 8.7 %collective-permute-start.4 = (bf16[128,2048]{1,0:T(8,128)(2,1)}, bf16[128,2048]{1,0:T(8,128)(2,1)}, u32[]{:S(2)}, u32[]{:S(2)}) collective-permute-start(bf16[128,2048]{1,0:T(8,128)(2,1)} %refs_0_), channel_id=1, source_target_pairs={{0,32},{32,0},{64,96},{96,64},{128,160},{160,128},{192,224},{224,1... | collective-permute-start | bytes 1572872 | tf_op jit(solution)/shard_map/ppermute | solution.py:26
  29.4 8.6 %collective-permute-start.5 = (bf16[128,2048]{1,0:T(8,128)(2,1)}, bf16[128,2048]{1,0:T(8,128)(2,1)}, u32[]{:S(2)}, u32[]{:S(2)}) collective-permute-start(bf16[128,2048]{1,0:T(8,128)(2,1)} %collective-permute-done.refs_1_), channel_id=1, source_target_pairs={{0,32},{32,0},{64,96},{96,64},{128,160},{160,128},{192,224},{224,1... | collective-permute-start | bytes 1572872 | tf_op jit(solution)/shard_map/ppermute | solution.py:26
  29.9 8.1 %collective-permute-start.6 = (bf16[128,2048]{1,0:T(8,128)(2,1)}, bf16[128,2048]{1,0:T(8,128)(2,1)}, u32[]{:S(2)}, u32[]{:S(2)}) collective-permute-start(bf16[128,2048]{1,0:T(8,128)(2,1)} %collective-permute-done.1.refs_2_), channel_id=1, source_target_pairs={{0,32},{32,0},{64,96},{96,64},{128,160},{160,128},{192,224},{224,1... | collective-permute-start | bytes 1572872 | tf_op jit(solution)/shard_map/ppermute | solution.py:26
  37.2 0.8 copy-start.1
  38.0 2.0 collective-permute-start.7
  40.1 127.7 %all-gather.3.cloned.1.call-start = ((), (), s32[]{:S(2)}) async-start(), calls=%async_computation.2 | async-start | bytes 12976128 | tf_op jit(solution)/shard_map/all_gather | solution.py:118
  167.8 6.7 %copy-start.4 = (bf16[2048,32]{0,1:T(8,128)(2,1)S(1)}, bf16[2048,32]{0,1:T(8,128)(2,1)}, u32[]{:S(2)}) copy-start(bf16[2048,32]{0,1:T(8,128)(2,1)} %param.15) | copy-start | bytes 393220
  167.8 8.0 %copy-start.5 = (s32[128,6]{0,1:T(8,128)S(1)}, s32[128,6]{0,1:T(8,128)}, u32[]{:S(2)}) copy-start(s32[128,6]{0,1:T(8,128)} %param.20) | copy-start | bytes 9220
  167.8 100.6 %all-to-all-start.1 = ((bf16[32,32,2048]{2,1,0:T(8,128)(2,1)}), bf16[32,32,2048]{2,1,0:T(8,128)(2,1)}, u32[]{:S(2)}, u32[]{:S(2)}) async-start(bf16[32,32,2048]{2,1,0:T(8,128)(2,1)} %bitcast.43), calls=%async_computation.1 | async-start | bytes 8388608 | tf_op jit(solution)/shard_map/all_to_all | solution.py:137
  176.3 7.4 %slice-start = ((s8[5767168]{0:T(1024)(128)(4,1)}), s8[4194304]{0:T(1024)(128)(4,1)S(1)}, s32[]{:S(2)}) async-start(s8[5767168]{0:T(1024)(128)(4,1)} %bitcast.48), calls=%async_computation.4 | async-start | bytes 8388608
  177.1 6.6 %slice-start.1 = ((s8[5767168]{0:T(1024)(128)(4,1)}), s8[1572864]{0:T(1024)(128)(4,1)S(1)}, s32[]{:S(2)}) async-start(s8[5767168]{0:T(1024)(128)(4,1)} %bitcast.48), calls=%async_computation.5 | async-start | bytes 3145728
  268.4 3.7 %copy-start.2 = (f32[128,2048]{1,0:T(8,128)S(1)}, f32[128,2048]{1,0:T(8,128)}, u32[]{:S(2)}) copy-start(f32[128,2048]{1,0:T(8,128)} %get-tuple-element.36) | copy-start | bytes 3145732
  268.4 3.7 %copy-start.3 = (f32[128,2048]{1,0:T(8,128)S(1)}, f32[128,2048]{1,0:T(8,128)}, u32[]{:S(2)}) copy-start(f32[128,2048]{1,0:T(8,128)} %fusion.18) | copy-start | bytes 3145732
Sparse Core Ops, SparseCore 0:
  40.2 45.2 all-gather.4
  87.3 66.4 all-gather.2

commit v18 on v15

--- a/solution.py
+++ b/solution.py
@@ -25,13 +25,13 @@
     def sib(x):
         return lax.ppermute(x, "group", [(i, i ^ 1) for i in range(groups)])
 
-    half = w.shape[0] // 2
     from_left = shift(w, 1)
     from_right = shift(w, -1)
     from_left, passenger = lax.optimization_barrier((from_left, passenger))
-    far = jnp.concatenate(
-        [shift(from_right[:half], -1), shift(from_left[half:], 1)], axis=0
-    )
+    onward = jnp.where(c == 0, from_left, from_right)
+    pairs = [(2 * q, 2 * ((q + 1) % ring)) for q in range(ring)]
+    pairs += [(2 * q + 1, 2 * ((q - 1) % ring) + 1) for q in range(ring)]
+    far = lax.ppermute(onward, "group", pairs)
     pieces = [w, from_left, from_right, far, sib(w), sib(from_left), sib(from_right), sib(far)]
     return pieces, passenger
 

time: 279 us -> 275 us (0.986)
    ppermute x4 -> x2, waiting for transfers between devices: 13.6 us -> 4.05 us  [shift(): return lax.ppermute(x, 'group', pairs)]
    ppermute x0 -> x1, waiting for transfers between devices: none -> 8.3 us  [gather_rows_by_chip(): far = lax.ppermute(onward, 'group', pairs)]
    ppermute x4 -> x2, starting transfers between devices: 6.33 us -> 3.24 us  [shift(): return lax.ppermute(x, 'group', pairs)]
  transfers between devices with their start and end apart: 11 -> 10, of which waited for: 5 -> 4; matrix products, arithmetic and copies ran while one was open for 13% -> 12% of each run, Pallas kernels for 2% -> 2%
where the time goes in v18:
time: 275 us; the launch traced here: 274 us
  blocking collectives  106 us (39%)
  waiting for transfers between devices  97.8 us (36%)
  matrix products  30.2 us (11%)
  between operations  13.6 us (5%)
  starting transfers between devices  12.1 us (4%)
  other arithmetic  7.36 us (3%)
  Pallas kernels  4.83 us (2%)
    all_to_all x1, blocking collectives, per_device(): lax.all_to_all(outgoing, 'expert', split_axis=0, concat_axis=0, tiled=True)  106 us
    all_to_all x1, waiting for transfers between devices, per_device(): lax.all_to_all(expert_rows.reshape(arrived.shape), 'expert', split_axis=0...  82.7 us
    ppermute x1, waiting for transfers between devices, gather_rows_by_chip(): far = lax.ppermute(onward, 'group', pairs)  8.3 us
    all_to_all x1, starting transfers between devices, per_device(): lax.all_to_all(expert_rows.reshape(arrived.shape), 'expert', split_axis=0...  6.66 us
    dot_general x1, matrix products, swiglu_rows(): mid = jnp.dot(rows, w_in, preferred_element_type=jnp.float32)  6.64 us
    dot_general x1, matrix products, per_device(): shared_mid = jnp.dot(normed, shared_in, preferred_element_type=jnp.float32)  6.57 us
  transfers between devices with their start and end apart: 10, of which 4 were waited for; matrix products, arithmetic and copies ran while one was open for 12% of the time, Pallas kernels for 2%

profile of v18, /device:TPU:32, one launch (start us, length us, event | category | flops | bytes accessed | tf_op | source)
XLA Modules:
  0.0 274.3 jit_solution(9383974412678046933)
XLA Ops:
  6.5 1.6 collective-permute-start
  8.1 1.7 collective-permute-start.1
  9.8 0.8 copy.33
  10.6 0.1 eq.89
  10.7 0.1 eq.85
  10.9 0.7 broadcast_add_fusion
  11.6 1.7 reduce-window.6
  13.3 0.3 slice_reduce_fusion
  13.6 0.1 fusion.23
  13.7 0.1 reduce_sum.39
  13.9 0.1 copy.36
  13.9 0.7 multiply_add_fusion
  14.6 0.5 fusion.5
  15.1 0.1 add_multiply_fusion
  15.2 0.1 add_bitcast_fusion.1
  15.3 2.5 fusion.10.ctx_ref
  17.8 4.0 %collective-permute-done.refs_1_ = bf16[128,2048]{1,0:T(8,128)(2,1)} collective-permute-done((bf16[128,2048]{1,0:T(8,128)(2,1)}, bf16[128,2048]{1,0:T(8,128)(2,1)}, u32[]{:S(2)}, u32[]{:S(2)}) %collective-permute-start) | collective-permute-done | bytes 524320 | tf_op jit(solution)/shard_map/ppermute | solution.py:23
  21.8 0.0 collective-permute-done.1.refs_2_
  21.8 1.1 broadcast_select_fusion
  22.9 1.7 collective-permute-start.2
  24.6 0.0 collective-permute-start.3
  24.6 0.5 collective-permute-start.4
  25.1 0.0 collective-permute-start.5
  25.1 8.3 %collective-permute-done.2.refs_3_ = bf16[128,2048]{1,0:T(8,128)(2,1)S(1)} collective-permute-done((bf16[128,2048]{1,0:T(8,128)(2,1)S(1)}, bf16[128,2048]{1,0:T(8,128)(2,1)S(1)}, u32[]{:S(2)}, u32[]{:S(2)}) %collective-permute-start.2) | collective-permute-done | bytes 524320 | tf_op jit(solution)/shard_map/ppermute | solution.py:34
  33.4 0.8 copy-done.3
  34.2 0.0 collective-permute-start.6
  34.2 0.0 collective-permute-done.5.refs_6_
  34.2 2.0 collective-permute-done.6.refs_7_
  36.2 0.0 all-gather.5.cloned.1.call-update
  36.3 0.0 all-gather.3.cloned.1.call-start
  36.3 0.7 all-gather.3.cloned.1.call-update
  37.0 4.8 %shard_map.109 = (f32[128,2048]{1,0:T(8,128)}, bf16[128,2048]{1,0:T(8,128)(2,1)}) custom-call(bf16[128,1024]{1,0:T(8,128)(2,1)} %fusion.10.ctx_ref, bf16[128,2048]{1,0:T(8,128)(2,1)} %res_ref.1, f32[1,2048]{1,0:T(1,128)} %bitcast.49, bf16[128,2048]{1,0:T(8,128)(2,1)} %refs_0_, bf16[128,2048]{1,0:T(8,128)(2,1)} %collective-permute-done.refs_1_, ...), custom_call_target="tpu_custom_call" | custom-call | tf_op jit(solution)/shard_map/pallas_call | solution.py:65
  41.8 2.5 convolution_convert_fusion.1
  44.3 0.0 slice-start.1
  44.3 106.0 %all_to_all.10 = bf16[32,32,2048]{2,1,0:T(8,128)(2,1)S(1)} all-to-all(bf16[32,32,2048]{2,1,0:T(8,128)(2,1)S(1)} %bitcast.45), channel_id=1, replica_groups=mesh['group'=8,'expert'=32] {'expert'}, dimensions={0} | all-to-all | bytes 8388608 | tf_op jit(solution)/shard_map/all_to_all | solution.py:129
  150.3 6.6 %fusion = f32[1024,1536]{1,0:T(8,128)S(1)} fusion(bf16[1024,2048]{1,0:T(8,128)(2,1)S(1)} %bitcast.47, bf16[1,2048,1536]{2,1,0:T(8,128)(2,1)S(1)} %bitcast.51), kind=kOutput, calls=%fused_computation | convolution fusion | flops 6442450944 | bytes 16777216 | tf_op jit(solution)/shard_map/dot_general | solution.py:10
  157.0 5.1 %convolution_convert_fusion = bf16[1024,2048]{1,0:T(8,128)(2,1)} fusion(bf16[1,768,2048]{2,1,0:T(8,128)(2,1)S(1)} %copy-done, f32[1024,1536]{1,0:T(8,128)S(1)} %fusion), kind=kOutput, calls=%fused_computation.4 | convolution fusion | flops 3228041216 | bytes 13631488 | tf_op jit(solution)/shard_map/dot_general | solution.py:12
  162.1 6.7 %all-to-all-start.1 = ((bf16[32,32,2048]{2,1,0:T(8,128)(2,1)}), bf16[32,32,2048]{2,1,0:T(8,128)(2,1)}, u32[]{:S(2)}, u32[]{:S(2)}) async-start(bf16[32,32,2048]{2,1,0:T(8,128)(2,1)} %bitcast.46), calls=%async_computation.1 | async-start | bytes 8388608 | tf_op jit(solution)/shard_map/all_to_all | solution.py:133
  168.8 1.3 fusion.32
  170.1 0.0 copy-done.5
  170.2 0.4 select_reduce_fusion
  170.6 0.0 slice-start.2
  170.7 0.8 subtract_convert_fusion
  171.4 6.6 %fusion.31 = f32[128,2816]{1,0:T(8,128)S(1)} fusion(bf16[128,2048]{1,0:T(8,128)(2,1)} %get-tuple-element.35, bf16[2048,2816]{1,0:T(8,128)(2,1)} %all-gather.3.cloned.1.call-done), kind=kOutput, calls=%fused_computation.57 | convolution fusion | flops 1476395008 | bytes 13500416 | tf_op jit(solution)/shard_map/dot_general | solution.py:146
  178.0 2.0 fusion.18
  180.0 82.7 %all-to-all-done.1 = bf16[32,32,2048]{2,1,0:T(8,128)(2,1)} async-done(((bf16[32,32,2048]{2,1,0:T(8,128)(2,1)}), bf16[32,32,2048]{2,1,0:T(8,128)(2,1)}, u32[]{:S(2)}, u32[]{:S(2)}) %all-to-all-start.1) | async-done | bytes 4194336 | tf_op jit(solution)/shard_map/all_to_all | solution.py:133
  262.8 3.7 %fusion.14 = f32[256,2048]{1,0:T(8,128)S(1)} fusion(bf16[1024,2048]{1,0:T(8,128)(2,1)} %bitcast.9, bf16[128,1024]{1,0:T(8,128)(2,1)S(1)} %get-tuple-element.43, bf16[128,1024]{1,0:T(8,128)(2,1)} %get-tuple-element.44), kind=kOutput, calls=%fused_computation.22 | convolution fusion | flops 1074790400 | bytes 6815744 | tf_op jit(solution)/shard_map/dot_general | solution.py:141
  266.4 1.1 fusion.12
  (30 shorter events, 0.2 us)
Async XLA Ops:
  6.5 150.4 %copy-start = (bf16[1,768,2048]{2,1,0:T(8,128)(2,1)S(1)}, bf16[1,768,2048]{2,1,0:T(8,128)(2,1)}, u32[]{:S(2)}) copy-start(bf16[1,768,2048]{2,1,0:T(8,128)(2,1)} %param.19) | copy-start | bytes 9437188
  6.5 155.6 %all-gather.5.cloned.1.call-start = ((), (), s32[]{:S(2)}) async-start(), calls=%async_computation.3 | async-start | bytes 6488064 | tf_op jit(solution)/shard_map/all_gather | solution.py:114
  6.5 15.3 %collective-permute-start = (bf16[128,2048]{1,0:T(8,128)(2,1)}, bf16[128,2048]{1,0:T(8,128)(2,1)}, u32[]{:S(2)}, u32[]{:S(2)}) collective-permute-start(bf16[128,2048]{1,0:T(8,128)(2,1)} %refs_0_), channel_id=1, source_target_pairs={{0,64},{32,96},{64,128},{96,160},{128,192},{160,224},{192,0},{224,... | collective-permute-start | bytes 1572872 | tf_op jit(solution)/shard_map/ppermute | solution.py:23
  8.1 13.7 %collective-permute-start.1 = (bf16[128,2048]{1,0:T(8,128)(2,1)}, bf16[128,2048]{1,0:T(8,128)(2,1)}, u32[]{:S(2)}, u32[]{:S(2)}) collective-permute-start(bf16[128,2048]{1,0:T(8,128)(2,1)} %refs_0_), channel_id=1, source_target_pairs={{0,192},{32,224},{64,0},{96,32},{128,64},{160,96},{192,128},{224,1... | collective-permute-start | bytes 1572872 | tf_op jit(solution)/shard_map/ppermute | solution.py:23
  22.9 10.5 %collective-permute-start.2 = (bf16[128,2048]{1,0:T(8,128)(2,1)S(1)}, bf16[128,2048]{1,0:T(8,128)(2,1)S(1)}, u32[]{:S(2)}, u32[]{:S(2)}) collective-permute-start(bf16[128,2048]{1,0:T(8,128)(2,1)S(1)} %broadcast_select_fusion), channel_id=1, source_target_pairs={{0,64},{64,128},{128,192},{192,0},{32,224},{96,32},{160,96},{224,1... | collective-permute-start | bytes 1572872 | tf_op jit(solution)/shard_map/ppermute | solution.py:34
  24.6 9.6 %collective-permute-start.3 = (bf16[128,2048]{1,0:T(8,128)(2,1)}, bf16[128,2048]{1,0:T(8,128)(2,1)}, u32[]{:S(2)}, u32[]{:S(2)}) collective-permute-start(bf16[128,2048]{1,0:T(8,128)(2,1)} %refs_0_), channel_id=1, source_target_pairs={{0,32},{32,0},{64,96},{96,64},{128,160},{160,128},{192,224},{224,1... | collective-permute-start | bytes 1572872 | tf_op jit(solution)/shard_map/ppermute | solution.py:26
  24.6 9.6 %collective-permute-start.4 = (bf16[128,2048]{1,0:T(8,128)(2,1)}, bf16[128,2048]{1,0:T(8,128)(2,1)}, u32[]{:S(2)}, u32[]{:S(2)}) collective-permute-start(bf16[128,2048]{1,0:T(8,128)(2,1)} %collective-permute-done.refs_1_), channel_id=1, source_target_pairs={{0,32},{32,0},{64,96},{96,64},{128,160},{160,128},{192,224},{224,1... | collective-permute-start | bytes 1572872 | tf_op jit(solution)/shard_map/ppermute | solution.py:26
  25.1 9.1 %collective-permute-start.5 = (bf16[128,2048]{1,0:T(8,128)(2,1)}, bf16[128,2048]{1,0:T(8,128)(2,1)}, u32[]{:S(2)}, u32[]{:S(2)}) collective-permute-start(bf16[128,2048]{1,0:T(8,128)(2,1)} %collective-permute-done.1.refs_2_), channel_id=1, source_target_pairs={{0,32},{32,0},{64,96},{96,64},{128,160},{160,128},{192,224},{224,1... | collective-permute-start | bytes 1572872 | tf_op jit(solution)/shard_map/ppermute | solution.py:26
  33.4 0.8 copy-start.3
  34.2 2.0 collective-permute-start.6
  36.3 125.9 %all-gather.3.cloned.1.call-start = ((), (), s32[]{:S(2)}) async-start(), calls=%async_computation.2 | async-start | bytes 12976128 | tf_op jit(solution)/shard_map/all_gather | solution.py:113
  41.8 108.5 %slice-start = ((s8[6291456]{0:T(1024)(128)(4,1)}), s8[4194304]{0:T(1024)(128)(4,1)S(1)}, s32[]{:S(2)}) async-start(s8[6291456]{0:T(1024)(128)(4,1)} %bitcast.50), calls=%async_computation.4 | async-start | bytes 8388608
  44.3 106.0 %slice-start.1 = ((s8[6291456]{0:T(1024)(128)(4,1)}), s8[2097152]{0:T(1024)(128)(4,1)S(1)}, s32[]{:S(2)}) async-start(s8[6291456]{0:T(1024)(128)(4,1)} %bitcast.50), calls=%async_computation.5 | async-start | bytes 4194304
  162.1 6.7 %copy-start.4 = (bf16[2048,32]{0,1:T(8,128)(2,1)S(1)}, bf16[2048,32]{0,1:T(8,128)(2,1)}, u32[]{:S(2)}) copy-start(bf16[2048,32]{0,1:T(8,128)(2,1)} %param.15) | copy-start | bytes 393220
  162.1 8.0 %copy-start.5 = (s32[128,6]{0,1:T(8,128)S(1)}, s32[128,6]{0,1:T(8,128)}, u32[]{:S(2)}) copy-start(s32[128,6]{0,1:T(8,128)} %param.20) | copy-start | bytes 9220
  162.1 100.6 %all-to-all-start.1 = ((bf16[32,32,2048]{2,1,0:T(8,128)(2,1)}), bf16[32,32,2048]{2,1,0:T(8,128)(2,1)}, u32[]{:S(2)}, u32[]{:S(2)}) async-start(bf16[32,32,2048]{2,1,0:T(8,128)(2,1)} %bitcast.46), calls=%async_computation.1 | async-start | bytes 8388608 | tf_op jit(solution)/shard_map/all_to_all | solution.py:133
  170.6 7.4 %slice-start.2 = ((s8[5767168]{0:T(1024)(128)(4,1)}), s8[4194304]{0:T(1024)(128)(4,1)S(1)}, s32[]{:S(2)}) async-start(s8[5767168]{0:T(1024)(128)(4,1)} %bitcast.52), calls=%async_computation.6 | async-start | bytes 8388608
  171.4 6.6 %slice-start.3 = ((s8[5767168]{0:T(1024)(128)(4,1)}), s8[1572864]{0:T(1024)(128)(4,1)S(1)}, s32[]{:S(2)}) async-start(s8[5767168]{0:T(1024)(128)(4,1)} %bitcast.52), calls=%async_computation.7 | async-start | bytes 3145728
  262.7 3.7 %copy-start.1 = (f32[128,2048]{1,0:T(8,128)S(1)}, f32[128,2048]{1,0:T(8,128)}, u32[]{:S(2)}) copy-start(f32[128,2048]{1,0:T(8,128)} %get-tuple-element.34) | copy-start | bytes 3145732
  262.8 3.7 %copy-start.2 = (f32[128,2048]{1,0:T(8,128)S(1)}, f32[128,2048]{1,0:T(8,128)}, u32[]{:S(2)}) copy-start(f32[128,2048]{1,0:T(8,128)} %fusion.18) | copy-start | bytes 3145732
Sparse Core Ops, SparseCore 0:
  36.4 46.4 all-gather.4
  84.7 66.4 all-gather.2

commit v19 on v18

--- a/solution.py
+++ b/solution.py
@@ -25,14 +25,16 @@
     def sib(x):
         return lax.ppermute(x, "group", [(i, i ^ 1) for i in range(groups)])
 
-    from_left = shift(w, 1)
-    from_right = shift(w, -1)
-    from_left, passenger = lax.optimization_barrier((from_left, passenger))
-    onward = jnp.where(c == 0, from_left, from_right)
-    pairs = [(2 * q, 2 * ((q + 1) % ring)) for q in range(ring)]
-    pairs += [(2 * q + 1, 2 * ((q - 1) % ring) + 1) for q in range(ring)]
-    far = lax.ppermute(onward, "group", pairs)
-    pieces = [w, from_left, from_right, far, sib(w), sib(from_left), sib(from_right), sib(far)]
+    def mirrored(x, s):
+        pairs = [(2 * q, 2 * ((q + s) % ring)) for q in range(ring)]
+        pairs += [(2 * q + 1, 2 * ((q - s) % ring) + 1) for q in range(ring)]
+        return lax.ppermute(x, "group", pairs)
+
+    near = mirrored(w, 1)
+    other = mirrored(w, -1)
+    near, passenger = lax.optimization_barrier((near, passenger))
+    far = mirrored(near, 1)
+    pieces = [w, near, other, far, sib(w), sib(near), sib(other), sib(far)]
     return pieces, passenger
 
 
@@ -40,8 +42,10 @@
     ring = lax.axis_size("group") // 2
     g = lax.axis_index("group")
     y, c = g // 2, g % 2
-    ys = (y + jnp.array([0, -1, 1, 2], jnp.int32) + ring) % ring
-    return jnp.concatenate([2 * ys + c, 2 * ys + 1 - c])
+    s = 1 - 2 * c
+    mine = (y + jnp.array([0, -1, 1, 2], jnp.int32) * jnp.array([1, s, s, 1], jnp.int32) + ring) % ring
+    theirs = (y + jnp.array([0, 1, -1, 2], jnp.int32) * jnp.array([1, s, s, 1], jnp.int32) + ring) % ring
+    return jnp.concatenate([2 * mine + c, 2 * theirs + 1 - c])
 
 
 def _attn_norm_kernel(ctx_ref, res_ref, gain_ref, *refs):

time: 275 us -> 273 us (level)
  no operation moved by 1% of the time
where the time goes in v19:
time: 273 us
  blocking collectives  106 us (39%)
  waiting for transfers between devices  96.9 us (35%)
  matrix products  30.3 us (11%)
  between operations  13.6 us (5%)
  starting transfers between devices  12.4 us (5%)
  other arithmetic  6.35 us (2%)
  Pallas kernels  4.82 us (2%)
    all_to_all x1, blocking collectives, per_device(): lax.all_to_all(outgoing, 'expert', split_axis=0, concat_axis=0, tiled=True)  106 us
    all_to_all x1, waiting for transfers between devices, per_device(): lax.all_to_all(expert_rows.reshape(arrived.shape), 'expert', split_axis=0...  82.7 us
    ppermute x3, waiting for transfers between devices, mirrored(): return lax.ppermute(x, 'group', pairs)  11.5 us
    all_to_all x1, starting transfers between devices, per_device(): lax.all_to_all(expert_rows.reshape(arrived.shape), 'expert', split_axis=0...  6.65 us
    dot_general x1, matrix products, swiglu_rows(): mid = jnp.dot(rows, w_in, preferred_element_type=jnp.float32)  6.64 us
    dot_general x1, matrix products, per_device(): shared_mid = jnp.dot(normed, shared_in, preferred_element_type=jnp.float32)  6.57 us
  transfers between devices with their start and end apart: 10, of which 4 were waited for; matrix products, arithmetic and copies ran while one was open for 12% of the time, Pallas kernels for 2%

profile of v19, /device:TPU:32, one launch (start us, length us, event | category | flops | bytes accessed | tf_op | source)
XLA Modules:
  0.0 272.7 jit_solution(103634287649543980)
XLA Ops:
  6.5 1.6 collective-permute-start
  8.1 1.7 collective-permute-start.1
  9.8 0.8 copy.34
  10.6 0.1 eq.86
  10.7 0.1 eq.82
  10.9 1.7 reduce-window.6
  12.6 0.3 slice_reduce_fusion
  12.9 0.1 fusion.23
  13.0 0.1 reduce_sum.39
  13.2 0.1 copy.37
  13.2 0.7 multiply_add_fusion
  13.9 0.5 fusion.5
  14.5 0.8 fusion.26
  15.2 0.1 add_multiply_fusion
  15.3 0.1 add_bitcast_fusion.1
  15.4 2.5 fusion.10.ctx_ref
  17.9 3.3 %collective-permute-done.refs_1_ = bf16[128,2048]{1,0:T(8,128)(2,1)} collective-permute-done((bf16[128,2048]{1,0:T(8,128)(2,1)}, bf16[128,2048]{1,0:T(8,128)(2,1)}, u32[]{:S(2)}, u32[]{:S(2)}) %collective-permute-start) | collective-permute-done | bytes 524320 | tf_op jit(solution)/shard_map/ppermute | solution.py:31
  21.2 1.7 collective-permute-start.2
  22.9 0.3 collective-permute-start.3
  23.2 0.2 collective-permute-start.4
  23.4 0.0 collective-permute-done.1.refs_2_
  23.4 0.3 collective-permute-start.5
  23.7 8.1 %collective-permute-done.2.refs_3_ = bf16[128,2048]{1,0:T(8,128)(2,1)S(1)} collective-permute-done((bf16[128,2048]{1,0:T(8,128)(2,1)}, bf16[128,2048]{1,0:T(8,128)(2,1)S(1)}, u32[]{:S(2)}, u32[]{:S(2)}) %collective-permute-start.2) | collective-permute-done | bytes 524320 | tf_op jit(solution)/shard_map/ppermute | solution.py:31
  31.8 0.8 copy-done.3
  32.6 0.0 collective-permute-start.6
  32.6 0.0 collective-permute-done.3.refs_4_
  32.6 0.0 collective-permute-done.4.refs_5_
  32.6 0.0 collective-permute-done.5.refs_6_
  32.6 2.0 collective-permute-done.6.refs_7_
  34.6 0.0 all-gather.5.cloned.1.call-update
  34.7 0.0 all-gather.3.cloned.1.call-start
  34.7 0.7 all-gather.3.cloned.1.call-update
  35.4 4.8 %shard_map.118 = (f32[128,2048]{1,0:T(8,128)}, bf16[128,2048]{1,0:T(8,128)(2,1)}) custom-call(bf16[128,1024]{1,0:T(8,128)(2,1)} %fusion.10.ctx_ref, bf16[128,2048]{1,0:T(8,128)(2,1)} %res_ref.1, f32[1,2048]{1,0:T(1,128)} %bitcast.50, bf16[128,2048]{1,0:T(8,128)(2,1)} %refs_0_, bf16[128,2048]{1,0:T(8,128)(2,1)} %collective-permute-done.refs_1_, ...), custom_call_target="tpu_custom_call" | custom-call | tf_op jit(solution)/shard_map/pallas_call | solution.py:69
  40.2 2.5 convolution_convert_fusion.1
  42.7 0.0 slice-start.1
  42.7 106.0 %all_to_all.10 = bf16[32,32,2048]{2,1,0:T(8,128)(2,1)S(1)} all-to-all(bf16[32,32,2048]{2,1,0:T(8,128)(2,1)S(1)} %bitcast.46), channel_id=1, replica_groups=mesh['group'=8,'expert'=32] {'expert'}, dimensions={0} | all-to-all | bytes 8388608 | tf_op jit(solution)/shard_map/all_to_all | solution.py:133
  148.7 6.6 %fusion = f32[1024,1536]{1,0:T(8,128)S(1)} fusion(bf16[1024,2048]{1,0:T(8,128)(2,1)S(1)} %bitcast.48, bf16[1,2048,1536]{2,1,0:T(8,128)(2,1)S(1)} %bitcast.52), kind=kOutput, calls=%fused_computation | convolution fusion | flops 6442450944 | bytes 16777216 | tf_op jit(solution)/shard_map/dot_general | solution.py:10
  155.4 5.1 %convolution_convert_fusion = bf16[1024,2048]{1,0:T(8,128)(2,1)} fusion(bf16[1,768,2048]{2,1,0:T(8,128)(2,1)S(1)} %copy-done, f32[1024,1536]{1,0:T(8,128)S(1)} %fusion), kind=kOutput, calls=%fused_computation.4 | convolution fusion | flops 3228041216 | bytes 13631488 | tf_op jit(solution)/shard_map/dot_general | solution.py:12
  160.5 6.6 %all-to-all-start.1 = ((bf16[32,32,2048]{2,1,0:T(8,128)(2,1)}), bf16[32,32,2048]{2,1,0:T(8,128)(2,1)}, u32[]{:S(2)}, u32[]{:S(2)}) async-start(bf16[32,32,2048]{2,1,0:T(8,128)(2,1)} %bitcast.47), calls=%async_computation.1 | async-start | bytes 8388608 | tf_op jit(solution)/shard_map/all_to_all | solution.py:137
  167.2 1.3 fusion.36
  168.5 0.0 copy-done.5
  168.6 0.4 select_reduce_fusion
  169.1 0.8 subtract_convert_fusion
  169.8 6.6 %fusion.35 = f32[128,2816]{1,0:T(8,128)S(1)} fusion(bf16[128,2048]{1,0:T(8,128)(2,1)} %get-tuple-element.35, bf16[2048,2816]{1,0:T(8,128)(2,1)} %all-gather.3.cloned.1.call-done), kind=kOutput, calls=%fused_computation.63 | convolution fusion | flops 1476395008 | bytes 13500416 | tf_op jit(solution)/shard_map/dot_general | solution.py:150
  176.4 2.0 fusion.18
  178.4 82.7 %all-to-all-done.1 = bf16[32,32,2048]{2,1,0:T(8,128)(2,1)} async-done(((bf16[32,32,2048]{2,1,0:T(8,128)(2,1)}), bf16[32,32,2048]{2,1,0:T(8,128)(2,1)}, u32[]{:S(2)}, u32[]{:S(2)}) %all-to-all-start.1) | async-done | bytes 4194336 | tf_op jit(solution)/shard_map/all_to_all | solution.py:137
  261.1 3.7 %fusion.14 = f32[256,2048]{1,0:T(8,128)S(1)} fusion(bf16[1024,2048]{1,0:T(8,128)(2,1)} %bitcast.10, bf16[128,1024]{1,0:T(8,128)(2,1)S(1)} %get-tuple-element.43, bf16[128,1024]{1,0:T(8,128)(2,1)} %get-tuple-element.44), kind=kOutput, calls=%fused_computation.22 | convolution fusion | flops 1074790400 | bytes 6815744 | tf_op jit(solution)/shard_map/dot_general | solution.py:145
  264.8 1.1 fusion.12
  (28 shorter events, 0.1 us)
Async XLA Ops:
  6.5 148.8 %copy-start = (bf16[1,768,2048]{2,1,0:T(8,128)(2,1)S(1)}, bf16[1,768,2048]{2,1,0:T(8,128)(2,1)}, u32[]{:S(2)}) copy-start(bf16[1,768,2048]{2,1,0:T(8,128)(2,1)} %param.20) | copy-start | bytes 9437188
  6.5 154.0 %all-gather.5.cloned.1.call-start = ((), (), s32[]{:S(2)}) async-start(), calls=%async_computation.3 | async-start | bytes 6488064 | tf_op jit(solution)/shard_map/all_gather | solution.py:118
  6.5 14.7 %collective-permute-start = (bf16[128,2048]{1,0:T(8,128)(2,1)}, bf16[128,2048]{1,0:T(8,128)(2,1)}, u32[]{:S(2)}, u32[]{:S(2)}) collective-permute-start(bf16[128,2048]{1,0:T(8,128)(2,1)} %refs_0_), channel_id=1, source_target_pairs={{0,64},{64,128},{128,192},{192,0},{32,224},{96,32},{160,96},{224,1... | collective-permute-start | bytes 1572872 | tf_op jit(solution)/shard_map/ppermute | solution.py:31
  8.1 15.3 %collective-permute-start.1 = (bf16[128,2048]{1,0:T(8,128)(2,1)}, bf16[128,2048]{1,0:T(8,128)(2,1)}, u32[]{:S(2)}, u32[]{:S(2)}) collective-permute-start(bf16[128,2048]{1,0:T(8,128)(2,1)} %refs_0_), channel_id=1, source_target_pairs={{0,192},{64,0},{128,64},{192,128},{32,96},{96,160},{160,224},{224,... | collective-permute-start | bytes 1572872 | tf_op jit(solution)/shard_map/ppermute | solution.py:31
  21.2 10.6 %collective-permute-start.2 = (bf16[128,2048]{1,0:T(8,128)(2,1)}, bf16[128,2048]{1,0:T(8,128)(2,1)S(1)}, u32[]{:S(2)}, u32[]{:S(2)}) collective-permute-start(bf16[128,2048]{1,0:T(8,128)(2,1)} %collective-permute-done.refs_1_), channel_id=1, source_target_pairs={{0,64},{64,128},{128,192},{192,0},{32,224},{96,32},{160,96},{224,1... | collective-permute-start | bytes 1572872 | tf_op jit(solution)/shard_map/ppermute | solution.py:31
  22.9 9.7 %collective-permute-start.3 = (bf16[128,2048]{1,0:T(8,128)(2,1)}, bf16[128,2048]{1,0:T(8,128)(2,1)}, u32[]{:S(2)}, u32[]{:S(2)}) collective-permute-start(bf16[128,2048]{1,0:T(8,128)(2,1)} %refs_0_), channel_id=1, source_target_pairs={{0,32},{32,0},{64,96},{96,64},{128,160},{160,128},{192,224},{224,1... | collective-permute-start | bytes 1572872 | tf_op jit(solution)/shard_map/ppermute | solution.py:26
  23.2 9.4 %collective-permute-start.4 = (bf16[128,2048]{1,0:T(8,128)(2,1)}, bf16[128,2048]{1,0:T(8,128)(2,1)}, u32[]{:S(2)}, u32[]{:S(2)}) collective-permute-start(bf16[128,2048]{1,0:T(8,128)(2,1)} %collective-permute-done.refs_1_), channel_id=1, source_target_pairs={{0,32},{32,0},{64,96},{96,64},{128,160},{160,128},{192,224},{224,1... | collective-permute-start | bytes 1572872 | tf_op jit(solution)/shard_map/ppermute | solution.py:26
  23.4 9.2 %collective-permute-start.5 = (bf16[128,2048]{1,0:T(8,128)(2,1)}, bf16[128,2048]{1,0:T(8,128)(2,1)}, u32[]{:S(2)}, u32[]{:S(2)}) collective-permute-start(bf16[128,2048]{1,0:T(8,128)(2,1)} %collective-permute-done.1.refs_2_), channel_id=1, source_target_pairs={{0,32},{32,0},{64,96},{96,64},{128,160},{160,128},{192,224},{224,1... | collective-permute-start | bytes 1572872 | tf_op jit(solution)/shard_map/ppermute | solution.py:26
  31.8 0.8 copy-start.3
  32.6 2.0 collective-permute-start.6
  34.7 125.9 %all-gather.3.cloned.1.call-start = ((), (), s32[]{:S(2)}) async-start(), calls=%async_computation.2 | async-start | bytes 12976128 | tf_op jit(solution)/shard_map/all_gather | solution.py:117
  40.2 108.5 %slice-start = ((s8[6291456]{0:T(1024)(128)(4,1)}), s8[4194304]{0:T(1024)(128)(4,1)S(1)}, s32[]{:S(2)}) async-start(s8[6291456]{0:T(1024)(128)(4,1)} %bitcast.51), calls=%async_computation.4 | async-start | bytes 8388608
  42.7 106.0 %slice-start.1 = ((s8[6291456]{0:T(1024)(128)(4,1)}), s8[2097152]{0:T(1024)(128)(4,1)S(1)}, s32[]{:S(2)}) async-start(s8[6291456]{0:T(1024)(128)(4,1)} %bitcast.51), calls=%async_computation.5 | async-start | bytes 4194304
  160.5 6.7 %copy-start.4 = (bf16[2048,32]{0,1:T(8,128)(2,1)S(1)}, bf16[2048,32]{0,1:T(8,128)(2,1)}, u32[]{:S(2)}) copy-start(bf16[2048,32]{0,1:T(8,128)(2,1)} %param.16) | copy-start | bytes 393220
  160.5 8.0 %copy-start.5 = (s32[128,6]{0,1:T(8,128)S(1)}, s32[128,6]{0,1:T(8,128)}, u32[]{:S(2)}) copy-start(s32[128,6]{0,1:T(8,128)} %param.21) | copy-start | bytes 9220
  160.5 100.6 %all-to-all-start.1 = ((bf16[32,32,2048]{2,1,0:T(8,128)(2,1)}), bf16[32,32,2048]{2,1,0:T(8,128)(2,1)}, u32[]{:S(2)}, u32[]{:S(2)}) async-start(bf16[32,32,2048]{2,1,0:T(8,128)(2,1)} %bitcast.47), calls=%async_computation.1 | async-start | bytes 8388608 | tf_op jit(solution)/shard_map/all_to_all | solution.py:137
  169.0 7.4 %slice-start.2 = ((s8[5767168]{0:T(1024)(128)(4,1)}), s8[4194304]{0:T(1024)(128)(4,1)S(1)}, s32[]{:S(2)}) async-start(s8[5767168]{0:T(1024)(128)(4,1)} %bitcast.53), calls=%async_computation.6 | async-start | bytes 8388608
  169.8 6.6 %slice-start.3 = ((s8[5767168]{0:T(1024)(128)(4,1)}), s8[1572864]{0:T(1024)(128)(4,1)S(1)}, s32[]{:S(2)}) async-start(s8[5767168]{0:T(1024)(128)(4,1)} %bitcast.53), calls=%async_computation.7 | async-start | bytes 3145728
  261.1 3.7 %copy-start.1 = (f32[128,2048]{1,0:T(8,128)S(1)}, f32[128,2048]{1,0:T(8,128)}, u32[]{:S(2)}) copy-start(f32[128,2048]{1,0:T(8,128)} %get-tuple-element.34) | copy-start | bytes 3145732
  261.1 3.7 %copy-start.2 = (f32[128,2048]{1,0:T(8,128)S(1)}, f32[128,2048]{1,0:T(8,128)}, u32[]{:S(2)}) copy-start(f32[128,2048]{1,0:T(8,128)} %fusion.18) | copy-start | bytes 3145732
Sparse Core Ops, SparseCore 0:
  34.8 46.2 all-gather.4
  83.0 66.4 all-gather.2

commit v20 on v19

--- a/solution.py
+++ b/solution.py
@@ -98,8 +98,8 @@
     rank = jnp.cumsum(onehot, axis=0) - onehot
     position = jnp.sum(rank * onehot, axis=1)
     slot_of = (flat_e * capacity + position).reshape(tok_rows, picks)
-    hit = slot_of[:, :, None] == jnp.arange(slots, dtype=jnp.int32)[None, None, :]
-    dispatch = jnp.any(hit, axis=1).astype(jnp.bfloat16)
+    dispatch = jnp.any(slot_of[None, :, :] == jnp.arange(slots, dtype=jnp.int32)[:, None, None], axis=2)
+    dispatch = dispatch.astype(jnp.bfloat16)
     block = attn_out_w.shape[0]
     groups = lax.axis_size("group")
     if groups == 8:
@@ -122,7 +122,7 @@
     picked = jnp.sum(jnp.where(chosen, logits[:, None, :], 0.0), axis=-1)
     sig = jax.nn.sigmoid(picked)
     gates = sig / jnp.sum(sig, axis=1, keepdims=True)
-    outgoing = jnp.dot(dispatch.T, normed, preferred_element_type=jnp.float32)
+    outgoing = jnp.dot(dispatch, normed, preferred_element_type=jnp.float32)
     outgoing = outgoing.astype(jnp.bfloat16).reshape(experts, capacity, width)
     hit = slot_of[:, :, None] == jnp.arange(slots, dtype=jnp.int32)[None, None, :]
     combine = jnp.sum(jnp.where(hit, gates[:, :, None], 0.0), axis=1)

time: 273 us -> 273 us (level)
  no operation moved by 1% of the time
where the time goes in v20:
time: 273 us
  blocking collectives  106 us (39%)
  waiting for transfers between devices  96.8 us (35%)
  matrix products  30.2 us (11%)
  between operations  13.6 us (5%)
  starting transfers between devices  12.4 us (5%)
  other arithmetic  6.4 us (2%)
  Pallas kernels  4.82 us (2%)
    all_to_all x1, blocking collectives, per_device(): lax.all_to_all(outgoing, 'expert', split_axis=0, concat_axis=0, tiled=True)  106 us
    all_to_all x1, waiting for transfers between devices, per_device(): lax.all_to_all(expert_rows.reshape(arrived.shape), 'expert', split_axis=0...  82.7 us
    ppermute x3, waiting for transfers between devices, mirrored(): return lax.ppermute(x, 'group', pairs)  11.4 us
    all_to_all x1, starting transfers between devices, per_device(): lax.all_to_all(expert_rows.reshape(arrived.shape), 'expert', split_axis=0...  6.68 us
    dot_general x1, matrix products, swiglu_rows(): mid = jnp.dot(rows, w_in, preferred_element_type=jnp.float32)  6.64 us
    dot_general x1, matrix products, per_device(): shared_mid = jnp.dot(normed, shared_in, preferred_element_type=jnp.float32)  6.57 us
  transfers between devices with their start and end apart: 10, of which 4 were waited for; matrix products, arithmetic and copies ran while one was open for 12% of the time, Pallas kernels for 2%

profile of v20, /device:TPU:32, one launch (start us, length us, event | category | flops | bytes accessed | tf_op | source)
XLA Modules:
  0.0 272.7 jit_solution(10244825326952972314)
XLA Ops:
  6.5 1.6 collective-permute-start
  8.1 1.7 collective-permute-start.1
  9.8 0.8 copy.34
  10.6 0.1 eq.86
  10.7 0.1 eq.82
  10.9 1.7 reduce-window.6
  12.6 0.3 slice_reduce_fusion
  12.9 0.1 fusion.23
  13.0 0.1 reduce_sum.39
  13.2 0.1 copy.37
  13.2 0.7 multiply_add_fusion
  13.9 0.5 fusion.5
  14.4 0.1 convert_element_type.43
  14.5 0.8 fusion.26
  15.3 0.1 add_multiply_fusion
  15.4 0.1 add_bitcast_fusion.1
  15.4 2.5 fusion.10.ctx_ref
  17.9 3.3 %collective-permute-done.refs_1_ = bf16[128,2048]{1,0:T(8,128)(2,1)} collective-permute-done((bf16[128,2048]{1,0:T(8,128)(2,1)}, bf16[128,2048]{1,0:T(8,128)(2,1)}, u32[]{:S(2)}, u32[]{:S(2)}) %collective-permute-start) | collective-permute-done | bytes 524320 | tf_op jit(solution)/shard_map/ppermute | solution.py:31
  21.2 1.7 collective-permute-start.2
  22.9 0.3 collective-permute-start.3
  23.2 0.2 collective-permute-start.4
  23.4 0.0 collective-permute-done.1.refs_2_
  23.4 0.3 collective-permute-start.5
  23.7 8.1 %collective-permute-done.2.refs_3_ = bf16[128,2048]{1,0:T(8,128)(2,1)S(1)} collective-permute-done((bf16[128,2048]{1,0:T(8,128)(2,1)}, bf16[128,2048]{1,0:T(8,128)(2,1)S(1)}, u32[]{:S(2)}, u32[]{:S(2)}) %collective-permute-start.2) | collective-permute-done | bytes 524320 | tf_op jit(solution)/shard_map/ppermute | solution.py:31
  31.8 0.8 copy-done.3
  32.6 0.0 collective-permute-start.6
  32.6 0.0 collective-permute-done.3.refs_4_
  32.6 0.0 collective-permute-done.4.refs_5_
  32.6 2.0 collective-permute-done.6.refs_7_
  34.6 0.0 all-gather.5.cloned.1.call-update
  34.7 0.0 all-gather.3.cloned.1.call-start
  34.7 0.7 all-gather.3.cloned.1.call-update
  35.4 4.8 %shard_map.118 = (f32[128,2048]{1,0:T(8,128)}, bf16[128,2048]{1,0:T(8,128)(2,1)}) custom-call(bf16[128,1024]{1,0:T(8,128)(2,1)} %fusion.10.ctx_ref, bf16[128,2048]{1,0:T(8,128)(2,1)} %res_ref.1, f32[1,2048]{1,0:T(1,128)} %bitcast.50, bf16[128,2048]{1,0:T(8,128)(2,1)} %refs_0_, bf16[128,2048]{1,0:T(8,128)(2,1)} %collective-permute-done.refs_1_, ...), custom_call_target="tpu_custom_call" | custom-call | tf_op jit(solution)/shard_map/pallas_call | solution.py:69
  40.2 2.4 convolution_convert_fusion.1
  42.7 0.0 slice-start.1
  42.7 106.0 %all_to_all.10 = bf16[32,32,2048]{2,1,0:T(8,128)(2,1)S(1)} all-to-all(bf16[32,32,2048]{2,1,0:T(8,128)(2,1)S(1)} %bitcast.46), channel_id=1, replica_groups=mesh['group'=8,'expert'=32] {'expert'}, dimensions={0} | all-to-all | bytes 8388608 | tf_op jit(solution)/shard_map/all_to_all | solution.py:133
  148.7 6.6 %fusion = f32[1024,1536]{1,0:T(8,128)S(1)} fusion(bf16[1024,2048]{1,0:T(8,128)(2,1)S(1)} %bitcast.48, bf16[1,2048,1536]{2,1,0:T(8,128)(2,1)S(1)} %bitcast.52), kind=kOutput, calls=%fused_computation | convolution fusion | flops 6442450944 | bytes 16777216 | tf_op jit(solution)/shard_map/dot_general | solution.py:10
  155.4 5.1 %convolution_convert_fusion = bf16[1024,2048]{1,0:T(8,128)(2,1)} fusion(bf16[1,768,2048]{2,1,0:T(8,128)(2,1)S(1)} %copy-done, f32[1024,1536]{1,0:T(8,128)S(1)} %fusion), kind=kOutput, calls=%fused_computation.4 | convolution fusion | flops 3228041216 | bytes 13631488 | tf_op jit(solution)/shard_map/dot_general | solution.py:12
  160.5 6.7 %all-to-all-start.1 = ((bf16[32,32,2048]{2,1,0:T(8,128)(2,1)}), bf16[32,32,2048]{2,1,0:T(8,128)(2,1)}, u32[]{:S(2)}, u32[]{:S(2)}) async-start(bf16[32,32,2048]{2,1,0:T(8,128)(2,1)} %bitcast.47), calls=%async_computation.1 | async-start | bytes 8388608 | tf_op jit(solution)/shard_map/all_to_all | solution.py:137
  167.2 1.3 fusion.36
  168.5 0.0 copy-done.5
  168.6 0.4 select_reduce_fusion
  169.0 0.8 subtract_convert_fusion
  169.8 6.6 %fusion.35 = f32[128,2816]{1,0:T(8,128)S(1)} fusion(bf16[128,2048]{1,0:T(8,128)(2,1)} %get-tuple-element.35, bf16[2048,2816]{1,0:T(8,128)(2,1)} %all-gather.3.cloned.1.call-done), kind=kOutput, calls=%fused_computation.63 | convolution fusion | flops 1476395008 | bytes 13500416 | tf_op jit(solution)/shard_map/dot_general | solution.py:150
  176.4 2.0 fusion.18
  178.4 82.7 %all-to-all-done.1 = bf16[32,32,2048]{2,1,0:T(8,128)(2,1)} async-done(((bf16[32,32,2048]{2,1,0:T(8,128)(2,1)}), bf16[32,32,2048]{2,1,0:T(8,128)(2,1)}, u32[]{:S(2)}, u32[]{:S(2)}) %all-to-all-start.1) | async-done | bytes 4194336 | tf_op jit(solution)/shard_map/all_to_all | solution.py:137
  261.1 3.7 %fusion.14 = f32[256,2048]{1,0:T(8,128)S(1)} fusion(bf16[1024,2048]{1,0:T(8,128)(2,1)} %bitcast.10, bf16[128,1024]{1,0:T(8,128)(2,1)S(1)} %get-tuple-element.43, bf16[128,1024]{1,0:T(8,128)(2,1)} %get-tuple-element.44), kind=kOutput, calls=%fused_computation.22 | convolution fusion | flops 1074790400 | bytes 6815744 | tf_op jit(solution)/shard_map/dot_general | solution.py:145
  264.8 1.1 fusion.12
  (28 shorter events, 0.1 us)
Async XLA Ops:
  6.5 148.8 %copy-start = (bf16[1,768,2048]{2,1,0:T(8,128)(2,1)S(1)}, bf16[1,768,2048]{2,1,0:T(8,128)(2,1)}, u32[]{:S(2)}) copy-start(bf16[1,768,2048]{2,1,0:T(8,128)(2,1)} %param.20) | copy-start | bytes 9437188
  6.5 154.0 %all-gather.5.cloned.1.call-start = ((), (), s32[]{:S(2)}) async-start(), calls=%async_computation.3 | async-start | bytes 6488064 | tf_op jit(solution)/shard_map/all_gather | solution.py:118
  6.5 14.7 %collective-permute-start = (bf16[128,2048]{1,0:T(8,128)(2,1)}, bf16[128,2048]{1,0:T(8,128)(2,1)}, u32[]{:S(2)}, u32[]{:S(2)}) collective-permute-start(bf16[128,2048]{1,0:T(8,128)(2,1)} %refs_0_), channel_id=1, source_target_pairs={{0,64},{64,128},{128,192},{192,0},{32,224},{96,32},{160,96},{224,1... | collective-permute-start | bytes 1572872 | tf_op jit(solution)/shard_map/ppermute | solution.py:31
  8.1 15.3 %collective-permute-start.1 = (bf16[128,2048]{1,0:T(8,128)(2,1)}, bf16[128,2048]{1,0:T(8,128)(2,1)}, u32[]{:S(2)}, u32[]{:S(2)}) collective-permute-start(bf16[128,2048]{1,0:T(8,128)(2,1)} %refs_0_), channel_id=1, source_target_pairs={{0,192},{64,0},{128,64},{192,128},{32,96},{96,160},{160,224},{224,... | collective-permute-start | bytes 1572872 | tf_op jit(solution)/shard_map/ppermute | solution.py:31
  21.2 10.6 %collective-permute-start.2 = (bf16[128,2048]{1,0:T(8,128)(2,1)}, bf16[128,2048]{1,0:T(8,128)(2,1)S(1)}, u32[]{:S(2)}, u32[]{:S(2)}) collective-permute-start(bf16[128,2048]{1,0:T(8,128)(2,1)} %collective-permute-done.refs_1_), channel_id=1, source_target_pairs={{0,64},{64,128},{128,192},{192,0},{32,224},{96,32},{160,96},{224,1... | collective-permute-start | bytes 1572872 | tf_op jit(solution)/shard_map/ppermute | solution.py:31
  22.9 9.7 %collective-permute-start.3 = (bf16[128,2048]{1,0:T(8,128)(2,1)}, bf16[128,2048]{1,0:T(8,128)(2,1)}, u32[]{:S(2)}, u32[]{:S(2)}) collective-permute-start(bf16[128,2048]{1,0:T(8,128)(2,1)} %refs_0_), channel_id=1, source_target_pairs={{0,32},{32,0},{64,96},{96,64},{128,160},{160,128},{192,224},{224,1... | collective-permute-start | bytes 1572872 | tf_op jit(solution)/shard_map/ppermute | solution.py:26
  23.2 9.4 %collective-permute-start.4 = (bf16[128,2048]{1,0:T(8,128)(2,1)}, bf16[128,2048]{1,0:T(8,128)(2,1)}, u32[]{:S(2)}, u32[]{:S(2)}) collective-permute-start(bf16[128,2048]{1,0:T(8,128)(2,1)} %collective-permute-done.refs_1_), channel_id=1, source_target_pairs={{0,32},{32,0},{64,96},{96,64},{128,160},{160,128},{192,224},{224,1... | collective-permute-start | bytes 1572872 | tf_op jit(solution)/shard_map/ppermute | solution.py:26
  23.4 9.2 %collective-permute-start.5 = (bf16[128,2048]{1,0:T(8,128)(2,1)}, bf16[128,2048]{1,0:T(8,128)(2,1)}, u32[]{:S(2)}, u32[]{:S(2)}) collective-permute-start(bf16[128,2048]{1,0:T(8,128)(2,1)} %collective-permute-done.1.refs_2_), channel_id=1, source_target_pairs={{0,32},{32,0},{64,96},{96,64},{128,160},{160,128},{192,224},{224,1... | collective-permute-start | bytes 1572872 | tf_op jit(solution)/shard_map/ppermute | solution.py:26
  31.8 0.8 copy-start.3
  32.6 2.0 collective-permute-start.6
  34.7 125.8 %all-gather.3.cloned.1.call-start = ((), (), s32[]{:S(2)}) async-start(), calls=%async_computation.2 | async-start | bytes 12976128 | tf_op jit(solution)/shard_map/all_gather | solution.py:117
  40.2 108.5 %slice-start = ((s8[6291456]{0:T(1024)(128)(4,1)}), s8[4194304]{0:T(1024)(128)(4,1)S(1)}, s32[]{:S(2)}) async-start(s8[6291456]{0:T(1024)(128)(4,1)} %bitcast.51), calls=%async_computation.4 | async-start | bytes 8388608
  42.7 106.0 %slice-start.1 = ((s8[6291456]{0:T(1024)(128)(4,1)}), s8[2097152]{0:T(1024)(128)(4,1)S(1)}, s32[]{:S(2)}) async-start(s8[6291456]{0:T(1024)(128)(4,1)} %bitcast.51), calls=%async_computation.5 | async-start | bytes 4194304
  160.5 6.7 %copy-start.4 = (bf16[2048,32]{0,1:T(8,128)(2,1)S(1)}, bf16[2048,32]{0,1:T(8,128)(2,1)}, u32[]{:S(2)}) copy-start(bf16[2048,32]{0,1:T(8,128)(2,1)} %param.16) | copy-start | bytes 393220
  160.5 8.0 %copy-start.5 = (s32[128,6]{0,1:T(8,128)S(1)}, s32[128,6]{0,1:T(8,128)}, u32[]{:S(2)}) copy-start(s32[128,6]{0,1:T(8,128)} %param.21) | copy-start | bytes 9220
  160.5 100.6 %all-to-all-start.1 = ((bf16[32,32,2048]{2,1,0:T(8,128)(2,1)}), bf16[32,32,2048]{2,1,0:T(8,128)(2,1)}, u32[]{:S(2)}, u32[]{:S(2)}) async-start(bf16[32,32,2048]{2,1,0:T(8,128)(2,1)} %bitcast.47), calls=%async_computation.1 | async-start | bytes 8388608 | tf_op jit(solution)/shard_map/all_to_all | solution.py:137
  169.0 7.4 %slice-start.2 = ((s8[5767168]{0:T(1024)(128)(4,1)}), s8[4194304]{0:T(1024)(128)(4,1)S(1)}, s32[]{:S(2)}) async-start(s8[5767168]{0:T(1024)(128)(4,1)} %bitcast.53), calls=%async_computation.6 | async-start | bytes 8388608
  169.8 6.6 %slice-start.3 = ((s8[5767168]{0:T(1024)(128)(4,1)}), s8[1572864]{0:T(1024)(128)(4,1)S(1)}, s32[]{:S(2)}) async-start(s8[5767168]{0:T(1024)(128)(4,1)} %bitcast.53), calls=%async_computation.7 | async-start | bytes 3145728
  261.1 3.7 %copy-start.1 = (f32[128,2048]{1,0:T(8,128)S(1)}, f32[128,2048]{1,0:T(8,128)}, u32[]{:S(2)}) copy-start(f32[128,2048]{1,0:T(8,128)} %get-tuple-element.34) | copy-start | bytes 3145732
  261.1 3.7 %copy-start.2 = (f32[128,2048]{1,0:T(8,128)S(1)}, f32[128,2048]{1,0:T(8,128)}, u32[]{:S(2)}) copy-start(f32[128,2048]{1,0:T(8,128)} %fusion.18) | copy-start | bytes 3145732
Sparse Core Ops, SparseCore 0:
  34.8 46.2 all-gather.4
  83.0 66.4 all-gather.2
